TPU v7x, 32 devices: a whole 2x2x4 slice. The times are simulated.
32 devices in a mesh: row: 4 (over y, core), col: 8 (over z, x).
Axes of the slice: x: 2, y: 2, z: 4, core: 2. Of those that a mesh axis runs over, the one named last changes fastest.
Arguments:
- node_feats: bfloat16 [8192, 256], P(('row', 'col')), may hold values from -6 to 6
- weight: bfloat16 [256, 256], replicated, may hold values from -0.375 to 0.375
- cotangent: bfloat16 [8192, 256], P(('row', 'col')), may hold values from -6 to 6
- band_tiles: bfloat16 [384, 128, 128], P(('row', 'col')), may hold values from 0 to 0.049804688
- band_coords: int32 [384, 2], P(('row', 'col')), may hold values from 0 to 5, as said below
- bound_tiles: bfloat16 [1280, 128, 128], P(('row', 'col')), may hold values from 0 to 0.049804688
- bound_coords: int32 [1280, 2], P(('row', 'col')), may hold values from 0 to 7, as said below
- bound_count: int32 [32], P(('row', 'col')), may hold values from 0 to 40, as said below
- recv_lists: int32 [32, 8], P(('row', 'col')), may hold values from -1 to 1, as said below
- send_lists: int32 [32, 8], P(('row', 'col')), may hold values from -1 to 1, as said below
- reorder: int32 [32, 256], P(('row', 'col')), may hold values from 0 to 255, each once within a row
Outputs:
- node_out: bfloat16 [8192, 256], P(('row', 'col'))
- feat_grad: bfloat16 [8192, 256], P(('row', 'col'))
- weight_grad: float32 [256, 256], replicated
Inputs may be any that keep to these rules, and one draw needn't show every extreme that they name: recv_lists[r * 8 + c, s] is a row block of device r * 8 + s, below 2, or -1 for none; it is -1 where s = c. In every row group one device receives a block from every other column. send_lists[r * 8 + s, c] equals recv_lists[r * 8 + c, s]. bound_count[d] is at least the number of entries of recv_lists[d] that are not -1; in every row group one device has all 40 slots live. `bound_coords`: pairs (row block below 2, owner column below 8); for k < bound_count[d] the owner column s of slot k has recv_lists[d, s] >= 0, and every such column is named by one of them; slots from bound_count[d] on are not used. `band_coords`: pairs (row block below 2, extended column block below (768) / 128); no pair twice on one device. `reorder`: each row is a permutation.
All inputs are finite; a program needn't handle non-finite values.
Results may differ from a plain program's by a relative error of at most 0.0095.
Values may be sent and summed in bfloat16 or wider, within the bound.
No kernel may reach another device: no remote copies, remote signals or barrier semaphores. Data moves between devices by JAX's collectives and lax.ppermute only.
A program may use at most 64 MiB of HBM per device.

v0:
```python
import jax
import jax.numpy as jnp
from jax import lax
from jax.sharding import PartitionSpec as P

BW = 256


def padded_2(cells, sides, width):
    for axis, dim in sides:
        count = lax.axis_size(axis)
        head = lax.slice_in_dim(cells, 0, width, axis=dim)
        tail = lax.slice_in_dim(cells, cells.shape[dim] - width, cells.shape[dim], axis=dim)
        cells = jnp.concatenate(
            [
                lax.ppermute(tail, axis, [(i, (i + 1) % count) for i in range(count)]),
                cells,
                lax.ppermute(head, axis, [((i + 1) % count, i) for i in range(count)]),
            ],
            axis=dim,
        )
    return cells


def split_sum(selector, terms):
    high_part = terms.astype(jnp.bfloat16)
    low_part = (terms - high_part.astype(jnp.float32)).astype(jnp.bfloat16)
    pick = selector.astype(jnp.bfloat16)
    upper_sum = jnp.einsum("rk,kaf->raf", pick, high_part, preferred_element_type=jnp.float32)
    lower_sum = jnp.einsum("rk,kaf->raf", pick, low_part, preferred_element_type=jnp.float32)
    return upper_sum + lower_sum


def on_device(
    node_feats,
    weight,
    cotangent,
    band_tiles,
    band_coords,
    bound_tiles,
    bound_coords,
    bound_count,
    recv_lists,
    send_lists,
    reorder,
):
    tile_size = band_tiles.shape[1]
    row_count = node_feats.shape[0]
    width_feat = node_feats.shape[1]
    tile_rows = row_count // tile_size
    rim_tiles = BW // tile_size
    col_tiles = tile_rows + 2 * rim_tiles
    ext_count = row_count + 2 * BW
    peers = lax.axis_size("col")
    slot_total = bound_tiles.shape[0]
    order = reorder[0]
    inverse = (
        jnp.zeros((row_count,), jnp.int32).at[order].set(jnp.arange(row_count, dtype=jnp.int32))
    )
    x_band = jnp.take(node_feats, order, axis=0)
    hidden = jnp.dot(x_band, weight, preferred_element_type=jnp.float32).astype(jnp.bfloat16)
    band_row_ids = band_coords[:, 0]
    band_col_ids = band_coords[:, 1]
    band_dense = jnp.zeros((tile_rows, tile_size, col_tiles, tile_size), jnp.bfloat16)
    band_dense = (
        band_dense.at[band_row_ids, :, band_col_ids].set(band_tiles).reshape(row_count, ext_count)
    )
    extended = padded_2(hidden, (("row", 0),), BW)
    mixed = jnp.dot(band_dense, extended, preferred_element_type=jnp.float32)
    blocks = hidden.reshape(tile_rows, tile_size, width_feat)
    giving = send_lists[0]
    outgoing = jnp.where(
        (giving >= 0)[:, None, None],
        jnp.take(blocks, jnp.maximum(giving, 0), axis=0),
        jnp.zeros((), jnp.bfloat16),
    )
    arrived = lax.all_to_all(outgoing, "col", split_axis=0, concat_axis=0, tiled=True)
    tile_range = jnp.arange(tile_rows, dtype=jnp.int32)
    live_slots = jnp.arange(slot_total, dtype=jnp.int32) < bound_count[0]
    bound_row_ids = bound_coords[:, 0]
    bound_owner = bound_coords[:, 1]
    bound_onehot = (bound_row_ids[None, :] == tile_range[:, None]) & live_slots[None, :]
    slot_rows = jnp.take(arrived, bound_owner, axis=0).reshape(slot_total * tile_size, width_feat)
    placed = jnp.einsum(
        "rk,kab->rakb",
        bound_onehot.astype(jnp.bfloat16),
        bound_tiles,
        preferred_element_type=jnp.bfloat16,
    )
    placed = placed.reshape(row_count, slot_total * tile_size)
    mixed = mixed + jnp.dot(placed, slot_rows, preferred_element_type=jnp.float32)
    out_band = jax.nn.silu(mixed).astype(jnp.bfloat16)
    node_out = jnp.take(out_band, inverse, axis=0)
    grad_band = jnp.take(cotangent, order, axis=0).astype(jnp.float32)
    sigma = jax.nn.sigmoid(mixed)
    slope = (grad_band * sigma * (1.0 + mixed * (1.0 - sigma))).astype(jnp.bfloat16)
    slope_blocks = slope.reshape(tile_rows, tile_size, width_feat)
    ext_grad = lax.dot_general(
        band_dense, slope, (((0,), (0,)), ((), ())), preferred_element_type=jnp.float32
    )
    rim_terms = jnp.concatenate([ext_grad[:BW], ext_grad[BW + row_count :]], axis=0).astype(
        jnp.bfloat16
    )
    padded = padded_2(rim_terms, (("row", 0),), BW)
    grad_hidden = ext_grad[BW : BW + row_count]
    grad_hidden = grad_hidden.at[:BW].add(padded[:BW].astype(jnp.float32))
    grad_hidden = grad_hidden.at[row_count - BW :].add(padded[3 * BW :].astype(jnp.float32))
    slot_back = jnp.einsum(
        "kab,kaf->kbf",
        bound_tiles,
        jnp.take(slope_blocks, bound_row_ids, axis=0),
        preferred_element_type=jnp.float32,
    )
    owner_range = jnp.arange(peers, dtype=jnp.int32)
    owner_onehot = (bound_owner[None, :] == owner_range[:, None]) & live_slots[None, :]
    to_owner = split_sum(owner_onehot, slot_back).astype(jnp.bfloat16)
    returned = lax.all_to_all(to_owner, "col", split_axis=0, concat_axis=0, tiled=True)
    block_onehot = (giving[None, :] == tile_range[:, None]).astype(jnp.bfloat16)
    from_peers = jnp.einsum(
        "bs,saf->baf", block_onehot, returned, preferred_element_type=jnp.float32
    )
    grad_hidden = grad_hidden + from_peers.reshape(row_count, width_feat)
    grad_round = grad_hidden.astype(jnp.bfloat16)
    partial_weight = lax.dot_general(
        x_band, grad_round, (((0,), (0,)), ((), ())), preferred_element_type=jnp.float32
    )
    nodes_all = row_count * lax.axis_size("row") * peers
    weight_grad = lax.psum(partial_weight, ("row", "col")) * nodes_all ** (-0.5)
    feat_band = lax.dot_general(
        grad_round, weight, (((1,), (1,)), ((), ())), preferred_element_type=jnp.float32
    ).astype(jnp.bfloat16)
    feat_grad = jnp.take(feat_band, inverse, axis=0)
    return (node_out, feat_grad, weight_grad)


def solution(mesh):
    in_specs = (
        P(("row", "col"), None),
        P(),
        P(("row", "col"), None),
        P(("row", "col"), None, None),
        P(("row", "col"), None),
        P(("row", "col"), None, None),
        P(("row", "col"), None),
        P(("row", "col")),
        P(("row", "col"), None),
        P(("row", "col"), None),
        P(("row", "col"), None),
    )
    out_specs = (P(("row", "col"), None), P(("row", "col"), None), P())
    return jax.shard_map(
        on_device, mesh=mesh, in_specs=in_specs, out_specs=out_specs, check_vma=False
    )
```

profile of v0, /device:TPU:0, one launch (start us, length us, event | category | flops | bytes accessed | tf_op | source)
XLA Modules:
  0.0 214.7 jit_solution(14946147041477789685)
XLA Ops:
  7.2 0.8 compare_select_fusion.2
  8.0 0.7 compare_and_fusion.1
  8.7 1.9 gather_fusion.3
  10.6 0.2 convolution_convert_fusion.1
  10.9 0.5 collective-permute-start
  11.4 2.0 collective-permute-start.1
  13.4 0.7 maximum_bitcast_fusion
  14.0 0.7 broadcast_compare_fusion
  14.7 0.6 gather_fusion
  15.3 0.9 select_select_fusion
  16.3 6.5 %all-to-all-start = ((bf16[8,128,256]{2,1,0:T(8,128)(2,1)}), bf16[8,128,256]{2,1,0:T(8,128)(2,1)S(1)}, u32[]{:S(2)}, u32[]{:S(2)}) async-start(bf16[8,128,256]{2,1,0:T(8,128)(2,1)} %select_select_fusion), calls=%async_computation | async-start | bytes 1048576 | tf_op jit(solution)/shard_map/all_to_all | solution.py:77
  22.8 0.6 compare_select_fusion
  23.4 0.6 slice_bitcast_fusion
  24.6 0.6 iota_compare_fusion.1
  25.2 0.8 copy.20
  26.1 1.8 gather_fusion.5
  27.9 0.1 broadcast_in_dim.61
  28.0 2.0 scatter_fusion
  30.1 1.1 copy.19
  31.2 2.1 scatter_custom_fusion.1
  33.3 0.5 and_bitcast_fusion
  33.8 1.7 broadcast_multiply_fusion
  35.6 1.8 all-to-all-done
  37.3 0.7 gather_fusion.1
  38.1 0.3 broadcast_select_fusion
  38.4 1.4 copy-done.4
  39.8 0.8 fusion.1
  40.7 0.1 copy-done.5
  40.8 1.3 multiply_convert_fusion
  42.2 2.4 %gather_fusion.2 = bf16[40,128,256]{2,1,0:T(8,128)(2,1)} fusion(bf16[2,128,256]{2,1,0:T(8,128)(2,1)S(1)} %bitcast.73, s32[1024]{0:T(1024)S(1)} %pad_clamp_fusion), kind=kCustom, calls=%fused_computation.6 | custom fusion | bytes 5243040 | tf_op jit(solution)/shard_map/jit(_take)/gather | solution.py:111
  44.6 4.9 %fusion = (bf16[40,128,256]{1,2,0:T(8,128)(2,1)S(1)}, bf16[40,128,256]{1,2,0:T(8,128)(2,1)}) fusion(bf16[40,128,128]{2,1,0:T(8,128)(2,1)} %param.26, bf16[40,128,256]{2,1,0:T(8,128)(2,1)} %gather_fusion.2, pred[40]{0:T(512)(128)(4,1)S(1)} %copy-done.16), kind=kOutput, calls=%fused_computation.11 | convolution fusion | flops 342097920 | bytes 9175080 | tf_op jit(solution)/shard_map/kab,kaf->kbf/dot_general | solution.py:108
  49.5 4.7 %copy.22 = bf16[40,128,256]{2,0,1:T(8,128)(2,1)} copy(bf16[40,128,256]{1,2,0:T(8,128)(2,1)} %get-tuple-element.45) | data formatting | bytes 5242880 | tf_op jit(solution)/shard_map/convert_element_type | solution.py:26
  54.2 3.4 %copy.23 = bf16[40,128,256]{2,0,1:T(8,128)(2,1)} copy(bf16[40,128,256]{1,2,0:T(8,128)(2,1)S(1)} %get-tuple-element.44) | data formatting | bytes 5242880 | tf_op jit(solution)/shard_map/convert_element_type | solution.py:27
  57.6 2.5 %fusion.28 = f32[8,128,256]{2,0,1:T(8,128)S(1)} fusion(bf16[40,128,256]{2,0,1:T(8,128)(2,1)} %copy.22, s32[40]{0:T(128)S(1)} %get-tuple-element.50, pred[40]{0:T(512)(128)(4,1)S(1)} %copy-done.15), kind=kOutput, calls=%fused_computation.62 | convolution fusion | flops 20972160 | bytes 3670216 | tf_op jit(solution)/shard_map/rk,kaf->raf/dot_general | solution.py:29
  60.1 0.6 fusion.8
  60.7 0.9 copy.24
  61.6 4.2 %all-to-all-start.1 = ((bf16[8,128,256]{2,1,0:T(8,128)(2,1)}), bf16[8,128,256]{2,1,0:T(8,128)(2,1)S(1)}, u32[]{:S(2)}, u32[]{:S(2)}) async-start(bf16[8,128,256]{2,1,0:T(8,128)(2,1)} %copy.24), calls=%async_computation.1 | async-start | bytes 1048576 | tf_op jit(solution)/shard_map/all_to_all | solution.py:117
  65.9 0.3 fusion.50
  66.3 1.7 collective-permute-start.3
  68.0 1.1 gather_fusion.4
  69.2 10.8 %all-to-all-done.1 = bf16[8,128,256]{2,1,0:T(8,128)(2,1)S(1)} async-done(((bf16[8,128,256]{2,1,0:T(8,128)(2,1)}), bf16[8,128,256]{2,1,0:T(8,128)(2,1)S(1)}, u32[]{:S(2)}, u32[]{:S(2)}) %all-to-all-start.1) | async-done | bytes 524320 | tf_op jit(solution)/shard_map/all_to_all | solution.py:117
  79.9 0.4 fusion.9
  80.4 0.2 convolution_convert_fusion
  80.7 1.0 fusion.24
  81.7 1.1 gather_fusion.6
  82.9 0.8 broadcast_select_fusion.1
  83.7 122.5 %all-reduce.2.cloned.1.call-done = f32[256,256]{1,0:T(8,128)} async-done(((f32[256,256]{1,0:T(8,128)}), f32[256,256]{1,0:T(8,128)}) %all-reduce.2.cloned.1.call-update) | async-done | bytes 262160 | tf_op jit(solution)/shard_map/psum | solution.py:128
  206.1 1.7 broadcast_multiply_fusion.1
  (62 shorter events, 0.5 us)
Async XLA Ops:
  7.2 3.4 %copy-start = (bf16[256,256]{1,0:T(8,128)(2,1)S(1)}, bf16[256,256]{1,0:T(8,128)(2,1)}, u32[]{:S(2)}) copy-start(bf16[256,256]{1,0:T(8,128)(2,1)} %param.22) | copy-start | bytes 393220
  7.2 15.6 %copy-start.11 = (s32[1,256]{1,0:T(1,128)S(1)}, s32[1,256]{1,0:T(1,128)}, u32[]{:S(2)}) copy-start(s32[1,256]{1,0:T(1,128)} %param.30) | copy-start | bytes 3076
  7.2 16.2 %copy-start.9 = (s32[40,2]{0,1:T(2,128)S(1)}, s32[40,2]{0,1:T(2,128)}, u32[]{:S(2)}) copy-start(s32[40,2]{0,1:T(2,128)} %param.27) | copy-start | bytes 964
  7.2 17.4 %copy-start.21 = (s32[12,2]{0,1:T(2,128)S(1)}, s32[12,2]{0,1:T(2,128)}, u32[]{:S(2)}) copy-start(s32[12,2]{0,1:T(2,128)} %param.25) | copy-start | bytes 292
  7.2 18.0 %copy-start.3 = (bf16[40,128,128]{2,1,0:T(8,128)(2,1)S(1)}, bf16[40,128,128]{2,1,0:T(8,128)(2,1)}, u32[]{:S(2)}) copy-start(bf16[40,128,128]{2,1,0:T(8,128)(2,1)} %param.26) | copy-start | bytes 3932164
  8.7 5.3 %copy-start.12 = (pred[256]{0:T(512)(128)(4,1)}, pred[256]{0:T(512)(128)(4,1)S(1)}, u32[]{:S(2)}) copy-start(pred[256]{0:T(512)(128)(4,1)S(1)} %compare_and_fusion.1) | copy-start | bytes 772
  10.6 4.1 %copy-start.6 = (bf16[256,256]{1,0:T(8,128)(2,1)}, bf16[256,256]{1,0:T(8,128)(2,1)S(1)}, u32[]{:S(2)}) copy-start(bf16[256,256]{1,0:T(8,128)(2,1)S(1)} %gather_fusion.3) | copy-start | bytes 393220
  10.9 29.8 %collective-permute-start = (bf16[256,256]{1,0:T(8,128)(2,1)S(1)}, bf16[256,256]{1,0:T(8,128)(2,1)}, u32[]{:S(2)}, u32[]{:S(2)}) collective-permute-start(bf16[256,256]{1,0:T(8,128)(2,1)S(1)} %convolution_convert_fusion.1), channel_id=1, source_target_pairs={{0,8},{8,16},{16,24},{24,0},{1,9},{9,17},{17,25},{25,1},{2,10},{10... | collective-permute-start | bytes 393224 | tf_op jit(solution)/shard_map/ppermute | solution.py:16
  11.4 29.3 %collective-permute-start.1 = (bf16[256,256]{1,0:T(8,128)(2,1)S(1)}, bf16[256,256]{1,0:T(8,128)(2,1)}, u32[]{:S(2)}, u32[]{:S(2)}) collective-permute-start(bf16[256,256]{1,0:T(8,128)(2,1)S(1)} %convolution_convert_fusion.1), channel_id=1, source_target_pairs={{8,0},{16,8},{24,16},{0,24},{9,1},{17,9},{25,17},{1,25},{10,2},{18... | collective-permute-start | bytes 393224 | tf_op jit(solution)/shard_map/ppermute | solution.py:18
  15.3 10.8 %copy-start.2 = (bf16[256,256]{1,0:T(8,128)(2,1)S(1)}, bf16[256,256]{1,0:T(8,128)(2,1)}, u32[]{:S(2)}) copy-start(bf16[256,256]{1,0:T(8,128)(2,1)} %param.23) | copy-start | bytes 393220
  16.3 21.1 %all-to-all-start = ((bf16[8,128,256]{2,1,0:T(8,128)(2,1)}), bf16[8,128,256]{2,1,0:T(8,128)(2,1)S(1)}, u32[]{:S(2)}, u32[]{:S(2)}) async-start(bf16[8,128,256]{2,1,0:T(8,128)(2,1)} %select_select_fusion), calls=%async_computation | async-start | bytes 1048576 | tf_op jit(solution)/shard_map/all_to_all | solution.py:77
  26.1 7.2 %copy-start.17 = (s32[40]{0:T(128)S(1)}, s32[40]{0:T(128)}, u32[]{:S(2)}) copy-start(s32[40]{0:T(128)} %get-tuple-element.51) | copy-start | bytes 484
  26.1 7.2 %copy-start.14 = (pred[40]{0:T(512)(128)(4,1)S(1)}, pred[40]{0:T(512)(128)(4,1)}, u32[]{:S(2)}) copy-start(pred[40]{0:T(512)(128)(4,1)} %iota_compare_fusion.1) | copy-start | bytes 124
  26.1 7.2 %copy-start.19 = (s32[40]{0:T(128)S(1)}, s32[40]{0:T(128)}, u32[]{:S(2)}) copy-start(s32[40]{0:T(128)} %get-tuple-element.53) | copy-start | bytes 484
  26.1 7.2 %copy-start.10 = (s32[40,2]{0,1:T(2,128)S(1)}, s32[40,2]{0,1:T(2,128)}, u32[]{:S(2)}) copy-start(s32[40,2]{0,1:T(2,128)} %param.27) | copy-start | bytes 964
  38.1 1.7 copy-start.4
  39.8 1.0 copy-start.5
  39.8 1.0 copy-start.8
  39.8 1.0 copy-start.13
  42.2 2.4 %copy-start.16 = (pred[40]{0:T(512)(128)(4,1)S(1)}, pred[40]{0:T(512)(128)(4,1)}, u32[]{:S(2)}) copy-start(pred[40]{0:T(512)(128)(4,1)} %get-tuple-element.54) | copy-start | bytes 124
  54.2 3.4 %copy-start.15 = (pred[40]{0:T(512)(128)(4,1)S(1)}, pred[40]{0:T(512)(128)(4,1)}, u32[]{:S(2)}) copy-start(pred[40]{0:T(512)(128)(4,1)} %iota_compare_fusion.1) | copy-start | bytes 124
  57.6 2.5 %copy-start.1 = (bf16[40,128,256]{2,0,1:T(8,128)(2,1)S(1)}, bf16[40,128,256]{2,0,1:T(8,128)(2,1)}, u32[]{:S(2)}) copy-start(bf16[40,128,256]{2,0,1:T(8,128)(2,1)} %copy.23) | copy-start | bytes 7864324
  60.1 5.8 %copy-start.18 = (s32[256]{0:T(256)S(1)}, s32[256]{0:T(256)}, u32[]{:S(2)}) copy-start(s32[256]{0:T(256)} %scatter_custom_fusion.1) | copy-start | bytes 3076
  60.7 19.3 %copy-start.20 = (s32[1,8]{1,0:T(1,128)S(1)}, s32[1,8]{1,0:T(1,128)}, u32[]{:S(2)}) copy-start(s32[1,8]{1,0:T(1,128)} %param.29) | copy-start | bytes 100
  61.6 18.4 %all-to-all-start.1 = ((bf16[8,128,256]{2,1,0:T(8,128)(2,1)}), bf16[8,128,256]{2,1,0:T(8,128)(2,1)S(1)}, u32[]{:S(2)}, u32[]{:S(2)}) async-start(bf16[8,128,256]{2,1,0:T(8,128)(2,1)} %copy.24), calls=%async_computation.1 | async-start | bytes 1048576 | tf_op jit(solution)/shard_map/all_to_all | solution.py:117
  65.8 140.3 %all-reduce.2.cloned.1.call-start = ((), (), s32[]{:S(2)}) async-start(), calls=%async_computation.2 | async-start | bytes 524288 | tf_op jit(solution)/shard_map/psum | solution.py:128
  65.9 14.8 %copy-start.7 = (bf16[256,256]{1,0:T(8,128)(2,1)S(1)}, bf16[256,256]{1,0:T(8,128)(2,1)}, u32[]{:S(2)}) copy-start(bf16[256,256]{1,0:T(8,128)(2,1)} %copy-done.6) | copy-start | bytes 393220
  66.2 14.1 %collective-permute-start.2 = (bf16[256,256]{1,0:T(8,128)(2,1)S(1)}, bf16[256,256]{1,0:T(8,128)(2,1)S(1)}, u32[]{:S(2)}, u32[]{:S(2)}) collective-permute-start(bf16[256,256]{1,0:T(8,128)(2,1)S(1)} %get-tuple-element.46), channel_id=1, source_target_pairs={{0,8},{8,16},{16,24},{24,0},{1,9},{9,17},{17,25},{25,1},{2,10},{10... | collective-permute-start | bytes 393224 | tf_op jit(solution)/shard_map/ppermute | solution.py:16
  66.3 14.1 %collective-permute-start.3 = (bf16[256,256]{1,0:T(8,128)(2,1)S(1)}, bf16[256,256]{1,0:T(8,128)(2,1)S(1)}, u32[]{:S(2)}, u32[]{:S(2)}) collective-permute-start(bf16[256,256]{1,0:T(8,128)(2,1)S(1)} %get-tuple-element.47), channel_id=1, source_target_pairs={{8,0},{16,8},{24,16},{0,24},{9,1},{17,9},{25,17},{1,25},{10,2},{18... | collective-permute-start | bytes 393224 | tf_op jit(solution)/shard_map/ppermute | solution.py:18
Sparse Core Ops, SparseCore 0:
  83.0 123.1 all-reduce.1
where the time goes:
time: 215 us
  waiting for transfers between devices  135 us (63%)
  local copies, waits for them, and re-layouts  26.5 us (12%)
  starting transfers between devices  15.1 us (7%)
  between operations  15.1 us (7%)
  matrix products  12.3 us (6%)
  other arithmetic  10.6 us (5%)
    psum x1, waiting for transfers between devices, on_device(): weight_grad = lax.psum(partial_weight, ('row', 'col')) * nodes_all ** (-0.5)  122 us
    all_to_all x1, waiting for transfers between devices, on_device(): lax.all_to_all(to_owner, 'col', split_axis=0, concat_axis=0, tiled=True)  10.8 us
    all_to_all x1, starting transfers between devices, on_device(): lax.all_to_all(outgoing, 'col', split_axis=0, concat_axis=0, tiled=True)  6.53 us
    dot_general x1, matrix products, on_device(): jnp.einsum('kab,kaf->kbf', bound_tiles, jnp.take(slope_blocks, bound_row_...  4.94 us
    convert_element_type x1, local copies, waits for them, and re-layouts, split_sum(): high_part = terms.astype(jnp.bfloat16)  4.69 us
  transfers between devices with their start and end apart: 7, of which 3 were waited for; matrix products, arithmetic and copies ran while one was open for 9% of the time, Pallas kernels for 0%

commit v1 on v0

--- a/solution.py
+++ b/solution.py
@@ -29,6 +29,15 @@
     upper_sum = jnp.einsum("rk,kaf->raf", pick, high_part, preferred_element_type=jnp.float32)
     lower_sum = jnp.einsum("rk,kaf->raf", pick, low_part, preferred_element_type=jnp.float32)
     return upper_sum + lower_sum
+
+
+def spread_sum(value, axes):
+    count = lax.axis_size(axes)
+    pieces = value.reshape(count, value.size // count)
+    gathered = lax.all_to_all(pieces, axes, 0, 0, tiled=True)
+    owned = jnp.sum(gathered.reshape(count, 1, value.size // count), axis=0)
+    copies = jnp.broadcast_to(owned, (count, value.size // count))
+    return lax.all_to_all(copies, axes, 0, 0, tiled=True).reshape(value.shape)
 
 
 def on_device(
@@ -125,7 +134,7 @@
         x_band, grad_round, (((0,), (0,)), ((), ())), preferred_element_type=jnp.float32
     )
     nodes_all = row_count * lax.axis_size("row") * peers
-    weight_grad = lax.psum(partial_weight, ("row", "col")) * nodes_all ** (-0.5)
+    weight_grad = spread_sum(partial_weight, ("row", "col")) * nodes_all ** (-0.5)
     feat_band = lax.dot_general(
         grad_round, weight, (((1,), (1,)), ((), ())), preferred_element_type=jnp.float32
     ).astype(jnp.bfloat16)

time: 215 us -> 105 us (0.49)
  waiting for transfers between devices: 135 us -> 33.5 us
  between operations: 15.1 us -> 1.72 us
  starting transfers between devices: 15.1 us -> 20.1 us
    psum x1 -> x0, waiting for transfers between devices: 122 us -> none  [on_device(): weight_grad = lax.psum(partial_weight, ('row', 'col')) * nodes_all ** (-0.5)]
    all_to_all x0 -> x2, waiting for transfers between devices: none -> 16.5 us  [the longest x1 9.19 us: spread_sum(): gathered = lax.all_to_all(pieces, axes, 0, 0, tiled=True)]
    all_to_all x0 -> x2, starting transfers between devices: none -> 5.49 us  [the longest x1 2.77 us: spread_sum(): return lax.all_to_all(copies, axes, 0, 0, tiled=True).reshape(value.shape)]
    all_to_all x1, waiting for transfers between devices: 1.76 us -> 4.44 us  [on_device(): lax.all_to_all(outgoing, 'col', split_axis=0, concat_axis=0, tiled=True)]
  transfers between devices with their start and end apart: 7 -> 8, of which waited for: 3 -> 4; matrix products, arithmetic and copies ran while one was open for 9% -> 19% of each run, Pallas kernels for 0% -> 0%
where the time goes in v1:
time: 105 us
  waiting for transfers between devices  33.5 us (32%)
  local copies, waits for them, and re-layouts  28.5 us (27%)
  starting transfers between devices  20.1 us (19%)
  matrix products  11.6 us (11%)
  other arithmetic  9.32 us (9%)
  between operations  1.72 us (2%)
    all_to_all x1, waiting for transfers between devices, on_device(): lax.all_to_all(to_owner, 'col', split_axis=0, concat_axis=0, tiled=True)  12.6 us
    all_to_all x1, waiting for transfers between devices, spread_sum(): gathered = lax.all_to_all(pieces, axes, 0, 0, tiled=True)  9.19 us
    all_to_all x1, waiting for transfers between devices, spread_sum(): return lax.all_to_all(copies, axes, 0, 0, tiled=True).reshape(value.shape)  7.3 us
    all_to_all x1, starting transfers between devices, on_device(): lax.all_to_all(outgoing, 'col', split_axis=0, concat_axis=0, tiled=True)  6.53 us
    dot_general x1, matrix products, on_device(): jnp.einsum('kab,kaf->kbf', bound_tiles, jnp.take(slope_blocks, bound_row_...  4.94 us
    convert_element_type x1, local copies, waits for them, and re-layouts, split_sum(): high_part = terms.astype(jnp.bfloat16)  4.76 us
    all_to_all x1, waiting for transfers between devices, on_device(): lax.all_to_all(outgoing, 'col', split_axis=0, concat_axis=0, tiled=True)  4.44 us
    all_to_all x1, starting transfers between devices, on_device(): lax.all_to_all(to_owner, 'col', split_axis=0, concat_axis=0, tiled=True)  3.77 us
  transfers between devices with their start and end apart: 8, of which 4 were waited for; matrix products, arithmetic and copies ran while one was open for 19% of the time, Pallas kernels for 0%

profile of v1, /device:TPU:0, one launch (start us, length us, event | category | flops | bytes accessed | tf_op | source)
XLA Modules:
  0.0 104.7 jit_solution(282931697207215189)
XLA Ops:
  0.7 0.8 compare_select_fusion.2
  1.5 0.7 compare_and_fusion.1
  2.2 1.9 %gather_fusion.3 = bf16[256,256]{1,0:T(8,128)(2,1)S(1)} fusion(bf16[256,256]{1,0:T(8,128)(2,1)} %param.21, s32[1024]{0:T(1024)S(1)} %pad_clamp_fusion.4), kind=kCustom, calls=%fused_computation.clone | custom fusion | bytes 263168 | tf_op jit(solution)/shard_map/jit(_take)/gather | solution.py:69
  4.3 0.5 collective-permute-start
  4.8 2.0 %collective-permute-start.1 = (bf16[256,256]{1,0:T(8,128)(2,1)S(1)}, bf16[256,256]{1,0:T(8,128)(2,1)}, u32[]{:S(2)}, u32[]{:S(2)}) collective-permute-start(bf16[256,256]{1,0:T(8,128)(2,1)S(1)} %convolution_convert_fusion.1), channel_id=1, source_target_pairs={{8,0},{16,8},{24,16},{0,24},{9,1},{17,9},{25,17},{1,25},{10,2},{18... | collective-permute-start | bytes 393224 | tf_op jit(solution)/shard_map/ppermute | solution.py:18
  6.8 0.7 maximum_bitcast_fusion
  7.5 0.7 broadcast_compare_fusion
  8.2 0.6 gather_fusion
  8.8 0.9 select_select_fusion
  9.7 6.5 %all-to-all-start = ((bf16[8,128,256]{2,1,0:T(8,128)(2,1)}), bf16[8,128,256]{2,1,0:T(8,128)(2,1)S(1)}, u32[]{:S(2)}, u32[]{:S(2)}) async-start(bf16[8,128,256]{2,1,0:T(8,128)(2,1)} %select_select_fusion), calls=%async_computation | async-start | bytes 1048576 | tf_op jit(solution)/shard_map/all_to_all | solution.py:86
  16.2 0.6 slice_bitcast_fusion
  17.5 0.6 iota_compare_fusion.1
  18.1 0.8 copy.20
  19.0 1.8 %gather_fusion.5 = bf16[256,256]{1,0:T(8,128)(2,1)} fusion(bf16[256,256]{1,0:T(8,128)(2,1)S(1)} %copy-done.2, s32[1024]{0:T(1024)S(1)} %pad_clamp_fusion.4), kind=kCustom, calls=%fused_computation.2.clone | custom fusion | bytes 263168 | tf_op jit(solution)/shard_map/jit(_take)/gather | solution.py:103
  20.9 2.0 %scatter_fusion = bf16[2,128,6,128]{3,1,2,0:T(8,128)(2,1)S(1)} fusion(bf16[2,128,6,128]{3,1,2,0:T(8,128)(2,1)S(1)} %broadcast_in_dim.66, s32[12]{0:T(128)S(1)} %fusion.42, bf16[12,128,128]{2,1,0:T(8,128)(2,1)} %param.24), kind=kCustom, calls=%fused_computation.7 | custom fusion | bytes 1179744 | tf_op jit(solution)/shard_map/scatter | solution.py:75
  22.9 1.1 %copy.19 = bf16[2,128,6,128]{1,0,3,2:T(2,128)(2,1)} copy(bf16[2,128,6,128]{3,1,2,0:T(8,128)(2,1)S(1)} %scatter_fusion) | data formatting | bytes 786432 | tf_op jit(solution)/shard_map/scatter | solution.py:75
  24.0 0.5 and_bitcast_fusion
  24.6 1.8 %broadcast_multiply_fusion = bf16[40,2,128,128]{3,0,2,1:T(8,128)(2,1)} fusion(bf16[40,128,128]{2,0,1:T(8,128)(2,1)S(1)} %copy.20, bf16[40,2]{0,1:T(2,128)(2,1)S(1)} %fusion.38), kind=kLoop, calls=%fused_computation.21 | loop fusion | flops 1310720 | bytes 3932320 | tf_op jit(solution)/shard_map/rk,kab->rakb/dot_general | solution.py:93
  26.4 4.4 %all-to-all-done = bf16[8,128,256]{2,1,0:T(8,128)(2,1)S(1)} async-done(((bf16[8,128,256]{2,1,0:T(8,128)(2,1)}), bf16[8,128,256]{2,1,0:T(8,128)(2,1)S(1)}, u32[]{:S(2)}, u32[]{:S(2)}) %all-to-all-start) | async-done | bytes 524320 | tf_op jit(solution)/shard_map/all_to_all | solution.py:86
  30.8 0.7 gather_fusion.1
  31.5 0.3 broadcast_select_fusion
  31.8 1.4 %copy-done.4 = bf16[40,2,128,128]{3,0,2,1:T(8,128)(2,1)S(1)} copy-done((bf16[40,2,128,128]{3,0,2,1:T(8,128)(2,1)S(1)}, bf16[40,2,128,128]{3,0,2,1:T(8,128)(2,1)}, u32[]{:S(2)}) %copy-start.4) | copy-done | bytes 2621464
  33.3 0.8 fusion.1
  34.3 1.3 %multiply_convert_fusion = (bf16[256,256]{1,0:T(8,128)(2,1)S(1)}, bf16[256,256]{1,0:T(8,128)(2,1)S(1)}) fusion(bf16[256,256]{1,0:T(8,128)(2,1)S(1)} %copy-done.8, pred[256]{0:T(512)(128)(4,1)S(1)} %copy-done.13, f32[256,256]{1,0:T(8,128)S(1)} %fusion.1, bf16[256,256]{1,0:T(8,128)(2,1)} %collective-permute-done.1, ...), kind=kOutput, calls=%fused_computation.44 | convolution fusion | flops 102760448 | bytes 1442048 | tf_op jit(solution)/shard_map/dot_general | solution.py:78
  35.6 2.4 %gather_fusion.2 = bf16[40,128,256]{2,1,0:T(8,128)(2,1)} fusion(bf16[2,128,256]{2,1,0:T(8,128)(2,1)S(1)} %bitcast.73, s32[1024]{0:T(1024)S(1)} %pad_clamp_fusion), kind=kCustom, calls=%fused_computation.6 | custom fusion | bytes 5243040 | tf_op jit(solution)/shard_map/jit(_take)/gather | solution.py:120
  38.0 4.9 %fusion = (bf16[40,128,256]{1,2,0:T(8,128)(2,1)S(1)}, bf16[40,128,256]{1,2,0:T(8,128)(2,1)}) fusion(bf16[40,128,128]{2,1,0:T(8,128)(2,1)} %param.26, bf16[40,128,256]{2,1,0:T(8,128)(2,1)} %gather_fusion.2, pred[40]{0:T(512)(128)(4,1)S(1)} %copy-done.16), kind=kOutput, calls=%fused_computation.11 | convolution fusion | flops 342097920 | bytes 9175080 | tf_op jit(solution)/shard_map/kab,kaf->kbf/dot_general | solution.py:117
  43.0 4.8 %copy.22 = bf16[40,128,256]{2,0,1:T(8,128)(2,1)} copy(bf16[40,128,256]{1,2,0:T(8,128)(2,1)} %get-tuple-element.45) | data formatting | bytes 5242880 | tf_op jit(solution)/shard_map/convert_element_type | solution.py:26
  47.7 3.4 %copy.23 = bf16[40,128,256]{2,0,1:T(8,128)(2,1)} copy(bf16[40,128,256]{1,2,0:T(8,128)(2,1)S(1)} %get-tuple-element.44) | data formatting | bytes 5242880 | tf_op jit(solution)/shard_map/convert_element_type | solution.py:27
  51.1 2.5 %fusion.28 = f32[8,128,256]{2,0,1:T(8,128)S(1)} fusion(bf16[40,128,256]{2,0,1:T(8,128)(2,1)} %copy.22, s32[40]{0:T(128)S(1)} %get-tuple-element.50, pred[40]{0:T(512)(128)(4,1)S(1)} %copy-done.15), kind=kOutput, calls=%fused_computation.62 | convolution fusion | flops 20972160 | bytes 3670216 | tf_op jit(solution)/shard_map/rk,kaf->raf/dot_general | solution.py:29
  53.7 0.6 fusion.8
  54.2 0.9 copy.24
  55.1 3.8 %all-to-all-start.1 = ((bf16[8,128,256]{2,1,0:T(8,128)(2,1)}), bf16[8,128,256]{2,1,0:T(8,128)(2,1)S(1)}, u32[]{:S(2)}, u32[]{:S(2)}) async-start(bf16[8,128,256]{2,1,0:T(8,128)(2,1)} %copy.24), calls=%async_computation.1 | async-start | bytes 1048576 | tf_op jit(solution)/shard_map/all_to_all | solution.py:126
  59.3 1.7 %collective-permute-start.3 = (bf16[256,256]{1,0:T(8,128)(2,1)S(1)}, bf16[256,256]{1,0:T(8,128)(2,1)S(1)}, u32[]{:S(2)}, u32[]{:S(2)}) collective-permute-start(bf16[256,256]{1,0:T(8,128)(2,1)S(1)} %get-tuple-element.47), channel_id=1, source_target_pairs={{8,0},{16,8},{24,16},{0,24},{9,1},{17,9},{25,17},{1,25},{10,2},{18... | collective-permute-start | bytes 393224 | tf_op jit(solution)/shard_map/ppermute | solution.py:18
  61.0 12.6 %all-to-all-done.1 = bf16[8,128,256]{2,1,0:T(8,128)(2,1)S(1)} async-done(((bf16[8,128,256]{2,1,0:T(8,128)(2,1)}), bf16[8,128,256]{2,1,0:T(8,128)(2,1)S(1)}, u32[]{:S(2)}, u32[]{:S(2)}) %all-to-all-start.1) | async-done | bytes 524320 | tf_op jit(solution)/shard_map/all_to_all | solution.py:126
  73.6 0.4 fusion.9
  74.1 0.3 fusion.24
  74.4 1.0 all_to_all.21
  75.4 2.7 %all-to-all-start.2 = ((f32[32,1,2048]{2,1,0:T(1,128)}), f32[32,1,2048]{2,1,0:T(1,128)S(1)}, u32[]{:S(2)}, u32[]{:S(2)}) async-start(f32[32,1,2048]{2,1,0:T(1,128)} %all_to_all.21), calls=%async_computation.2 | async-start | bytes 524288 | tf_op jit(solution)/shard_map/all_to_all | solution.py:37
  78.2 1.4 %scatter_custom_fusion.1 = s32[256]{0:T(256)S(1)} fusion(s32[256]{0:T(256)S(1)} %bitcast.81, s32[256]{0:T(256)S(1)} %iota.18, s32[]{:T(128)} %constant.132.clone.1), kind=kCustom, calls=%fused_computation.85 | custom fusion | bytes 1028 | tf_op jit(solution)/shard_map/scatter | solution.py:67
  79.6 9.2 %all-to-all-done.2 = f32[32,1,2048]{2,1,0:T(1,128)S(1)} async-done(((f32[32,1,2048]{2,1,0:T(1,128)}), f32[32,1,2048]{2,1,0:T(1,128)S(1)}, u32[]{:S(2)}, u32[]{:S(2)}) %all-to-all-start.2) | async-done | bytes 262176 | tf_op jit(solution)/shard_map/all_to_all | solution.py:37
  88.9 0.8 broadcast_in_dim.74
  89.8 2.8 %all-to-all-start.3 = ((f32[32,1,2048]{2,1,0:T(1,128)}), f32[32,1,2048]{2,1,0:T(1,128)S(1)}, u32[]{:S(2)}, u32[]{:S(2)}) async-start(f32[32,1,2048]{2,1,0:T(1,128)} %broadcast_in_dim.74), calls=%async_computation.3 | async-start | bytes 524288 | tf_op jit(solution)/shard_map/all_to_all | solution.py:40
  92.6 1.2 %gather_fusion.4 = bf16[256,256]{1,0:T(8,128)(2,1)S(1)} fusion(bf16[256,256]{1,0:T(8,128)(2,1)S(1)} %get-tuple-element.49, s32[1024]{0:T(1024)S(1)} %pad_clamp_fusion.1), kind=kCustom, calls=%fused_computation.1.clone | custom fusion | bytes 263168 | tf_op jit(solution)/shard_map/jit(_take)/gather | solution.py:102
  93.9 1.2 %gather_fusion.6 = bf16[256,256]{1,0:T(8,128)(2,1)S(1)} fusion(bf16[256,256]{1,0:T(8,128)(2,1)S(1)} %convolution_convert_fusion, s32[1024]{0:T(1024)S(1)} %pad_clamp_fusion.1), kind=kCustom, calls=%fused_computation.3.clone | custom fusion | bytes 263168 | tf_op jit(solution)/shard_map/jit(_take)/gather | solution.py:141
  95.1 0.8 broadcast_select_fusion.1
  95.9 7.3 %all-to-all-done.3 = f32[32,1,2048]{2,1,0:T(1,128)S(1)} async-done(((f32[32,1,2048]{2,1,0:T(1,128)}), f32[32,1,2048]{2,1,0:T(1,128)S(1)}, u32[]{:S(2)}, u32[]{:S(2)}) %all-to-all-start.3) | async-done | bytes 262176 | tf_op jit(solution)/shard_map/all_to_all | solution.py:40
  103.2 0.8 multiply_reduce_fusion
  104.0 0.7 mul.28
  (65 shorter events, 1.4 us)
Async XLA Ops:
  0.6 3.4 %copy-start = (bf16[256,256]{1,0:T(8,128)(2,1)S(1)}, bf16[256,256]{1,0:T(8,128)(2,1)}, u32[]{:S(2)}) copy-start(bf16[256,256]{1,0:T(8,128)(2,1)} %param.22) | copy-start | bytes 393220
  0.6 15.6 %copy-start.9 = (s32[40,2]{0,1:T(2,128)S(1)}, s32[40,2]{0,1:T(2,128)}, u32[]{:S(2)}) copy-start(s32[40,2]{0,1:T(2,128)} %param.27) | copy-start | bytes 964
  0.7 16.8 %copy-start.20 = (s32[12,2]{0,1:T(2,128)S(1)}, s32[12,2]{0,1:T(2,128)}, u32[]{:S(2)}) copy-start(s32[12,2]{0,1:T(2,128)} %param.25) | copy-start | bytes 292
  0.7 17.4 %copy-start.3 = (bf16[40,128,128]{2,1,0:T(8,128)(2,1)S(1)}, bf16[40,128,128]{2,1,0:T(8,128)(2,1)}, u32[]{:S(2)}) copy-start(bf16[40,128,128]{2,1,0:T(8,128)(2,1)} %param.26) | copy-start | bytes 3932164
  2.2 5.3 %copy-start.12 = (pred[256]{0:T(512)(128)(4,1)}, pred[256]{0:T(512)(128)(4,1)S(1)}, u32[]{:S(2)}) copy-start(pred[256]{0:T(512)(128)(4,1)S(1)} %compare_and_fusion.1) | copy-start | bytes 772
  4.1 4.1 %copy-start.6 = (bf16[256,256]{1,0:T(8,128)(2,1)}, bf16[256,256]{1,0:T(8,128)(2,1)S(1)}, u32[]{:S(2)}) copy-start(bf16[256,256]{1,0:T(8,128)(2,1)S(1)} %gather_fusion.3) | copy-start | bytes 393220
  4.3 29.8 %collective-permute-start = (bf16[256,256]{1,0:T(8,128)(2,1)S(1)}, bf16[256,256]{1,0:T(8,128)(2,1)}, u32[]{:S(2)}, u32[]{:S(2)}) collective-permute-start(bf16[256,256]{1,0:T(8,128)(2,1)S(1)} %convolution_convert_fusion.1), channel_id=1, source_target_pairs={{0,8},{8,16},{16,24},{24,0},{1,9},{9,17},{17,25},{25,1},{2,10},{10... | collective-permute-start | bytes 393224 | tf_op jit(solution)/shard_map/ppermute | solution.py:16
  4.8 29.3 %collective-permute-start.1 = (bf16[256,256]{1,0:T(8,128)(2,1)S(1)}, bf16[256,256]{1,0:T(8,128)(2,1)}, u32[]{:S(2)}, u32[]{:S(2)}) collective-permute-start(bf16[256,256]{1,0:T(8,128)(2,1)S(1)} %convolution_convert_fusion.1), channel_id=1, source_target_pairs={{8,0},{16,8},{24,16},{0,24},{9,1},{17,9},{25,17},{1,25},{10,2},{18... | collective-permute-start | bytes 393224 | tf_op jit(solution)/shard_map/ppermute | solution.py:18
  8.8 10.2 %copy-start.2 = (bf16[256,256]{1,0:T(8,128)(2,1)S(1)}, bf16[256,256]{1,0:T(8,128)(2,1)}, u32[]{:S(2)}) copy-start(bf16[256,256]{1,0:T(8,128)(2,1)} %param.23) | copy-start | bytes 393220
  9.7 21.1 %all-to-all-start = ((bf16[8,128,256]{2,1,0:T(8,128)(2,1)}), bf16[8,128,256]{2,1,0:T(8,128)(2,1)S(1)}, u32[]{:S(2)}, u32[]{:S(2)}) async-start(bf16[8,128,256]{2,1,0:T(8,128)(2,1)} %select_select_fusion), calls=%async_computation | async-start | bytes 1048576 | tf_op jit(solution)/shard_map/all_to_all | solution.py:86
  18.9 5.0 %copy-start.17 = (s32[40]{0:T(128)S(1)}, s32[40]{0:T(128)}, u32[]{:S(2)}) copy-start(s32[40]{0:T(128)} %get-tuple-element.51) | copy-start | bytes 484
  19.0 5.0 %copy-start.14 = (pred[40]{0:T(512)(128)(4,1)S(1)}, pred[40]{0:T(512)(128)(4,1)}, u32[]{:S(2)}) copy-start(pred[40]{0:T(512)(128)(4,1)} %iota_compare_fusion.1) | copy-start | bytes 124
  19.0 5.0 %copy-start.18 = (s32[40]{0:T(128)S(1)}, s32[40]{0:T(128)}, u32[]{:S(2)}) copy-start(s32[40]{0:T(128)} %get-tuple-element.53) | copy-start | bytes 484
  19.0 5.1 %copy-start.10 = (s32[40,2]{0,1:T(2,128)S(1)}, s32[40,2]{0,1:T(2,128)}, u32[]{:S(2)}) copy-start(s32[40,2]{0,1:T(2,128)} %param.27) | copy-start | bytes 964
  31.5 1.7 %copy-start.4 = (bf16[40,2,128,128]{3,0,2,1:T(8,128)(2,1)S(1)}, bf16[40,2,128,128]{3,0,2,1:T(8,128)(2,1)}, u32[]{:S(2)}) copy-start(bf16[40,2,128,128]{3,0,2,1:T(8,128)(2,1)} %broadcast_multiply_fusion) | copy-start | bytes 7864324
  33.3 1.0 copy-start.5
  33.3 1.0 copy-start.8
  33.3 1.0 copy-start.13
  35.6 2.4 %copy-start.16 = (pred[40]{0:T(512)(128)(4,1)S(1)}, pred[40]{0:T(512)(128)(4,1)}, u32[]{:S(2)}) copy-start(pred[40]{0:T(512)(128)(4,1)} %get-tuple-element.54) | copy-start | bytes 124
  47.7 3.4 %copy-start.15 = (pred[40]{0:T(512)(128)(4,1)S(1)}, pred[40]{0:T(512)(128)(4,1)}, u32[]{:S(2)}) copy-start(pred[40]{0:T(512)(128)(4,1)} %iota_compare_fusion.1) | copy-start | bytes 124
  51.1 2.5 %copy-start.1 = (bf16[40,128,256]{2,0,1:T(8,128)(2,1)S(1)}, bf16[40,128,256]{2,0,1:T(8,128)(2,1)}, u32[]{:S(2)}) copy-start(bf16[40,128,256]{2,0,1:T(8,128)(2,1)} %copy.23) | copy-start | bytes 7864324
  54.2 19.4 %copy-start.19 = (s32[1,8]{1,0:T(1,128)S(1)}, s32[1,8]{1,0:T(1,128)}, u32[]{:S(2)}) copy-start(s32[1,8]{1,0:T(1,128)} %param.29) | copy-start | bytes 100
  55.1 19.0 %copy-start.7 = (bf16[256,256]{1,0:T(8,128)(2,1)S(1)}, bf16[256,256]{1,0:T(8,128)(2,1)}, u32[]{:S(2)}) copy-start(bf16[256,256]{1,0:T(8,128)(2,1)} %copy-done.6) | copy-start | bytes 393220
  55.1 18.4 %all-to-all-start.1 = ((bf16[8,128,256]{2,1,0:T(8,128)(2,1)}), bf16[8,128,256]{2,1,0:T(8,128)(2,1)S(1)}, u32[]{:S(2)}, u32[]{:S(2)}) async-start(bf16[8,128,256]{2,1,0:T(8,128)(2,1)} %copy.24), calls=%async_computation.1 | async-start | bytes 1048576 | tf_op jit(solution)/shard_map/all_to_all | solution.py:126
  58.9 19.2 %copy-start.11 = (s32[1,256]{1,0:T(1,128)S(1)}, s32[1,256]{1,0:T(1,128)}, u32[]{:S(2)}) copy-start(s32[1,256]{1,0:T(1,128)} %param.30) | copy-start | bytes 3076
  59.2 14.8 %collective-permute-start.2 = (bf16[256,256]{1,0:T(8,128)(2,1)S(1)}, bf16[256,256]{1,0:T(8,128)(2,1)S(1)}, u32[]{:S(2)}, u32[]{:S(2)}) collective-permute-start(bf16[256,256]{1,0:T(8,128)(2,1)S(1)} %get-tuple-element.46), channel_id=1, source_target_pairs={{0,8},{8,16},{16,24},{24,0},{1,9},{9,17},{17,25},{25,1},{2,10},{10... | collective-permute-start | bytes 393224 | tf_op jit(solution)/shard_map/ppermute | solution.py:16
  59.3 14.8 %collective-permute-start.3 = (bf16[256,256]{1,0:T(8,128)(2,1)S(1)}, bf16[256,256]{1,0:T(8,128)(2,1)S(1)}, u32[]{:S(2)}, u32[]{:S(2)}) collective-permute-start(bf16[256,256]{1,0:T(8,128)(2,1)S(1)} %get-tuple-element.47), channel_id=1, source_target_pairs={{8,0},{16,8},{24,16},{0,24},{9,1},{17,9},{25,17},{1,25},{10,2},{18... | collective-permute-start | bytes 393224 | tf_op jit(solution)/shard_map/ppermute | solution.py:18
  75.4 13.4 %all-to-all-start.2 = ((f32[32,1,2048]{2,1,0:T(1,128)}), f32[32,1,2048]{2,1,0:T(1,128)S(1)}, u32[]{:S(2)}, u32[]{:S(2)}) async-start(f32[32,1,2048]{2,1,0:T(1,128)} %all_to_all.21), calls=%async_computation.2 | async-start | bytes 524288 | tf_op jit(solution)/shard_map/all_to_all | solution.py:37
  89.8 13.4 %all-to-all-start.3 = ((f32[32,1,2048]{2,1,0:T(1,128)}), f32[32,1,2048]{2,1,0:T(1,128)S(1)}, u32[]{:S(2)}, u32[]{:S(2)}) async-start(f32[32,1,2048]{2,1,0:T(1,128)} %broadcast_in_dim.74), calls=%async_computation.3 | async-start | bytes 524288 | tf_op jit(solution)/shard_map/all_to_all | solution.py:40

commit v2 on v1

--- a/solution.py
+++ b/solution.py
@@ -20,15 +20,6 @@
             axis=dim,
         )
     return cells
-
-
-def split_sum(selector, terms):
-    high_part = terms.astype(jnp.bfloat16)
-    low_part = (terms - high_part.astype(jnp.float32)).astype(jnp.bfloat16)
-    pick = selector.astype(jnp.bfloat16)
-    upper_sum = jnp.einsum("rk,kaf->raf", pick, high_part, preferred_element_type=jnp.float32)
-    lower_sum = jnp.einsum("rk,kaf->raf", pick, low_part, preferred_element_type=jnp.float32)
-    return upper_sum + lower_sum
 
 
 def spread_sum(value, axes):
@@ -70,9 +61,14 @@
     hidden = jnp.dot(x_band, weight, preferred_element_type=jnp.float32).astype(jnp.bfloat16)
     band_row_ids = band_coords[:, 0]
     band_col_ids = band_coords[:, 1]
-    band_dense = jnp.zeros((tile_rows, tile_size, col_tiles, tile_size), jnp.bfloat16)
+    band_onehot = (
+        (band_row_ids[:, None, None] == jnp.arange(tile_rows, dtype=jnp.int32)[None, :, None])
+        & (band_col_ids[:, None, None] == jnp.arange(col_tiles, dtype=jnp.int32)[None, None, :])
+    ).astype(jnp.bfloat16)
     band_dense = (
-        band_dense.at[band_row_ids, :, band_col_ids].set(band_tiles).reshape(row_count, ext_count)
+        jnp.einsum("krc,kab->racb", band_onehot, band_tiles, preferred_element_type=jnp.float32)
+        .astype(jnp.bfloat16)
+        .reshape(row_count, ext_count)
     )
     extended = padded_2(hidden, (("row", 0),), BW)
     mixed = jnp.dot(band_dense, extended, preferred_element_type=jnp.float32)
@@ -85,25 +81,28 @@
     )
     arrived = lax.all_to_all(outgoing, "col", split_axis=0, concat_axis=0, tiled=True)
     tile_range = jnp.arange(tile_rows, dtype=jnp.int32)
+    owner_range = jnp.arange(peers, dtype=jnp.int32)
     live_slots = jnp.arange(slot_total, dtype=jnp.int32) < bound_count[0]
     bound_row_ids = bound_coords[:, 0]
     bound_owner = bound_coords[:, 1]
-    bound_onehot = (bound_row_ids[None, :] == tile_range[:, None]) & live_slots[None, :]
-    slot_rows = jnp.take(arrived, bound_owner, axis=0).reshape(slot_total * tile_size, width_feat)
-    placed = jnp.einsum(
-        "rk,kab->rakb",
-        bound_onehot.astype(jnp.bfloat16),
-        bound_tiles,
-        preferred_element_type=jnp.bfloat16,
-    )
-    placed = placed.reshape(row_count, slot_total * tile_size)
-    mixed = mixed + jnp.dot(placed, slot_rows, preferred_element_type=jnp.float32)
+    slot_onehot = (
+        (bound_row_ids[:, None, None] == tile_range[None, :, None])
+        & (bound_owner[:, None, None] == owner_range[None, None, :])
+        & live_slots[:, None, None]
+    ).astype(jnp.bfloat16)
+    bound_dense = jnp.einsum(
+        "krs,kab->rasb", slot_onehot, bound_tiles, preferred_element_type=jnp.float32
+    ).reshape(row_count, peers * tile_size)
+    dense_high = bound_dense.astype(jnp.bfloat16)
+    dense_low = (bound_dense - dense_high.astype(jnp.float32)).astype(jnp.bfloat16)
+    arrived_rows = arrived.reshape(peers * tile_size, width_feat)
+    mixed = mixed + jnp.dot(dense_high, arrived_rows, preferred_element_type=jnp.float32)
+    mixed = mixed + jnp.dot(dense_low, arrived_rows, preferred_element_type=jnp.float32)
     out_band = jax.nn.silu(mixed).astype(jnp.bfloat16)
     node_out = jnp.take(out_band, inverse, axis=0)
     grad_band = jnp.take(cotangent, order, axis=0).astype(jnp.float32)
     sigma = jax.nn.sigmoid(mixed)
     slope = (grad_band * sigma * (1.0 + mixed * (1.0 - sigma))).astype(jnp.bfloat16)
-    slope_blocks = slope.reshape(tile_rows, tile_size, width_feat)
     ext_grad = lax.dot_general(
         band_dense, slope, (((0,), (0,)), ((), ())), preferred_element_type=jnp.float32
     )
@@ -114,15 +113,11 @@
     grad_hidden = ext_grad[BW : BW + row_count]
     grad_hidden = grad_hidden.at[:BW].add(padded[:BW].astype(jnp.float32))
     grad_hidden = grad_hidden.at[row_count - BW :].add(padded[3 * BW :].astype(jnp.float32))
-    slot_back = jnp.einsum(
-        "kab,kaf->kbf",
-        bound_tiles,
-        jnp.take(slope_blocks, bound_row_ids, axis=0),
-        preferred_element_type=jnp.float32,
-    )
-    owner_range = jnp.arange(peers, dtype=jnp.int32)
-    owner_onehot = (bound_owner[None, :] == owner_range[:, None]) & live_slots[None, :]
-    to_owner = split_sum(owner_onehot, slot_back).astype(jnp.bfloat16)
+    contract_rows = (((0,), (0,)), ((), ()))
+    owner_terms = lax.dot_general(
+        dense_high, slope, contract_rows, preferred_element_type=jnp.float32
+    ) + lax.dot_general(dense_low, slope, contract_rows, preferred_element_type=jnp.float32)
+    to_owner = owner_terms.astype(jnp.bfloat16).reshape(peers, tile_size, width_feat)
     returned = lax.all_to_all(to_owner, "col", split_axis=0, concat_axis=0, tiled=True)
     block_onehot = (giving[None, :] == tile_range[:, None]).astype(jnp.bfloat16)
     from_peers = jnp.einsum(

time: 105 us -> 83.1 us (0.79)
  local copies, waits for them, and re-layouts: 28.5 us -> 10.9 us
  other arithmetic: 9.32 us -> 4.2 us
  waiting for transfers between devices: 33.5 us -> 38.3 us
  matrix products: 11.6 us -> 7.54 us
    convert_element_type x3 -> x0, local copies, waits for them, and re-layouts: 9.07 us -> none  [the longest x1 4.76 us: split_sum(): high_part = terms.astype(jnp.bfloat16)]
    all_to_all x1, waiting for transfers between devices: 4.44 us -> 9.33 us  [on_device(): lax.all_to_all(outgoing, 'col', split_axis=0, concat_axis=0, tiled=True)]
    dot_general x4 -> x6, matrix products: 8.83 us -> 4.77 us  [the longest x1 2.28 us: on_device(): jnp.einsum('krs,kab->rasb', slot_onehot, bound_tiles, preferred_element_t...]
    scatter x2 -> x0, local copies, waits for them, and re-layouts: 3.12 us -> none  [on_device(): band_dense.at[band_row_ids, :, band_col_ids].set(band_tiles)]
    gather x2 -> x0, local copies, waits for them, and re-layouts: 3.09 us -> none  [the longest x1 2.38 us: on_device(): jnp.take(slope_blocks, bound_row_ids, axis=0)]
    unnamed x43 -> x20, local copies, waits for them, and re-layouts: 2.55 us -> 0.32 us
    dot_general x1 -> x0, other arithmetic: 1.75 us -> none  [on_device(): jnp.einsum('rk,kab->rakb', bound_onehot.astype(jnp.bfloat16), bound_tiles...]
  transfers between devices with their start and end apart: 8 -> 8, of which waited for: 4 -> 4; matrix products, arithmetic and copies ran while one was open for 19% -> 15% of each run, Pallas kernels for 0% -> 0%
where the time goes in v2:
time: 83.1 us; the launch traced here: 82.6 us
  waiting for transfers between devices  38.3 us (46%)
  starting transfers between devices  19.9 us (24%)
  local copies, waits for them, and re-layouts  10.9 us (13%)
  matrix products  7.54 us (9%)
  other arithmetic  4.2 us (5%)
  between operations  1.67 us (2%)
    all_to_all x1, waiting for transfers between devices, on_device(): lax.all_to_all(to_owner, 'col', split_axis=0, concat_axis=0, tiled=True)  12.5 us
    all_to_all x1, waiting for transfers between devices, on_device(): lax.all_to_all(outgoing, 'col', split_axis=0, concat_axis=0, tiled=True)  9.33 us
    all_to_all x1, waiting for transfers between devices, spread_sum(): gathered = lax.all_to_all(pieces, axes, 0, 0, tiled=True)  9.19 us
    all_to_all x1, waiting for transfers between devices, spread_sum(): return lax.all_to_all(copies, axes, 0, 0, tiled=True).reshape(value.shape)  7.3 us
    all_to_all x1, starting transfers between devices, on_device(): lax.all_to_all(outgoing, 'col', split_axis=0, concat_axis=0, tiled=True)  6.66 us
    ppermute x2, starting transfers between devices, padded_2(): lax.ppermute(head, axis, [((i + 1) % count, i) for i in range(count)])  3.75 us
    all_to_all x1, starting transfers between devices, on_device(): lax.all_to_all(to_owner, 'col', split_axis=0, concat_axis=0, tiled=True)  3.64 us
    all_to_all x1, starting transfers between devices, spread_sum(): gathered = lax.all_to_all(pieces, axes, 0, 0, tiled=True)  2.72 us
  transfers between devices with their start and end apart: 8, of which 4 were waited for; matrix products, arithmetic and copies ran while one was open for 15% of the time, Pallas kernels for 0%

profile of v2, /device:TPU:0, one launch (start us, length us, event | category | flops | bytes accessed | tf_op | source)
XLA Modules:
  0.0 82.6 jit_solution(4654018305692980824)
XLA Ops:
  0.6 0.0 copy-start
  0.7 0.7 compare_select_fusion.2
  1.4 0.7 compare_and_fusion.1
  2.1 1.9 %gather_fusion.1 = bf16[256,256]{1,0:T(8,128)(2,1)S(1)} fusion(bf16[256,256]{1,0:T(8,128)(2,1)} %param.21, s32[1024]{0:T(1024)S(1)} %pad_clamp_fusion.2), kind=kCustom, calls=%fused_computation.clone | custom fusion | bytes 263168 | tf_op jit(solution)/shard_map/jit(_take)/gather | solution.py:60
  4.0 0.0 copy-start.2
  4.0 0.2 convolution_convert_fusion.2
  4.2 0.5 collective-permute-start
  4.7 2.0 %collective-permute-start.1 = (bf16[256,256]{1,0:T(8,128)(2,1)S(1)}, bf16[256,256]{1,0:T(8,128)(2,1)}, u32[]{:S(2)}, u32[]{:S(2)}) collective-permute-start(bf16[256,256]{1,0:T(8,128)(2,1)S(1)} %convolution_convert_fusion.2), channel_id=1, source_target_pairs={{8,0},{16,8},{24,16},{0,24},{9,1},{17,9},{25,17},{1,25},{10,2},{18... | collective-permute-start | bytes 393224 | tf_op jit(solution)/shard_map/ppermute | solution.py:18
  6.8 0.6 gather_fusion
  7.4 0.0 copy-start.7
  7.4 0.0 copy-start.8
  7.4 0.0 copy-start.1
  7.4 1.0 %select_select_fusion = bf16[8,128,256]{2,1,0:T(8,128)(2,1)} fusion(bf16[8,128,256]{2,1,0:T(8,128)(2,1)S(1)} %gather_fusion, pred[8]{0:T(512)(128)(4,1)S(1)} %get-tuple-element.57, pred[8]{0:T(512)(128)(4,1)S(1)} %get-tuple-element.56), kind=kLoop, calls=%fused_computation.33 | loop fusion | flops 524288 | bytes 1048592 | tf_op jit(solution)/shard_map/jit(_where)/select_n | solution.py:77
  8.4 6.7 %all-to-all-start = ((bf16[8,128,256]{2,1,0:T(8,128)(2,1)}), bf16[8,128,256]{2,1,0:T(8,128)(2,1)S(1)}, u32[]{:S(2)}, u32[]{:S(2)}) async-start(bf16[8,128,256]{2,1,0:T(8,128)(2,1)} %select_select_fusion), calls=%async_computation | async-start | bytes 1048576 | tf_op jit(solution)/shard_map/all_to_all | solution.py:82
  15.8 1.8 %gather_fusion.3 = bf16[256,256]{1,0:T(8,128)(2,1)} fusion(bf16[256,256]{1,0:T(8,128)(2,1)S(1)} %copy-done.1, s32[1024]{0:T(1024)S(1)} %pad_clamp_fusion.2), kind=kCustom, calls=%fused_computation.2.clone | custom fusion | bytes 263168 | tf_op jit(solution)/shard_map/jit(_take)/gather | solution.py:103
  17.6 0.4 convolution_convert_fusion
  18.0 2.3 %fusion.6 = (bf16[2,128,8,128]{3,2,1,0:T(8,128)(2,1)S(1)}, bf16[2,128,8,128]{3,2,1,0:T(8,128)(2,1)S(1)}, f32[2,8,128,128]{3,1,2,0:T(8,128)S(1)}) fusion(bf16[40,128,128]{2,1,0:T(8,128)(2,1)} %param.26, pred[40]{0:T(512)(128)(4,1)S(1)} %iota_compare_fusion.4, pred[40,8]{0,1:T(8,128)(4,1)S(1)} %iota_compare_fusion, pred[40,2]{0,1:T(4,128)(4,1)S(1)} %iota_compare_fusion.2), kind=kOutput, calls=%fused_computation.21 | convolution fusion | flops 22021376 | bytes 3408312 | tf_op jit(solution)/shard_map/krs,kab->rasb/dot_general | solution.py:93
  20.2 9.3 %all-to-all-done = bf16[8,128,256]{2,1,0:T(8,128)(2,1)S(1)} async-done(((bf16[8,128,256]{2,1,0:T(8,128)(2,1)}), bf16[8,128,256]{2,1,0:T(8,128)(2,1)S(1)}, u32[]{:S(2)}, u32[]{:S(2)}) %all-to-all-start) | async-done | bytes 524320 | tf_op jit(solution)/shard_map/all_to_all | solution.py:82
  29.6 0.3 fusion.12
  29.9 0.3 fusion.9
  30.2 0.3 copy-done.5
  30.5 1.3 %multiply_convert_fusion = (bf16[256,256]{1,0:T(8,128)(2,1)S(1)}, bf16[256,256]{1,0:T(8,128)(2,1)S(1)}) fusion(bf16[256,256]{1,0:T(8,128)(2,1)S(1)} %copy-done.5, pred[256]{0:T(512)(128)(4,1)S(1)} %compare_and_fusion.1, f32[256,256]{1,0:T(8,128)S(1)} %fusion.9, f32[256,256]{1,0:T(8,128)S(1)} %fusion.12, bf16[256,256]{1,0:T(8,128)(2,1)} %collective-permute-done.1, ...), kind=kOutput, calls=%fused_computation.49 | convolution fusion | flops 102825984 | bytes 1704192 | tf_op jit(solution)/shard_map/dot_general | solution.py:74
  31.8 0.4 fusion.7
  32.2 1.2 %fusion.3 = bf16[1024,256]{1,0:T(8,128)(2,1)} fusion(f32[1024,256]{1,0:T(8,128)S(1)} %fusion.7, bf16[256,256]{1,0:T(8,128)(2,1)S(1)} %get-tuple-element.48, f32[32,8,8,128]{3,2,1,0:T(8,128)S(1)} %bitcast.96), kind=kOutput, calls=%fused_computation.11 | convolution fusion | flops 135790592 | bytes 2752512 | tf_op jit(solution)/shard_map/dot_general | solution.py:119
  33.3 3.6 %all-to-all-start.1 = ((bf16[8,128,256]{2,1,0:T(8,128)(2,1)}), bf16[8,128,256]{2,1,0:T(8,128)(2,1)S(1)}, u32[]{:S(2)}, u32[]{:S(2)}) async-start(bf16[8,128,256]{2,1,0:T(8,128)(2,1)} %bitcast.21), calls=%async_computation.1 | async-start | bytes 1048576 | tf_op jit(solution)/shard_map/all_to_all | solution.py:121
  37.0 0.3 fusion.53
  37.3 0.0 copy-start.3
  37.3 0.1 collective-permute-start.2
  37.4 1.7 %collective-permute-start.3 = (bf16[256,256]{1,0:T(8,128)(2,1)S(1)}, bf16[256,256]{1,0:T(8,128)(2,1)S(1)}, u32[]{:S(2)}, u32[]{:S(2)}) collective-permute-start(bf16[256,256]{1,0:T(8,128)(2,1)S(1)} %get-tuple-element.47), channel_id=1, source_target_pairs={{8,0},{16,8},{24,16},{0,24},{9,1},{17,9},{25,17},{1,25},{10,2},{18... | collective-permute-start | bytes 393224 | tf_op jit(solution)/shard_map/ppermute | solution.py:18
  39.1 12.5 %all-to-all-done.1 = bf16[8,128,256]{2,1,0:T(8,128)(2,1)S(1)} async-done(((bf16[8,128,256]{2,1,0:T(8,128)(2,1)}), bf16[8,128,256]{2,1,0:T(8,128)(2,1)S(1)}, u32[]{:S(2)}, u32[]{:S(2)}) %all-to-all-start.1) | async-done | bytes 524320 | tf_op jit(solution)/shard_map/all_to_all | solution.py:121
  51.6 0.4 fusion.16
  52.1 0.0 copy-start.6
  52.1 0.1 fusion.31
  52.2 0.3 fusion.32
  52.5 1.0 %all_to_all.21 = f32[32,1,2048]{2,1,0:T(1,128)} reshape(f32[256,256]{1,0:T(8,128)S(1)} %fusion.32) | data formatting | bytes 524288 | tf_op jit(solution)/shard_map/all_to_all | solution.py:28
  53.5 2.7 %all-to-all-start.2 = ((f32[32,1,2048]{2,1,0:T(1,128)}), f32[32,1,2048]{2,1,0:T(1,128)S(1)}, u32[]{:S(2)}, u32[]{:S(2)}) async-start(f32[32,1,2048]{2,1,0:T(1,128)} %all_to_all.21), calls=%async_computation.2 | async-start | bytes 524288 | tf_op jit(solution)/shard_map/all_to_all | solution.py:28
  56.2 1.4 %scatter_custom_fusion = s32[256]{0:T(256)S(1)} fusion(s32[256]{0:T(256)S(1)} %bitcast.106, s32[256]{0:T(256)S(1)} %iota.42, s32[]{:T(128)} %constant.103.clone.1), kind=kCustom, calls=%fused_computation.82 | custom fusion | bytes 1028 | tf_op jit(solution)/shard_map/scatter | solution.py:58
  57.6 9.2 %all-to-all-done.2 = f32[32,1,2048]{2,1,0:T(1,128)S(1)} async-done(((f32[32,1,2048]{2,1,0:T(1,128)}), f32[32,1,2048]{2,1,0:T(1,128)S(1)}, u32[]{:S(2)}, u32[]{:S(2)}) %all-to-all-start.2) | async-done | bytes 262176 | tf_op jit(solution)/shard_map/all_to_all | solution.py:28
  66.8 0.2 reduce_sum.9
  67.0 0.8 %broadcast_in_dim.48 = f32[32,1,2048]{2,1,0:T(1,128)} broadcast(f32[2048]{0:T(1024)S(1)} %reduce_sum.9), dimensions={2} | broadcast | bytes 270336 | tf_op jit(solution)/shard_map/broadcast_in_dim | solution.py:30
  67.8 2.6 %all-to-all-start.3 = ((f32[32,1,2048]{2,1,0:T(1,128)}), f32[32,1,2048]{2,1,0:T(1,128)S(1)}, u32[]{:S(2)}, u32[]{:S(2)}) async-start(f32[32,1,2048]{2,1,0:T(1,128)} %broadcast_in_dim.48), calls=%async_computation.3 | async-start | bytes 524288 | tf_op jit(solution)/shard_map/all_to_all | solution.py:31
  70.4 1.2 %gather_fusion.2 = bf16[256,256]{1,0:T(8,128)(2,1)S(1)} fusion(bf16[256,256]{1,0:T(8,128)(2,1)S(1)} %get-tuple-element.49, s32[1024]{0:T(1024)S(1)} %pad_clamp_fusion), kind=kCustom, calls=%fused_computation.1.clone | custom fusion | bytes 263168 | tf_op jit(solution)/shard_map/jit(_take)/gather | solution.py:102
  71.6 0.2 convolution_convert_fusion.1
  71.8 1.2 %gather_fusion.4 = bf16[256,256]{1,0:T(8,128)(2,1)S(1)} fusion(bf16[256,256]{1,0:T(8,128)(2,1)S(1)} %convolution_convert_fusion.1, s32[1024]{0:T(1024)S(1)} %pad_clamp_fusion), kind=kCustom, calls=%fused_computation.3.clone | custom fusion | bytes 263168 | tf_op jit(solution)/shard_map/jit(_take)/gather | solution.py:136
  73.0 0.8 broadcast_select_fusion
  73.8 7.3 %all-to-all-done.3 = f32[32,1,2048]{2,1,0:T(1,128)S(1)} async-done(((f32[32,1,2048]{2,1,0:T(1,128)}), f32[32,1,2048]{2,1,0:T(1,128)S(1)}, u32[]{:S(2)}, u32[]{:S(2)}) %all-to-all-start.3) | async-done | bytes 262176 | tf_op jit(solution)/shard_map/all_to_all | solution.py:31
  81.1 0.8 multiply_reduce_fusion
  81.8 0.7 mul.28
  (34 shorter events, 0.2 us)
Async XLA Ops:
  0.6 3.3 %copy-start = (bf16[256,256]{1,0:T(8,128)(2,1)S(1)}, bf16[256,256]{1,0:T(8,128)(2,1)}, u32[]{:S(2)}) copy-start(bf16[256,256]{1,0:T(8,128)(2,1)} %param.22) | copy-start | bytes 393220
  0.6 6.1 %copy-start.9 = (s32[1,8]{1,0:T(1,128)S(1)}, s32[1,8]{1,0:T(1,128)}, u32[]{:S(2)}) copy-start(s32[1,8]{1,0:T(1,128)} %param.29) | copy-start | bytes 100
  4.0 2.8 %copy-start.2 = (bf16[256,256]{1,0:T(8,128)(2,1)}, bf16[256,256]{1,0:T(8,128)(2,1)S(1)}, u32[]{:S(2)}) copy-start(bf16[256,256]{1,0:T(8,128)(2,1)S(1)} %gather_fusion.1) | copy-start | bytes 393220
  4.2 26.0 %collective-permute-start = (bf16[256,256]{1,0:T(8,128)(2,1)S(1)}, bf16[256,256]{1,0:T(8,128)(2,1)}, u32[]{:S(2)}, u32[]{:S(2)}) collective-permute-start(bf16[256,256]{1,0:T(8,128)(2,1)S(1)} %convolution_convert_fusion.2), channel_id=1, source_target_pairs={{0,8},{8,16},{16,24},{24,0},{1,9},{9,17},{17,25},{25,1},{2,10},{10... | collective-permute-start | bytes 393224 | tf_op jit(solution)/shard_map/ppermute | solution.py:16
  4.7 25.5 %collective-permute-start.1 = (bf16[256,256]{1,0:T(8,128)(2,1)S(1)}, bf16[256,256]{1,0:T(8,128)(2,1)}, u32[]{:S(2)}, u32[]{:S(2)}) collective-permute-start(bf16[256,256]{1,0:T(8,128)(2,1)S(1)} %convolution_convert_fusion.2), channel_id=1, source_target_pairs={{8,0},{16,8},{24,16},{0,24},{9,1},{17,9},{25,17},{1,25},{10,2},{18... | collective-permute-start | bytes 393224 | tf_op jit(solution)/shard_map/ppermute | solution.py:18
  7.4 7.7 %copy-start.7 = (s32[40,2]{0,1:T(2,128)S(1)}, s32[40,2]{0,1:T(2,128)}, u32[]{:S(2)}) copy-start(s32[40,2]{0,1:T(2,128)} %param.27) | copy-start | bytes 964
  7.4 7.7 %copy-start.8 = (s32[12,2]{0,1:T(2,128)S(1)}, s32[12,2]{0,1:T(2,128)}, u32[]{:S(2)}) copy-start(s32[12,2]{0,1:T(2,128)} %param.25) | copy-start | bytes 292
  7.4 8.4 %copy-start.1 = (bf16[256,256]{1,0:T(8,128)(2,1)S(1)}, bf16[256,256]{1,0:T(8,128)(2,1)}, u32[]{:S(2)}) copy-start(bf16[256,256]{1,0:T(8,128)(2,1)} %param.23) | copy-start | bytes 393220
  8.4 9.2 %copy-start.4 = (bf16[12,128,128]{2,1,0:T(8,128)(2,1)S(1)}, bf16[12,128,128]{2,1,0:T(8,128)(2,1)}, u32[]{:S(2)}) copy-start(bf16[12,128,128]{2,1,0:T(8,128)(2,1)} %param.24) | copy-start | bytes 1179652
  8.4 21.2 %all-to-all-start = ((bf16[8,128,256]{2,1,0:T(8,128)(2,1)}), bf16[8,128,256]{2,1,0:T(8,128)(2,1)S(1)}, u32[]{:S(2)}, u32[]{:S(2)}) async-start(bf16[8,128,256]{2,1,0:T(8,128)(2,1)} %select_select_fusion), calls=%async_computation | async-start | bytes 1048576 | tf_op jit(solution)/shard_map/all_to_all | solution.py:82
  29.6 0.9 %copy-start.5 = (bf16[256,256]{1,0:T(8,128)(2,1)S(1)}, bf16[256,256]{1,0:T(8,128)(2,1)}, u32[]{:S(2)}) copy-start(bf16[256,256]{1,0:T(8,128)(2,1)} %gather_fusion.3) | copy-start | bytes 393220
  33.3 18.3 %all-to-all-start.1 = ((bf16[8,128,256]{2,1,0:T(8,128)(2,1)}), bf16[8,128,256]{2,1,0:T(8,128)(2,1)S(1)}, u32[]{:S(2)}, u32[]{:S(2)}) async-start(bf16[8,128,256]{2,1,0:T(8,128)(2,1)} %bitcast.21), calls=%async_computation.1 | async-start | bytes 1048576 | tf_op jit(solution)/shard_map/all_to_all | solution.py:121
  37.3 14.9 %copy-start.3 = (bf16[256,256]{1,0:T(8,128)(2,1)S(1)}, bf16[256,256]{1,0:T(8,128)(2,1)}, u32[]{:S(2)}) copy-start(bf16[256,256]{1,0:T(8,128)(2,1)} %copy-done.2) | copy-start | bytes 393220
  37.3 14.8 %collective-permute-start.2 = (bf16[256,256]{1,0:T(8,128)(2,1)S(1)}, bf16[256,256]{1,0:T(8,128)(2,1)S(1)}, u32[]{:S(2)}, u32[]{:S(2)}) collective-permute-start(bf16[256,256]{1,0:T(8,128)(2,1)S(1)} %get-tuple-element.46), channel_id=1, source_target_pairs={{0,8},{8,16},{16,24},{24,0},{1,9},{9,17},{17,25},{25,1},{2,10},{10... | collective-permute-start | bytes 393224 | tf_op jit(solution)/shard_map/ppermute | solution.py:16
  37.4 14.7 %collective-permute-start.3 = (bf16[256,256]{1,0:T(8,128)(2,1)S(1)}, bf16[256,256]{1,0:T(8,128)(2,1)S(1)}, u32[]{:S(2)}, u32[]{:S(2)}) collective-permute-start(bf16[256,256]{1,0:T(8,128)(2,1)S(1)} %get-tuple-element.47), channel_id=1, source_target_pairs={{8,0},{16,8},{24,16},{0,24},{9,1},{17,9},{25,17},{1,25},{10,2},{18... | collective-permute-start | bytes 393224 | tf_op jit(solution)/shard_map/ppermute | solution.py:18
  52.1 4.1 %copy-start.6 = (s32[1,256]{1,0:T(1,128)S(1)}, s32[1,256]{1,0:T(1,128)}, u32[]{:S(2)}) copy-start(s32[1,256]{1,0:T(1,128)} %param.30) | copy-start | bytes 3076
  53.5 13.4 %all-to-all-start.2 = ((f32[32,1,2048]{2,1,0:T(1,128)}), f32[32,1,2048]{2,1,0:T(1,128)S(1)}, u32[]{:S(2)}, u32[]{:S(2)}) async-start(f32[32,1,2048]{2,1,0:T(1,128)} %all_to_all.21), calls=%async_computation.2 | async-start | bytes 524288 | tf_op jit(solution)/shard_map/all_to_all | solution.py:28
  67.8 13.2 %all-to-all-start.3 = ((f32[32,1,2048]{2,1,0:T(1,128)}), f32[32,1,2048]{2,1,0:T(1,128)S(1)}, u32[]{:S(2)}, u32[]{:S(2)}) async-start(f32[32,1,2048]{2,1,0:T(1,128)} %broadcast_in_dim.48), calls=%async_computation.3 | async-start | bytes 524288 | tf_op jit(solution)/shard_map/all_to_all | solution.py:31

commit v3 on v2

--- a/solution.py
+++ b/solution.py
@@ -74,28 +74,35 @@
     mixed = jnp.dot(band_dense, extended, preferred_element_type=jnp.float32)
     blocks = hidden.reshape(tile_rows, tile_size, width_feat)
     giving = send_lists[0]
+    here = lax.axis_index("col")
+    shifts = jnp.arange(1, peers, dtype=jnp.int32)
+    giving_rel = jnp.take(giving, (here + shifts) % peers)
     outgoing = jnp.where(
-        (giving >= 0)[:, None, None],
-        jnp.take(blocks, jnp.maximum(giving, 0), axis=0),
+        (giving_rel >= 0)[:, None, None],
+        jnp.take(blocks, jnp.maximum(giving_rel, 0), axis=0),
         jnp.zeros((), jnp.bfloat16),
     )
-    arrived = lax.all_to_all(outgoing, "col", split_axis=0, concat_axis=0, tiled=True)
+    arrived = jnp.stack(
+        [
+            lax.ppermute(outgoing[k - 1], "col", [(i, (i + k) % peers) for i in range(peers)])
+            for k in range(1, peers)
+        ]
+    )
     tile_range = jnp.arange(tile_rows, dtype=jnp.int32)
-    owner_range = jnp.arange(peers, dtype=jnp.int32)
     live_slots = jnp.arange(slot_total, dtype=jnp.int32) < bound_count[0]
     bound_row_ids = bound_coords[:, 0]
-    bound_owner = bound_coords[:, 1]
+    bound_shift = (here - bound_coords[:, 1]) % peers
     slot_onehot = (
         (bound_row_ids[:, None, None] == tile_range[None, :, None])
-        & (bound_owner[:, None, None] == owner_range[None, None, :])
+        & (bound_shift[:, None, None] == shifts[None, None, :])
         & live_slots[:, None, None]
     ).astype(jnp.bfloat16)
     bound_dense = jnp.einsum(
         "krs,kab->rasb", slot_onehot, bound_tiles, preferred_element_type=jnp.float32
-    ).reshape(row_count, peers * tile_size)
+    ).reshape(row_count, (peers - 1) * tile_size)
     dense_high = bound_dense.astype(jnp.bfloat16)
     dense_low = (bound_dense - dense_high.astype(jnp.float32)).astype(jnp.bfloat16)
-    arrived_rows = arrived.reshape(peers * tile_size, width_feat)
+    arrived_rows = arrived.reshape((peers - 1) * tile_size, width_feat)
     mixed = mixed + jnp.dot(dense_high, arrived_rows, preferred_element_type=jnp.float32)
     mixed = mixed + jnp.dot(dense_low, arrived_rows, preferred_element_type=jnp.float32)
     out_band = jax.nn.silu(mixed).astype(jnp.bfloat16)
@@ -117,9 +124,14 @@
     owner_terms = lax.dot_general(
         dense_high, slope, contract_rows, preferred_element_type=jnp.float32
     ) + lax.dot_general(dense_low, slope, contract_rows, preferred_element_type=jnp.float32)
-    to_owner = owner_terms.astype(jnp.bfloat16).reshape(peers, tile_size, width_feat)
-    returned = lax.all_to_all(to_owner, "col", split_axis=0, concat_axis=0, tiled=True)
-    block_onehot = (giving[None, :] == tile_range[:, None]).astype(jnp.bfloat16)
+    to_owner = owner_terms.astype(jnp.bfloat16).reshape(peers - 1, tile_size, width_feat)
+    returned = jnp.stack(
+        [
+            lax.ppermute(to_owner[k - 1], "col", [((i + k) % peers, i) for i in range(peers)])
+            for k in range(1, peers)
+        ]
+    )
+    block_onehot = (giving_rel[None, :] == tile_range[:, None]).astype(jnp.bfloat16)
     from_peers = jnp.einsum(
         "bs,saf->baf", block_onehot, returned, preferred_element_type=jnp.float32
     )

time: 83.1 us -> 88.7 us (1.067)
  starting transfers between devices: 19.9 us -> 33.5 us
  waiting for transfers between devices: 38.3 us -> 24.9 us
  local copies, waits for them, and re-layouts: 10.9 us -> 19.1 us
  matrix products: 7.54 us -> 5.27 us
    ppermute x0 -> x14, starting transfers between devices: none -> 23.8 us  [the longest x7 13.1 us: on_device(): lax.ppermute(outgoing[k - 1], 'col', [(i, (i + k) % peers) for i in range...]
    all_to_all x2 -> x0, waiting for transfers between devices: 21.8 us -> none  [the longest x1 12.5 us: on_device(): lax.all_to_all(to_owner, 'col', split_axis=0, concat_axis=0, tiled=True)]
    all_to_all x2 -> x0, starting transfers between devices: 10.3 us -> none  [the longest x1 6.66 us: on_device(): lax.all_to_all(outgoing, 'col', split_axis=0, concat_axis=0, tiled=True)]
    ppermute x0 -> x14, waiting for transfers between devices: none -> 8.26 us  [the longest x7 5.45 us: on_device(): lax.ppermute(to_owner[k - 1], 'col', [((i + k) % peers, i) for i in range...]
    unnamed x20 -> x43, local copies, waits for them, and re-layouts: 0.32 us -> 4.08 us
    convert_element_type x0 -> x2, local copies, waits for them, and re-layouts: none -> 2.48 us  [the longest x1 1.25 us: on_device(): dense_high = bound_dense.astype(jnp.bfloat16)]
    all_to_all x1, starting transfers between devices: 2.72 us -> 4.52 us  [spread_sum(): gathered = lax.all_to_all(pieces, axes, 0, 0, tiled=True)]
    ppermute x2, starting transfers between devices: 3.75 us -> 2.02 us  [padded_2(): lax.ppermute(head, axis, [((i + 1) % count, i) for i in range(count)])]
  transfers between devices with their start and end apart: 8 -> 20, of which waited for: 4 -> 10; matrix products, arithmetic and copies ran while one was open for 15% -> 18% of each run, Pallas kernels for 0% -> 0%
where the time goes in v3:
time: 88.7 us; the launch traced here: 88.2 us
  starting transfers between devices  33.5 us (38%)
  waiting for transfers between devices  24.9 us (28%)
  local copies, waits for them, and re-layouts  19.1 us (22%)
  matrix products  5.27 us (6%)
  other arithmetic  3.7 us (4%)
  between operations  1.78 us (2%)
    ppermute x7, starting transfers between devices, on_device(): lax.ppermute(outgoing[k - 1], 'col', [(i, (i + k) % peers) for i in range...  13.1 us
    ppermute x7, starting transfers between devices, on_device(): lax.ppermute(to_owner[k - 1], 'col', [((i + k) % peers, i) for i in range...  10.7 us
    all_to_all x1, waiting for transfers between devices, spread_sum(): gathered = lax.all_to_all(pieces, axes, 0, 0, tiled=True)  9.19 us
    all_to_all x1, waiting for transfers between devices, spread_sum(): return lax.all_to_all(copies, axes, 0, 0, tiled=True).reshape(value.shape)  7.3 us
    ppermute x7, waiting for transfers between devices, on_device(): lax.ppermute(to_owner[k - 1], 'col', [((i + k) % peers, i) for i in range...  5.45 us
    all_to_all x1, starting transfers between devices, spread_sum(): gathered = lax.all_to_all(pieces, axes, 0, 0, tiled=True)  4.52 us
    unnamed x43, local copies, waits for them, and re-layouts  4.08 us
    ppermute x7, waiting for transfers between devices, on_device(): lax.ppermute(outgoing[k - 1], 'col', [(i, (i + k) % peers) for i in range...  2.81 us
  transfers between devices with their start and end apart: 20, of which 10 were waited for; matrix products, arithmetic and copies ran while one was open for 18% of the time, Pallas kernels for 0%

profile of v3, /device:TPU:0, one launch (start us, length us, event | category | flops | bytes accessed | tf_op | source)
XLA Modules:
  0.0 88.2 jit_solution(6829059304144034708)
XLA Ops:
  0.6 0.7 compare_select_fusion.2
  1.4 0.7 compare_and_fusion.1
  2.1 1.3 %gather_fusion = s32[7]{0:T(128)S(1)} fusion(s32[8]{0:T(128)} %bitcast.137, s32[1024]{0:T(1024)S(1)} %pad_clamp_fusion.2), kind=kCustom, calls=%fused_computation.4 | custom fusion | bytes 84 | tf_op jit(solution)/shard_map/jit(_take)/gather | solution.py:79
  3.4 1.9 %gather_fusion.2 = bf16[256,256]{1,0:T(8,128)(2,1)S(1)} fusion(bf16[256,256]{1,0:T(8,128)(2,1)} %param.21, s32[1024]{0:T(1024)S(1)} %get-tuple-element.71), kind=kCustom, calls=%fused_computation.clone | custom fusion | bytes 263168 | tf_op jit(solution)/shard_map/jit(_take)/gather | solution.py:60
  5.6 0.5 collective-permute-start
  6.1 2.0 %collective-permute-start.1 = (bf16[256,256]{1,0:T(8,128)(2,1)S(1)}, bf16[256,256]{1,0:T(8,128)(2,1)}, u32[]{:S(2)}, u32[]{:S(2)}) collective-permute-start(bf16[256,256]{1,0:T(8,128)(2,1)S(1)} %convolution_convert_fusion.2), channel_id=1, source_target_pairs={{8,0},{16,8},{24,16},{0,24},{9,1},{17,9},{25,17},{1,25},{10,2},{18... | collective-permute-start | bytes 393224 | tf_op jit(solution)/shard_map/ppermute | solution.py:18
  8.2 0.6 gather_fusion.1
  8.9 0.8 slice_bitcast_fusion
  9.6 2.2 %collective-permute-start.2 = (bf16[128,256]{1,0:T(8,128)(2,1)}, bf16[128,256]{1,0:T(8,128)(2,1)}, u32[]{:S(2)}, u32[]{:S(2)}) collective-permute-start(bf16[128,256]{1,0:T(8,128)(2,1)} %get-tuple-element.59), channel_id=1, source_target_pairs={{0,1},{1,2},{2,3},{3,4},{4,5},{5,6},{6,7},{7,0},{8,9},{9,10},{10,1... | collective-permute-start | bytes 196616 | tf_op jit(solution)/shard_map/ppermute | solution.py:87
  11.9 1.6 %collective-permute-start.3 = (bf16[128,256]{1,0:T(8,128)(2,1)}, bf16[128,256]{1,0:T(8,128)(2,1)}, u32[]{:S(2)}, u32[]{:S(2)}) collective-permute-start(bf16[128,256]{1,0:T(8,128)(2,1)} %get-tuple-element.58), channel_id=1, source_target_pairs={{0,2},{1,3},{2,4},{3,5},{4,6},{5,7},{6,0},{7,1},{8,10},{9,11},{10,... | collective-permute-start | bytes 196616 | tf_op jit(solution)/shard_map/ppermute | solution.py:87
  13.4 2.6 %collective-permute-start.4 = (bf16[128,256]{1,0:T(8,128)(2,1)}, bf16[128,256]{1,0:T(8,128)(2,1)}, u32[]{:S(2)}, u32[]{:S(2)}) collective-permute-start(bf16[128,256]{1,0:T(8,128)(2,1)} %get-tuple-element.57), channel_id=1, source_target_pairs={{0,3},{1,4},{2,5},{3,6},{4,7},{5,0},{6,1},{7,2},{8,11},{9,12},{10,... | collective-permute-start | bytes 196616 | tf_op jit(solution)/shard_map/ppermute | solution.py:87
  16.8 0.9 %fusion = f32[2,7,128,128]{3,1,2,0:T(8,128)S(1)} fusion(bf16[40,128,128]{2,1,0:T(8,128)(2,1)S(1)} %copy-done.2, pred[40]{0:T(512)(128)(4,1)S(1)} %iota_compare_fusion.3, pred[40,7]{0,1:T(8,128)(4,1)S(1)} %broadcast_compare_fusion, pred[40,2]{0,1:T(4,128)(4,1)S(1)} %iota_compare_fusion.1), kind=kOutput, calls=%fused_computation.8 | convolution fusion | flops 18351200 | bytes 2228624 | tf_op jit(solution)/shard_map/krs,kab->rasb/dot_general | solution.py:100
  17.9 0.5 copy-done.13
  19.3 1.3 %copy.38 = bf16[2,128,7,128]{1,0,3,2:T(2,128)(2,1)} copy(bf16[2,128,7,128]{3,1,2,0:T(8,128)(2,1)S(1)} %bitcast.141) | data formatting | bytes 917504 | tf_op jit(solution)/shard_map/convert_element_type | solution.py:103
  20.5 1.2 %copy.39 = bf16[2,128,7,128]{1,0,3,2:T(2,128)(2,1)} copy(bf16[2,128,7,128]{3,1,2,0:T(8,128)(2,1)S(1)} %fusion.5) | data formatting | bytes 917504 | tf_op jit(solution)/shard_map/convert_element_type | solution.py:104
  21.8 1.2 %gather_fusion.4 = bf16[256,256]{1,0:T(8,128)(2,1)S(1)} fusion(bf16[256,256]{1,0:T(8,128)(2,1)S(1)} %copy-done.1, s32[1024]{0:T(1024)S(1)} %get-tuple-element.71), kind=kCustom, calls=%fused_computation.2.clone | custom fusion | bytes 263168 | tf_op jit(solution)/shard_map/jit(_take)/gather | solution.py:110
  23.5 0.5 copy-done.11
  23.9 1.2 %collective-permute-start.5 = (bf16[128,256]{1,0:T(8,128)(2,1)S(1)}, bf16[128,256]{1,0:T(8,128)(2,1)S(1)}, u32[]{:S(2)}, u32[]{:S(2)}) collective-permute-start(bf16[128,256]{1,0:T(8,128)(2,1)S(1)} %copy-done.11), channel_id=1, source_target_pairs={{0,4},{1,5},{2,6},{3,7},{4,0},{5,1},{6,2},{7,3},{8,12},{9,13},{10,... | collective-permute-start | bytes 196616 | tf_op jit(solution)/shard_map/ppermute | solution.py:87
  25.2 0.8 bitcast_dynamic-update-slice_fusion.13
  26.0 2.7 %collective-permute-start.6 = (bf16[128,256]{1,0:T(8,128)(2,1)S(1)}, bf16[128,256]{1,0:T(8,128)(2,1)S(1)}, u32[]{:S(2)}, u32[]{:S(2)}) collective-permute-start(bf16[128,256]{1,0:T(8,128)(2,1)S(1)} %copy-done.10), channel_id=1, source_target_pairs={{0,5},{1,6},{2,7},{3,0},{4,1},{5,2},{6,3},{7,4},{8,13},{9,14},{10,... | collective-permute-start | bytes 196616 | tf_op jit(solution)/shard_map/ppermute | solution.py:87
  28.7 0.8 bitcast_dynamic-update-slice_fusion.12
  29.6 1.4 %collective-permute-start.7 = (bf16[128,256]{1,0:T(8,128)(2,1)S(1)}, bf16[128,256]{1,0:T(8,128)(2,1)S(1)}, u32[]{:S(2)}, u32[]{:S(2)}) collective-permute-start(bf16[128,256]{1,0:T(8,128)(2,1)S(1)} %copy-done.9), channel_id=1, source_target_pairs={{0,6},{1,7},{2,0},{3,1},{4,2},{5,3},{6,4},{7,5},{8,14},{9,15},{10,... | collective-permute-start | bytes 196616 | tf_op jit(solution)/shard_map/ppermute | solution.py:87
  31.0 0.8 bitcast_dynamic-update-slice_fusion.11
  31.8 1.5 %collective-permute-start.8 = (bf16[128,256]{1,0:T(8,128)(2,1)S(1)}, bf16[128,256]{1,0:T(8,128)(2,1)S(1)}, u32[]{:S(2)}, u32[]{:S(2)}) collective-permute-start(bf16[128,256]{1,0:T(8,128)(2,1)S(1)} %copy-done.8), channel_id=1, source_target_pairs={{0,7},{1,0},{2,1},{3,2},{4,3},{5,4},{6,5},{7,6},{8,15},{9,8},{10,9... | collective-permute-start | bytes 196616 | tf_op jit(solution)/shard_map/ppermute | solution.py:87
  33.3 0.9 collective-permute-done.7
  34.2 1.9 %collective-permute-done.8 = bf16[128,256]{1,0:T(8,128)(2,1)S(1)} collective-permute-done((bf16[128,256]{1,0:T(8,128)(2,1)S(1)}, bf16[128,256]{1,0:T(8,128)(2,1)S(1)}, u32[]{:S(2)}, u32[]{:S(2)}) %collective-permute-start.8) | collective-permute-done | bytes 65568 | tf_op jit(solution)/shard_map/ppermute | solution.py:87
  36.9 1.3 %multiply_convert_fusion = (bf16[256,256]{1,0:T(8,128)(2,1)S(1)}, bf16[256,256]{1,0:T(8,128)(2,1)S(1)}) fusion(bf16[256,256]{1,0:T(8,128)(2,1)S(1)} %gather_fusion.4, pred[256]{0:T(512)(128)(4,1)S(1)} %compare_and_fusion.1, f32[256,256]{1,0:T(8,128)S(1)} %fusion.10, f32[256,256]{1,0:T(8,128)S(1)} %fusion.13, bf16[256,256]{1,0:T(8,128)(2,1)} %collective-permute-done.1, ...), kind=kOutput, calls=%fused_computation.48 | convolution fusion | flops 102825984 | bytes 1704192 | tf_op jit(solution)/shard_map/dot_general | solution.py:74
  39.1 4.2 %collective-permute-start.11 = (bf16[128,256]{1,0:T(8,128)(2,1)S(1)}, bf16[128,256]{1,0:T(8,128)(2,1)S(1)}, u32[]{:S(2)}, u32[]{:S(2)}) collective-permute-start(bf16[128,256]{1,0:T(8,128)(2,1)S(1)} %get-tuple-element.52), channel_id=1, source_target_pairs={{1,0},{2,1},{3,2},{4,3},{5,4},{6,5},{7,6},{0,7},{9,8},{10,9},{11,1... | collective-permute-start | bytes 196616 | tf_op jit(solution)/shard_map/ppermute | solution.py:130
  43.3 3.0 %collective-permute-start.14 = (bf16[128,256]{1,0:T(8,128)(2,1)S(1)}, bf16[128,256]{1,0:T(8,128)(2,1)S(1)}, u32[]{:S(2)}, u32[]{:S(2)}) collective-permute-start(bf16[128,256]{1,0:T(8,128)(2,1)S(1)} %get-tuple-element.49), channel_id=1, source_target_pairs={{4,0},{5,1},{6,2},{7,3},{0,4},{1,5},{2,6},{3,7},{12,8},{13,9},{14,... | collective-permute-start | bytes 196616 | tf_op jit(solution)/shard_map/ppermute | solution.py:130
  46.6 1.7 %collective-permute-start.16 = (bf16[128,256]{1,0:T(8,128)(2,1)S(1)}, bf16[128,256]{1,0:T(8,128)(2,1)S(1)}, u32[]{:S(2)}, u32[]{:S(2)}) collective-permute-start(bf16[128,256]{1,0:T(8,128)(2,1)S(1)} %get-tuple-element.47), channel_id=1, source_target_pairs={{6,0},{7,1},{0,2},{1,3},{2,4},{3,5},{4,6},{5,7},{14,8},{15,9},{8,1... | collective-permute-start | bytes 196616 | tf_op jit(solution)/shard_map/ppermute | solution.py:130
  48.3 1.5 %collective-permute-start.17 = (bf16[128,256]{1,0:T(8,128)(2,1)S(1)}, bf16[128,256]{1,0:T(8,128)(2,1)S(1)}, u32[]{:S(2)}, u32[]{:S(2)}) collective-permute-start(bf16[128,256]{1,0:T(8,128)(2,1)S(1)} %get-tuple-element.46), channel_id=1, source_target_pairs={{7,0},{0,1},{1,2},{2,3},{3,4},{4,5},{5,6},{6,7},{15,8},{8,9},{9,10... | collective-permute-start | bytes 196616 | tf_op jit(solution)/shard_map/ppermute | solution.py:130
  49.9 0.8 collective-permute-done.13
  50.7 0.7 collective-permute-done.14
  51.3 2.9 %collective-permute-done.15 = bf16[128,256]{1,0:T(8,128)(2,1)S(1)} collective-permute-done((bf16[128,256]{1,0:T(8,128)(2,1)S(1)}, bf16[128,256]{1,0:T(8,128)(2,1)S(1)}, u32[]{:S(2)}, u32[]{:S(2)}) %collective-permute-start.15) | collective-permute-done | bytes 65568 | tf_op jit(solution)/shard_map/ppermute | solution.py:130
  54.4 0.9 %collective-permute-done.17 = bf16[128,256]{1,0:T(8,128)(2,1)S(1)} collective-permute-done((bf16[128,256]{1,0:T(8,128)(2,1)S(1)}, bf16[128,256]{1,0:T(8,128)(2,1)S(1)}, u32[]{:S(2)}, u32[]{:S(2)}) %collective-permute-start.17) | collective-permute-done | bytes 65568 | tf_op jit(solution)/shard_map/ppermute | solution.py:130
  55.4 0.4 fusion.7
  56.3 1.0 %all_to_all.13 = f32[32,1,2048]{2,1,0:T(1,128)} reshape(f32[256,256]{1,0:T(8,128)S(1)} %fusion.32) | data formatting | bytes 524288 | tf_op jit(solution)/shard_map/all_to_all | solution.py:28
  57.3 4.5 %all-to-all-start = ((f32[32,1,2048]{2,1,0:T(1,128)}), f32[32,1,2048]{2,1,0:T(1,128)S(1)}, u32[]{:S(2)}, u32[]{:S(2)}) async-start(f32[32,1,2048]{2,1,0:T(1,128)} %all_to_all.13), calls=%async_computation | async-start | bytes 524288 | tf_op jit(solution)/shard_map/all_to_all | solution.py:28
  61.8 1.4 %scatter_custom_fusion = s32[256]{0:T(256)S(1)} fusion(s32[256]{0:T(256)S(1)} %bitcast.150, s32[256]{0:T(256)S(1)} %iota.51, s32[]{:T(128)} %constant.146.clone.1), kind=kCustom, calls=%fused_computation.122 | custom fusion | bytes 1028 | tf_op jit(solution)/shard_map/scatter | solution.py:58
  63.3 9.2 %all-to-all-done = f32[32,1,2048]{2,1,0:T(1,128)S(1)} async-done(((f32[32,1,2048]{2,1,0:T(1,128)}), f32[32,1,2048]{2,1,0:T(1,128)S(1)}, u32[]{:S(2)}, u32[]{:S(2)}) %all-to-all-start) | async-done | bytes 262176 | tf_op jit(solution)/shard_map/all_to_all | solution.py:28
  72.6 0.8 broadcast_in_dim.52
  73.5 2.6 %all-to-all-start.1 = ((f32[32,1,2048]{2,1,0:T(1,128)}), f32[32,1,2048]{2,1,0:T(1,128)S(1)}, u32[]{:S(2)}, u32[]{:S(2)}) async-start(f32[32,1,2048]{2,1,0:T(1,128)} %broadcast_in_dim.52), calls=%async_computation.1 | async-start | bytes 524288 | tf_op jit(solution)/shard_map/all_to_all | solution.py:31
  76.1 1.2 %gather_fusion.3 = bf16[256,256]{1,0:T(8,128)(2,1)S(1)} fusion(bf16[256,256]{1,0:T(8,128)(2,1)S(1)} %get-tuple-element.63, s32[1024]{0:T(1024)S(1)} %pad_clamp_fusion), kind=kCustom, calls=%fused_computation.1.clone | custom fusion | bytes 263168 | tf_op jit(solution)/shard_map/jit(_take)/gather | solution.py:109
  77.4 1.2 %gather_fusion.5 = bf16[256,256]{1,0:T(8,128)(2,1)S(1)} fusion(bf16[256,256]{1,0:T(8,128)(2,1)S(1)} %convolution_convert_fusion.1, s32[1024]{0:T(1024)S(1)} %pad_clamp_fusion), kind=kCustom, calls=%fused_computation.3.clone | custom fusion | bytes 263168 | tf_op jit(solution)/shard_map/jit(_take)/gather | solution.py:148
  78.6 0.8 broadcast_select_fusion
  79.4 7.3 %all-to-all-done.1 = f32[32,1,2048]{2,1,0:T(1,128)S(1)} async-done(((f32[32,1,2048]{2,1,0:T(1,128)}), f32[32,1,2048]{2,1,0:T(1,128)S(1)}, u32[]{:S(2)}, u32[]{:S(2)}) %all-to-all-start.1) | async-done | bytes 262176 | tf_op jit(solution)/shard_map/all_to_all | solution.py:31
  86.7 0.8 multiply_reduce_fusion
  87.4 0.7 mul.28
  (95 shorter events, 5.2 us)
Async XLA Ops:
  0.6 4.7 %copy-start = (bf16[256,256]{1,0:T(8,128)(2,1)S(1)}, bf16[256,256]{1,0:T(8,128)(2,1)}, u32[]{:S(2)}) copy-start(bf16[256,256]{1,0:T(8,128)(2,1)} %param.22) | copy-start | bytes 393220
  5.3 3.4 %copy-start.3 = (bf16[256,256]{1,0:T(8,128)(2,1)}, bf16[256,256]{1,0:T(8,128)(2,1)S(1)}, u32[]{:S(2)}) copy-start(bf16[256,256]{1,0:T(8,128)(2,1)S(1)} %gather_fusion.2) | copy-start | bytes 393220
  5.6 31.3 %collective-permute-start = (bf16[256,256]{1,0:T(8,128)(2,1)S(1)}, bf16[256,256]{1,0:T(8,128)(2,1)}, u32[]{:S(2)}, u32[]{:S(2)}) collective-permute-start(bf16[256,256]{1,0:T(8,128)(2,1)S(1)} %convolution_convert_fusion.2), channel_id=1, source_target_pairs={{0,8},{8,16},{16,24},{24,0},{1,9},{9,17},{17,25},{25,1},{2,10},{10... | collective-permute-start | bytes 393224 | tf_op jit(solution)/shard_map/ppermute | solution.py:16
  6.1 30.8 %collective-permute-start.1 = (bf16[256,256]{1,0:T(8,128)(2,1)S(1)}, bf16[256,256]{1,0:T(8,128)(2,1)}, u32[]{:S(2)}, u32[]{:S(2)}) collective-permute-start(bf16[256,256]{1,0:T(8,128)(2,1)S(1)} %convolution_convert_fusion.2), channel_id=1, source_target_pairs={{8,0},{16,8},{24,16},{0,24},{9,1},{17,9},{25,17},{1,25},{10,2},{18... | collective-permute-start | bytes 393224 | tf_op jit(solution)/shard_map/ppermute | solution.py:18
  8.1 7.9 %copy-start.14 = (s32[40,2]{0,1:T(2,128)S(1)}, s32[40,2]{0,1:T(2,128)}, u32[]{:S(2)}) copy-start(s32[40,2]{0,1:T(2,128)} %param.27) | copy-start | bytes 964
  8.1 8.6 %copy-start.2 = (bf16[40,128,128]{2,1,0:T(8,128)(2,1)S(1)}, bf16[40,128,128]{2,1,0:T(8,128)(2,1)}, u32[]{:S(2)}) copy-start(bf16[40,128,128]{2,1,0:T(8,128)(2,1)} %param.26) | copy-start | bytes 3932164
  9.6 13.8 %collective-permute-start.2 = (bf16[128,256]{1,0:T(8,128)(2,1)}, bf16[128,256]{1,0:T(8,128)(2,1)}, u32[]{:S(2)}, u32[]{:S(2)}) collective-permute-start(bf16[128,256]{1,0:T(8,128)(2,1)} %get-tuple-element.59), channel_id=1, source_target_pairs={{0,1},{1,2},{2,3},{3,4},{4,5},{5,6},{6,7},{7,0},{8,9},{9,10},{10,1... | collective-permute-start | bytes 196616 | tf_op jit(solution)/shard_map/ppermute | solution.py:87
  11.9 14.2 %collective-permute-start.3 = (bf16[128,256]{1,0:T(8,128)(2,1)}, bf16[128,256]{1,0:T(8,128)(2,1)}, u32[]{:S(2)}, u32[]{:S(2)}) collective-permute-start(bf16[128,256]{1,0:T(8,128)(2,1)} %get-tuple-element.58), channel_id=1, source_target_pairs={{0,2},{1,3},{2,4},{3,5},{4,6},{5,7},{6,0},{7,1},{8,10},{9,11},{10,... | collective-permute-start | bytes 196616 | tf_op jit(solution)/shard_map/ppermute | solution.py:87
  13.4 16.1 %collective-permute-start.4 = (bf16[128,256]{1,0:T(8,128)(2,1)}, bf16[128,256]{1,0:T(8,128)(2,1)}, u32[]{:S(2)}, u32[]{:S(2)}) collective-permute-start(bf16[128,256]{1,0:T(8,128)(2,1)} %get-tuple-element.57), channel_id=1, source_target_pairs={{0,3},{1,4},{2,5},{3,6},{4,7},{5,0},{6,1},{7,2},{8,11},{9,12},{10,... | collective-permute-start | bytes 196616 | tf_op jit(solution)/shard_map/ppermute | solution.py:87
  17.7 0.7 copy-start.13
  17.7 1.0 %copy-start.5 = (bf16[12,128,128]{2,1,0:T(8,128)(2,1)S(1)}, bf16[12,128,128]{2,1,0:T(8,128)(2,1)}, u32[]{:S(2)}) copy-start(bf16[12,128,128]{2,1,0:T(8,128)(2,1)} %param.24) | copy-start | bytes 1179652
  19.1 2.7 %copy-start.1 = (bf16[256,256]{1,0:T(8,128)(2,1)S(1)}, bf16[256,256]{1,0:T(8,128)(2,1)}, u32[]{:S(2)}) copy-start(bf16[256,256]{1,0:T(8,128)(2,1)} %param.23) | copy-start | bytes 393220
  23.1 0.8 copy-start.11
  23.1 2.9 %copy-start.10 = (bf16[128,256]{1,0:T(8,128)(2,1)S(1)}, bf16[128,256]{1,0:T(8,128)(2,1)}, u32[]{:S(2)}) copy-start(bf16[128,256]{1,0:T(8,128)(2,1)} %get-tuple-element.55) | copy-start | bytes 196612
  23.1 6.4 %copy-start.9 = (bf16[128,256]{1,0:T(8,128)(2,1)S(1)}, bf16[128,256]{1,0:T(8,128)(2,1)}, u32[]{:S(2)}) copy-start(bf16[128,256]{1,0:T(8,128)(2,1)} %get-tuple-element.54) | copy-start | bytes 196612
  23.1 8.7 %copy-start.8 = (bf16[128,256]{1,0:T(8,128)(2,1)S(1)}, bf16[128,256]{1,0:T(8,128)(2,1)}, u32[]{:S(2)}) copy-start(bf16[128,256]{1,0:T(8,128)(2,1)} %get-tuple-element.53) | copy-start | bytes 196612
  23.1 13.0 %copy-start.6 = (bf16[2,128,7,128]{1,0,3,2:T(2,128)(2,1)S(1)}, bf16[2,128,7,128]{1,0,3,2:T(2,128)(2,1)}, u32[]{:S(2)}) copy-start(bf16[2,128,7,128]{1,0,3,2:T(2,128)(2,1)} %copy.38) | copy-start | bytes 1376260
  23.5 13.0 %copy-start.7 = (bf16[2,128,7,128]{1,0,3,2:T(2,128)(2,1)S(1)}, bf16[2,128,7,128]{1,0,3,2:T(2,128)(2,1)}, u32[]{:S(2)}) copy-start(bf16[2,128,7,128]{1,0,3,2:T(2,128)(2,1)} %copy.39) | copy-start | bytes 1376260
  23.9 7.9 %collective-permute-start.5 = (bf16[128,256]{1,0:T(8,128)(2,1)S(1)}, bf16[128,256]{1,0:T(8,128)(2,1)S(1)}, u32[]{:S(2)}, u32[]{:S(2)}) collective-permute-start(bf16[128,256]{1,0:T(8,128)(2,1)S(1)} %copy-done.11), channel_id=1, source_target_pairs={{0,4},{1,5},{2,6},{3,7},{4,0},{5,1},{6,2},{7,3},{8,12},{9,13},{10,... | collective-permute-start | bytes 196616 | tf_op jit(solution)/shard_map/ppermute | solution.py:87
  26.0 7.3 %collective-permute-start.6 = (bf16[128,256]{1,0:T(8,128)(2,1)S(1)}, bf16[128,256]{1,0:T(8,128)(2,1)S(1)}, u32[]{:S(2)}, u32[]{:S(2)}) collective-permute-start(bf16[128,256]{1,0:T(8,128)(2,1)S(1)} %copy-done.10), channel_id=1, source_target_pairs={{0,5},{1,6},{2,7},{3,0},{4,1},{5,2},{6,3},{7,4},{8,13},{9,14},{10,... | collective-permute-start | bytes 196616 | tf_op jit(solution)/shard_map/ppermute | solution.py:87
  29.6 4.6 %collective-permute-start.7 = (bf16[128,256]{1,0:T(8,128)(2,1)S(1)}, bf16[128,256]{1,0:T(8,128)(2,1)S(1)}, u32[]{:S(2)}, u32[]{:S(2)}) collective-permute-start(bf16[128,256]{1,0:T(8,128)(2,1)S(1)} %copy-done.9), channel_id=1, source_target_pairs={{0,6},{1,7},{2,0},{3,1},{4,2},{5,3},{6,4},{7,5},{8,14},{9,15},{10,... | collective-permute-start | bytes 196616 | tf_op jit(solution)/shard_map/ppermute | solution.py:87
  31.8 4.3 %collective-permute-start.8 = (bf16[128,256]{1,0:T(8,128)(2,1)S(1)}, bf16[128,256]{1,0:T(8,128)(2,1)S(1)}, u32[]{:S(2)}, u32[]{:S(2)}) collective-permute-start(bf16[128,256]{1,0:T(8,128)(2,1)S(1)} %copy-done.8), channel_id=1, source_target_pairs={{0,7},{1,0},{2,1},{3,2},{4,3},{5,4},{6,5},{7,6},{8,15},{9,8},{10,9... | collective-permute-start | bytes 196616 | tf_op jit(solution)/shard_map/ppermute | solution.py:87
  39.1 7.5 %collective-permute-start.11 = (bf16[128,256]{1,0:T(8,128)(2,1)S(1)}, bf16[128,256]{1,0:T(8,128)(2,1)S(1)}, u32[]{:S(2)}, u32[]{:S(2)}) collective-permute-start(bf16[128,256]{1,0:T(8,128)(2,1)S(1)} %get-tuple-element.52), channel_id=1, source_target_pairs={{1,0},{2,1},{3,2},{4,3},{5,4},{6,5},{7,6},{0,7},{9,8},{10,9},{11,1... | collective-permute-start | bytes 196616 | tf_op jit(solution)/shard_map/ppermute | solution.py:130
  43.3 5.0 %collective-permute-start.12 = (bf16[128,256]{1,0:T(8,128)(2,1)S(1)}, bf16[128,256]{1,0:T(8,128)(2,1)S(1)}, u32[]{:S(2)}, u32[]{:S(2)}) collective-permute-start(bf16[128,256]{1,0:T(8,128)(2,1)S(1)} %get-tuple-element.51), channel_id=1, source_target_pairs={{2,0},{3,1},{4,2},{5,3},{6,4},{7,5},{0,6},{1,7},{10,8},{11,9},{12,... | collective-permute-start | bytes 196616 | tf_op jit(solution)/shard_map/ppermute | solution.py:130
  43.3 7.4 %collective-permute-start.13 = (bf16[128,256]{1,0:T(8,128)(2,1)S(1)}, bf16[128,256]{1,0:T(8,128)(2,1)S(1)}, u32[]{:S(2)}, u32[]{:S(2)}) collective-permute-start(bf16[128,256]{1,0:T(8,128)(2,1)S(1)} %get-tuple-element.50), channel_id=1, source_target_pairs={{3,0},{4,1},{5,2},{6,3},{7,4},{0,5},{1,6},{2,7},{11,8},{12,9},{13,... | collective-permute-start | bytes 196616 | tf_op jit(solution)/shard_map/ppermute | solution.py:130
  43.3 8.0 %collective-permute-start.14 = (bf16[128,256]{1,0:T(8,128)(2,1)S(1)}, bf16[128,256]{1,0:T(8,128)(2,1)S(1)}, u32[]{:S(2)}, u32[]{:S(2)}) collective-permute-start(bf16[128,256]{1,0:T(8,128)(2,1)S(1)} %get-tuple-element.49), channel_id=1, source_target_pairs={{4,0},{5,1},{6,2},{7,3},{0,4},{1,5},{2,6},{3,7},{12,8},{13,9},{14,... | collective-permute-start | bytes 196616 | tf_op jit(solution)/shard_map/ppermute | solution.py:130
  46.3 8.0 %collective-permute-start.15 = (bf16[128,256]{1,0:T(8,128)(2,1)S(1)}, bf16[128,256]{1,0:T(8,128)(2,1)S(1)}, u32[]{:S(2)}, u32[]{:S(2)}) collective-permute-start(bf16[128,256]{1,0:T(8,128)(2,1)S(1)} %get-tuple-element.48), channel_id=1, source_target_pairs={{5,0},{6,1},{7,2},{0,3},{1,4},{2,5},{3,6},{4,7},{13,8},{14,9},{15,... | collective-permute-start | bytes 196616 | tf_op jit(solution)/shard_map/ppermute | solution.py:130
  46.6 7.9 %collective-permute-start.16 = (bf16[128,256]{1,0:T(8,128)(2,1)S(1)}, bf16[128,256]{1,0:T(8,128)(2,1)S(1)}, u32[]{:S(2)}, u32[]{:S(2)}) collective-permute-start(bf16[128,256]{1,0:T(8,128)(2,1)S(1)} %get-tuple-element.47), channel_id=1, source_target_pairs={{6,0},{7,1},{0,2},{1,3},{2,4},{3,5},{4,6},{5,7},{14,8},{15,9},{8,1... | collective-permute-start | bytes 196616 | tf_op jit(solution)/shard_map/ppermute | solution.py:130
  48.3 7.0 %collective-permute-start.17 = (bf16[128,256]{1,0:T(8,128)(2,1)S(1)}, bf16[128,256]{1,0:T(8,128)(2,1)S(1)}, u32[]{:S(2)}, u32[]{:S(2)}) collective-permute-start(bf16[128,256]{1,0:T(8,128)(2,1)S(1)} %get-tuple-element.46), channel_id=1, source_target_pairs={{7,0},{0,1},{1,2},{2,3},{3,4},{4,5},{5,6},{6,7},{15,8},{8,9},{9,10... | collective-permute-start | bytes 196616 | tf_op jit(solution)/shard_map/ppermute | solution.py:130
  50.7 5.1 %collective-permute-start.10 = (bf16[256,256]{1,0:T(8,128)(2,1)S(1)}, bf16[256,256]{1,0:T(8,128)(2,1)S(1)}, u32[]{:S(2)}, u32[]{:S(2)}) collective-permute-start(bf16[256,256]{1,0:T(8,128)(2,1)S(1)} %get-tuple-element.61), channel_id=1, source_target_pairs={{8,0},{16,8},{24,16},{0,24},{9,1},{17,9},{25,17},{1,25},{10,2},{18... | collective-permute-start | bytes 393224 | tf_op jit(solution)/shard_map/ppermute | solution.py:18
  51.3 4.6 %collective-permute-start.9 = (bf16[256,256]{1,0:T(8,128)(2,1)S(1)}, bf16[256,256]{1,0:T(8,128)(2,1)S(1)}, u32[]{:S(2)}, u32[]{:S(2)}) collective-permute-start(bf16[256,256]{1,0:T(8,128)(2,1)S(1)} %get-tuple-element.60), channel_id=1, source_target_pairs={{0,8},{8,16},{16,24},{24,0},{1,9},{9,17},{17,25},{25,1},{2,10},{10... | collective-permute-start | bytes 393224 | tf_op jit(solution)/shard_map/ppermute | solution.py:16
  51.3 4.6 %copy-start.4 = (bf16[256,256]{1,0:T(8,128)(2,1)S(1)}, bf16[256,256]{1,0:T(8,128)(2,1)}, u32[]{:S(2)}) copy-start(bf16[256,256]{1,0:T(8,128)(2,1)} %copy-done.3) | copy-start | bytes 393220
  55.7 6.1 %copy-start.12 = (s32[1,256]{1,0:T(1,128)S(1)}, s32[1,256]{1,0:T(1,128)}, u32[]{:S(2)}) copy-start(s32[1,256]{1,0:T(1,128)} %param.30) | copy-start | bytes 3076
  57.3 15.2 %all-to-all-start = ((f32[32,1,2048]{2,1,0:T(1,128)}), f32[32,1,2048]{2,1,0:T(1,128)S(1)}, u32[]{:S(2)}, u32[]{:S(2)}) async-start(f32[32,1,2048]{2,1,0:T(1,128)} %all_to_all.13), calls=%async_computation | async-start | bytes 524288 | tf_op jit(solution)/shard_map/all_to_all | solution.py:28
  73.5 13.2 %all-to-all-start.1 = ((f32[32,1,2048]{2,1,0:T(1,128)}), f32[32,1,2048]{2,1,0:T(1,128)S(1)}, u32[]{:S(2)}, u32[]{:S(2)}) async-start(f32[32,1,2048]{2,1,0:T(1,128)} %broadcast_in_dim.52), calls=%async_computation.1 | async-start | bytes 524288 | tf_op jit(solution)/shard_map/all_to_all | solution.py:31

commit v4 on v2

--- a/solution.py
+++ b/solution.py
@@ -70,9 +70,11 @@
         .astype(jnp.bfloat16)
         .reshape(row_count, ext_count)
     )
-    extended = padded_2(hidden, (("row", 0),), BW)
+    paired = padded_2(jnp.concatenate([hidden, x_band], axis=1), (("row", 0),), BW)
+    extended = paired[:, :width_feat]
+    x_extended = paired[:, width_feat:]
     mixed = jnp.dot(band_dense, extended, preferred_element_type=jnp.float32)
-    blocks = hidden.reshape(tile_rows, tile_size, width_feat)
+    blocks = jnp.concatenate([hidden, x_band], axis=1).reshape(tile_rows, tile_size, 2 * width_feat)
     giving = send_lists[0]
     outgoing = jnp.where(
         (giving >= 0)[:, None, None],
@@ -95,7 +97,9 @@
     ).reshape(row_count, peers * tile_size)
     dense_high = bound_dense.astype(jnp.bfloat16)
     dense_low = (bound_dense - dense_high.astype(jnp.float32)).astype(jnp.bfloat16)
-    arrived_rows = arrived.reshape(peers * tile_size, width_feat)
+    arrived_pairs = arrived.reshape(peers * tile_size, 2 * width_feat)
+    arrived_rows = arrived_pairs[:, :width_feat]
+    arrived_x = arrived_pairs[:, width_feat:]
     mixed = mixed + jnp.dot(dense_high, arrived_rows, preferred_element_type=jnp.float32)
     mixed = mixed + jnp.dot(dense_low, arrived_rows, preferred_element_type=jnp.float32)
     out_band = jax.nn.silu(mixed).astype(jnp.bfloat16)
@@ -110,14 +114,26 @@
         jnp.bfloat16
     )
     padded = padded_2(rim_terms, (("row", 0),), BW)
+    own_terms = ext_grad[BW : BW + row_count]
+    own_high = own_terms.astype(jnp.bfloat16)
+    own_low = (own_terms - own_high.astype(jnp.float32)).astype(jnp.bfloat16)
+    contract_rows = (((0,), (0,)), ((), ()))
     grad_hidden = ext_grad[BW : BW + row_count]
     grad_hidden = grad_hidden.at[:BW].add(padded[:BW].astype(jnp.float32))
     grad_hidden = grad_hidden.at[row_count - BW :].add(padded[3 * BW :].astype(jnp.float32))
-    contract_rows = (((0,), (0,)), ((), ()))
     owner_terms = lax.dot_general(
         dense_high, slope, contract_rows, preferred_element_type=jnp.float32
     ) + lax.dot_general(dense_low, slope, contract_rows, preferred_element_type=jnp.float32)
-    to_owner = owner_terms.astype(jnp.bfloat16).reshape(peers, tile_size, width_feat)
+    owner_round = owner_terms.astype(jnp.bfloat16)
+    to_owner = owner_round.reshape(peers, tile_size, width_feat)
+    x_rims = jnp.concatenate([x_extended[:BW], x_extended[BW + row_count :]], axis=0)
+    x_own = x_extended[BW : BW + row_count]
+    partial_weight = (
+        lax.dot_general(x_own, own_high, contract_rows, preferred_element_type=jnp.float32)
+        + lax.dot_general(x_own, own_low, contract_rows, preferred_element_type=jnp.float32)
+        + lax.dot_general(x_rims, rim_terms, contract_rows, preferred_element_type=jnp.float32)
+        + lax.dot_general(arrived_x, owner_round, contract_rows, preferred_element_type=jnp.float32)
+    )
     returned = lax.all_to_all(to_owner, "col", split_axis=0, concat_axis=0, tiled=True)
     block_onehot = (giving[None, :] == tile_range[:, None]).astype(jnp.bfloat16)
     from_peers = jnp.einsum(
@@ -125,9 +141,6 @@
     )
     grad_hidden = grad_hidden + from_peers.reshape(row_count, width_feat)
     grad_round = grad_hidden.astype(jnp.bfloat16)
-    partial_weight = lax.dot_general(
-        x_band, grad_round, (((0,), (0,)), ((), ())), preferred_element_type=jnp.float32
-    )
     nodes_all = row_count * lax.axis_size("row") * peers
     weight_grad = spread_sum(partial_weight, ("row", "col")) * nodes_all ** (-0.5)
     feat_band = lax.dot_general(

time: 83.1 us -> 97.8 us (1.18)
  blocking collectives: 0 us -> 13 us
  starting transfers between devices: 19.9 us -> 15.9 us
  matrix products: 7.54 us -> 10.2 us
  local copies, waits for them, and re-layouts: 10.9 us -> 12.9 us
    all_to_all x0 -> x1, blocking collectives: none -> 13 us  [spread_sum(): gathered = lax.all_to_all(pieces, axes, 0, 0, tiled=True)]
    all_to_all x1, waiting for transfers between devices: 9.33 us -> 19.7 us  [on_device(): lax.all_to_all(outgoing, 'col', split_axis=0, concat_axis=0, tiled=True)]
    all_to_all x1 -> x0, waiting for transfers between devices: 9.19 us -> none  [spread_sum(): gathered = lax.all_to_all(pieces, axes, 0, 0, tiled=True)]
    all_to_all x1 -> x0, starting transfers between devices: 2.72 us -> none  [spread_sum(): gathered = lax.all_to_all(pieces, axes, 0, 0, tiled=True)]
    slice x0 -> x3, local copies, waits for them, and re-layouts: none -> 1.74 us  [the longest x1 1.73 us: on_device(): x_extended[:BW]]
    dot_general x1 -> x4, matrix products: 0.31 us -> 2.02 us  [the longest x1 1.42 us: on_device(): lax.dot_general(arrived_x, owner_round, contract_rows, preferred_element_...]
    all_to_all x1, waiting for transfers between devices: 12.5 us -> 11.2 us  [on_device(): lax.all_to_all(to_owner, 'col', split_axis=0, concat_axis=0, tiled=True)]
    dot_general x1, matrix products: 0.36 us -> 1.35 us  [on_device(): jnp.einsum('krc,kab->racb', band_onehot, band_tiles, preferred_element_ty...]
  transfers between devices with their start and end apart: 8 -> 7, of which waited for: 4 -> 3; matrix products, arithmetic and copies ran while one was open for 15% -> 16% of each run, Pallas kernels for 0% -> 0%
where the time goes in v4:
time: 97.8 us; the launch traced here: 97.2 us
  waiting for transfers between devices  38.8 us (40%)
  starting transfers between devices  15.9 us (16%)
  blocking collectives  13 us (13%)
  local copies, waits for them, and re-layouts  12.9 us (13%)
  matrix products  10.2 us (10%)
  other arithmetic  4.48 us (5%)
  between operations  1.82 us (2%)
    all_to_all x1, waiting for transfers between devices, on_device(): lax.all_to_all(outgoing, 'col', split_axis=0, concat_axis=0, tiled=True)  19.7 us
    all_to_all x1, blocking collectives, spread_sum(): gathered = lax.all_to_all(pieces, axes, 0, 0, tiled=True)  13 us
    all_to_all x1, waiting for transfers between devices, on_device(): lax.all_to_all(to_owner, 'col', split_axis=0, concat_axis=0, tiled=True)  11.2 us
    all_to_all x1, waiting for transfers between devices, spread_sum(): return lax.all_to_all(copies, axes, 0, 0, tiled=True).reshape(value.shape)  7.95 us
    all_to_all x1, starting transfers between devices, on_device(): lax.all_to_all(outgoing, 'col', split_axis=0, concat_axis=0, tiled=True)  5.94 us
    all_to_all x1, starting transfers between devices, on_device(): lax.all_to_all(to_owner, 'col', split_axis=0, concat_axis=0, tiled=True)  3.49 us
    all_to_all x1, starting transfers between devices, spread_sum(): return lax.all_to_all(copies, axes, 0, 0, tiled=True).reshape(value.shape)  3.4 us
    ppermute x2, starting transfers between devices, padded_2(): lax.ppermute(head, axis, [((i + 1) % count, i) for i in range(count)])  3.06 us
  transfers between devices with their start and end apart: 7, of which 3 were waited for; matrix products, arithmetic and copies ran while one was open for 16% of the time, Pallas kernels for 0%

profile of v4, /device:TPU:0, one launch (start us, length us, event | category | flops | bytes accessed | tf_op | source)
XLA Modules:
  0.0 97.2 jit_solution(4225636215159345098)
XLA Ops:
  0.6 0.0 copy-start
  0.6 0.7 compare_select_fusion.2
  1.4 0.7 compare_and_fusion.1
  2.1 1.9 %gather_fusion.1 = bf16[256,256]{1,0:T(8,128)(2,1)S(1)} fusion(bf16[256,256]{1,0:T(8,128)(2,1)} %param.21, s32[1024]{0:T(1024)S(1)} %pad_clamp_fusion.2), kind=kCustom, calls=%fused_computation.clone | custom fusion | bytes 263168 | tf_op jit(solution)/shard_map/jit(_take)/gather | solution.py:60
  4.0 0.1 copy.27
  4.1 0.2 convolution_convert_fusion.2
  4.4 2.5 %collective-permute-start.1 = (bf16[256,512]{0,1:T(8,128)(2,1)S(1)}, bf16[256,512]{0,1:T(8,128)(2,1)S(1)}, u32[]{:S(2)}, u32[]{:S(2)}) collective-permute-start(bf16[256,512]{0,1:T(8,128)(2,1)S(1)} %pad_maximum_fusion.6), channel_id=1, source_target_pairs={{8,0},{16,8},{24,16},{0,24},{9,1},{17,9},{25,17},{1,25},{10,2},{18... | collective-permute-start | bytes 786440 | tf_op jit(solution)/shard_map/ppermute | solution.py:18
  6.8 0.1 copy.36
  7.0 0.6 gather_fusion
  7.7 1.2 %select_select_fusion = bf16[8,128,512]{2,1,0:T(8,128)(2,1)} fusion(bf16[8,128,512]{2,1,0:T(8,128)(2,1)S(1)} %gather_fusion, pred[8]{0:T(512)(128)(4,1)S(1)} %get-tuple-element.55, pred[8]{0:T(512)(128)(4,1)S(1)} %get-tuple-element.54), kind=kLoop, calls=%fused_computation.22 | loop fusion | flops 1048576 | bytes 2097168 | tf_op jit(solution)/shard_map/jit(_where)/select_n | solution.py:79
  8.9 5.9 %all-to-all-start = ((bf16[8,128,512]{2,1,0:T(8,128)(2,1)}), bf16[8,128,512]{2,1,0:T(8,128)(2,1)S(1)}, u32[]{:S(2)}, u32[]{:S(2)}) async-start(bf16[8,128,512]{2,1,0:T(8,128)(2,1)} %select_select_fusion), calls=%async_computation | async-start | bytes 2097152 | tf_op jit(solution)/shard_map/all_to_all | solution.py:84
  15.6 2.2 %fusion = f32[2,8,128,128]{3,1,2,0:T(8,128)S(1)} fusion(bf16[40,128,128]{2,1,0:T(8,128)(2,1)} %param.26, pred[40]{0:T(512)(128)(4,1)S(1)} %iota_compare_fusion.4, pred[40,8]{0,1:T(8,128)(4,1)S(1)} %iota_compare_fusion, pred[40,2]{0,1:T(4,128)(4,1)S(1)} %iota_compare_fusion.2), kind=kOutput, calls=%fused_computation.7 | convolution fusion | flops 20972800 | bytes 2359736 | tf_op jit(solution)/shard_map/krs,kab->rasb/dot_general | solution.py:95
  17.8 1.8 %gather_fusion.3 = bf16[256,256]{1,0:T(8,128)(2,1)} fusion(bf16[256,256]{1,0:T(8,128)(2,1)S(1)} %copy-done.1, s32[1024]{0:T(1024)S(1)} %pad_clamp_fusion.2), kind=kCustom, calls=%fused_computation.2.clone | custom fusion | bytes 263168 | tf_op jit(solution)/shard_map/jit(_take)/gather | solution.py:107
  19.7 1.4 %convolution_convert_fusion = bf16[2,6,128,128]{3,1,2,0:T(8,128)(2,1)S(1)} fusion(bf16[12,128,128]{2,1,0:T(8,128)(2,1)} %param.24, pred[12,6]{0,1:T(8,128)(4,1)S(1)} %iota_compare_fusion.1, pred[12,2]{0,1:T(4,128)(4,1)S(1)} %iota_compare_fusion.3), kind=kOutput, calls=%fused_computation.10 | convolution fusion | flops 4915344 | bytes 786528 | tf_op jit(solution)/shard_map/krc,kab->racb/dot_general | solution.py:69
  21.1 1.7 %slice.109 = bf16[256,256]{0,1:T(8,128)(2,1)} slice(bf16[256,512]{0,1:T(8,128)(2,1)} %collective-permute-done), slice={[0:256], [256:512]} | slice | bytes 262144 | tf_op jit(solution)/shard_map/slice | solution.py:129
  22.8 19.7 %all-to-all-done = bf16[8,128,512]{2,1,0:T(8,128)(2,1)S(1)} async-done(((bf16[8,128,512]{2,1,0:T(8,128)(2,1)}), bf16[8,128,512]{2,1,0:T(8,128)(2,1)S(1)}, u32[]{:S(2)}, u32[]{:S(2)}) %all-to-all-start) | async-done | bytes 1048608 | tf_op jit(solution)/shard_map/all_to_all | solution.py:84
  42.4 0.3 fusion.13
  42.8 0.3 fusion.15
  43.1 0.2 copy-done.7
  43.3 0.1 copy-done.8
  43.4 1.3 %multiply_convert_fusion = (bf16[256,256]{1,0:T(8,128)(2,1)S(1)}, bf16[256,256]{1,0:T(8,128)(2,1)S(1)}) fusion(bf16[256,256]{1,0:T(8,128)(2,1)S(1)} %copy-done.8, pred[256]{0:T(512)(128)(4,1)S(1)} %compare_and_fusion.1, f32[256,256]{1,0:T(8,128)S(1)} %fusion.13, f32[256,256]{1,0:T(8,128)S(1)} %fusion.15, bf16[256,512]{0,1:T(8,128)(2,1)S(1)} %collective-permute-done.1, ...), kind=kOutput, calls=%fused_computation.54 | convolution fusion | flops 103219200 | bytes 2097408 | tf_op jit(solution)/shard_map/dot_general | solution.py:76
  44.7 0.4 fusion.17
  45.1 0.7 copy-done.3
  45.8 0.3 fusion.53
  46.1 1.2 %fusion.3 = bf16[1024,256]{1,0:T(8,128)(2,1)} fusion(f32[1024,256]{1,0:T(8,128)S(1)} %fusion.17, bf16[256,256]{1,0:T(8,128)(2,1)S(1)} %get-tuple-element.46, f32[32,8,8,128]{3,2,1,0:T(8,128)S(1)} %bitcast.84), kind=kOutput, calls=%fused_computation.11 | convolution fusion | flops 135790592 | bytes 2752512 | tf_op jit(solution)/shard_map/dot_general | solution.py:126
  47.3 0.0 slice-start
  47.3 1.4 %fusion.7 = f32[256,256]{1,0:T(8,128)S(1)} fusion(bf16[1024,256]{1,0:T(8,128)(2,1)} %fusion.3, bf16[1024,512]{1,0:T(8,128)(2,1)S(1)} %bitcast.88), kind=kOutput, calls=%fused_computation.23 | convolution fusion | flops 134217728 | bytes 1310720 | tf_op jit(solution)/shard_map/dot_general | solution.py:135
  48.7 0.2 fusion.33
  48.9 0.2 convolution_add_fusion.2
  49.1 0.2 fusion.4
  49.4 0.3 all_to_all.21
  49.6 13.0 %all_to_all.26 = f32[32,1,2048]{2,1,0:T(1,128)S(1)} all-to-all(f32[32,1,2048]{2,1,0:T(1,128)S(1)} %all_to_all.21), channel_id=1, replica_groups=mesh['row'=4,'col'=8] {'row','col'}, dimensions={0} | all-to-all | bytes 524288 | tf_op jit(solution)/shard_map/all_to_all | solution.py:28
  62.7 3.5 %all-to-all-start.1 = ((bf16[8,128,256]{2,1,0:T(8,128)(2,1)}), bf16[8,128,256]{2,1,0:T(8,128)(2,1)S(1)}, u32[]{:S(2)}, u32[]{:S(2)}) async-start(bf16[8,128,256]{2,1,0:T(8,128)(2,1)} %bitcast.21), calls=%async_computation.1 | async-start | bytes 1048576 | tf_op jit(solution)/shard_map/all_to_all | solution.py:137
  66.2 1.4 %scatter_custom_fusion = s32[256]{0:T(256)S(1)} fusion(s32[256]{0:T(256)S(1)} %bitcast.93, s32[256]{0:T(256)S(1)} %iota.42, s32[]{:T(128)} %constant.103.clone.1), kind=kCustom, calls=%fused_computation.88 | custom fusion | bytes 1028 | tf_op jit(solution)/shard_map/scatter | solution.py:58
  67.7 0.6 collective-permute-start.3
  68.3 1.2 %gather_fusion.2 = bf16[256,256]{1,0:T(8,128)(2,1)S(1)} fusion(bf16[256,256]{1,0:T(8,128)(2,1)S(1)} %get-tuple-element.47, s32[1024]{0:T(1024)S(1)} %pad_clamp_fusion), kind=kCustom, calls=%fused_computation.1.clone | custom fusion | bytes 263168 | tf_op jit(solution)/shard_map/jit(_take)/gather | solution.py:106
  69.4 0.2 reduce_sum.9
  69.6 11.2 %all-to-all-done.1 = bf16[8,128,256]{2,1,0:T(8,128)(2,1)S(1)} async-done(((bf16[8,128,256]{2,1,0:T(8,128)(2,1)}), bf16[8,128,256]{2,1,0:T(8,128)(2,1)S(1)}, u32[]{:S(2)}, u32[]{:S(2)}) %all-to-all-start.1) | async-done | bytes 524320 | tf_op jit(solution)/shard_map/all_to_all | solution.py:137
  80.8 0.8 broadcast_in_dim.48
  81.6 3.4 %all-to-all-start.3 = ((f32[32,1,2048]{2,1,0:T(1,128)}), f32[32,1,2048]{2,1,0:T(1,128)S(1)}, u32[]{:S(2)}, u32[]{:S(2)}) async-start(f32[32,1,2048]{2,1,0:T(1,128)} %broadcast_in_dim.48), calls=%async_computation.3 | async-start | bytes 524288 | tf_op jit(solution)/shard_map/all_to_all | solution.py:31
  85.1 0.4 fusion.10
  85.5 0.1 fusion.30
  85.6 0.2 convolution_convert_fusion.1
  85.8 1.2 %gather_fusion.4 = bf16[256,256]{1,0:T(8,128)(2,1)S(1)} fusion(bf16[256,256]{1,0:T(8,128)(2,1)S(1)} %convolution_convert_fusion.1, s32[1024]{0:T(1024)S(1)} %pad_clamp_fusion), kind=kCustom, calls=%fused_computation.3.clone | custom fusion | bytes 263168 | tf_op jit(solution)/shard_map/jit(_take)/gather | solution.py:149
  86.9 0.8 broadcast_select_fusion
  87.7 7.9 %all-to-all-done.3 = f32[32,1,2048]{2,1,0:T(1,128)S(1)} async-done(((f32[32,1,2048]{2,1,0:T(1,128)}), f32[32,1,2048]{2,1,0:T(1,128)S(1)}, u32[]{:S(2)}, u32[]{:S(2)}) %all-to-all-start.3) | async-done | bytes 262176 | tf_op jit(solution)/shard_map/all_to_all | solution.py:31
  95.7 0.8 multiply_reduce_fusion
  96.4 0.7 mul.28
  (51 shorter events, 0.2 us)
Async XLA Ops:
  0.6 3.5 %copy-start = (bf16[256,256]{1,0:T(8,128)(2,1)S(1)}, bf16[256,256]{1,0:T(8,128)(2,1)}, u32[]{:S(2)}) copy-start(bf16[256,256]{1,0:T(8,128)(2,1)} %param.22) | copy-start | bytes 393220
  2.1 4.9 %copy-start.12 = (s32[1,8]{1,0:T(1,128)S(1)}, s32[1,8]{1,0:T(1,128)}, u32[]{:S(2)}) copy-start(s32[1,8]{1,0:T(1,128)} %param.29) | copy-start | bytes 100
  4.3 2.5 %copy-start.6 = (bf16[256,256]{0,1:T(8,128)(2,1)}, bf16[256,256]{0,1:T(8,128)(2,1)S(1)}, u32[]{:S(2)}) copy-start(bf16[256,256]{0,1:T(8,128)(2,1)S(1)} %convolution_convert_fusion.2) | copy-start | bytes 393220
  4.4 16.6 %collective-permute-start.1 = (bf16[256,512]{0,1:T(8,128)(2,1)S(1)}, bf16[256,512]{0,1:T(8,128)(2,1)S(1)}, u32[]{:S(2)}, u32[]{:S(2)}) collective-permute-start(bf16[256,512]{0,1:T(8,128)(2,1)S(1)} %pad_maximum_fusion.6), channel_id=1, source_target_pairs={{8,0},{16,8},{24,16},{0,24},{9,1},{17,9},{25,17},{1,25},{10,2},{18... | collective-permute-start | bytes 786440 | tf_op jit(solution)/shard_map/ppermute | solution.py:18
  6.8 14.2 %collective-permute-start = (bf16[256,512]{0,1:T(8,128)(2,1)S(1)}, bf16[256,512]{0,1:T(8,128)(2,1)}, u32[]{:S(2)}, u32[]{:S(2)}) collective-permute-start(bf16[256,512]{0,1:T(8,128)(2,1)S(1)} %pad_maximum_fusion.6), channel_id=1, source_target_pairs={{0,8},{8,16},{16,24},{24,0},{1,9},{9,17},{17,25},{25,1},{2,10},{10... | collective-permute-start | bytes 786440 | tf_op jit(solution)/shard_map/ppermute | solution.py:16
  8.9 6.6 %copy-start.10 = (s32[40,2]{0,1:T(2,128)S(1)}, s32[40,2]{0,1:T(2,128)}, u32[]{:S(2)}) copy-start(s32[40,2]{0,1:T(2,128)} %param.27) | copy-start | bytes 964
  8.9 6.7 %copy-start.11 = (s32[12,2]{0,1:T(2,128)S(1)}, s32[12,2]{0,1:T(2,128)}, u32[]{:S(2)}) copy-start(s32[12,2]{0,1:T(2,128)} %param.25) | copy-start | bytes 292
  8.9 33.6 %all-to-all-start = ((bf16[8,128,512]{2,1,0:T(8,128)(2,1)}), bf16[8,128,512]{2,1,0:T(8,128)(2,1)S(1)}, u32[]{:S(2)}, u32[]{:S(2)}) async-start(bf16[8,128,512]{2,1,0:T(8,128)(2,1)} %select_select_fusion), calls=%async_computation | async-start | bytes 2097152 | tf_op jit(solution)/shard_map/all_to_all | solution.py:84
  14.8 3.0 %copy-start.1 = (bf16[256,256]{1,0:T(8,128)(2,1)S(1)}, bf16[256,256]{1,0:T(8,128)(2,1)}, u32[]{:S(2)}) copy-start(bf16[256,256]{1,0:T(8,128)(2,1)} %param.23) | copy-start | bytes 393220
  21.0 22.1 %copy-start.2 = (bf16[2,6,128,128]{3,1,2,0:T(8,128)(2,1)}, bf16[2,6,128,128]{3,1,2,0:T(8,128)(2,1)S(1)}, u32[]{:S(2)}) copy-start(bf16[2,6,128,128]{3,1,2,0:T(8,128)(2,1)S(1)} %convolution_convert_fusion) | copy-start | bytes 1179652
  21.0 22.1 %copy-start.4 = (bf16[256,512]{0,1:T(8,128)(2,1)}, bf16[256,512]{0,1:T(8,128)(2,1)S(1)}, u32[]{:S(2)}) copy-start(bf16[256,512]{0,1:T(8,128)(2,1)S(1)} %collective-permute-done.1) | copy-start | bytes 786436
  42.4 0.9 copy-start.7
  42.4 1.0 copy-start.8
  44.7 1.0 %copy-start.3 = (bf16[2,6,128,128]{3,1,2,0:T(8,128)(2,1)S(1)}, bf16[2,6,128,128]{3,1,2,0:T(8,128)(2,1)}, u32[]{:S(2)}) copy-start(bf16[2,6,128,128]{3,1,2,0:T(8,128)(2,1)} %copy-done.2) | copy-start | bytes 1179652
  47.3 1.8 %slice-start = ((bf16[256,512]{0,1:T(8,128)(2,1)}), bf16[256,256]{0,1:T(8,128)(2,1)S(1)}, s32[]{:S(2)}) async-start(bf16[256,512]{0,1:T(8,128)(2,1)} %copy-done.4), calls=%async_computation.4 | async-start | bytes 262144 | tf_op jit(solution)/shard_map/slice | solution.py:129
  47.3 1.8 %copy-start.5 = (bf16[256,256]{0,1:T(8,128)(2,1)S(1)}, bf16[256,256]{0,1:T(8,128)(2,1)}, u32[]{:S(2)}) copy-start(bf16[256,256]{0,1:T(8,128)(2,1)} %slice.109) | copy-start | bytes 393220
  49.4 16.8 %copy-start.9 = (s32[1,256]{1,0:T(1,128)S(1)}, s32[1,256]{1,0:T(1,128)}, u32[]{:S(2)}) copy-start(s32[1,256]{1,0:T(1,128)} %param.30) | copy-start | bytes 3076
  62.7 18.1 %all-to-all-start.1 = ((bf16[8,128,256]{2,1,0:T(8,128)(2,1)}), bf16[8,128,256]{2,1,0:T(8,128)(2,1)S(1)}, u32[]{:S(2)}, u32[]{:S(2)}) async-start(bf16[8,128,256]{2,1,0:T(8,128)(2,1)} %bitcast.21), calls=%async_computation.1 | async-start | bytes 1048576 | tf_op jit(solution)/shard_map/all_to_all | solution.py:137
  66.2 18.8 %copy-start.13 = (s32[1,8]{1,0:T(1,128)S(1)}, s32[1,8]{1,0:T(1,128)}, u32[]{:S(2)}) copy-start(s32[1,8]{1,0:T(1,128)} %param.29) | copy-start | bytes 100
  67.7 17.8 %collective-permute-start.3 = (bf16[256,256]{1,0:T(8,128)(2,1)S(1)}, bf16[256,256]{1,0:T(8,128)(2,1)S(1)}, u32[]{:S(2)}, u32[]{:S(2)}) collective-permute-start(bf16[256,256]{1,0:T(8,128)(2,1)S(1)} %get-tuple-element.45), channel_id=1, source_target_pairs={{8,0},{16,8},{24,16},{0,24},{9,1},{17,9},{25,17},{1,25},{10,2},{18... | collective-permute-start | bytes 393224 | tf_op jit(solution)/shard_map/ppermute | solution.py:18
  68.3 17.2 %collective-permute-start.2 = (bf16[256,256]{1,0:T(8,128)(2,1)S(1)}, bf16[256,256]{1,0:T(8,128)(2,1)S(1)}, u32[]{:S(2)}, u32[]{:S(2)}) collective-permute-start(bf16[256,256]{1,0:T(8,128)(2,1)S(1)} %get-tuple-element.44), channel_id=1, source_target_pairs={{0,8},{8,16},{16,24},{24,0},{1,9},{9,17},{17,25},{25,1},{2,10},{10... | collective-permute-start | bytes 393224 | tf_op jit(solution)/shard_map/ppermute | solution.py:16
  81.6 14.1 %all-to-all-start.3 = ((f32[32,1,2048]{2,1,0:T(1,128)}), f32[32,1,2048]{2,1,0:T(1,128)S(1)}, u32[]{:S(2)}, u32[]{:S(2)}) async-start(f32[32,1,2048]{2,1,0:T(1,128)} %broadcast_in_dim.48), calls=%async_computation.3 | async-start | bytes 524288 | tf_op jit(solution)/shard_map/all_to_all | solution.py:31

commit v5 on v2

--- a/solution.py
+++ b/solution.py
@@ -54,10 +54,12 @@
     peers = lax.axis_size("col")
     slot_total = bound_tiles.shape[0]
     order = reorder[0]
-    inverse = (
-        jnp.zeros((row_count,), jnp.int32).at[order].set(jnp.arange(row_count, dtype=jnp.int32))
+    node_range = jnp.arange(row_count, dtype=jnp.int32)
+    band_perm = (order[:, None] == node_range[None, :]).astype(jnp.bfloat16)
+    contract_rows = (((0,), (0,)), ((), ()))
+    x_band = jnp.dot(band_perm, node_feats, preferred_element_type=jnp.float32).astype(
+        jnp.bfloat16
     )
-    x_band = jnp.take(node_feats, order, axis=0)
     hidden = jnp.dot(x_band, weight, preferred_element_type=jnp.float32).astype(jnp.bfloat16)
     band_row_ids = band_coords[:, 0]
     band_col_ids = band_coords[:, 1]
@@ -74,13 +76,12 @@
     mixed = jnp.dot(band_dense, extended, preferred_element_type=jnp.float32)
     blocks = hidden.reshape(tile_rows, tile_size, width_feat)
     giving = send_lists[0]
-    outgoing = jnp.where(
-        (giving >= 0)[:, None, None],
-        jnp.take(blocks, jnp.maximum(giving, 0), axis=0),
-        jnp.zeros((), jnp.bfloat16),
-    )
+    tile_range = jnp.arange(tile_rows, dtype=jnp.int32)
+    give_onehot = (giving[:, None] == tile_range[None, :]).astype(jnp.bfloat16)
+    outgoing = jnp.einsum(
+        "sb,baf->saf", give_onehot, blocks, preferred_element_type=jnp.float32
+    ).astype(jnp.bfloat16)
     arrived = lax.all_to_all(outgoing, "col", split_axis=0, concat_axis=0, tiled=True)
-    tile_range = jnp.arange(tile_rows, dtype=jnp.int32)
     owner_range = jnp.arange(peers, dtype=jnp.int32)
     live_slots = jnp.arange(slot_total, dtype=jnp.int32) < bound_count[0]
     bound_row_ids = bound_coords[:, 0]
@@ -99,8 +100,10 @@
     mixed = mixed + jnp.dot(dense_high, arrived_rows, preferred_element_type=jnp.float32)
     mixed = mixed + jnp.dot(dense_low, arrived_rows, preferred_element_type=jnp.float32)
     out_band = jax.nn.silu(mixed).astype(jnp.bfloat16)
-    node_out = jnp.take(out_band, inverse, axis=0)
-    grad_band = jnp.take(cotangent, order, axis=0).astype(jnp.float32)
+    node_out = lax.dot_general(
+        band_perm, out_band, contract_rows, preferred_element_type=jnp.float32
+    ).astype(jnp.bfloat16)
+    grad_band = jnp.dot(band_perm, cotangent, preferred_element_type=jnp.float32)
     sigma = jax.nn.sigmoid(mixed)
     slope = (grad_band * sigma * (1.0 + mixed * (1.0 - sigma))).astype(jnp.bfloat16)
     ext_grad = lax.dot_general(
@@ -113,7 +116,6 @@
     grad_hidden = ext_grad[BW : BW + row_count]
     grad_hidden = grad_hidden.at[:BW].add(padded[:BW].astype(jnp.float32))
     grad_hidden = grad_hidden.at[row_count - BW :].add(padded[3 * BW :].astype(jnp.float32))
-    contract_rows = (((0,), (0,)), ((), ()))
     owner_terms = lax.dot_general(
         dense_high, slope, contract_rows, preferred_element_type=jnp.float32
     ) + lax.dot_general(dense_low, slope, contract_rows, preferred_element_type=jnp.float32)
@@ -133,7 +135,9 @@
     feat_band = lax.dot_general(
         grad_round, weight, (((1,), (1,)), ((), ())), preferred_element_type=jnp.float32
     ).astype(jnp.bfloat16)
-    feat_grad = jnp.take(feat_band, inverse, axis=0)
+    feat_grad = lax.dot_general(
+        band_perm, feat_band, contract_rows, preferred_element_type=jnp.float32
+    ).astype(jnp.bfloat16)
     return (node_out, feat_grad, weight_grad)
 
 

time: 83.1 us -> 80.1 us (0.964)
  blocking collectives: 0 us -> 13.2 us
  local copies, waits for them, and re-layouts: 10.9 us -> 2.95 us
  waiting for transfers between devices: 38.3 us -> 32.2 us
  matrix products: 7.54 us -> 11.7 us
  other arithmetic: 4.2 us -> 1 us
  starting transfers between devices: 19.9 us -> 17.1 us
    all_to_all x0 -> x1, blocking collectives: none -> 13.2 us  [spread_sum(): gathered = lax.all_to_all(pieces, axes, 0, 0, tiled=True)]
    all_to_all x1 -> x0, waiting for transfers between devices: 9.19 us -> none  [spread_sum(): gathered = lax.all_to_all(pieces, axes, 0, 0, tiled=True)]
    gather x5 -> x0, local copies, waits for them, and re-layouts: 6.58 us -> none  [the longest x1 1.89 us: on_device(): x_band = jnp.take(node_feats, order, axis=0)]
    dot_general x1 -> x5, matrix products: 0.21 us -> 4.54 us  [the longest x1 1.18 us: on_device(): jnp.dot(band_perm, node_feats, preferred_element_type=jnp.float32)]
    all_to_all x1 -> x0, starting transfers between devices: 2.72 us -> none  [spread_sum(): gathered = lax.all_to_all(pieces, axes, 0, 0, tiled=True)]
    select_n x5 -> x0, other arithmetic: 2.48 us -> none  [the longest x1 0.95 us: on_device(): jnp.where((giving >= 0)[:, None, None], jnp.take(blocks, jnp.maximum(givi...]
    all_to_all x1, waiting for transfers between devices: 9.33 us -> 11.1 us  [on_device(): lax.all_to_all(outgoing, 'col', split_axis=0, concat_axis=0, tiled=True)]
    scatter x1 -> x0, local copies, waits for them, and re-layouts: 1.4 us -> none  [on_device(): jnp.zeros((row_count,), jnp.int32).at[order]]
  transfers between devices with their start and end apart: 8 -> 7, of which waited for: 4 -> 3; matrix products, arithmetic and copies ran while one was open for 15% -> 10% of each run, Pallas kernels for 0% -> 0%
where the time goes in v5:
time: 80.1 us; the launch traced here: 79.7 us
  waiting for transfers between devices  32.2 us (40%)
  starting transfers between devices  17.1 us (21%)
  blocking collectives  13.2 us (16%)
  matrix products  11.7 us (15%)
  local copies, waits for them, and re-layouts  2.95 us (4%)
  between operations  1.6 us (2%)
  other arithmetic  1 us (1%)
    all_to_all x1, blocking collectives, spread_sum(): gathered = lax.all_to_all(pieces, axes, 0, 0, tiled=True)  13.2 us
    all_to_all x1, waiting for transfers between devices, on_device(): lax.all_to_all(to_owner, 'col', split_axis=0, concat_axis=0, tiled=True)  12.5 us
    all_to_all x1, waiting for transfers between devices, on_device(): lax.all_to_all(outgoing, 'col', split_axis=0, concat_axis=0, tiled=True)  11.1 us
    all_to_all x1, waiting for transfers between devices, spread_sum(): return lax.all_to_all(copies, axes, 0, 0, tiled=True).reshape(value.shape)  8.56 us
    all_to_all x1, starting transfers between devices, on_device(): lax.all_to_all(outgoing, 'col', split_axis=0, concat_axis=0, tiled=True)  6.53 us
    ppermute x2, starting transfers between devices, padded_2(): lax.ppermute(head, axis, [((i + 1) % count, i) for i in range(count)])  3.75 us
    all_to_all x1, starting transfers between devices, on_device(): lax.all_to_all(to_owner, 'col', split_axis=0, concat_axis=0, tiled=True)  3.64 us
    all_to_all x1, starting transfers between devices, spread_sum(): return lax.all_to_all(copies, axes, 0, 0, tiled=True).reshape(value.shape)  2.58 us
  transfers between devices with their start and end apart: 7, of which 3 were waited for; matrix products, arithmetic and copies ran while one was open for 10% of the time, Pallas kernels for 0%

profile of v5, /device:TPU:0, one launch (start us, length us, event | category | flops | bytes accessed | tf_op | source)
XLA Modules:
  0.0 79.7 jit_solution(2326769386620154304)
XLA Ops:
  0.6 0.0 copy-start
  0.6 1.2 %convolution_convert_fusion.6 = bf16[256,256]{1,0:T(8,128)(2,1)S(1)} fusion(bf16[256,256]{1,0:T(8,128)(2,1)} %param.19, s32[256]{0:T(256)} %bitcast.102), kind=kOutput, calls=%fused_computation.16 | convolution fusion | flops 33685504 | bytes 263168 | tf_op jit(solution)/shard_map/dot_general | solution.py:60
  1.8 0.0 copy-done
  1.8 0.2 convolution_convert_fusion.5
  2.0 0.5 collective-permute-start
  2.5 2.0 %collective-permute-start.1 = (bf16[256,256]{1,0:T(8,128)(2,1)S(1)}, bf16[256,256]{1,0:T(8,128)(2,1)}, u32[]{:S(2)}, u32[]{:S(2)}) collective-permute-start(bf16[256,256]{1,0:T(8,128)(2,1)S(1)} %convolution_convert_fusion.5), channel_id=1, source_target_pairs={{8,0},{16,8},{24,16},{0,24},{9,1},{17,9},{25,17},{1,25},{10,2},{18... | collective-permute-start | bytes 393224 | tf_op jit(solution)/shard_map/ppermute | solution.py:18
  4.6 1.1 %convolution_convert_fusion = bf16[8,128,256]{2,0,1:T(8,128)(2,1)S(1)} fusion(bf16[2,128,256]{2,1,0:T(8,128)(2,1)S(1)} %bitcast.101, s32[8]{0:T(128)} %bitcast.106), kind=kOutput, calls=%fused_computation.4 | convolution fusion | flops 1310736 | bytes 655392 | tf_op jit(solution)/shard_map/sb,baf->saf/dot_general | solution.py:81
  5.6 0.9 %copy.29 = bf16[8,128,256]{2,1,0:T(8,128)(2,1)} copy(bf16[8,128,256]{2,0,1:T(8,128)(2,1)S(1)} %convolution_convert_fusion) | data formatting | bytes 1048576 | tf_op jit(solution)/shard_map/convert_element_type | solution.py:83
  6.5 6.5 %all-to-all-start = ((bf16[8,128,256]{2,1,0:T(8,128)(2,1)}), bf16[8,128,256]{2,1,0:T(8,128)(2,1)S(1)}, u32[]{:S(2)}, u32[]{:S(2)}) async-start(bf16[8,128,256]{2,1,0:T(8,128)(2,1)} %copy.29), calls=%async_computation | async-start | bytes 1048576 | tf_op jit(solution)/shard_map/all_to_all | solution.py:84
  13.1 0.0 copy-done.5
  13.8 0.4 convolution_convert_fusion.1
  14.2 2.3 %fusion.8 = (bf16[2,128,8,128]{3,2,1,0:T(8,128)(2,1)S(1)}, bf16[2,128,8,128]{3,2,1,0:T(8,128)(2,1)S(1)}, f32[2,8,128,128]{3,1,2,0:T(8,128)S(1)}) fusion(bf16[40,128,128]{2,1,0:T(8,128)(2,1)} %param.24, pred[40]{0:T(512)(128)(4,1)S(1)} %iota_compare_fusion.9, pred[40,8]{0,1:T(8,128)(4,1)S(1)} %iota_compare_fusion.5, pred[40,2]{0,1:T(4,128)(4,1)S(1)} %iota_compare_fusion.7), kind=kOutput, calls=%fused_computation.22 | convolution fusion | flops 22021376 | bytes 3408312 | tf_op jit(solution)/shard_map/krs,kab->rasb/dot_general | solution.py:94
  16.5 11.1 %all-to-all-done = bf16[8,128,256]{2,1,0:T(8,128)(2,1)S(1)} async-done(((bf16[8,128,256]{2,1,0:T(8,128)(2,1)}), bf16[8,128,256]{2,1,0:T(8,128)(2,1)S(1)}, u32[]{:S(2)}, u32[]{:S(2)}) %all-to-all-start) | async-done | bytes 524320 | tf_op jit(solution)/shard_map/all_to_all | solution.py:84
  27.6 0.3 fusion.14
  27.9 0.0 copy-start.2
  27.9 0.0 copy-start.6
  27.9 0.3 fusion.11
  28.3 0.0 collective-permute-done
  28.3 0.0 collective-permute-done.1
  28.3 1.2 %fusion.5 = f32[256,256]{1,0:T(8,128)S(1)} fusion(f32[256,256]{1,0:T(8,128)S(1)} %fusion.11, f32[256,256]{1,0:T(8,128)S(1)} %fusion.14, bf16[256,256]{1,0:T(8,128)(2,1)} %collective-permute-done.1, bf16[256,256]{1,0:T(8,128)(2,1)S(1)} %convolution_convert_fusion.5, bf16[256,256]{1,0:T(8,128)(2,1)} %collective-permute-done, ...), kind=kOutput, calls=%fused_computation.10 | convolution fusion | flops 101974016 | bytes 1572864 | tf_op jit(solution)/shard_map/dot_general | solution.py:76
  29.5 0.0 copy-start.7
  29.6 0.2 fusion.6
  29.8 0.4 fusion.9
  30.2 0.1 copy-done.7
  30.3 1.2 %fusion.3 = bf16[1024,256]{1,0:T(8,128)(2,1)} fusion(f32[1024,256]{1,0:T(8,128)S(1)} %fusion.9, bf16[256,256]{1,0:T(8,128)(2,1)S(1)} %fusion.6, f32[32,8,8,128]{3,2,1,0:T(8,128)S(1)} %bitcast.94), kind=kOutput, calls=%fused_computation.6 | convolution fusion | flops 135790592 | bytes 2752512 | tf_op jit(solution)/shard_map/dot_general | solution.py:121
  31.4 3.6 %all-to-all-start.1 = ((bf16[8,128,256]{2,1,0:T(8,128)(2,1)}), bf16[8,128,256]{2,1,0:T(8,128)(2,1)S(1)}, u32[]{:S(2)}, u32[]{:S(2)}) async-start(bf16[8,128,256]{2,1,0:T(8,128)(2,1)} %bitcast.19), calls=%async_computation.1 | async-start | bytes 1048576 | tf_op jit(solution)/shard_map/all_to_all | solution.py:123
  35.1 0.3 fusion.60
  35.4 0.1 collective-permute-start.2
  35.5 1.7 %collective-permute-start.3 = (bf16[256,256]{1,0:T(8,128)(2,1)S(1)}, bf16[256,256]{1,0:T(8,128)(2,1)S(1)}, u32[]{:S(2)}, u32[]{:S(2)}) collective-permute-start(bf16[256,256]{1,0:T(8,128)(2,1)S(1)} %get-tuple-element.46), channel_id=1, source_target_pairs={{8,0},{16,8},{24,16},{0,24},{9,1},{17,9},{25,17},{1,25},{10,2},{18... | collective-permute-start | bytes 393224 | tf_op jit(solution)/shard_map/ppermute | solution.py:18
  37.2 12.5 %all-to-all-done.1 = bf16[8,128,256]{2,1,0:T(8,128)(2,1)S(1)} async-done(((bf16[8,128,256]{2,1,0:T(8,128)(2,1)}), bf16[8,128,256]{2,1,0:T(8,128)(2,1)S(1)}, u32[]{:S(2)}, u32[]{:S(2)}) %all-to-all-start.1) | async-done | bytes 524320 | tf_op jit(solution)/shard_map/all_to_all | solution.py:123
  49.7 0.0 copy-done.3
  49.7 0.4 fusion.18
  50.2 0.0 collective-permute-done.2
  50.2 0.0 collective-permute-done.3
  50.2 0.1 fusion.33
  50.2 0.0 copy-start.8
  50.3 0.2 fusion.61
  50.5 0.3 all_to_all.21
  50.8 13.2 %all_to_all.26 = f32[32,1,2048]{2,1,0:T(1,128)S(1)} all-to-all(f32[32,1,2048]{2,1,0:T(1,128)S(1)} %all_to_all.21), channel_id=1, replica_groups=mesh['row'=4,'col'=8] {'row','col'}, dimensions={0} | all-to-all | bytes 524288 | tf_op jit(solution)/shard_map/all_to_all | solution.py:28
  63.9 0.2 reduce_sum.9
  64.1 0.8 %broadcast_in_dim.2 = f32[32,1,2048]{2,1,0:T(1,128)} broadcast(f32[2048]{0:T(1024)S(1)} %reduce_sum.9), dimensions={2} | broadcast | bytes 270336 | tf_op jit(solution)/shard_map/broadcast_in_dim | solution.py:30
  64.9 2.6 %all-to-all-start.3 = ((f32[32,1,2048]{2,1,0:T(1,128)}), f32[32,1,2048]{2,1,0:T(1,128)S(1)}, u32[]{:S(2)}, u32[]{:S(2)}) async-start(f32[32,1,2048]{2,1,0:T(1,128)} %broadcast_in_dim.2), calls=%async_computation.3 | async-start | bytes 524288 | tf_op jit(solution)/shard_map/all_to_all | solution.py:31
  67.5 0.0 copy-done.8
  67.5 1.0 %convolution_convert_fusion.4 = bf16[256,256]{1,0:T(8,128)(2,1)} fusion(s32[256]{0:T(256)S(1)} %bitcast.104, f32[256,256]{1,0:T(8,128)S(1)} %copy-done.8), kind=kOutput, calls=%fused_computation.14 | convolution fusion | flops 34013184 | bytes 394240 | tf_op jit(solution)/shard_map/dot_general | solution.py:103
  68.5 1.1 %convolution_convert_fusion.2 = bf16[256,256]{1,0:T(8,128)(2,1)} fusion(bf16[256,256]{1,0:T(8,128)(2,1)S(1)} %fusion.33, bf16[256,256]{1,0:T(8,128)(2,1)S(1)} %copy-done, s32[256]{0:T(256)S(1)} %bitcast.105), kind=kOutput, calls=%fused_computation.12 | convolution fusion | flops 67305472 | bytes 394240 | tf_op jit(solution)/shard_map/dot_general | solution.py:138
  69.6 8.6 %all-to-all-done.3 = f32[32,1,2048]{2,1,0:T(1,128)S(1)} async-done(((f32[32,1,2048]{2,1,0:T(1,128)}), f32[32,1,2048]{2,1,0:T(1,128)S(1)}, u32[]{:S(2)}, u32[]{:S(2)}) %all-to-all-start.3) | async-done | bytes 262176 | tf_op jit(solution)/shard_map/all_to_all | solution.py:31
  78.2 0.8 multiply_reduce_fusion
  78.9 0.7 mul.28
  (17 shorter events, 0.1 us)
Async XLA Ops:
  0.6 1.2 %copy-start = (bf16[256,256]{1,0:T(8,128)(2,1)S(1)}, bf16[256,256]{1,0:T(8,128)(2,1)}, u32[]{:S(2)}) copy-start(bf16[256,256]{1,0:T(8,128)(2,1)} %param.20) | copy-start | bytes 393220
  2.0 26.2 %collective-permute-start = (bf16[256,256]{1,0:T(8,128)(2,1)S(1)}, bf16[256,256]{1,0:T(8,128)(2,1)}, u32[]{:S(2)}, u32[]{:S(2)}) collective-permute-start(bf16[256,256]{1,0:T(8,128)(2,1)S(1)} %convolution_convert_fusion.5), channel_id=1, source_target_pairs={{0,8},{8,16},{16,24},{24,0},{1,9},{9,17},{17,25},{25,1},{2,10},{10... | collective-permute-start | bytes 393224 | tf_op jit(solution)/shard_map/ppermute | solution.py:16
  2.5 25.7 %collective-permute-start.1 = (bf16[256,256]{1,0:T(8,128)(2,1)S(1)}, bf16[256,256]{1,0:T(8,128)(2,1)}, u32[]{:S(2)}, u32[]{:S(2)}) collective-permute-start(bf16[256,256]{1,0:T(8,128)(2,1)S(1)} %convolution_convert_fusion.5), channel_id=1, source_target_pairs={{8,0},{16,8},{24,16},{0,24},{9,1},{17,9},{25,17},{1,25},{10,2},{18... | collective-permute-start | bytes 393224 | tf_op jit(solution)/shard_map/ppermute | solution.py:18
  4.6 8.5 %copy-start.4 = (s32[40,2]{0,1:T(2,128)S(1)}, s32[40,2]{0,1:T(2,128)}, u32[]{:S(2)}) copy-start(s32[40,2]{0,1:T(2,128)} %param.25) | copy-start | bytes 964
  4.6 8.5 %copy-start.5 = (s32[12,2]{0,1:T(2,128)S(1)}, s32[12,2]{0,1:T(2,128)}, u32[]{:S(2)}) copy-start(s32[12,2]{0,1:T(2,128)} %param.23) | copy-start | bytes 292
  4.6 9.3 %copy-start.1 = (bf16[12,128,128]{2,1,0:T(8,128)(2,1)S(1)}, bf16[12,128,128]{2,1,0:T(8,128)(2,1)}, u32[]{:S(2)}) copy-start(bf16[12,128,128]{2,1,0:T(8,128)(2,1)} %param.22) | copy-start | bytes 1179652
  6.5 21.1 %all-to-all-start = ((bf16[8,128,256]{2,1,0:T(8,128)(2,1)}), bf16[8,128,256]{2,1,0:T(8,128)(2,1)S(1)}, u32[]{:S(2)}, u32[]{:S(2)}) async-start(bf16[8,128,256]{2,1,0:T(8,128)(2,1)} %copy.29), calls=%async_computation | async-start | bytes 1048576 | tf_op jit(solution)/shard_map/all_to_all | solution.py:84
  27.9 1.6 %copy-start.2 = (s32[1,256]{1,0:T(1,128)S(1)}, s32[1,256]{1,0:T(1,128)}, u32[]{:S(2)}) copy-start(s32[1,256]{1,0:T(1,128)} %param.28) | copy-start | bytes 3076
  27.9 1.6 %copy-start.6 = (bf16[256,256]{1,0:T(8,128)(2,1)S(1)}, bf16[256,256]{1,0:T(8,128)(2,1)}, u32[]{:S(2)}) copy-start(bf16[256,256]{1,0:T(8,128)(2,1)} %param.21) | copy-start | bytes 393220
  29.5 0.7 copy-start.7
  31.4 18.3 %all-to-all-start.1 = ((bf16[8,128,256]{2,1,0:T(8,128)(2,1)}), bf16[8,128,256]{2,1,0:T(8,128)(2,1)S(1)}, u32[]{:S(2)}, u32[]{:S(2)}) async-start(bf16[8,128,256]{2,1,0:T(8,128)(2,1)} %bitcast.19), calls=%async_computation.1 | async-start | bytes 1048576 | tf_op jit(solution)/shard_map/all_to_all | solution.py:123
  35.1 14.7 %copy-start.3 = (s32[1,8]{1,0:T(1,128)S(1)}, s32[1,8]{1,0:T(1,128)}, u32[]{:S(2)}) copy-start(s32[1,8]{1,0:T(1,128)} %param.27) | copy-start | bytes 100
  35.4 14.8 %collective-permute-start.2 = (bf16[256,256]{1,0:T(8,128)(2,1)S(1)}, bf16[256,256]{1,0:T(8,128)(2,1)S(1)}, u32[]{:S(2)}, u32[]{:S(2)}) collective-permute-start(bf16[256,256]{1,0:T(8,128)(2,1)S(1)} %get-tuple-element.45), channel_id=1, source_target_pairs={{0,8},{8,16},{16,24},{24,0},{1,9},{9,17},{17,25},{25,1},{2,10},{10... | collective-permute-start | bytes 393224 | tf_op jit(solution)/shard_map/ppermute | solution.py:16
  35.5 14.7 %collective-permute-start.3 = (bf16[256,256]{1,0:T(8,128)(2,1)S(1)}, bf16[256,256]{1,0:T(8,128)(2,1)S(1)}, u32[]{:S(2)}, u32[]{:S(2)}) collective-permute-start(bf16[256,256]{1,0:T(8,128)(2,1)S(1)} %get-tuple-element.46), channel_id=1, source_target_pairs={{8,0},{16,8},{24,16},{0,24},{9,1},{17,9},{25,17},{1,25},{10,2},{18... | collective-permute-start | bytes 393224 | tf_op jit(solution)/shard_map/ppermute | solution.py:18
  50.2 17.3 %copy-start.8 = (f32[256,256]{1,0:T(8,128)S(1)}, f32[256,256]{1,0:T(8,128)}, u32[]{:S(2)}) copy-start(f32[256,256]{1,0:T(8,128)} %copy-done.7) | copy-start | bytes 786436
  64.9 13.2 %all-to-all-start.3 = ((f32[32,1,2048]{2,1,0:T(1,128)}), f32[32,1,2048]{2,1,0:T(1,128)S(1)}, u32[]{:S(2)}, u32[]{:S(2)}) async-start(f32[32,1,2048]{2,1,0:T(1,128)} %broadcast_in_dim.2), calls=%async_computation.3 | async-start | bytes 524288 | tf_op jit(solution)/shard_map/all_to_all | solution.py:31

commit v6 on v5

--- a/solution.py
+++ b/solution.py
@@ -22,12 +22,15 @@
     return cells
 
 
-def spread_sum(value, axes):
+def spread_sum(value, axes, scale):
     count = lax.axis_size(axes)
-    pieces = value.reshape(count, value.size // count)
-    gathered = lax.all_to_all(pieces, axes, 0, 0, tiled=True)
-    owned = jnp.sum(gathered.reshape(count, 1, value.size // count), axis=0)
-    copies = jnp.broadcast_to(owned, (count, value.size // count))
+    if value.shape[0] % count == 0:
+        piece = (count, value.shape[0] // count, value.shape[1])
+    else:
+        piece = (count, value.size // count // 128, 128)
+    gathered = lax.all_to_all(value.reshape(piece), axes, 0, 0, tiled=True)
+    owned = jnp.sum(gathered, axis=0, keepdims=True) * scale
+    copies = jnp.broadcast_to(owned, piece)
     return lax.all_to_all(copies, axes, 0, 0, tiled=True).reshape(value.shape)
 
 
@@ -131,7 +134,7 @@
         x_band, grad_round, (((0,), (0,)), ((), ())), preferred_element_type=jnp.float32
     )
     nodes_all = row_count * lax.axis_size("row") * peers
-    weight_grad = spread_sum(partial_weight, ("row", "col")) * nodes_all ** (-0.5)
+    weight_grad = spread_sum(partial_weight, ("row", "col"), nodes_all ** (-0.5))
     feat_band = lax.dot_general(
         grad_round, weight, (((1,), (1,)), ((), ())), preferred_element_type=jnp.float32
     ).astype(jnp.bfloat16)

time: 80.1 us -> 78.8 us (0.984)
  other arithmetic: 1 us -> 0.13 us
where the time goes in v6:
time: 78.8 us; the launch traced here: 78.4 us
  waiting for transfers between devices  32.2 us (41%)
  starting transfers between devices  17.1 us (22%)
  blocking collectives  13.2 us (17%)
  matrix products  11.7 us (15%)
  local copies, waits for them, and re-layouts  2.51 us (3%)
  between operations  1.6 us (2%)
    all_to_all x1, blocking collectives, spread_sum(): gathered = lax.all_to_all(value.reshape(piece), axes, 0, 0, tiled=True)  13.2 us
    all_to_all x1, waiting for transfers between devices, on_device(): lax.all_to_all(to_owner, 'col', split_axis=0, concat_axis=0, tiled=True)  12.5 us
    all_to_all x1, waiting for transfers between devices, on_device(): lax.all_to_all(outgoing, 'col', split_axis=0, concat_axis=0, tiled=True)  11.1 us
    all_to_all x1, waiting for transfers between devices, spread_sum(): return lax.all_to_all(copies, axes, 0, 0, tiled=True).reshape(value.shape)  8.56 us
    all_to_all x1, starting transfers between devices, on_device(): lax.all_to_all(outgoing, 'col', split_axis=0, concat_axis=0, tiled=True)  6.53 us
    ppermute x2, starting transfers between devices, padded_2(): lax.ppermute(head, axis, [((i + 1) % count, i) for i in range(count)])  3.75 us
    all_to_all x1, starting transfers between devices, on_device(): lax.all_to_all(to_owner, 'col', split_axis=0, concat_axis=0, tiled=True)  3.63 us
    all_to_all x1, starting transfers between devices, spread_sum(): return lax.all_to_all(copies, axes, 0, 0, tiled=True).reshape(value.shape)  2.58 us
  transfers between devices with their start and end apart: 7, of which 3 were waited for; matrix products, arithmetic and copies ran while one was open for 10% of the time, Pallas kernels for 0%

profile of v6, /device:TPU:0, one launch (start us, length us, event | category | flops | bytes accessed | tf_op | source)
XLA Modules:
  0.0 78.4 jit_solution(11423440603721464966)
XLA Ops:
  0.6 0.0 copy-start
  0.6 1.2 %convolution_convert_fusion.6 = bf16[256,256]{1,0:T(8,128)(2,1)S(1)} fusion(bf16[256,256]{1,0:T(8,128)(2,1)} %param.19, s32[256]{0:T(256)} %bitcast.106), kind=kOutput, calls=%fused_computation.17 | convolution fusion | flops 33685504 | bytes 263168 | tf_op jit(solution)/shard_map/dot_general | solution.py:63
  1.8 0.0 copy-done
  1.8 0.2 convolution_convert_fusion.5
  2.0 0.5 collective-permute-start
  2.5 2.0 %collective-permute-start.1 = (bf16[256,256]{1,0:T(8,128)(2,1)S(1)}, bf16[256,256]{1,0:T(8,128)(2,1)}, u32[]{:S(2)}, u32[]{:S(2)}) collective-permute-start(bf16[256,256]{1,0:T(8,128)(2,1)S(1)} %convolution_convert_fusion.5), channel_id=1, source_target_pairs={{8,0},{16,8},{24,16},{0,24},{9,1},{17,9},{25,17},{1,25},{10,2},{18... | collective-permute-start | bytes 393224 | tf_op jit(solution)/shard_map/ppermute | solution.py:18
  4.6 1.1 %convolution_convert_fusion = bf16[8,128,256]{2,0,1:T(8,128)(2,1)S(1)} fusion(bf16[2,128,256]{2,1,0:T(8,128)(2,1)S(1)} %bitcast.105, s32[8]{0:T(128)} %bitcast.110), kind=kOutput, calls=%fused_computation.4 | convolution fusion | flops 1310736 | bytes 655392 | tf_op jit(solution)/shard_map/sb,baf->saf/dot_general | solution.py:84
  5.6 0.9 %copy.29 = bf16[8,128,256]{2,1,0:T(8,128)(2,1)} copy(bf16[8,128,256]{2,0,1:T(8,128)(2,1)S(1)} %convolution_convert_fusion) | data formatting | bytes 1048576 | tf_op jit(solution)/shard_map/convert_element_type | solution.py:86
  6.5 6.5 %all-to-all-start = ((bf16[8,128,256]{2,1,0:T(8,128)(2,1)}), bf16[8,128,256]{2,1,0:T(8,128)(2,1)S(1)}, u32[]{:S(2)}, u32[]{:S(2)}) async-start(bf16[8,128,256]{2,1,0:T(8,128)(2,1)} %copy.29), calls=%async_computation | async-start | bytes 1048576 | tf_op jit(solution)/shard_map/all_to_all | solution.py:87
  13.1 0.0 copy-done.4
  13.1 0.0 copy-done.5
  13.8 0.0 copy-done.1
  13.8 0.4 convolution_convert_fusion.1
  14.2 2.3 %fusion.8 = (bf16[2,128,8,128]{3,2,1,0:T(8,128)(2,1)S(1)}, bf16[2,128,8,128]{3,2,1,0:T(8,128)(2,1)S(1)}, f32[2,8,128,128]{3,1,2,0:T(8,128)S(1)}) fusion(bf16[40,128,128]{2,1,0:T(8,128)(2,1)} %param.24, pred[40]{0:T(512)(128)(4,1)S(1)} %iota_compare_fusion.9, pred[40,8]{0,1:T(8,128)(4,1)S(1)} %iota_compare_fusion.5, pred[40,2]{0,1:T(4,128)(4,1)S(1)} %iota_compare_fusion.7), kind=kOutput, calls=%fused_computation.23 | convolution fusion | flops 22021376 | bytes 3408312 | tf_op jit(solution)/shard_map/krs,kab->rasb/dot_general | solution.py:97
  16.5 11.1 %all-to-all-done = bf16[8,128,256]{2,1,0:T(8,128)(2,1)S(1)} async-done(((bf16[8,128,256]{2,1,0:T(8,128)(2,1)}), bf16[8,128,256]{2,1,0:T(8,128)(2,1)S(1)}, u32[]{:S(2)}, u32[]{:S(2)}) %all-to-all-start) | async-done | bytes 524320 | tf_op jit(solution)/shard_map/all_to_all | solution.py:87
  27.6 0.3 fusion.14
  27.9 0.0 copy-start.2
  27.9 0.0 copy-start.6
  27.9 0.3 fusion.11
  28.3 0.0 collective-permute-done
  28.3 0.0 collective-permute-done.1
  28.3 1.2 %fusion.5 = f32[256,256]{1,0:T(8,128)S(1)} fusion(f32[256,256]{1,0:T(8,128)S(1)} %fusion.11, f32[256,256]{1,0:T(8,128)S(1)} %fusion.14, bf16[256,256]{1,0:T(8,128)(2,1)} %collective-permute-done.1, bf16[256,256]{1,0:T(8,128)(2,1)S(1)} %convolution_convert_fusion.5, bf16[256,256]{1,0:T(8,128)(2,1)} %collective-permute-done, ...), kind=kOutput, calls=%fused_computation.10 | convolution fusion | flops 101974016 | bytes 1572864 | tf_op jit(solution)/shard_map/dot_general | solution.py:79
  29.5 0.0 copy-done.2
  29.5 0.0 copy-done.6
  29.5 0.0 copy-start.7
  29.6 0.2 fusion.6
  29.8 0.4 fusion.9
  30.2 0.1 copy-done.7
  30.3 1.2 %fusion.3 = bf16[1024,256]{1,0:T(8,128)(2,1)} fusion(f32[1024,256]{1,0:T(8,128)S(1)} %fusion.9, bf16[256,256]{1,0:T(8,128)(2,1)S(1)} %fusion.6, f32[32,8,8,128]{3,2,1,0:T(8,128)S(1)} %bitcast.97), kind=kOutput, calls=%fused_computation.6 | convolution fusion | flops 135790592 | bytes 2752512 | tf_op jit(solution)/shard_map/dot_general | solution.py:124
  31.4 3.6 %all-to-all-start.1 = ((bf16[8,128,256]{2,1,0:T(8,128)(2,1)}), bf16[8,128,256]{2,1,0:T(8,128)(2,1)S(1)}, u32[]{:S(2)}, u32[]{:S(2)}) async-start(bf16[8,128,256]{2,1,0:T(8,128)(2,1)} %bitcast.19), calls=%async_computation.1 | async-start | bytes 1048576 | tf_op jit(solution)/shard_map/all_to_all | solution.py:126
  35.1 0.3 fusion.60
  35.4 0.1 collective-permute-start.2
  35.5 1.7 %collective-permute-start.3 = (bf16[256,256]{1,0:T(8,128)(2,1)S(1)}, bf16[256,256]{1,0:T(8,128)(2,1)S(1)}, u32[]{:S(2)}, u32[]{:S(2)}) collective-permute-start(bf16[256,256]{1,0:T(8,128)(2,1)S(1)} %get-tuple-element.46), channel_id=1, source_target_pairs={{8,0},{16,8},{24,16},{0,24},{9,1},{17,9},{25,17},{1,25},{10,2},{18... | collective-permute-start | bytes 393224 | tf_op jit(solution)/shard_map/ppermute | solution.py:18
  37.2 12.5 %all-to-all-done.1 = bf16[8,128,256]{2,1,0:T(8,128)(2,1)S(1)} async-done(((bf16[8,128,256]{2,1,0:T(8,128)(2,1)}), bf16[8,128,256]{2,1,0:T(8,128)(2,1)S(1)}, u32[]{:S(2)}, u32[]{:S(2)}) %all-to-all-start.1) | async-done | bytes 524320 | tf_op jit(solution)/shard_map/all_to_all | solution.py:126
  49.7 0.0 copy-done.3
  49.7 0.4 fusion.18
  50.2 0.0 collective-permute-done.2
  50.2 0.0 collective-permute-done.3
  50.2 0.0 copy-start.8
  50.2 0.1 fusion.33
  50.3 0.2 convolution_bitcast_fusion
  50.5 13.2 %all_to_all.20 = f32[32,8,256]{2,1,0:T(8,128)S(1)} all-to-all(f32[32,8,256]{2,1,0:T(8,128)S(1)} %convolution_bitcast_fusion), channel_id=1, replica_groups=mesh['row'=4,'col'=8] {'row','col'}, dimensions={0} | all-to-all | bytes 524288 | tf_op jit(solution)/shard_map/all_to_all | solution.py:31
  63.7 0.7 broadcast_in_dim.2
  64.4 2.6 %all-to-all-start.3 = ((f32[32,8,256]{2,1,0:T(8,128)}), f32[32,8,256]{2,1,0:T(8,128)S(1)}, u32[]{:S(2)}, u32[]{:S(2)}) async-start(f32[32,8,256]{2,1,0:T(8,128)} %broadcast_in_dim.2), calls=%async_computation.3 | async-start | bytes 524288 | tf_op jit(solution)/shard_map/all_to_all | solution.py:34
  67.0 1.0 %convolution_convert_fusion.4 = bf16[256,256]{1,0:T(8,128)(2,1)} fusion(s32[256]{0:T(256)S(1)} %bitcast.108, f32[256,256]{1,0:T(8,128)S(1)} %copy-done.8), kind=kOutput, calls=%fused_computation.15 | convolution fusion | flops 34013184 | bytes 394240 | tf_op jit(solution)/shard_map/dot_general | solution.py:106
  68.0 1.1 %convolution_convert_fusion.2 = bf16[256,256]{1,0:T(8,128)(2,1)} fusion(bf16[256,256]{1,0:T(8,128)(2,1)S(1)} %fusion.33, bf16[256,256]{1,0:T(8,128)(2,1)S(1)} %copy-done, s32[256]{0:T(256)S(1)} %bitcast.109), kind=kOutput, calls=%fused_computation.13 | convolution fusion | flops 67305472 | bytes 394240 | tf_op jit(solution)/shard_map/dot_general | solution.py:141
  69.1 8.6 %all-to-all-done.3 = f32[32,8,256]{2,1,0:T(8,128)S(1)} async-done(((f32[32,8,256]{2,1,0:T(8,128)}), f32[32,8,256]{2,1,0:T(8,128)S(1)}, u32[]{:S(2)}, u32[]{:S(2)}) %all-to-all-start.3) | async-done | bytes 262176 | tf_op jit(solution)/shard_map/all_to_all | solution.py:34
  77.7 0.7 copy.79
  (16 shorter events, 0.1 us)
Async XLA Ops:
  0.6 1.2 %copy-start = (bf16[256,256]{1,0:T(8,128)(2,1)S(1)}, bf16[256,256]{1,0:T(8,128)(2,1)}, u32[]{:S(2)}) copy-start(bf16[256,256]{1,0:T(8,128)(2,1)} %param.20) | copy-start | bytes 393220
  2.0 26.2 %collective-permute-start = (bf16[256,256]{1,0:T(8,128)(2,1)S(1)}, bf16[256,256]{1,0:T(8,128)(2,1)}, u32[]{:S(2)}, u32[]{:S(2)}) collective-permute-start(bf16[256,256]{1,0:T(8,128)(2,1)S(1)} %convolution_convert_fusion.5), channel_id=1, source_target_pairs={{0,8},{8,16},{16,24},{24,0},{1,9},{9,17},{17,25},{25,1},{2,10},{10... | collective-permute-start | bytes 393224 | tf_op jit(solution)/shard_map/ppermute | solution.py:16
  2.5 25.7 %collective-permute-start.1 = (bf16[256,256]{1,0:T(8,128)(2,1)S(1)}, bf16[256,256]{1,0:T(8,128)(2,1)}, u32[]{:S(2)}, u32[]{:S(2)}) collective-permute-start(bf16[256,256]{1,0:T(8,128)(2,1)S(1)} %convolution_convert_fusion.5), channel_id=1, source_target_pairs={{8,0},{16,8},{24,16},{0,24},{9,1},{17,9},{25,17},{1,25},{10,2},{18... | collective-permute-start | bytes 393224 | tf_op jit(solution)/shard_map/ppermute | solution.py:18
  4.6 8.5 %copy-start.4 = (s32[40,2]{0,1:T(2,128)S(1)}, s32[40,2]{0,1:T(2,128)}, u32[]{:S(2)}) copy-start(s32[40,2]{0,1:T(2,128)} %param.25) | copy-start | bytes 964
  4.6 8.5 %copy-start.5 = (s32[12,2]{0,1:T(2,128)S(1)}, s32[12,2]{0,1:T(2,128)}, u32[]{:S(2)}) copy-start(s32[12,2]{0,1:T(2,128)} %param.23) | copy-start | bytes 292
  4.6 9.3 %copy-start.1 = (bf16[12,128,128]{2,1,0:T(8,128)(2,1)S(1)}, bf16[12,128,128]{2,1,0:T(8,128)(2,1)}, u32[]{:S(2)}) copy-start(bf16[12,128,128]{2,1,0:T(8,128)(2,1)} %param.22) | copy-start | bytes 1179652
  6.5 21.1 %all-to-all-start = ((bf16[8,128,256]{2,1,0:T(8,128)(2,1)}), bf16[8,128,256]{2,1,0:T(8,128)(2,1)S(1)}, u32[]{:S(2)}, u32[]{:S(2)}) async-start(bf16[8,128,256]{2,1,0:T(8,128)(2,1)} %copy.29), calls=%async_computation | async-start | bytes 1048576 | tf_op jit(solution)/shard_map/all_to_all | solution.py:87
  27.9 1.6 %copy-start.2 = (s32[1,256]{1,0:T(1,128)S(1)}, s32[1,256]{1,0:T(1,128)}, u32[]{:S(2)}) copy-start(s32[1,256]{1,0:T(1,128)} %param.28) | copy-start | bytes 3076
  27.9 1.6 %copy-start.6 = (bf16[256,256]{1,0:T(8,128)(2,1)S(1)}, bf16[256,256]{1,0:T(8,128)(2,1)}, u32[]{:S(2)}) copy-start(bf16[256,256]{1,0:T(8,128)(2,1)} %param.21) | copy-start | bytes 393220
  29.5 0.7 copy-start.7
  31.4 18.3 %all-to-all-start.1 = ((bf16[8,128,256]{2,1,0:T(8,128)(2,1)}), bf16[8,128,256]{2,1,0:T(8,128)(2,1)S(1)}, u32[]{:S(2)}, u32[]{:S(2)}) async-start(bf16[8,128,256]{2,1,0:T(8,128)(2,1)} %bitcast.19), calls=%async_computation.1 | async-start | bytes 1048576 | tf_op jit(solution)/shard_map/all_to_all | solution.py:126
  35.1 14.7 %copy-start.3 = (s32[1,8]{1,0:T(1,128)S(1)}, s32[1,8]{1,0:T(1,128)}, u32[]{:S(2)}) copy-start(s32[1,8]{1,0:T(1,128)} %param.27) | copy-start | bytes 100
  35.4 14.8 %collective-permute-start.2 = (bf16[256,256]{1,0:T(8,128)(2,1)S(1)}, bf16[256,256]{1,0:T(8,128)(2,1)S(1)}, u32[]{:S(2)}, u32[]{:S(2)}) collective-permute-start(bf16[256,256]{1,0:T(8,128)(2,1)S(1)} %get-tuple-element.45), channel_id=1, source_target_pairs={{0,8},{8,16},{16,24},{24,0},{1,9},{9,17},{17,25},{25,1},{2,10},{10... | collective-permute-start | bytes 393224 | tf_op jit(solution)/shard_map/ppermute | solution.py:16
  35.5 14.7 %collective-permute-start.3 = (bf16[256,256]{1,0:T(8,128)(2,1)S(1)}, bf16[256,256]{1,0:T(8,128)(2,1)S(1)}, u32[]{:S(2)}, u32[]{:S(2)}) collective-permute-start(bf16[256,256]{1,0:T(8,128)(2,1)S(1)} %get-tuple-element.46), channel_id=1, source_target_pairs={{8,0},{16,8},{24,16},{0,24},{9,1},{17,9},{25,17},{1,25},{10,2},{18... | collective-permute-start | bytes 393224 | tf_op jit(solution)/shard_map/ppermute | solution.py:18
  50.2 16.8 %copy-start.8 = (f32[256,256]{1,0:T(8,128)S(1)}, f32[256,256]{1,0:T(8,128)}, u32[]{:S(2)}) copy-start(f32[256,256]{1,0:T(8,128)} %copy-done.7) | copy-start | bytes 786436
  64.4 13.2 %all-to-all-start.3 = ((f32[32,8,256]{2,1,0:T(8,128)}), f32[32,8,256]{2,1,0:T(8,128)S(1)}, u32[]{:S(2)}, u32[]{:S(2)}) async-start(f32[32,8,256]{2,1,0:T(8,128)} %broadcast_in_dim.2), calls=%async_computation.3 | async-start | bytes 524288 | tf_op jit(solution)/shard_map/all_to_all | solution.py:34

commit v7 on v6

--- a/solution.py
+++ b/solution.py
@@ -63,7 +63,23 @@
     x_band = jnp.dot(band_perm, node_feats, preferred_element_type=jnp.float32).astype(
         jnp.bfloat16
     )
-    hidden = jnp.dot(x_band, weight, preferred_element_type=jnp.float32).astype(jnp.bfloat16)
+    giving = send_lists[0]
+    tile_range = jnp.arange(tile_rows, dtype=jnp.int32)
+    give_onehot = (giving[:, None] == tile_range[None, :]).astype(jnp.bfloat16)
+    send_pick = jnp.einsum(
+        "sb,bai->sai",
+        give_onehot,
+        band_perm.reshape(tile_rows, tile_size, row_count),
+        preferred_element_type=jnp.float32,
+    ).astype(jnp.bfloat16)
+    outgoing = jnp.dot(
+        send_pick.reshape(peers * tile_size, row_count),
+        node_feats,
+        preferred_element_type=jnp.float32,
+    ).astype(jnp.bfloat16)
+    arrived = lax.all_to_all(
+        outgoing.reshape(peers, tile_size, width_feat), "col", split_axis=0, concat_axis=0, tiled=True
+    )
     band_row_ids = band_coords[:, 0]
     band_col_ids = band_coords[:, 1]
     band_onehot = (
@@ -75,16 +91,9 @@
         .astype(jnp.bfloat16)
         .reshape(row_count, ext_count)
     )
-    extended = padded_2(hidden, (("row", 0),), BW)
+    x_extended = padded_2(x_band, (("row", 0),), BW)
+    extended = jnp.dot(x_extended, weight, preferred_element_type=jnp.float32).astype(jnp.bfloat16)
     mixed = jnp.dot(band_dense, extended, preferred_element_type=jnp.float32)
-    blocks = hidden.reshape(tile_rows, tile_size, width_feat)
-    giving = send_lists[0]
-    tile_range = jnp.arange(tile_rows, dtype=jnp.int32)
-    give_onehot = (giving[:, None] == tile_range[None, :]).astype(jnp.bfloat16)
-    outgoing = jnp.einsum(
-        "sb,baf->saf", give_onehot, blocks, preferred_element_type=jnp.float32
-    ).astype(jnp.bfloat16)
-    arrived = lax.all_to_all(outgoing, "col", split_axis=0, concat_axis=0, tiled=True)
     owner_range = jnp.arange(peers, dtype=jnp.int32)
     live_slots = jnp.arange(slot_total, dtype=jnp.int32) < bound_count[0]
     bound_row_ids = bound_coords[:, 0]
@@ -99,7 +108,9 @@
     ).reshape(row_count, peers * tile_size)
     dense_high = bound_dense.astype(jnp.bfloat16)
     dense_low = (bound_dense - dense_high.astype(jnp.float32)).astype(jnp.bfloat16)
-    arrived_rows = arrived.reshape(peers * tile_size, width_feat)
+    arrived_rows = jnp.dot(
+        arrived.reshape(peers * tile_size, width_feat), weight, preferred_element_type=jnp.float32
+    ).astype(jnp.bfloat16)
     mixed = mixed + jnp.dot(dense_high, arrived_rows, preferred_element_type=jnp.float32)
     mixed = mixed + jnp.dot(dense_low, arrived_rows, preferred_element_type=jnp.float32)
     out_band = jax.nn.silu(mixed).astype(jnp.bfloat16)

time: 78.8 us -> 82.1 us (1.042)
  matrix products: 11.7 us -> 13.6 us
  waiting for transfers between devices: 32.2 us -> 33.6 us
    dot_general x1, matrix products: 2.28 us -> 0.92 us  [on_device(): jnp.einsum('krs,kab->rasb', slot_onehot, bound_tiles, preferred_element_t...]
    all_to_all x1, waiting for transfers between devices: 11.1 us -> 12.5 us  [on_device(): lax.all_to_all(outgoing.reshape(peers, tile_size, width_feat), 'col', spl...]
    dot_general x2 -> x3, matrix products: 1.24 us -> 2.54 us  [the longest x1 1.16 us: on_device(): jnp.einsum('sb,bai->sai', give_onehot, band_perm.reshape(tile_rows, tile_...]
    dot_general x1, matrix products: 0.22 us -> 1.12 us  [on_device(): lax.dot_general(x_band, grad_round, (((0,), (0,)), ((), ())), preferred_e...]
where the time goes in v7:
time: 82.1 us; the launch traced here: 81.6 us
  waiting for transfers between devices  33.6 us (41%)
  starting transfers between devices  17.1 us (21%)
  matrix products  13.6 us (17%)
  blocking collectives  13.2 us (16%)
  local copies, waits for them, and re-layouts  2.41 us (3%)
  between operations  1.6 us (2%)
    all_to_all x1, blocking collectives, spread_sum(): gathered = lax.all_to_all(value.reshape(piece), axes, 0, 0, tiled=True)  13.2 us
    all_to_all x1, waiting for transfers between devices, on_device(): lax.all_to_all(to_owner, 'col', split_axis=0, concat_axis=0, tiled=True)  12.5 us
    all_to_all x1, waiting for transfers between devices, on_device(): lax.all_to_all(outgoing.reshape(peers, tile_size, width_feat), 'col', spl...  12.5 us
    all_to_all x1, waiting for transfers between devices, spread_sum(): return lax.all_to_all(copies, axes, 0, 0, tiled=True).reshape(value.shape)  8.57 us
    all_to_all x1, starting transfers between devices, on_device(): lax.all_to_all(outgoing.reshape(peers, tile_size, width_feat), 'col', spl...  6.72 us
    ppermute x2, starting transfers between devices, padded_2(): lax.ppermute(head, axis, [((i + 1) % count, i) for i in range(count)])  3.69 us
    all_to_all x1, starting transfers between devices, on_device(): lax.all_to_all(to_owner, 'col', split_axis=0, concat_axis=0, tiled=True)  3.63 us
    all_to_all x1, starting transfers between devices, spread_sum(): return lax.all_to_all(copies, axes, 0, 0, tiled=True).reshape(value.shape)  2.59 us
  transfers between devices with their start and end apart: 7, of which 3 were waited for; matrix products, arithmetic and copies ran while one was open for 10% of the time, Pallas kernels for 0%

profile of v7, /device:TPU:0, one launch (start us, length us, event | category | flops | bytes accessed | tf_op | source)
XLA Modules:
  0.0 81.6 jit_solution(6518992282440661921)
XLA Ops:
  0.6 0.0 copy-start
  0.6 0.0 copy-start.3
  0.7 1.9 %convolution_convert_fusion.8 = bf16[256,256]{1,0:T(8,128)(2,1)} fusion(bf16[256,256]{1,0:T(8,128)(2,1)} %param.19, s32[256]{0:T(256)} %bitcast.93), kind=kOutput, calls=%fused_computation.20 | convolution fusion | flops 33685504 | bytes 263168 | tf_op jit(solution)/shard_map/dot_general | solution.py:63
  2.5 0.5 collective-permute-start
  3.0 2.0 %collective-permute-start.1 = (bf16[256,256]{1,0:T(8,128)(2,1)}, bf16[256,256]{1,0:T(8,128)(2,1)}, u32[]{:S(2)}, u32[]{:S(2)}) collective-permute-start(bf16[256,256]{1,0:T(8,128)(2,1)} %convolution_convert_fusion.8), channel_id=1, source_target_pairs={{8,0},{16,8},{24,16},{0,24},{9,1},{17,9},{25,17},{1,25},{10,2},{18... | collective-permute-start | bytes 393224 | tf_op jit(solution)/shard_map/ppermute | solution.py:18
  4.9 0.8 copy.28
  5.7 1.2 %convolution_convert_fusion.2 = bf16[8,128,256]{2,0,1:T(8,128)(2,1)S(1)} fusion(s32[2,128]{0,1:T(8,128)S(1)} %copy.28, s32[8]{0:T(128)} %bitcast.98), kind=kOutput, calls=%fused_computation.6 | convolution fusion | flops 1376272 | bytes 525344 | tf_op jit(solution)/shard_map/sb,bai->sai/dot_general | solution.py:69
  6.9 0.1 copy.29
  7.0 0.0 copy-start.5
  7.0 0.0 copy-start.6
  7.0 0.0 copy-start.2
  7.0 0.0 copy-done.3
  7.0 1.1 %convolution_convert_fusion.1 = bf16[1024,256]{1,0:T(8,128)(2,1)} fusion(bf16[1024,256]{1,0:T(8,128)(2,1)S(1)} %bitcast.89, bf16[256,256]{1,0:T(8,128)(2,1)S(1)} %copy-done.3), kind=kOutput, calls=%fused_computation.5 | convolution fusion | flops 134479872 | bytes 1179648 | tf_op jit(solution)/shard_map/dot_general | solution.py:75
  8.1 6.7 %all-to-all-start = ((bf16[8,128,256]{2,1,0:T(8,128)(2,1)}), bf16[8,128,256]{2,1,0:T(8,128)(2,1)S(1)}, u32[]{:S(2)}, u32[]{:S(2)}) async-start(bf16[8,128,256]{2,1,0:T(8,128)(2,1)} %bitcast.18), calls=%async_computation | async-start | bytes 1048576 | tf_op jit(solution)/shard_map/all_to_all | solution.py:80
  14.8 0.0 copy-done.5
  14.9 0.0 copy-done.6
  15.6 0.4 convolution_convert_fusion.3
  16.0 0.0 copy-done.1
  16.0 0.9 %fusion = f32[2,8,128,128]{3,1,2,0:T(8,128)S(1)} fusion(bf16[40,128,128]{2,1,0:T(8,128)(2,1)S(1)} %copy-done.1, pred[40]{0:T(512)(128)(4,1)S(1)} %iota_compare_fusion.9, pred[40,8]{0,1:T(8,128)(4,1)S(1)} %iota_compare_fusion.5, pred[40,2]{0,1:T(4,128)(4,1)S(1)} %iota_compare_fusion.7), kind=kOutput, calls=%fused_computation.1 | convolution fusion | flops 20972800 | bytes 2359736 | tf_op jit(solution)/shard_map/krs,kab->rasb/dot_general | solution.py:106
  16.9 12.5 %all-to-all-done = bf16[8,128,256]{2,1,0:T(8,128)(2,1)S(1)} async-done(((bf16[8,128,256]{2,1,0:T(8,128)(2,1)}), bf16[8,128,256]{2,1,0:T(8,128)(2,1)S(1)}, u32[]{:S(2)}, u32[]{:S(2)}) %all-to-all-start) | async-done | bytes 524320 | tf_op jit(solution)/shard_map/all_to_all | solution.py:80
  29.4 0.3 convolution_convert_fusion
  29.7 0.3 fusion.42
  30.0 0.3 fusion.16
  30.3 0.0 copy-start.4
  30.3 0.0 copy-start.8
  30.4 0.0 collective-permute-done
  30.4 0.0 collective-permute-done.1
  30.4 1.6 %fusion.7 = f32[256,256]{1,0:T(8,128)S(1)} fusion(f32[256,256]{1,0:T(8,128)S(1)} %fusion.42, f32[256,256]{1,0:T(8,128)S(1)} %fusion.16, bf16[256,256]{1,0:T(8,128)(2,1)S(1)} %copy-done, bf16[256,256]{1,0:T(8,128)(2,1)} %collective-permute-done.1, bf16[256,256]{1,0:T(8,128)(2,1)} %convolution_convert_fusion.8, bf16[256,256]{1,0:T(8,128)(2,1)} %collective-permute-done, ...), kind=kOutput, calls=%fused_computation.15 | convolution fusion | flops 202833920 | bytes 1703936 | tf_op jit(solution)/shard_map/dot_general | solution.py:96
  32.0 0.2 fusion.8
  32.2 0.4 fusion.15
  32.6 1.2 %fusion.3 = bf16[1024,256]{1,0:T(8,128)(2,1)} fusion(f32[1024,256]{1,0:T(8,128)S(1)} %fusion.15, bf16[256,256]{1,0:T(8,128)(2,1)S(1)} %fusion.8, f32[32,8,8,128]{3,2,1,0:T(8,128)S(1)} %bitcast.87), kind=kOutput, calls=%fused_computation.8 | convolution fusion | flops 135790592 | bytes 2752512 | tf_op jit(solution)/shard_map/dot_general | solution.py:135
  33.8 3.6 %all-to-all-start.1 = ((bf16[8,128,256]{2,1,0:T(8,128)(2,1)}), bf16[8,128,256]{2,1,0:T(8,128)(2,1)S(1)}, u32[]{:S(2)}, u32[]{:S(2)}) async-start(bf16[8,128,256]{2,1,0:T(8,128)(2,1)} %bitcast.21), calls=%async_computation.1 | async-start | bytes 1048576 | tf_op jit(solution)/shard_map/all_to_all | solution.py:137
  37.4 0.3 fusion.66
  37.7 0.1 collective-permute-start.2
  37.8 1.7 %collective-permute-start.3 = (bf16[256,256]{1,0:T(8,128)(2,1)S(1)}, bf16[256,256]{1,0:T(8,128)(2,1)S(1)}, u32[]{:S(2)}, u32[]{:S(2)}) collective-permute-start(bf16[256,256]{1,0:T(8,128)(2,1)S(1)} %get-tuple-element.44), channel_id=1, source_target_pairs={{8,0},{16,8},{24,16},{0,24},{9,1},{17,9},{25,17},{1,25},{10,2},{18... | collective-permute-start | bytes 393224 | tf_op jit(solution)/shard_map/ppermute | solution.py:18
  39.5 12.5 %all-to-all-done.1 = bf16[8,128,256]{2,1,0:T(8,128)(2,1)S(1)} async-done(((bf16[8,128,256]{2,1,0:T(8,128)(2,1)}), bf16[8,128,256]{2,1,0:T(8,128)(2,1)S(1)}, u32[]{:S(2)}, u32[]{:S(2)}) %all-to-all-start.1) | async-done | bytes 524320 | tf_op jit(solution)/shard_map/all_to_all | solution.py:137
  52.1 0.4 fusion.11
  52.5 0.0 collective-permute-done.2
  52.5 0.0 collective-permute-done.3
  52.5 0.1 fusion.34
  52.6 1.1 %convolution_bitcast_fusion = f32[32,8,256]{2,1,0:T(8,128)S(1)} fusion(bf16[256,256]{1,0:T(8,128)(2,1)} %convolution_convert_fusion.8, bf16[256,256]{1,0:T(8,128)(2,1)S(1)} %fusion.34), kind=kOutput, calls=%fused_computation.14 | convolution fusion | flops 33554432 | bytes 524288 | tf_op jit(solution)/shard_map/dot_general | solution.py:144
  53.7 13.2 %all_to_all.20 = f32[32,8,256]{2,1,0:T(8,128)S(1)} all-to-all(f32[32,8,256]{2,1,0:T(8,128)S(1)} %convolution_bitcast_fusion), channel_id=1, replica_groups=mesh['row'=4,'col'=8] {'row','col'}, dimensions={0} | all-to-all | bytes 524288 | tf_op jit(solution)/shard_map/all_to_all | solution.py:31
  66.9 0.7 broadcast_in_dim.2
  67.7 2.6 %all-to-all-start.3 = ((f32[32,8,256]{2,1,0:T(8,128)}), f32[32,8,256]{2,1,0:T(8,128)S(1)}, u32[]{:S(2)}, u32[]{:S(2)}) async-start(f32[32,8,256]{2,1,0:T(8,128)} %broadcast_in_dim.2), calls=%async_computation.3 | async-start | bytes 524288 | tf_op jit(solution)/shard_map/all_to_all | solution.py:34
  70.2 1.0 %convolution_convert_fusion.7 = bf16[256,256]{1,0:T(8,128)(2,1)} fusion(s32[256]{0:T(256)S(1)} %bitcast.96, f32[256,256]{1,0:T(8,128)S(1)} %fusion.7), kind=kOutput, calls=%fused_computation.19 | convolution fusion | flops 34013184 | bytes 394240 | tf_op jit(solution)/shard_map/dot_general | solution.py:117
  71.2 1.1 %convolution_convert_fusion.5 = bf16[256,256]{1,0:T(8,128)(2,1)} fusion(bf16[256,256]{1,0:T(8,128)(2,1)S(1)} %fusion.34, bf16[256,256]{1,0:T(8,128)(2,1)S(1)} %copy-done, s32[256]{0:T(256)S(1)} %bitcast.97), kind=kOutput, calls=%fused_computation.17 | convolution fusion | flops 67305472 | bytes 394240 | tf_op jit(solution)/shard_map/dot_general | solution.py:152
  72.3 8.6 %all-to-all-done.3 = f32[32,8,256]{2,1,0:T(8,128)S(1)} async-done(((f32[32,8,256]{2,1,0:T(8,128)}), f32[32,8,256]{2,1,0:T(8,128)S(1)}, u32[]{:S(2)}, u32[]{:S(2)}) %all-to-all-start.3) | async-done | bytes 262176 | tf_op jit(solution)/shard_map/all_to_all | solution.py:34
  80.9 0.7 copy.67
  (18 shorter events, 0.1 us)
Async XLA Ops:
  0.6 28.8 %copy-start = (bf16[256,256]{1,0:T(8,128)(2,1)S(1)}, bf16[256,256]{1,0:T(8,128)(2,1)}, u32[]{:S(2)}) copy-start(bf16[256,256]{1,0:T(8,128)(2,1)} %param.20) | copy-start | bytes 393220
  0.6 6.4 %copy-start.3 = (bf16[256,256]{1,0:T(8,128)(2,1)S(1)}, bf16[256,256]{1,0:T(8,128)(2,1)}, u32[]{:S(2)}) copy-start(bf16[256,256]{1,0:T(8,128)(2,1)} %param.19) | copy-start | bytes 393220
  2.5 27.8 %collective-permute-start = (bf16[256,256]{1,0:T(8,128)(2,1)}, bf16[256,256]{1,0:T(8,128)(2,1)}, u32[]{:S(2)}, u32[]{:S(2)}) collective-permute-start(bf16[256,256]{1,0:T(8,128)(2,1)} %convolution_convert_fusion.8), channel_id=1, source_target_pairs={{0,8},{8,16},{16,24},{24,0},{1,9},{9,17},{17,25},{25,1},{2,10},{10... | collective-permute-start | bytes 393224 | tf_op jit(solution)/shard_map/ppermute | solution.py:16
  3.0 27.4 %collective-permute-start.1 = (bf16[256,256]{1,0:T(8,128)(2,1)}, bf16[256,256]{1,0:T(8,128)(2,1)}, u32[]{:S(2)}, u32[]{:S(2)}) collective-permute-start(bf16[256,256]{1,0:T(8,128)(2,1)} %convolution_convert_fusion.8), channel_id=1, source_target_pairs={{8,0},{16,8},{24,16},{0,24},{9,1},{17,9},{25,17},{1,25},{10,2},{18... | collective-permute-start | bytes 393224 | tf_op jit(solution)/shard_map/ppermute | solution.py:18
  7.0 7.9 %copy-start.5 = (s32[40,2]{0,1:T(2,128)S(1)}, s32[40,2]{0,1:T(2,128)}, u32[]{:S(2)}) copy-start(s32[40,2]{0,1:T(2,128)} %param.25) | copy-start | bytes 964
  7.0 7.9 %copy-start.6 = (s32[12,2]{0,1:T(2,128)S(1)}, s32[12,2]{0,1:T(2,128)}, u32[]{:S(2)}) copy-start(s32[12,2]{0,1:T(2,128)} %param.23) | copy-start | bytes 292
  7.0 8.6 %copy-start.2 = (bf16[12,128,128]{2,1,0:T(8,128)(2,1)S(1)}, bf16[12,128,128]{2,1,0:T(8,128)(2,1)}, u32[]{:S(2)}) copy-start(bf16[12,128,128]{2,1,0:T(8,128)(2,1)} %param.22) | copy-start | bytes 1179652
  8.1 7.9 %copy-start.1 = (bf16[40,128,128]{2,1,0:T(8,128)(2,1)S(1)}, bf16[40,128,128]{2,1,0:T(8,128)(2,1)}, u32[]{:S(2)}) copy-start(bf16[40,128,128]{2,1,0:T(8,128)(2,1)} %param.24) | copy-start | bytes 3932164
  8.1 21.3 %all-to-all-start = ((bf16[8,128,256]{2,1,0:T(8,128)(2,1)}), bf16[8,128,256]{2,1,0:T(8,128)(2,1)S(1)}, u32[]{:S(2)}, u32[]{:S(2)}) async-start(bf16[8,128,256]{2,1,0:T(8,128)(2,1)} %bitcast.18), calls=%async_computation | async-start | bytes 1048576 | tf_op jit(solution)/shard_map/all_to_all | solution.py:80
  30.3 1.7 %copy-start.4 = (s32[1,256]{1,0:T(1,128)S(1)}, s32[1,256]{1,0:T(1,128)}, u32[]{:S(2)}) copy-start(s32[1,256]{1,0:T(1,128)} %param.28) | copy-start | bytes 3076
  30.3 1.7 %copy-start.8 = (bf16[256,256]{1,0:T(8,128)(2,1)S(1)}, bf16[256,256]{1,0:T(8,128)(2,1)}, u32[]{:S(2)}) copy-start(bf16[256,256]{1,0:T(8,128)(2,1)} %param.21) | copy-start | bytes 393220
  33.8 18.3 %all-to-all-start.1 = ((bf16[8,128,256]{2,1,0:T(8,128)(2,1)}), bf16[8,128,256]{2,1,0:T(8,128)(2,1)S(1)}, u32[]{:S(2)}, u32[]{:S(2)}) async-start(bf16[8,128,256]{2,1,0:T(8,128)(2,1)} %bitcast.21), calls=%async_computation.1 | async-start | bytes 1048576 | tf_op jit(solution)/shard_map/all_to_all | solution.py:137
  37.4 14.7 %copy-start.7 = (s32[1,8]{1,0:T(1,128)S(1)}, s32[1,8]{1,0:T(1,128)}, u32[]{:S(2)}) copy-start(s32[1,8]{1,0:T(1,128)} %param.27) | copy-start | bytes 100
  37.7 14.8 %collective-permute-start.2 = (bf16[256,256]{1,0:T(8,128)(2,1)S(1)}, bf16[256,256]{1,0:T(8,128)(2,1)S(1)}, u32[]{:S(2)}, u32[]{:S(2)}) collective-permute-start(bf16[256,256]{1,0:T(8,128)(2,1)S(1)} %get-tuple-element.43), channel_id=1, source_target_pairs={{0,8},{8,16},{16,24},{24,0},{1,9},{9,17},{17,25},{25,1},{2,10},{10... | collective-permute-start | bytes 393224 | tf_op jit(solution)/shard_map/ppermute | solution.py:16
  37.8 14.7 %collective-permute-start.3 = (bf16[256,256]{1,0:T(8,128)(2,1)S(1)}, bf16[256,256]{1,0:T(8,128)(2,1)S(1)}, u32[]{:S(2)}, u32[]{:S(2)}) collective-permute-start(bf16[256,256]{1,0:T(8,128)(2,1)S(1)} %get-tuple-element.44), channel_id=1, source_target_pairs={{8,0},{16,8},{24,16},{0,24},{9,1},{17,9},{25,17},{1,25},{10,2},{18... | collective-permute-start | bytes 393224 | tf_op jit(solution)/shard_map/ppermute | solution.py:18
  67.7 13.2 %all-to-all-start.3 = ((f32[32,8,256]{2,1,0:T(8,128)}), f32[32,8,256]{2,1,0:T(8,128)S(1)}, u32[]{:S(2)}, u32[]{:S(2)}) async-start(f32[32,8,256]{2,1,0:T(8,128)} %broadcast_in_dim.2), calls=%async_computation.3 | async-start | bytes 524288 | tf_op jit(solution)/shard_map/all_to_all | solution.py:34

commit v8 on v6

--- a/solution.py
+++ b/solution.py
@@ -77,13 +77,19 @@
     )
     extended = padded_2(hidden, (("row", 0),), BW)
     mixed = jnp.dot(band_dense, extended, preferred_element_type=jnp.float32)
-    blocks = hidden.reshape(tile_rows, tile_size, width_feat)
     giving = send_lists[0]
     tile_range = jnp.arange(tile_rows, dtype=jnp.int32)
-    give_onehot = (giving[:, None] == tile_range[None, :]).astype(jnp.bfloat16)
-    outgoing = jnp.einsum(
-        "sb,baf->saf", give_onehot, blocks, preferred_element_type=jnp.float32
-    ).astype(jnp.bfloat16)
+    send_rows = jnp.where(
+        giving[:, None] >= 0,
+        giving[:, None] * tile_size + jnp.arange(tile_size, dtype=jnp.int32)[None, :],
+        -1,
+    ).reshape(peers * tile_size)
+    send_pick = (send_rows[:, None] == node_range[None, :]).astype(jnp.bfloat16)
+    outgoing = (
+        jnp.dot(send_pick, hidden, preferred_element_type=jnp.float32)
+        .astype(jnp.bfloat16)
+        .reshape(peers, tile_size, width_feat)
+    )
     arrived = lax.all_to_all(outgoing, "col", split_axis=0, concat_axis=0, tiled=True)
     owner_range = jnp.arange(peers, dtype=jnp.int32)
     live_slots = jnp.arange(slot_total, dtype=jnp.int32) < bound_count[0]

time: 78.8 us -> 79.5 us (level)
  other arithmetic: 0.13 us -> 1.52 us
  local copies, waits for them, and re-layouts: 2.51 us -> 1.6 us
    convert_element_type x1 -> x0, local copies, waits for them, and re-layouts: 0.91 us -> none  [on_device(): outgoing = jnp.einsum('sb,baf->saf', give_onehot, blocks, preferred_eleme...]
  transfers between devices with their start and end apart: 7 -> 7, of which waited for: 3 -> 3; matrix products, arithmetic and copies ran while one was open for 10% -> 11% of each run, Pallas kernels for 0% -> 0%
where the time goes in v8:
time: 79.5 us; the launch traced here: 79 us
  waiting for transfers between devices  32.2 us (41%)
  starting transfers between devices  17.1 us (22%)
  blocking collectives  13.2 us (17%)
  matrix products  11.8 us (15%)
  between operations  1.61 us (2%)
  local copies, waits for them, and re-layouts  1.6 us (2%)
  other arithmetic  1.52 us (2%)
    all_to_all x1, blocking collectives, spread_sum(): gathered = lax.all_to_all(value.reshape(piece), axes, 0, 0, tiled=True)  13.2 us
    all_to_all x1, waiting for transfers between devices, on_device(): lax.all_to_all(to_owner, 'col', split_axis=0, concat_axis=0, tiled=True)  12.5 us
    all_to_all x1, waiting for transfers between devices, on_device(): lax.all_to_all(outgoing, 'col', split_axis=0, concat_axis=0, tiled=True)  11.1 us
    all_to_all x1, waiting for transfers between devices, spread_sum(): return lax.all_to_all(copies, axes, 0, 0, tiled=True).reshape(value.shape)  8.56 us
    all_to_all x1, starting transfers between devices, on_device(): lax.all_to_all(outgoing, 'col', split_axis=0, concat_axis=0, tiled=True)  6.52 us
    ppermute x2, starting transfers between devices, padded_2(): lax.ppermute(head, axis, [((i + 1) % count, i) for i in range(count)])  3.75 us
    all_to_all x1, starting transfers between devices, on_device(): lax.all_to_all(to_owner, 'col', split_axis=0, concat_axis=0, tiled=True)  3.64 us
    all_to_all x1, starting transfers between devices, spread_sum(): return lax.all_to_all(copies, axes, 0, 0, tiled=True).reshape(value.shape)  2.58 us
  transfers between devices with their start and end apart: 7, of which 3 were waited for; matrix products, arithmetic and copies ran while one was open for 11% of the time, Pallas kernels for 0%

profile of v8, /device:TPU:0, one launch (start us, length us, event | category | flops | bytes accessed | tf_op | source)
XLA Modules:
  0.0 79.0 jit_solution(14693904079604727743)
XLA Ops:
  0.6 0.0 copy-start
  0.6 0.0 copy-start.3
  0.7 0.0 copy-start.4
  0.7 0.0 copy-start.1
  0.7 1.2 %convolution_convert_fusion.6 = bf16[256,256]{1,0:T(8,128)(2,1)S(1)} fusion(bf16[256,256]{1,0:T(8,128)(2,1)} %param.19, s32[256]{0:T(256)} %bitcast.107), kind=kOutput, calls=%fused_computation.17 | convolution fusion | flops 33685504 | bytes 263168 | tf_op jit(solution)/shard_map/dot_general | solution.py:63
  1.9 0.0 copy-done
  1.9 0.2 convolution_convert_fusion.5
  2.1 0.5 collective-permute-start
  2.6 2.0 %collective-permute-start.1 = (bf16[256,256]{1,0:T(8,128)(2,1)S(1)}, bf16[256,256]{1,0:T(8,128)(2,1)}, u32[]{:S(2)}, u32[]{:S(2)}) collective-permute-start(bf16[256,256]{1,0:T(8,128)(2,1)S(1)} %convolution_convert_fusion.5), channel_id=1, source_target_pairs={{8,0},{16,8},{24,16},{0,24},{9,1},{17,9},{25,17},{1,25},{10,2},{18... | collective-permute-start | bytes 393224 | tf_op jit(solution)/shard_map/ppermute | solution.py:18
  4.6 0.7 broadcast_compare_fusion
  5.3 0.7 broadcast_multiply_fusion.1
  5.9 0.1 select_bitcast_fusion
  6.0 1.2 %convolution_convert_fusion = bf16[1024,256]{1,0:T(8,128)(2,1)} fusion(bf16[256,256]{1,0:T(8,128)(2,1)S(1)} %convolution_convert_fusion.5, s32[1024]{0:T(1024)S(1)} %select_bitcast_fusion), kind=kOutput, calls=%fused_computation.4 | convolution fusion | flops 134742016 | bytes 659456 | tf_op jit(solution)/shard_map/dot_general | solution.py:89
  7.2 6.5 %all-to-all-start = ((bf16[8,128,256]{2,1,0:T(8,128)(2,1)}), bf16[8,128,256]{2,1,0:T(8,128)(2,1)S(1)}, u32[]{:S(2)}, u32[]{:S(2)}) async-start(bf16[8,128,256]{2,1,0:T(8,128)(2,1)} %bitcast.16), calls=%async_computation | async-start | bytes 1048576 | tf_op jit(solution)/shard_map/all_to_all | solution.py:93
  14.5 0.4 convolution_convert_fusion.1
  14.8 2.3 %fusion.8 = (bf16[2,128,8,128]{3,2,1,0:T(8,128)(2,1)S(1)}, bf16[2,128,8,128]{3,2,1,0:T(8,128)(2,1)S(1)}, f32[2,8,128,128]{3,1,2,0:T(8,128)S(1)}) fusion(bf16[40,128,128]{2,1,0:T(8,128)(2,1)} %param.24, pred[40]{0:T(512)(128)(4,1)S(1)} %iota_compare_fusion.11, pred[40,8]{0,1:T(8,128)(4,1)S(1)} %iota_compare_fusion.7, pred[40,2]{0,1:T(4,128)(4,1)S(1)} %iota_compare_fusion.9), kind=kOutput, calls=%fused_computation.23 | convolution fusion | flops 22021376 | bytes 3408312 | tf_op jit(solution)/shard_map/krs,kab->rasb/dot_general | solution.py:103
  17.1 11.1 %all-to-all-done = bf16[8,128,256]{2,1,0:T(8,128)(2,1)S(1)} async-done(((bf16[8,128,256]{2,1,0:T(8,128)(2,1)}), bf16[8,128,256]{2,1,0:T(8,128)(2,1)S(1)}, u32[]{:S(2)}, u32[]{:S(2)}) %all-to-all-start) | async-done | bytes 524320 | tf_op jit(solution)/shard_map/all_to_all | solution.py:93
  28.3 0.3 fusion.14
  28.6 0.0 copy-start.2
  28.6 0.0 copy-start.6
  28.6 0.3 fusion.11
  28.9 0.0 collective-permute-done
  28.9 0.0 collective-permute-done.1
  28.9 1.2 %fusion.5 = f32[256,256]{1,0:T(8,128)S(1)} fusion(f32[256,256]{1,0:T(8,128)S(1)} %fusion.11, f32[256,256]{1,0:T(8,128)S(1)} %fusion.14, bf16[256,256]{1,0:T(8,128)(2,1)} %collective-permute-done.1, bf16[256,256]{1,0:T(8,128)(2,1)S(1)} %convolution_convert_fusion.5, bf16[256,256]{1,0:T(8,128)(2,1)} %collective-permute-done, ...), kind=kOutput, calls=%fused_computation.10 | convolution fusion | flops 101974016 | bytes 1572864 | tf_op jit(solution)/shard_map/dot_general | solution.py:79
  30.2 0.0 copy-start.7
  30.2 0.2 fusion.6
  30.4 0.4 fusion.9
  30.8 0.1 copy-done.7
  30.9 1.2 %fusion.3 = bf16[1024,256]{1,0:T(8,128)(2,1)} fusion(f32[1024,256]{1,0:T(8,128)S(1)} %fusion.9, bf16[256,256]{1,0:T(8,128)(2,1)S(1)} %fusion.6, f32[32,8,8,128]{3,2,1,0:T(8,128)S(1)} %bitcast.99), kind=kOutput, calls=%fused_computation.6 | convolution fusion | flops 135790592 | bytes 2752512 | tf_op jit(solution)/shard_map/dot_general | solution.py:130
  32.1 3.6 %all-to-all-start.1 = ((bf16[8,128,256]{2,1,0:T(8,128)(2,1)}), bf16[8,128,256]{2,1,0:T(8,128)(2,1)S(1)}, u32[]{:S(2)}, u32[]{:S(2)}) async-start(bf16[8,128,256]{2,1,0:T(8,128)(2,1)} %bitcast.19), calls=%async_computation.1 | async-start | bytes 1048576 | tf_op jit(solution)/shard_map/all_to_all | solution.py:132
  35.7 0.3 fusion.56
  36.1 0.1 collective-permute-start.2
  36.1 1.7 %collective-permute-start.3 = (bf16[256,256]{1,0:T(8,128)(2,1)S(1)}, bf16[256,256]{1,0:T(8,128)(2,1)S(1)}, u32[]{:S(2)}, u32[]{:S(2)}) collective-permute-start(bf16[256,256]{1,0:T(8,128)(2,1)S(1)} %get-tuple-element.46), channel_id=1, source_target_pairs={{8,0},{16,8},{24,16},{0,24},{9,1},{17,9},{25,17},{1,25},{10,2},{18... | collective-permute-start | bytes 393224 | tf_op jit(solution)/shard_map/ppermute | solution.py:18
  37.9 12.5 %all-to-all-done.1 = bf16[8,128,256]{2,1,0:T(8,128)(2,1)S(1)} async-done(((bf16[8,128,256]{2,1,0:T(8,128)(2,1)}), bf16[8,128,256]{2,1,0:T(8,128)(2,1)S(1)}, u32[]{:S(2)}, u32[]{:S(2)}) %all-to-all-start.1) | async-done | bytes 524320 | tf_op jit(solution)/shard_map/all_to_all | solution.py:132
  50.4 0.0 copy-done.5
  50.4 0.4 fusion.18
  50.8 0.0 collective-permute-done.2
  50.8 0.0 collective-permute-done.3
  50.8 0.0 copy-start.8
  50.8 0.1 fusion.34
  50.9 0.2 convolution_bitcast_fusion
  51.1 13.2 %all_to_all.20 = f32[32,8,256]{2,1,0:T(8,128)S(1)} all-to-all(f32[32,8,256]{2,1,0:T(8,128)S(1)} %convolution_bitcast_fusion), channel_id=1, replica_groups=mesh['row'=4,'col'=8] {'row','col'}, dimensions={0} | all-to-all | bytes 524288 | tf_op jit(solution)/shard_map/all_to_all | solution.py:31
  64.4 0.7 broadcast_in_dim.16
  65.1 2.6 %all-to-all-start.3 = ((f32[32,8,256]{2,1,0:T(8,128)}), f32[32,8,256]{2,1,0:T(8,128)S(1)}, u32[]{:S(2)}, u32[]{:S(2)}) async-start(f32[32,8,256]{2,1,0:T(8,128)} %broadcast_in_dim.16), calls=%async_computation.3 | async-start | bytes 524288 | tf_op jit(solution)/shard_map/all_to_all | solution.py:34
  67.7 1.0 %convolution_convert_fusion.4 = bf16[256,256]{1,0:T(8,128)(2,1)} fusion(s32[256]{0:T(256)S(1)} %bitcast.109, f32[256,256]{1,0:T(8,128)S(1)} %copy-done.8), kind=kOutput, calls=%fused_computation.15 | convolution fusion | flops 34013184 | bytes 394240 | tf_op jit(solution)/shard_map/dot_general | solution.py:112
  68.7 1.1 %convolution_convert_fusion.2 = bf16[256,256]{1,0:T(8,128)(2,1)} fusion(bf16[256,256]{1,0:T(8,128)(2,1)S(1)} %fusion.34, bf16[256,256]{1,0:T(8,128)(2,1)S(1)} %copy-done, s32[256]{0:T(256)S(1)} %bitcast.110), kind=kOutput, calls=%fused_computation.13 | convolution fusion | flops 67305472 | bytes 394240 | tf_op jit(solution)/shard_map/dot_general | solution.py:147
  69.7 8.6 %all-to-all-done.3 = f32[32,8,256]{2,1,0:T(8,128)S(1)} async-done(((f32[32,8,256]{2,1,0:T(8,128)}), f32[32,8,256]{2,1,0:T(8,128)S(1)}, u32[]{:S(2)}, u32[]{:S(2)}) %all-to-all-start.3) | async-done | bytes 262176 | tf_op jit(solution)/shard_map/all_to_all | solution.py:34
  78.3 0.7 copy.72
  (18 shorter events, 0.1 us)
Async XLA Ops:
  0.6 1.3 %copy-start = (bf16[256,256]{1,0:T(8,128)(2,1)S(1)}, bf16[256,256]{1,0:T(8,128)(2,1)}, u32[]{:S(2)}) copy-start(bf16[256,256]{1,0:T(8,128)(2,1)} %param.20) | copy-start | bytes 393220
  0.6 13.1 %copy-start.3 = (s32[40,2]{0,1:T(2,128)S(1)}, s32[40,2]{0,1:T(2,128)}, u32[]{:S(2)}) copy-start(s32[40,2]{0,1:T(2,128)} %param.25) | copy-start | bytes 964
  0.7 13.1 %copy-start.4 = (s32[12,2]{0,1:T(2,128)S(1)}, s32[12,2]{0,1:T(2,128)}, u32[]{:S(2)}) copy-start(s32[12,2]{0,1:T(2,128)} %param.23) | copy-start | bytes 292
  0.7 13.8 %copy-start.1 = (bf16[12,128,128]{2,1,0:T(8,128)(2,1)S(1)}, bf16[12,128,128]{2,1,0:T(8,128)(2,1)}, u32[]{:S(2)}) copy-start(bf16[12,128,128]{2,1,0:T(8,128)(2,1)} %param.22) | copy-start | bytes 1179652
  2.1 26.8 %collective-permute-start = (bf16[256,256]{1,0:T(8,128)(2,1)S(1)}, bf16[256,256]{1,0:T(8,128)(2,1)}, u32[]{:S(2)}, u32[]{:S(2)}) collective-permute-start(bf16[256,256]{1,0:T(8,128)(2,1)S(1)} %convolution_convert_fusion.5), channel_id=1, source_target_pairs={{0,8},{8,16},{16,24},{24,0},{1,9},{9,17},{17,25},{25,1},{2,10},{10... | collective-permute-start | bytes 393224 | tf_op jit(solution)/shard_map/ppermute | solution.py:16
  2.6 26.3 %collective-permute-start.1 = (bf16[256,256]{1,0:T(8,128)(2,1)S(1)}, bf16[256,256]{1,0:T(8,128)(2,1)}, u32[]{:S(2)}, u32[]{:S(2)}) collective-permute-start(bf16[256,256]{1,0:T(8,128)(2,1)S(1)} %convolution_convert_fusion.5), channel_id=1, source_target_pairs={{8,0},{16,8},{24,16},{0,24},{9,1},{17,9},{25,17},{1,25},{10,2},{18... | collective-permute-start | bytes 393224 | tf_op jit(solution)/shard_map/ppermute | solution.py:18
  7.2 21.1 %all-to-all-start = ((bf16[8,128,256]{2,1,0:T(8,128)(2,1)}), bf16[8,128,256]{2,1,0:T(8,128)(2,1)S(1)}, u32[]{:S(2)}, u32[]{:S(2)}) async-start(bf16[8,128,256]{2,1,0:T(8,128)(2,1)} %bitcast.16), calls=%async_computation | async-start | bytes 1048576 | tf_op jit(solution)/shard_map/all_to_all | solution.py:93
  28.6 1.6 %copy-start.2 = (s32[1,256]{1,0:T(1,128)S(1)}, s32[1,256]{1,0:T(1,128)}, u32[]{:S(2)}) copy-start(s32[1,256]{1,0:T(1,128)} %param.28) | copy-start | bytes 3076
  28.6 1.6 %copy-start.6 = (bf16[256,256]{1,0:T(8,128)(2,1)S(1)}, bf16[256,256]{1,0:T(8,128)(2,1)}, u32[]{:S(2)}) copy-start(bf16[256,256]{1,0:T(8,128)(2,1)} %param.21) | copy-start | bytes 393220
  30.2 0.7 copy-start.7
  32.1 18.3 %all-to-all-start.1 = ((bf16[8,128,256]{2,1,0:T(8,128)(2,1)}), bf16[8,128,256]{2,1,0:T(8,128)(2,1)S(1)}, u32[]{:S(2)}, u32[]{:S(2)}) async-start(bf16[8,128,256]{2,1,0:T(8,128)(2,1)} %bitcast.19), calls=%async_computation.1 | async-start | bytes 1048576 | tf_op jit(solution)/shard_map/all_to_all | solution.py:132
  35.7 14.7 %copy-start.5 = (s32[1,8]{1,0:T(1,128)S(1)}, s32[1,8]{1,0:T(1,128)}, u32[]{:S(2)}) copy-start(s32[1,8]{1,0:T(1,128)} %param.27) | copy-start | bytes 100
  36.1 14.8 %collective-permute-start.2 = (bf16[256,256]{1,0:T(8,128)(2,1)S(1)}, bf16[256,256]{1,0:T(8,128)(2,1)S(1)}, u32[]{:S(2)}, u32[]{:S(2)}) collective-permute-start(bf16[256,256]{1,0:T(8,128)(2,1)S(1)} %get-tuple-element.45), channel_id=1, source_target_pairs={{0,8},{8,16},{16,24},{24,0},{1,9},{9,17},{17,25},{25,1},{2,10},{10... | collective-permute-start | bytes 393224 | tf_op jit(solution)/shard_map/ppermute | solution.py:16
  36.1 14.7 %collective-permute-start.3 = (bf16[256,256]{1,0:T(8,128)(2,1)S(1)}, bf16[256,256]{1,0:T(8,128)(2,1)S(1)}, u32[]{:S(2)}, u32[]{:S(2)}) collective-permute-start(bf16[256,256]{1,0:T(8,128)(2,1)S(1)} %get-tuple-element.46), channel_id=1, source_target_pairs={{8,0},{16,8},{24,16},{0,24},{9,1},{17,9},{25,17},{1,25},{10,2},{18... | collective-permute-start | bytes 393224 | tf_op jit(solution)/shard_map/ppermute | solution.py:18
  50.8 16.8 %copy-start.8 = (f32[256,256]{1,0:T(8,128)S(1)}, f32[256,256]{1,0:T(8,128)}, u32[]{:S(2)}) copy-start(f32[256,256]{1,0:T(8,128)} %copy-done.7) | copy-start | bytes 786436
  65.1 13.2 %all-to-all-start.3 = ((f32[32,8,256]{2,1,0:T(8,128)}), f32[32,8,256]{2,1,0:T(8,128)S(1)}, u32[]{:S(2)}, u32[]{:S(2)}) async-start(f32[32,8,256]{2,1,0:T(8,128)} %broadcast_in_dim.16), calls=%async_computation.3 | async-start | bytes 524288 | tf_op jit(solution)/shard_map/all_to_all | solution.py:34

commit v9 on v8

--- a/solution.py
+++ b/solution.py
@@ -63,7 +63,6 @@
     x_band = jnp.dot(band_perm, node_feats, preferred_element_type=jnp.float32).astype(
         jnp.bfloat16
     )
-    hidden = jnp.dot(x_band, weight, preferred_element_type=jnp.float32).astype(jnp.bfloat16)
     band_row_ids = band_coords[:, 0]
     band_col_ids = band_coords[:, 1]
     band_onehot = (
@@ -75,7 +74,8 @@
         .astype(jnp.bfloat16)
         .reshape(row_count, ext_count)
     )
-    extended = padded_2(hidden, (("row", 0),), BW)
+    x_extended = padded_2(x_band, (("row", 0),), BW)
+    extended = jnp.dot(x_extended, weight, preferred_element_type=jnp.float32).astype(jnp.bfloat16)
     mixed = jnp.dot(band_dense, extended, preferred_element_type=jnp.float32)
     giving = send_lists[0]
     tile_range = jnp.arange(tile_rows, dtype=jnp.int32)
@@ -84,9 +84,12 @@
         giving[:, None] * tile_size + jnp.arange(tile_size, dtype=jnp.int32)[None, :],
         -1,
     ).reshape(peers * tile_size)
-    send_pick = (send_rows[:, None] == node_range[None, :]).astype(jnp.bfloat16)
+    send_nodes = jnp.take(order, jnp.maximum(send_rows, 0))
+    send_pick = ((send_nodes[:, None] == node_range[None, :]) & (send_rows[:, None] >= 0)).astype(
+        jnp.bfloat16
+    )
     outgoing = (
-        jnp.dot(send_pick, hidden, preferred_element_type=jnp.float32)
+        jnp.dot(send_pick, node_feats, preferred_element_type=jnp.float32)
         .astype(jnp.bfloat16)
         .reshape(peers, tile_size, width_feat)
     )
@@ -105,7 +108,10 @@
     ).reshape(row_count, peers * tile_size)
     dense_high = bound_dense.astype(jnp.bfloat16)
     dense_low = (bound_dense - dense_high.astype(jnp.float32)).astype(jnp.bfloat16)
-    arrived_rows = arrived.reshape(peers * tile_size, width_feat)
+    arrived_x = arrived.reshape(peers * tile_size, width_feat)
+    arrived_rows = jnp.dot(arrived_x, weight, preferred_element_type=jnp.float32).astype(
+        jnp.bfloat16
+    )
     mixed = mixed + jnp.dot(dense_high, arrived_rows, preferred_element_type=jnp.float32)
     mixed = mixed + jnp.dot(dense_low, arrived_rows, preferred_element_type=jnp.float32)
     out_band = jax.nn.silu(mixed).astype(jnp.bfloat16)
@@ -128,17 +134,37 @@
     owner_terms = lax.dot_general(
         dense_high, slope, contract_rows, preferred_element_type=jnp.float32
     ) + lax.dot_general(dense_low, slope, contract_rows, preferred_element_type=jnp.float32)
-    to_owner = owner_terms.astype(jnp.bfloat16).reshape(peers, tile_size, width_feat)
-    returned = lax.all_to_all(to_owner, "col", split_axis=0, concat_axis=0, tiled=True)
-    block_onehot = (giving[None, :] == tile_range[:, None]).astype(jnp.bfloat16)
+    owner_round = owner_terms.astype(jnp.bfloat16)
+    to_owner = owner_round.reshape(peers, tile_size, width_feat)
+    own_terms = ext_grad[BW : BW + row_count]
+    local_high = own_terms.astype(jnp.bfloat16)
+    local_low = (own_terms - local_high.astype(jnp.float32)).astype(jnp.bfloat16)
+    x_rims = jnp.concatenate([x_extended[:BW], x_extended[BW + row_count :]], axis=0)
+    partial_weight = (
+        lax.dot_general(x_band, local_high, contract_rows, preferred_element_type=jnp.float32)
+        + lax.dot_general(x_band, local_low, contract_rows, preferred_element_type=jnp.float32)
+        + lax.dot_general(x_rims, rim_terms, contract_rows, preferred_element_type=jnp.float32)
+        + lax.dot_general(arrived_x, owner_round, contract_rows, preferred_element_type=jnp.float32)
+    )
+    here = lax.axis_index("col")
+    returned = jnp.stack(
+        [
+            lax.ppermute(
+                jnp.take(to_owner, (here + k) % peers, axis=0),
+                "col",
+                [(i, (i + k) % peers) for i in range(peers)],
+            )
+            for k in range(1, peers)
+        ]
+    )
+    source_cols = (here - jnp.arange(1, peers, dtype=jnp.int32)) % peers
+    back_blocks = jnp.take(giving, source_cols)
+    block_onehot = (back_blocks[None, :] == tile_range[:, None]).astype(jnp.bfloat16)
     from_peers = jnp.einsum(
         "bs,saf->baf", block_onehot, returned, preferred_element_type=jnp.float32
     )
     grad_hidden = grad_hidden + from_peers.reshape(row_count, width_feat)
     grad_round = grad_hidden.astype(jnp.bfloat16)
-    partial_weight = lax.dot_general(
-        x_band, grad_round, (((0,), (0,)), ((), ())), preferred_element_type=jnp.float32
-    )
     nodes_all = row_count * lax.axis_size("row") * peers
     weight_grad = spread_sum(partial_weight, ("row", "col"), nodes_all ** (-0.5))
     feat_band = lax.dot_general(

time: 79.5 us -> 87.9 us (1.11)
  blocking collectives: 13.2 us -> 0 us
  starting transfers between devices: 17.1 us -> 30.1 us
  local copies, waits for them, and re-layouts: 1.6 us -> 11.1 us
  waiting for transfers between devices: 32.2 us -> 27.6 us
  matrix products: 11.8 us -> 15.1 us
    all_to_all x1 -> x0, blocking collectives: 13.2 us -> none  [spread_sum(): gathered = lax.all_to_all(value.reshape(piece), axes, 0, 0, tiled=True)]
    all_to_all x1, waiting for transfers between devices: 12.5 us -> 0.01 us  [spread_sum(): gathered = lax.all_to_all(value.reshape(piece), axes, 0, 0, tiled=True)]
    ppermute x0 -> x7, starting transfers between devices: none -> 11 us  [on_device(): lax.ppermute(jnp.take(to_owner, (here + k) % peers, axis=0), 'col', [(i,...]
    gather x0 -> x2, local copies, waits for them, and re-layouts: none -> 7.48 us  [the longest x1 6.83 us: on_device(): send_nodes = jnp.take(order, jnp.maximum(send_rows, 0))]
    ppermute x0 -> x7, waiting for transfers between devices: none -> 5.93 us  [on_device(): lax.ppermute(jnp.take(to_owner, (here + k) % peers, axis=0), 'col', [(i,...]
    dot_general x3 -> x6, matrix products: 1.57 us -> 6.11 us  [the longest x1 1.95 us: on_device(): lax.dot_general(x_rims, rim_terms, contract_rows, preferred_element_type=...]
    all_to_all x1, starting transfers between devices: 2.58 us -> 6.54 us  [spread_sum(): return lax.all_to_all(copies, axes, 0, 0, tiled=True).reshape(value.shape)]
    another operation x0 -> x8, local copies, waits for them, and re-layouts: none -> 2.13 us  [on_device(): jnp.stack([lax.ppermute(jnp.take(to_owner, (here + k) % peers, axis=0), '...]
  transfers between devices with their start and end apart: 7 -> 14, of which waited for: 3 -> 5; matrix products, arithmetic and copies ran while one was open for 11% -> 21% of each run, Pallas kernels for 0% -> 0%
where the time goes in v9:
time: 87.9 us; the launch traced here: 87.5 us
  starting transfers between devices  30.1 us (34%)
  waiting for transfers between devices  27.6 us (31%)
  matrix products  15.1 us (17%)
  local copies, waits for them, and re-layouts  11.1 us (13%)
  between operations  1.85 us (2%)
  other arithmetic  1.77 us (2%)
    all_to_all x1, waiting for transfers between devices, on_device(): lax.all_to_all(outgoing, 'col', split_axis=0, concat_axis=0, tiled=True)  12.5 us
    ppermute x7, starting transfers between devices, on_device(): lax.ppermute(jnp.take(to_owner, (here + k) % peers, axis=0), 'col', [(i,...  11 us
    all_to_all x1, waiting for transfers between devices, spread_sum(): return lax.all_to_all(copies, axes, 0, 0, tiled=True).reshape(value.shape)  9.16 us
    gather x1, local copies, waits for them, and re-layouts, on_device(): send_nodes = jnp.take(order, jnp.maximum(send_rows, 0))  6.83 us
    all_to_all x1, starting transfers between devices, spread_sum(): return lax.all_to_all(copies, axes, 0, 0, tiled=True).reshape(value.shape)  6.54 us
    all_to_all x1, starting transfers between devices, on_device(): lax.all_to_all(outgoing, 'col', split_axis=0, concat_axis=0, tiled=True)  5.94 us
    ppermute x7, waiting for transfers between devices, on_device(): lax.ppermute(jnp.take(to_owner, (here + k) % peers, axis=0), 'col', [(i,...  5.93 us
    all_to_all x1, starting transfers between devices, spread_sum(): gathered = lax.all_to_all(value.reshape(piece), axes, 0, 0, tiled=True)  3.62 us
  transfers between devices with their start and end apart: 14, of which 5 were waited for; matrix products, arithmetic and copies ran while one was open for 21% of the time, Pallas kernels for 0%

profile of v9, /device:TPU:0, one launch (start us, length us, event | category | flops | bytes accessed | tf_op | source)
XLA Modules:
  0.0 87.5 jit_solution(14171564779471550964)
XLA Ops:
  0.7 1.8 %convolution_convert_fusion.7 = bf16[256,256]{1,0:T(8,128)(2,1)} fusion(bf16[256,256]{1,0:T(8,128)(2,1)} %param.21, s32[256]{0:T(256)} %bitcast.116), kind=kOutput, calls=%fused_computation.24 | convolution fusion | flops 33685504 | bytes 263168 | tf_op jit(solution)/shard_map/dot_general | solution.py:63
  2.5 2.4 %collective-permute-start.1 = (bf16[256,256]{1,0:T(8,128)(2,1)}, bf16[256,256]{1,0:T(8,128)(2,1)}, u32[]{:S(2)}, u32[]{:S(2)}) collective-permute-start(bf16[256,256]{1,0:T(8,128)(2,1)} %convolution_convert_fusion.7), channel_id=1, source_target_pairs={{8,0},{16,8},{24,16},{0,24},{9,1},{17,9},{25,17},{1,25},{10,2},{18... | collective-permute-start | bytes 393224 | tf_op jit(solution)/shard_map/ppermute | solution.py:18
  4.9 0.7 broadcast_multiply_fusion.1
  5.6 0.7 broadcast_compare_fusion
  6.4 6.8 %gather_fusion = s32[1024]{0:T(1024)S(1)} fusion(s32[256]{0:T(256)S(1)} %bitcast.117, s32[1024]{0:T(1024)S(1)} %bitcast_clamp_fusion), kind=kCustom, calls=%fused_computation | custom fusion | bytes 12288 | tf_op jit(solution)/shard_map/jit(_take)/gather | solution.py:87
  13.3 1.3 %convolution_convert_fusion.1 = bf16[1024,256]{1,0:T(8,128)(2,1)} fusion(bf16[256,256]{1,0:T(8,128)(2,1)S(1)} %copy-done.5, s32[1024]{0:T(1024)S(1)} %fusion.59, pred[1024]{0:T(1024)(128)(4,1)S(1)} %fusion.60), kind=kOutput, calls=%fused_computation.7 | convolution fusion | flops 135004160 | bytes 660480 | tf_op jit(solution)/shard_map/dot_general | solution.py:92
  14.6 5.9 %all-to-all-start = ((bf16[8,128,256]{2,1,0:T(8,128)(2,1)}), bf16[8,128,256]{2,1,0:T(8,128)(2,1)S(1)}, u32[]{:S(2)}, u32[]{:S(2)}) async-start(bf16[8,128,256]{2,1,0:T(8,128)(2,1)} %bitcast.18), calls=%async_computation | async-start | bytes 1048576 | tf_op jit(solution)/shard_map/all_to_all | solution.py:96
  21.5 0.6 gather_fusion.1
  22.1 0.4 convolution_convert_fusion.2
  22.5 0.9 %fusion = f32[2,8,128,128]{3,1,2,0:T(8,128)S(1)} fusion(bf16[40,128,128]{2,1,0:T(8,128)(2,1)S(1)} %copy-done.3, pred[40]{0:T(512)(128)(4,1)S(1)} %iota_compare_fusion.10, pred[40,8]{0,1:T(8,128)(4,1)S(1)} %iota_compare_fusion.6, pred[40,2]{0,1:T(4,128)(4,1)S(1)} %iota_compare_fusion.8), kind=kOutput, calls=%fused_computation.3 | convolution fusion | flops 20972800 | bytes 2359736 | tf_op jit(solution)/shard_map/krs,kab->rasb/dot_general | solution.py:106
  23.4 12.5 %all-to-all-done = bf16[8,128,256]{2,1,0:T(8,128)(2,1)S(1)} async-done(((bf16[8,128,256]{2,1,0:T(8,128)(2,1)}), bf16[8,128,256]{2,1,0:T(8,128)(2,1)S(1)}, u32[]{:S(2)}, u32[]{:S(2)}) %all-to-all-start) | async-done | bytes 524320 | tf_op jit(solution)/shard_map/all_to_all | solution.py:96
  35.9 0.3 convolution_convert_fusion
  36.2 0.3 fusion.47
  36.6 0.3 fusion.19
  36.9 1.6 %fusion.9 = f32[256,256]{1,0:T(8,128)S(1)} fusion(f32[256,256]{1,0:T(8,128)S(1)} %fusion.47, f32[256,256]{1,0:T(8,128)S(1)} %fusion.19, bf16[256,256]{1,0:T(8,128)(2,1)S(1)} %copy-done, bf16[256,256]{1,0:T(8,128)(2,1)} %collective-permute-done.1, bf16[256,256]{1,0:T(8,128)(2,1)} %convolution_convert_fusion.7, bf16[256,256]{1,0:T(8,128)(2,1)} %collective-permute-done, ...), kind=kOutput, calls=%fused_computation.19 | convolution fusion | flops 202833920 | bytes 1703936 | tf_op jit(solution)/shard_map/dot_general | solution.py:79
  38.5 0.2 fusion.10
  38.8 0.4 fusion.18
  39.1 0.3 fusion.79
  39.4 0.4 fusion.3
  39.8 0.3 fusion.80
  40.2 1.1 %fusion.49 = f32[256,256]{1,0:T(8,128)S(1)} fusion(bf16[256,256]{1,0:T(8,128)(2,1)} %convolution_convert_fusion.7, f32[768,256]{1,0:T(8,128)S(1)} %get-tuple-element.69), kind=kOutput, calls=%fused_computation.71 | convolution fusion | flops 33554432 | bytes 524288 | tf_op jit(solution)/shard_map/dot_general | solution.py:144
  41.3 1.1 %convolution_add_fusion.2 = f32[256,256]{1,0:T(8,128)S(1)} fusion(f32[256,256]{1,0:T(8,128)S(1)} %fusion.49, bf16[256,256]{1,0:T(8,128)(2,1)} %convolution_convert_fusion.7, f32[768,256]{1,0:T(8,128)S(1)} %get-tuple-element.69), kind=kOutput, calls=%fused_computation.15 | convolution fusion | flops 33882112 | bytes 917504 | tf_op jit(solution)/shard_map/dot_general | solution.py:145
  42.5 1.9 %fusion.6 = f32[32,8,256]{2,1,0:T(8,128)} fusion(f32[256,256]{1,0:T(8,128)S(1)} %fusion.80, f32[256,256]{1,0:T(8,128)S(1)} %convolution_add_fusion.2, bf16[256,256]{1,0:T(8,128)(2,1)} %collective-permute-done.1, bf16[256,256]{1,0:T(8,128)(2,1)} %collective-permute-done, bf16[256,256]{1,0:T(8,128)(2,1)S(1)} %get-tuple-element.62, ...), kind=kOutput, calls=%fused_computation.14 | convolution fusion | flops 68288512 | bytes 1310720 | tf_op jit(solution)/shard_map/dot_general | solution.py:146
  44.4 3.6 %all-to-all-start.1 = ((f32[32,8,256]{2,1,0:T(8,128)}), f32[32,8,256]{2,1,0:T(8,128)S(1)}, u32[]{:S(2)}, u32[]{:S(2)}) async-start(f32[32,8,256]{2,1,0:T(8,128)} %fusion.6), calls=%async_computation.1 | async-start | bytes 524288 | tf_op jit(solution)/shard_map/all_to_all | solution.py:31
  48.1 1.8 %collective-permute-start.4 = (bf16[128,256]{1,0:T(8,128)(2,1)S(1)}, bf16[128,256]{1,0:T(8,128)(2,1)S(1)}, u32[]{:S(2)}, u32[]{:S(2)}) collective-permute-start(bf16[128,256]{1,0:T(8,128)(2,1)S(1)} %get-tuple-element.61), channel_id=1, source_target_pairs={{0,1},{1,2},{2,3},{3,4},{4,5},{5,6},{6,7},{7,0},{8,9},{9,10},{10,1... | collective-permute-start | bytes 196616 | tf_op jit(solution)/shard_map/ppermute | solution.py:152
  49.9 1.5 %collective-permute-start.5 = (bf16[128,256]{1,0:T(8,128)(2,1)S(1)}, bf16[128,256]{1,0:T(8,128)(2,1)S(1)}, u32[]{:S(2)}, u32[]{:S(2)}) collective-permute-start(bf16[128,256]{1,0:T(8,128)(2,1)S(1)} %get-tuple-element.60), channel_id=1, source_target_pairs={{0,2},{1,3},{2,4},{3,5},{4,6},{5,7},{6,0},{7,1},{8,10},{9,11},{10,... | collective-permute-start | bytes 196616 | tf_op jit(solution)/shard_map/ppermute | solution.py:152
  51.4 2.5 %collective-permute-start.6 = (bf16[128,256]{1,0:T(8,128)(2,1)S(1)}, bf16[128,256]{1,0:T(8,128)(2,1)S(1)}, u32[]{:S(2)}, u32[]{:S(2)}) collective-permute-start(bf16[128,256]{1,0:T(8,128)(2,1)S(1)} %get-tuple-element.59), channel_id=1, source_target_pairs={{0,3},{1,4},{2,5},{3,6},{4,7},{5,0},{6,1},{7,2},{8,11},{9,12},{10,... | collective-permute-start | bytes 196616 | tf_op jit(solution)/shard_map/ppermute | solution.py:152
  53.9 1.4 %collective-permute-start.7 = (bf16[128,256]{1,0:T(8,128)(2,1)S(1)}, bf16[128,256]{1,0:T(8,128)(2,1)S(1)}, u32[]{:S(2)}, u32[]{:S(2)}) collective-permute-start(bf16[128,256]{1,0:T(8,128)(2,1)S(1)} %get-tuple-element.58), channel_id=1, source_target_pairs={{0,4},{1,5},{2,6},{3,7},{4,0},{5,1},{6,2},{7,3},{8,12},{9,13},{10,... | collective-permute-start | bytes 196616 | tf_op jit(solution)/shard_map/ppermute | solution.py:152
  55.3 2.4 %collective-permute-start.8 = (bf16[128,256]{1,0:T(8,128)(2,1)S(1)}, bf16[128,256]{1,0:T(8,128)(2,1)S(1)}, u32[]{:S(2)}, u32[]{:S(2)}) collective-permute-start(bf16[128,256]{1,0:T(8,128)(2,1)S(1)} %get-tuple-element.57), channel_id=1, source_target_pairs={{0,5},{1,6},{2,7},{3,0},{4,1},{5,2},{6,3},{7,4},{8,13},{9,14},{10,... | collective-permute-start | bytes 196616 | tf_op jit(solution)/shard_map/ppermute | solution.py:152
  57.7 2.0 %collective-permute-done.4 = bf16[128,256]{1,0:T(8,128)(2,1)S(1)} collective-permute-done((bf16[128,256]{1,0:T(8,128)(2,1)S(1)}, bf16[128,256]{1,0:T(8,128)(2,1)S(1)}, u32[]{:S(2)}, u32[]{:S(2)}) %collective-permute-start.4) | collective-permute-done | bytes 65568 | tf_op jit(solution)/shard_map/ppermute | solution.py:152
  59.8 0.2 collective-permute-start.9
  60.0 1.2 %collective-permute-start.10 = (bf16[128,256]{1,0:T(8,128)(2,1)S(1)}, bf16[128,256]{1,0:T(8,128)(2,1)S(1)}, u32[]{:S(2)}, u32[]{:S(2)}) collective-permute-start(bf16[128,256]{1,0:T(8,128)(2,1)S(1)} %get-tuple-element.55), channel_id=1, source_target_pairs={{0,7},{1,0},{2,1},{3,2},{4,3},{5,4},{6,5},{7,6},{8,15},{9,8},{10,9... | collective-permute-start | bytes 196616 | tf_op jit(solution)/shard_map/ppermute | solution.py:152
  61.2 1.0 %convolution_convert_fusion.6 = bf16[256,256]{1,0:T(8,128)(2,1)} fusion(s32[256]{0:T(256)S(1)} %bitcast.119, f32[256,256]{1,0:T(8,128)S(1)} %fusion.9), kind=kOutput, calls=%fused_computation.23 | convolution fusion | flops 34013184 | bytes 394240 | tf_op jit(solution)/shard_map/dot_general | solution.py:118
  62.3 0.1 copy.86
  62.4 3.4 %collective-permute-done.6 = bf16[128,256]{1,0:T(8,128)(2,1)S(1)} collective-permute-done((bf16[128,256]{1,0:T(8,128)(2,1)S(1)}, bf16[128,256]{1,0:T(8,128)(2,1)S(1)}, u32[]{:S(2)}, u32[]{:S(2)}) %collective-permute-start.6) | collective-permute-done | bytes 65568 | tf_op jit(solution)/shard_map/ppermute | solution.py:152
  65.8 0.3 collective-permute-start.3
  66.1 0.1 copy.87
  66.2 0.3 collective-permute-start.2
  66.6 0.1 copy.89
  66.7 0.4 collective-permute-done.9
  67.3 0.1 copy.91
  67.4 1.4 %stack.31 = bf16[7,128,256]{2,0,1:T(8,128)(2,1)S(1)} concatenate(bf16[1,128,256]{2,0,1:T(2,128)(2,1)S(1)} %copy.85, bf16[1,128,256]{2,0,1:T(2,128)(2,1)S(1)} %copy.86, bf16[1,128,256]{2,0,1:T(2,128)(2,1)S(1)} %copy.87, bf16[1,128,256]{2,0,1:T(2,128)(2,1)S(1)} %copy.88, bf16[1,128,256]{2,0,1:T(2,128)(2,1)S(1)} %copy.89, bf16[1,128,256]{2,0,1:T(2,128)(2,1)S(1)} %copy.90, ...), dimensions={0} | concatenate | bytes 917504 | tf_op jit(solution)/shard_map/stack | solution.py:150
  68.9 0.7 broadcast_in_dim.34
  69.6 6.5 %all-to-all-start.2 = ((f32[32,8,256]{2,1,0:T(8,128)}), f32[32,8,256]{2,1,0:T(8,128)S(1)}, u32[]{:S(2)}, u32[]{:S(2)}) async-start(f32[32,8,256]{2,1,0:T(8,128)} %broadcast_in_dim.34), calls=%async_computation.2 | async-start | bytes 524288 | tf_op jit(solution)/shard_map/all_to_all | solution.py:34
  76.1 0.3 fusion.66
  76.5 1.1 %convolution_convert_fusion.4 = bf16[256,256]{1,0:T(8,128)(2,1)} fusion(bf16[256,256]{1,0:T(8,128)(2,1)S(1)} %fusion.41, bf16[256,256]{1,0:T(8,128)(2,1)S(1)} %copy-done, s32[256]{0:T(256)S(1)} %bitcast.120), kind=kOutput, calls=%fused_computation.21 | convolution fusion | flops 67305472 | bytes 394240 | tf_op jit(solution)/shard_map/dot_general | solution.py:173
  77.6 9.2 %all-to-all-done.2 = f32[32,8,256]{2,1,0:T(8,128)S(1)} async-done(((f32[32,8,256]{2,1,0:T(8,128)}), f32[32,8,256]{2,1,0:T(8,128)S(1)}, u32[]{:S(2)}, u32[]{:S(2)}) %all-to-all-start.2) | async-done | bytes 262176 | tf_op jit(solution)/shard_map/all_to_all | solution.py:34
  86.8 0.7 copy.126
  (50 shorter events, 0.9 us)
Async XLA Ops:
  0.6 35.3 %copy-start = (bf16[256,256]{1,0:T(8,128)(2,1)S(1)}, bf16[256,256]{1,0:T(8,128)(2,1)}, u32[]{:S(2)}) copy-start(bf16[256,256]{1,0:T(8,128)(2,1)} %param.22) | copy-start | bytes 393220
  0.6 5.7 %copy-start.1 = (s32[1,256]{1,0:T(1,128)S(1)}, s32[1,256]{1,0:T(1,128)}, u32[]{:S(2)}) copy-start(s32[1,256]{1,0:T(1,128)} %param.30) | copy-start | bytes 3076
  2.5 34.4 %collective-permute-start.1 = (bf16[256,256]{1,0:T(8,128)(2,1)}, bf16[256,256]{1,0:T(8,128)(2,1)}, u32[]{:S(2)}, u32[]{:S(2)}) collective-permute-start(bf16[256,256]{1,0:T(8,128)(2,1)} %convolution_convert_fusion.7), channel_id=1, source_target_pairs={{8,0},{16,8},{24,16},{0,24},{9,1},{17,9},{25,17},{1,25},{10,2},{18... | collective-permute-start | bytes 393224 | tf_op jit(solution)/shard_map/ppermute | solution.py:18
  4.9 32.0 %collective-permute-start = (bf16[256,256]{1,0:T(8,128)(2,1)}, bf16[256,256]{1,0:T(8,128)(2,1)}, u32[]{:S(2)}, u32[]{:S(2)}) collective-permute-start(bf16[256,256]{1,0:T(8,128)(2,1)} %convolution_convert_fusion.7), channel_id=1, source_target_pairs={{0,8},{8,16},{16,24},{24,0},{1,9},{9,17},{17,25},{25,1},{2,10},{10... | collective-permute-start | bytes 393224 | tf_op jit(solution)/shard_map/ppermute | solution.py:16
  6.4 7.0 %copy-start.5 = (bf16[256,256]{1,0:T(8,128)(2,1)S(1)}, bf16[256,256]{1,0:T(8,128)(2,1)}, u32[]{:S(2)}) copy-start(bf16[256,256]{1,0:T(8,128)(2,1)} %param.21) | copy-start | bytes 393220
  13.2 7.3 %copy-start.6 = (s32[40,2]{0,1:T(2,128)S(1)}, s32[40,2]{0,1:T(2,128)}, u32[]{:S(2)}) copy-start(s32[40,2]{0,1:T(2,128)} %param.27) | copy-start | bytes 964
  13.2 7.4 %copy-start.7 = (s32[12,2]{0,1:T(2,128)S(1)}, s32[12,2]{0,1:T(2,128)}, u32[]{:S(2)}) copy-start(s32[12,2]{0,1:T(2,128)} %param.25) | copy-start | bytes 292
  13.3 8.2 %copy-start.2 = (s32[1,8]{1,0:T(1,128)S(1)}, s32[1,8]{1,0:T(1,128)}, u32[]{:S(2)}) copy-start(s32[1,8]{1,0:T(1,128)} %param.29) | copy-start | bytes 100
  13.3 8.8 %copy-start.4 = (bf16[12,128,128]{2,1,0:T(8,128)(2,1)S(1)}, bf16[12,128,128]{2,1,0:T(8,128)(2,1)}, u32[]{:S(2)}) copy-start(bf16[12,128,128]{2,1,0:T(8,128)(2,1)} %param.24) | copy-start | bytes 1179652
  14.6 7.9 %copy-start.3 = (bf16[40,128,128]{2,1,0:T(8,128)(2,1)S(1)}, bf16[40,128,128]{2,1,0:T(8,128)(2,1)}, u32[]{:S(2)}) copy-start(bf16[40,128,128]{2,1,0:T(8,128)(2,1)} %param.26) | copy-start | bytes 3932164
  14.6 21.3 %all-to-all-start = ((bf16[8,128,256]{2,1,0:T(8,128)(2,1)}), bf16[8,128,256]{2,1,0:T(8,128)(2,1)S(1)}, u32[]{:S(2)}, u32[]{:S(2)}) async-start(bf16[8,128,256]{2,1,0:T(8,128)(2,1)} %bitcast.18), calls=%async_computation | async-start | bytes 1048576 | tf_op jit(solution)/shard_map/all_to_all | solution.py:96
  36.9 1.6 %copy-start.8 = (bf16[256,256]{1,0:T(8,128)(2,1)S(1)}, bf16[256,256]{1,0:T(8,128)(2,1)}, u32[]{:S(2)}) copy-start(bf16[256,256]{1,0:T(8,128)(2,1)} %param.23) | copy-start | bytes 393220
  44.4 24.4 %all-to-all-start.1 = ((f32[32,8,256]{2,1,0:T(8,128)}), f32[32,8,256]{2,1,0:T(8,128)S(1)}, u32[]{:S(2)}, u32[]{:S(2)}) async-start(f32[32,8,256]{2,1,0:T(8,128)} %fusion.6), calls=%async_computation.1 | async-start | bytes 524288 | tf_op jit(solution)/shard_map/all_to_all | solution.py:31
  48.1 11.7 %collective-permute-start.4 = (bf16[128,256]{1,0:T(8,128)(2,1)S(1)}, bf16[128,256]{1,0:T(8,128)(2,1)S(1)}, u32[]{:S(2)}, u32[]{:S(2)}) collective-permute-start(bf16[128,256]{1,0:T(8,128)(2,1)S(1)} %get-tuple-element.61), channel_id=1, source_target_pairs={{0,1},{1,2},{2,3},{3,4},{4,5},{5,6},{6,7},{7,0},{8,9},{9,10},{10,1... | collective-permute-start | bytes 196616 | tf_op jit(solution)/shard_map/ppermute | solution.py:152
  49.9 10.0 %collective-permute-start.5 = (bf16[128,256]{1,0:T(8,128)(2,1)S(1)}, bf16[128,256]{1,0:T(8,128)(2,1)S(1)}, u32[]{:S(2)}, u32[]{:S(2)}) collective-permute-start(bf16[128,256]{1,0:T(8,128)(2,1)S(1)} %get-tuple-element.60), channel_id=1, source_target_pairs={{0,2},{1,3},{2,4},{3,5},{4,6},{5,7},{6,0},{7,1},{8,10},{9,11},{10,... | collective-permute-start | bytes 196616 | tf_op jit(solution)/shard_map/ppermute | solution.py:152
  51.4 14.4 %collective-permute-start.6 = (bf16[128,256]{1,0:T(8,128)(2,1)S(1)}, bf16[128,256]{1,0:T(8,128)(2,1)S(1)}, u32[]{:S(2)}, u32[]{:S(2)}) collective-permute-start(bf16[128,256]{1,0:T(8,128)(2,1)S(1)} %get-tuple-element.59), channel_id=1, source_target_pairs={{0,3},{1,4},{2,5},{3,6},{4,7},{5,0},{6,1},{7,2},{8,11},{9,12},{10,... | collective-permute-start | bytes 196616 | tf_op jit(solution)/shard_map/ppermute | solution.py:152
  53.9 12.3 %collective-permute-start.7 = (bf16[128,256]{1,0:T(8,128)(2,1)S(1)}, bf16[128,256]{1,0:T(8,128)(2,1)S(1)}, u32[]{:S(2)}, u32[]{:S(2)}) collective-permute-start(bf16[128,256]{1,0:T(8,128)(2,1)S(1)} %get-tuple-element.58), channel_id=1, source_target_pairs={{0,4},{1,5},{2,6},{3,7},{4,0},{5,1},{6,2},{7,3},{8,12},{9,13},{10,... | collective-permute-start | bytes 196616 | tf_op jit(solution)/shard_map/ppermute | solution.py:152
  55.3 11.3 %collective-permute-start.8 = (bf16[128,256]{1,0:T(8,128)(2,1)S(1)}, bf16[128,256]{1,0:T(8,128)(2,1)S(1)}, u32[]{:S(2)}, u32[]{:S(2)}) collective-permute-start(bf16[128,256]{1,0:T(8,128)(2,1)S(1)} %get-tuple-element.57), channel_id=1, source_target_pairs={{0,5},{1,6},{2,7},{3,0},{4,1},{5,2},{6,3},{7,4},{8,13},{9,14},{10,... | collective-permute-start | bytes 196616 | tf_op jit(solution)/shard_map/ppermute | solution.py:152
  59.8 7.4 %collective-permute-start.9 = (bf16[128,256]{1,0:T(8,128)(2,1)S(1)}, bf16[128,256]{1,0:T(8,128)(2,1)S(1)}, u32[]{:S(2)}, u32[]{:S(2)}) collective-permute-start(bf16[128,256]{1,0:T(8,128)(2,1)S(1)} %get-tuple-element.56), channel_id=1, source_target_pairs={{0,6},{1,7},{2,0},{3,1},{4,2},{5,3},{6,4},{7,5},{8,14},{9,15},{10,... | collective-permute-start | bytes 196616 | tf_op jit(solution)/shard_map/ppermute | solution.py:152
  60.0 7.3 %collective-permute-start.10 = (bf16[128,256]{1,0:T(8,128)(2,1)S(1)}, bf16[128,256]{1,0:T(8,128)(2,1)S(1)}, u32[]{:S(2)}, u32[]{:S(2)}) collective-permute-start(bf16[128,256]{1,0:T(8,128)(2,1)S(1)} %get-tuple-element.55), channel_id=1, source_target_pairs={{0,7},{1,0},{2,1},{3,2},{4,3},{5,4},{6,5},{7,6},{8,15},{9,8},{10,9... | collective-permute-start | bytes 196616 | tf_op jit(solution)/shard_map/ppermute | solution.py:152
  65.8 10.7 %collective-permute-start.3 = (bf16[256,256]{1,0:T(8,128)(2,1)S(1)}, bf16[256,256]{1,0:T(8,128)(2,1)S(1)}, u32[]{:S(2)}, u32[]{:S(2)}) collective-permute-start(bf16[256,256]{1,0:T(8,128)(2,1)S(1)} %get-tuple-element.63), channel_id=1, source_target_pairs={{8,0},{16,8},{24,16},{0,24},{9,1},{17,9},{25,17},{1,25},{10,2},{18... | collective-permute-start | bytes 393224 | tf_op jit(solution)/shard_map/ppermute | solution.py:18
  66.2 10.3 %collective-permute-start.2 = (bf16[256,256]{1,0:T(8,128)(2,1)S(1)}, bf16[256,256]{1,0:T(8,128)(2,1)S(1)}, u32[]{:S(2)}, u32[]{:S(2)}) collective-permute-start(bf16[256,256]{1,0:T(8,128)(2,1)S(1)} %get-tuple-element.62), channel_id=1, source_target_pairs={{0,8},{8,16},{16,24},{24,0},{1,9},{9,17},{17,25},{25,1},{2,10},{10... | collective-permute-start | bytes 393224 | tf_op jit(solution)/shard_map/ppermute | solution.py:16
  69.6 17.2 %all-to-all-start.2 = ((f32[32,8,256]{2,1,0:T(8,128)}), f32[32,8,256]{2,1,0:T(8,128)S(1)}, u32[]{:S(2)}, u32[]{:S(2)}) async-start(f32[32,8,256]{2,1,0:T(8,128)} %broadcast_in_dim.34), calls=%async_computation.2 | async-start | bytes 524288 | tf_op jit(solution)/shard_map/all_to_all | solution.py:34

commit v10 on v8

--- a/solution.py
+++ b/solution.py
@@ -76,7 +76,7 @@
         .reshape(row_count, ext_count)
     )
     extended = padded_2(hidden, (("row", 0),), BW)
-    mixed = jnp.dot(band_dense, extended, preferred_element_type=jnp.float32)
+    band_mixed = jnp.dot(band_dense, extended, preferred_element_type=jnp.float32)
     giving = send_lists[0]
     tile_range = jnp.arange(tile_rows, dtype=jnp.int32)
     send_rows = jnp.where(
@@ -105,8 +105,9 @@
     ).reshape(row_count, peers * tile_size)
     dense_high = bound_dense.astype(jnp.bfloat16)
     dense_low = (bound_dense - dense_high.astype(jnp.float32)).astype(jnp.bfloat16)
+    band_mixed, arrived = lax.optimization_barrier((band_mixed, arrived))
     arrived_rows = arrived.reshape(peers * tile_size, width_feat)
-    mixed = mixed + jnp.dot(dense_high, arrived_rows, preferred_element_type=jnp.float32)
+    mixed = band_mixed + jnp.dot(dense_high, arrived_rows, preferred_element_type=jnp.float32)
     mixed = mixed + jnp.dot(dense_low, arrived_rows, preferred_element_type=jnp.float32)
     out_band = jax.nn.silu(mixed).astype(jnp.bfloat16)
     node_out = lax.dot_general(

time: 79.5 us -> 79 us (level)
  waiting for transfers between devices: 32.2 us -> 30.2 us
  matrix products: 11.8 us -> 13.5 us
    all_to_all x1, waiting for transfers between devices: 11.1 us -> 9.1 us  [on_device(): lax.all_to_all(outgoing, 'col', split_axis=0, concat_axis=0, tiled=True)]
    dot_general x1, matrix products: 0.3 us -> 1.29 us  [on_device(): jnp.dot(dense_high, arrived_rows, preferred_element_type=jnp.float32)]
  transfers between devices with their start and end apart: 7 -> 7, of which waited for: 3 -> 3; matrix products, arithmetic and copies ran while one was open for 11% -> 13% of each run, Pallas kernels for 0% -> 0%
where the time goes in v10:
time: 79 us; the launch traced here: 78.6 us
  waiting for transfers between devices  30.2 us (38%)
  starting transfers between devices  17.1 us (22%)
  matrix products  13.5 us (17%)
  blocking collectives  13.2 us (17%)
  between operations  1.57 us (2%)
  other arithmetic  1.52 us (2%)
  local copies, waits for them, and re-layouts  1.51 us (2%)
    all_to_all x1, blocking collectives, spread_sum(): gathered = lax.all_to_all(value.reshape(piece), axes, 0, 0, tiled=True)  13.2 us
    all_to_all x1, waiting for transfers between devices, on_device(): lax.all_to_all(to_owner, 'col', split_axis=0, concat_axis=0, tiled=True)  12.5 us
    all_to_all x1, waiting for transfers between devices, on_device(): lax.all_to_all(outgoing, 'col', split_axis=0, concat_axis=0, tiled=True)  9.1 us
    all_to_all x1, waiting for transfers between devices, spread_sum(): return lax.all_to_all(copies, axes, 0, 0, tiled=True).reshape(value.shape)  8.57 us
    all_to_all x1, starting transfers between devices, on_device(): lax.all_to_all(outgoing, 'col', split_axis=0, concat_axis=0, tiled=True)  6.53 us
    ppermute x2, starting transfers between devices, padded_2(): lax.ppermute(head, axis, [((i + 1) % count, i) for i in range(count)])  3.75 us
    all_to_all x1, starting transfers between devices, on_device(): lax.all_to_all(to_owner, 'col', split_axis=0, concat_axis=0, tiled=True)  3.64 us
    all_to_all x1, starting transfers between devices, spread_sum(): return lax.all_to_all(copies, axes, 0, 0, tiled=True).reshape(value.shape)  2.59 us
  transfers between devices with their start and end apart: 7, of which 3 were waited for; matrix products, arithmetic and copies ran while one was open for 13% of the time, Pallas kernels for 0%

profile of v10, /device:TPU:0, one launch (start us, length us, event | category | flops | bytes accessed | tf_op | source)
XLA Modules:
  0.0 78.6 jit_solution(3510848295939392519)
XLA Ops:
  0.6 0.0 copy-start
  0.6 0.0 copy-start.3
  0.7 0.0 copy-start.4
  0.7 1.2 %convolution_convert_fusion.6 = bf16[256,256]{1,0:T(8,128)(2,1)S(1)} fusion(bf16[256,256]{1,0:T(8,128)(2,1)} %param.19, s32[256]{0:T(256)} %bitcast.107), kind=kOutput, calls=%fused_computation.17 | convolution fusion | flops 33685504 | bytes 263168 | tf_op jit(solution)/shard_map/dot_general | solution.py:63
  1.9 0.0 copy-done
  1.9 0.2 convolution_convert_fusion.5
  2.1 0.5 collective-permute-start
  2.6 2.0 %collective-permute-start.1 = (bf16[256,256]{1,0:T(8,128)(2,1)S(1)}, bf16[256,256]{1,0:T(8,128)(2,1)}, u32[]{:S(2)}, u32[]{:S(2)}) collective-permute-start(bf16[256,256]{1,0:T(8,128)(2,1)S(1)} %convolution_convert_fusion.5), channel_id=1, source_target_pairs={{8,0},{16,8},{24,16},{0,24},{9,1},{17,9},{25,17},{1,25},{10,2},{18... | collective-permute-start | bytes 393224 | tf_op jit(solution)/shard_map/ppermute | solution.py:18
  4.6 0.7 broadcast_compare_fusion
  5.3 0.7 broadcast_multiply_fusion.1
  5.9 0.1 select_bitcast_fusion
  6.0 1.2 %convolution_convert_fusion = bf16[1024,256]{1,0:T(8,128)(2,1)} fusion(bf16[256,256]{1,0:T(8,128)(2,1)S(1)} %convolution_convert_fusion.5, s32[1024]{0:T(1024)S(1)} %select_bitcast_fusion), kind=kOutput, calls=%fused_computation.4 | convolution fusion | flops 134742016 | bytes 659456 | tf_op jit(solution)/shard_map/dot_general | solution.py:89
  7.2 6.5 %all-to-all-start = ((bf16[8,128,256]{2,1,0:T(8,128)(2,1)}), bf16[8,128,256]{2,1,0:T(8,128)(2,1)S(1)}, u32[]{:S(2)}, u32[]{:S(2)}) async-start(bf16[8,128,256]{2,1,0:T(8,128)(2,1)} %bitcast.9), calls=%async_computation | async-start | bytes 1048576 | tf_op jit(solution)/shard_map/all_to_all | solution.py:93
  13.7 0.0 copy-done.3
  13.7 0.0 copy-done.4
  14.4 0.0 copy-start.1
  14.5 2.3 %fusion.7 = (bf16[2,128,8,128]{3,2,1,0:T(8,128)(2,1)S(1)}, bf16[2,128,8,128]{3,2,1,0:T(8,128)(2,1)S(1)}, f32[2,8,128,128]{3,1,2,0:T(8,128)S(1)}) fusion(bf16[40,128,128]{2,1,0:T(8,128)(2,1)} %param.24, pred[40]{0:T(512)(128)(4,1)S(1)} %iota_compare_fusion.11, pred[40,8]{0,1:T(8,128)(4,1)S(1)} %iota_compare_fusion.7, pred[40,2]{0,1:T(4,128)(4,1)S(1)} %iota_compare_fusion.9), kind=kOutput, calls=%fused_computation.23 | convolution fusion | flops 22021376 | bytes 3408312 | tf_op jit(solution)/shard_map/krs,kab->rasb/dot_general | solution.py:103
  16.8 0.0 copy-done.1
  16.8 0.4 convolution_convert_fusion.1
  17.2 0.0 collective-permute-done
  17.2 0.0 collective-permute-done.1
  17.2 1.9 %fusion.19 = f32[256,256]{1,0:T(8,128)} fusion(bf16[256,256]{1,0:T(8,128)(2,1)} %collective-permute-done.1, bf16[256,256]{1,0:T(8,128)(2,1)S(1)} %convolution_convert_fusion.5, bf16[256,256]{1,0:T(8,128)(2,1)} %collective-permute-done, bf16[32,8,6,128]{3,2,1,0:T(8,128)(2,1)S(1)} %bitcast.104), kind=kOutput, calls=%fused_computation.35 | convolution fusion | flops 101842944 | bytes 1048576 | tf_op jit(solution)/shard_map/dot_general | solution.py:79
  19.1 9.1 %all-to-all-done = bf16[8,128,256]{2,1,0:T(8,128)(2,1)S(1)} async-done(((bf16[8,128,256]{2,1,0:T(8,128)(2,1)}), bf16[8,128,256]{2,1,0:T(8,128)(2,1)S(1)}, u32[]{:S(2)}, u32[]{:S(2)}) %all-to-all-start) | async-done | bytes 524320 | tf_op jit(solution)/shard_map/all_to_all | solution.py:93
  28.2 1.3 %convolution_add_fusion.2 = f32[256,256]{1,0:T(8,128)S(1)} fusion(f32[256,256]{1,0:T(8,128)} %fusion.19, bf16[1024,256]{1,0:T(8,128)(2,1)S(1)} %bitcast.100, bf16[32,8,8,128]{3,2,1,0:T(8,128)(2,1)S(1)} %bitcast.103), kind=kOutput, calls=%fused_computation.11 | convolution fusion | flops 134283264 | bytes 1572864 | tf_op jit(solution)/shard_map/dot_general | solution.py:110
  29.5 0.3 convolution_add_fusion.1
  29.8 0.0 copy-done.2
  29.9 0.0 copy-done.6
  29.9 0.2 fusion.5
  30.1 0.4 fusion.8
  30.5 1.2 %fusion.3 = bf16[1024,256]{1,0:T(8,128)(2,1)} fusion(f32[1024,256]{1,0:T(8,128)S(1)} %fusion.8, bf16[256,256]{1,0:T(8,128)(2,1)S(1)} %fusion.5, f32[32,8,8,128]{3,2,1,0:T(8,128)S(1)} %bitcast.99), kind=kOutput, calls=%fused_computation.6 | convolution fusion | flops 135790592 | bytes 2752512 | tf_op jit(solution)/shard_map/dot_general | solution.py:131
  31.6 3.6 %all-to-all-start.1 = ((bf16[8,128,256]{2,1,0:T(8,128)(2,1)}), bf16[8,128,256]{2,1,0:T(8,128)(2,1)S(1)}, u32[]{:S(2)}, u32[]{:S(2)}) async-start(bf16[8,128,256]{2,1,0:T(8,128)(2,1)} %bitcast.19), calls=%async_computation.1 | async-start | bytes 1048576 | tf_op jit(solution)/shard_map/all_to_all | solution.py:133
  35.3 0.3 fusion.54
  35.6 0.1 collective-permute-start.2
  35.7 1.7 %collective-permute-start.3 = (bf16[256,256]{1,0:T(8,128)(2,1)S(1)}, bf16[256,256]{1,0:T(8,128)(2,1)S(1)}, u32[]{:S(2)}, u32[]{:S(2)}) collective-permute-start(bf16[256,256]{1,0:T(8,128)(2,1)S(1)} %get-tuple-element.50), channel_id=1, source_target_pairs={{8,0},{16,8},{24,16},{0,24},{9,1},{17,9},{25,17},{1,25},{10,2},{18... | collective-permute-start | bytes 393224 | tf_op jit(solution)/shard_map/ppermute | solution.py:18
  37.4 12.5 %all-to-all-done.1 = bf16[8,128,256]{2,1,0:T(8,128)(2,1)S(1)} async-done(((bf16[8,128,256]{2,1,0:T(8,128)(2,1)}), bf16[8,128,256]{2,1,0:T(8,128)(2,1)S(1)}, u32[]{:S(2)}, u32[]{:S(2)}) %all-to-all-start.1) | async-done | bytes 524320 | tf_op jit(solution)/shard_map/all_to_all | solution.py:133
  49.9 0.0 copy-done.5
  49.9 0.4 fusion.15
  50.4 0.0 collective-permute-done.2
  50.4 0.0 collective-permute-done.3
  50.4 0.1 fusion.32
  50.4 0.2 convolution_bitcast_fusion
  50.7 13.2 %all_to_all.20 = f32[32,8,256]{2,1,0:T(8,128)S(1)} all-to-all(f32[32,8,256]{2,1,0:T(8,128)S(1)} %convolution_bitcast_fusion), channel_id=1, replica_groups=mesh['row'=4,'col'=8] {'row','col'}, dimensions={0} | all-to-all | bytes 524288 | tf_op jit(solution)/shard_map/all_to_all | solution.py:31
  63.9 0.7 broadcast_in_dim.16
  64.6 2.6 %all-to-all-start.3 = ((f32[32,8,256]{2,1,0:T(8,128)}), f32[32,8,256]{2,1,0:T(8,128)S(1)}, u32[]{:S(2)}, u32[]{:S(2)}) async-start(f32[32,8,256]{2,1,0:T(8,128)} %broadcast_in_dim.16), calls=%async_computation.3 | async-start | bytes 524288 | tf_op jit(solution)/shard_map/all_to_all | solution.py:34
  67.2 1.0 %convolution_convert_fusion.4 = bf16[256,256]{1,0:T(8,128)(2,1)} fusion(s32[256]{0:T(256)S(1)} %bitcast.109, f32[256,256]{1,0:T(8,128)S(1)} %convolution_add_fusion.1), kind=kOutput, calls=%fused_computation.15 | convolution fusion | flops 34013184 | bytes 394240 | tf_op jit(solution)/shard_map/dot_general | solution.py:113
  68.2 1.1 %convolution_convert_fusion.2 = bf16[256,256]{1,0:T(8,128)(2,1)} fusion(bf16[256,256]{1,0:T(8,128)(2,1)S(1)} %fusion.32, bf16[256,256]{1,0:T(8,128)(2,1)S(1)} %copy-done, s32[256]{0:T(256)S(1)} %bitcast.110), kind=kOutput, calls=%fused_computation.13 | convolution fusion | flops 67305472 | bytes 394240 | tf_op jit(solution)/shard_map/dot_general | solution.py:148
  69.3 8.6 %all-to-all-done.3 = f32[32,8,256]{2,1,0:T(8,128)S(1)} async-done(((f32[32,8,256]{2,1,0:T(8,128)}), f32[32,8,256]{2,1,0:T(8,128)S(1)}, u32[]{:S(2)}, u32[]{:S(2)}) %all-to-all-start.3) | async-done | bytes 262176 | tf_op jit(solution)/shard_map/all_to_all | solution.py:34
  77.9 0.7 copy.72
  (14 shorter events, 0.1 us)
Async XLA Ops:
  0.6 1.3 %copy-start = (bf16[256,256]{1,0:T(8,128)(2,1)S(1)}, bf16[256,256]{1,0:T(8,128)(2,1)}, u32[]{:S(2)}) copy-start(bf16[256,256]{1,0:T(8,128)(2,1)} %param.20) | copy-start | bytes 393220
  0.6 13.0 %copy-start.3 = (s32[12,2]{0,1:T(2,128)S(1)}, s32[12,2]{0,1:T(2,128)}, u32[]{:S(2)}) copy-start(s32[12,2]{0,1:T(2,128)} %param.23) | copy-start | bytes 292
  0.7 13.1 %copy-start.4 = (s32[40,2]{0,1:T(2,128)S(1)}, s32[40,2]{0,1:T(2,128)}, u32[]{:S(2)}) copy-start(s32[40,2]{0,1:T(2,128)} %param.25) | copy-start | bytes 964
  2.1 15.1 %collective-permute-start = (bf16[256,256]{1,0:T(8,128)(2,1)S(1)}, bf16[256,256]{1,0:T(8,128)(2,1)}, u32[]{:S(2)}, u32[]{:S(2)}) collective-permute-start(bf16[256,256]{1,0:T(8,128)(2,1)S(1)} %convolution_convert_fusion.5), channel_id=1, source_target_pairs={{0,8},{8,16},{16,24},{24,0},{1,9},{9,17},{17,25},{25,1},{2,10},{10... | collective-permute-start | bytes 393224 | tf_op jit(solution)/shard_map/ppermute | solution.py:16
  2.6 14.6 %collective-permute-start.1 = (bf16[256,256]{1,0:T(8,128)(2,1)S(1)}, bf16[256,256]{1,0:T(8,128)(2,1)}, u32[]{:S(2)}, u32[]{:S(2)}) collective-permute-start(bf16[256,256]{1,0:T(8,128)(2,1)S(1)} %convolution_convert_fusion.5), channel_id=1, source_target_pairs={{8,0},{16,8},{24,16},{0,24},{9,1},{17,9},{25,17},{1,25},{10,2},{18... | collective-permute-start | bytes 393224 | tf_op jit(solution)/shard_map/ppermute | solution.py:18
  7.2 21.1 %all-to-all-start = ((bf16[8,128,256]{2,1,0:T(8,128)(2,1)}), bf16[8,128,256]{2,1,0:T(8,128)(2,1)S(1)}, u32[]{:S(2)}, u32[]{:S(2)}) async-start(bf16[8,128,256]{2,1,0:T(8,128)(2,1)} %bitcast.9), calls=%async_computation | async-start | bytes 1048576 | tf_op jit(solution)/shard_map/all_to_all | solution.py:93
  14.4 2.4 %copy-start.1 = (bf16[12,128,128]{2,1,0:T(8,128)(2,1)S(1)}, bf16[12,128,128]{2,1,0:T(8,128)(2,1)}, u32[]{:S(2)}) copy-start(bf16[12,128,128]{2,1,0:T(8,128)(2,1)} %param.22) | copy-start | bytes 1179652
  28.2 1.6 %copy-start.2 = (s32[1,256]{1,0:T(1,128)S(1)}, s32[1,256]{1,0:T(1,128)}, u32[]{:S(2)}) copy-start(s32[1,256]{1,0:T(1,128)} %param.28) | copy-start | bytes 3076
  28.2 1.6 %copy-start.6 = (bf16[256,256]{1,0:T(8,128)(2,1)S(1)}, bf16[256,256]{1,0:T(8,128)(2,1)}, u32[]{:S(2)}) copy-start(bf16[256,256]{1,0:T(8,128)(2,1)} %param.21) | copy-start | bytes 393220
  31.6 18.3 %all-to-all-start.1 = ((bf16[8,128,256]{2,1,0:T(8,128)(2,1)}), bf16[8,128,256]{2,1,0:T(8,128)(2,1)S(1)}, u32[]{:S(2)}, u32[]{:S(2)}) async-start(bf16[8,128,256]{2,1,0:T(8,128)(2,1)} %bitcast.19), calls=%async_computation.1 | async-start | bytes 1048576 | tf_op jit(solution)/shard_map/all_to_all | solution.py:133
  35.3 14.7 %copy-start.5 = (s32[1,8]{1,0:T(1,128)S(1)}, s32[1,8]{1,0:T(1,128)}, u32[]{:S(2)}) copy-start(s32[1,8]{1,0:T(1,128)} %param.27) | copy-start | bytes 100
  35.6 14.8 %collective-permute-start.2 = (bf16[256,256]{1,0:T(8,128)(2,1)S(1)}, bf16[256,256]{1,0:T(8,128)(2,1)S(1)}, u32[]{:S(2)}, u32[]{:S(2)}) collective-permute-start(bf16[256,256]{1,0:T(8,128)(2,1)S(1)} %get-tuple-element.49), channel_id=1, source_target_pairs={{0,8},{8,16},{16,24},{24,0},{1,9},{9,17},{17,25},{25,1},{2,10},{10... | collective-permute-start | bytes 393224 | tf_op jit(solution)/shard_map/ppermute | solution.py:16
  35.7 14.7 %collective-permute-start.3 = (bf16[256,256]{1,0:T(8,128)(2,1)S(1)}, bf16[256,256]{1,0:T(8,128)(2,1)S(1)}, u32[]{:S(2)}, u32[]{:S(2)}) collective-permute-start(bf16[256,256]{1,0:T(8,128)(2,1)S(1)} %get-tuple-element.50), channel_id=1, source_target_pairs={{8,0},{16,8},{24,16},{0,24},{9,1},{17,9},{25,17},{1,25},{10,2},{18... | collective-permute-start | bytes 393224 | tf_op jit(solution)/shard_map/ppermute | solution.py:18
  64.6 13.2 %all-to-all-start.3 = ((f32[32,8,256]{2,1,0:T(8,128)}), f32[32,8,256]{2,1,0:T(8,128)S(1)}, u32[]{:S(2)}, u32[]{:S(2)}) async-start(f32[32,8,256]{2,1,0:T(8,128)} %broadcast_in_dim.16), calls=%async_computation.3 | async-start | bytes 524288 | tf_op jit(solution)/shard_map/all_to_all | solution.py:34

commit v11 on v6

--- a/solution.py
+++ b/solution.py
@@ -29,9 +29,10 @@
     else:
         piece = (count, value.size // count // 128, 128)
     gathered = lax.all_to_all(value.reshape(piece), axes, 0, 0, tiled=True)
-    owned = jnp.sum(gathered, axis=0, keepdims=True) * scale
+    owned = (jnp.sum(gathered, axis=0, keepdims=True) * scale).astype(jnp.bfloat16)
     copies = jnp.broadcast_to(owned, piece)
-    return lax.all_to_all(copies, axes, 0, 0, tiled=True).reshape(value.shape)
+    spread = lax.all_to_all(copies, axes, 0, 0, tiled=True)
+    return spread.astype(jnp.float32).reshape(value.shape)
 
 
 def on_device(

time: 78.8 us -> 75.8 us (0.962)
  waiting for transfers between devices: 32.2 us -> 29.3 us
    all_to_all x1, waiting for transfers between devices: 8.56 us -> 5.65 us  [spread_sum(): spread = lax.all_to_all(copies, axes, 0, 0, tiled=True)]
  transfers between devices with their start and end apart: 7 -> 7, of which waited for: 3 -> 3; matrix products, arithmetic and copies ran while one was open for 10% -> 11% of each run, Pallas kernels for 0% -> 0%
where the time goes in v11:
time: 75.8 us; the launch traced here: 75.4 us
  waiting for transfers between devices  29.3 us (39%)
  starting transfers between devices  17 us (22%)
  blocking collectives  13.2 us (17%)
  matrix products  11.7 us (15%)
  local copies, waits for them, and re-layouts  1.74 us (2%)
  between operations  1.6 us (2%)
  other arithmetic  0.85 us (1%)
    all_to_all x1, blocking collectives, spread_sum(): gathered = lax.all_to_all(value.reshape(piece), axes, 0, 0, tiled=True)  13.2 us
    all_to_all x1, waiting for transfers between devices, on_device(): lax.all_to_all(to_owner, 'col', split_axis=0, concat_axis=0, tiled=True)  12.5 us
    all_to_all x1, waiting for transfers between devices, on_device(): lax.all_to_all(outgoing, 'col', split_axis=0, concat_axis=0, tiled=True)  11.1 us
    all_to_all x1, starting transfers between devices, on_device(): lax.all_to_all(outgoing, 'col', split_axis=0, concat_axis=0, tiled=True)  6.53 us
    all_to_all x1, waiting for transfers between devices, spread_sum(): spread = lax.all_to_all(copies, axes, 0, 0, tiled=True)  5.65 us
    ppermute x2, starting transfers between devices, padded_2(): lax.ppermute(head, axis, [((i + 1) % count, i) for i in range(count)])  3.75 us
    all_to_all x1, starting transfers between devices, on_device(): lax.all_to_all(to_owner, 'col', split_axis=0, concat_axis=0, tiled=True)  3.63 us
    all_to_all x1, starting transfers between devices, spread_sum(): spread = lax.all_to_all(copies, axes, 0, 0, tiled=True)  2.56 us
  transfers between devices with their start and end apart: 7, of which 3 were waited for; matrix products, arithmetic and copies ran while one was open for 11% of the time, Pallas kernels for 0%

profile of v11, /device:TPU:0, one launch (start us, length us, event | category | flops | bytes accessed | tf_op | source)
XLA Modules:
  0.0 75.4 jit_solution(11521754456911214876)
XLA Ops:
  0.6 0.0 copy-start
  0.6 1.2 %convolution_convert_fusion.6 = bf16[256,256]{1,0:T(8,128)(2,1)S(1)} fusion(bf16[256,256]{1,0:T(8,128)(2,1)} %param.19, s32[256]{0:T(256)} %bitcast.107), kind=kOutput, calls=%fused_computation.17 | convolution fusion | flops 33685504 | bytes 263168 | tf_op jit(solution)/shard_map/dot_general | solution.py:64
  1.8 0.0 copy-done
  1.8 0.2 convolution_convert_fusion.5
  2.0 0.5 collective-permute-start
  2.5 2.0 %collective-permute-start.1 = (bf16[256,256]{1,0:T(8,128)(2,1)S(1)}, bf16[256,256]{1,0:T(8,128)(2,1)}, u32[]{:S(2)}, u32[]{:S(2)}) collective-permute-start(bf16[256,256]{1,0:T(8,128)(2,1)S(1)} %convolution_convert_fusion.5), channel_id=1, source_target_pairs={{8,0},{16,8},{24,16},{0,24},{9,1},{17,9},{25,17},{1,25},{10,2},{18... | collective-permute-start | bytes 393224 | tf_op jit(solution)/shard_map/ppermute | solution.py:18
  4.6 1.1 %convolution_convert_fusion = bf16[8,128,256]{2,0,1:T(8,128)(2,1)S(1)} fusion(bf16[2,128,256]{2,1,0:T(8,128)(2,1)S(1)} %bitcast.106, s32[8]{0:T(128)} %bitcast.111), kind=kOutput, calls=%fused_computation.4 | convolution fusion | flops 1310736 | bytes 655392 | tf_op jit(solution)/shard_map/sb,baf->saf/dot_general | solution.py:85
  5.6 0.9 %copy.29 = bf16[8,128,256]{2,1,0:T(8,128)(2,1)} copy(bf16[8,128,256]{2,0,1:T(8,128)(2,1)S(1)} %convolution_convert_fusion) | data formatting | bytes 1048576 | tf_op jit(solution)/shard_map/convert_element_type | solution.py:87
  6.5 6.5 %all-to-all-start = ((bf16[8,128,256]{2,1,0:T(8,128)(2,1)}), bf16[8,128,256]{2,1,0:T(8,128)(2,1)S(1)}, u32[]{:S(2)}, u32[]{:S(2)}) async-start(bf16[8,128,256]{2,1,0:T(8,128)(2,1)} %copy.29), calls=%async_computation | async-start | bytes 1048576 | tf_op jit(solution)/shard_map/all_to_all | solution.py:88
  13.1 0.0 copy-done.4
  13.1 0.0 copy-done.5
  13.8 0.0 copy-done.1
  13.8 0.4 convolution_convert_fusion.1
  14.2 2.3 %fusion.8 = (bf16[2,128,8,128]{3,2,1,0:T(8,128)(2,1)S(1)}, bf16[2,128,8,128]{3,2,1,0:T(8,128)(2,1)S(1)}, f32[2,8,128,128]{3,1,2,0:T(8,128)S(1)}) fusion(bf16[40,128,128]{2,1,0:T(8,128)(2,1)} %param.24, pred[40]{0:T(512)(128)(4,1)S(1)} %iota_compare_fusion.9, pred[40,8]{0,1:T(8,128)(4,1)S(1)} %iota_compare_fusion.5, pred[40,2]{0,1:T(4,128)(4,1)S(1)} %iota_compare_fusion.7), kind=kOutput, calls=%fused_computation.23 | convolution fusion | flops 22021376 | bytes 3408312 | tf_op jit(solution)/shard_map/krs,kab->rasb/dot_general | solution.py:98
  16.5 11.1 %all-to-all-done = bf16[8,128,256]{2,1,0:T(8,128)(2,1)S(1)} async-done(((bf16[8,128,256]{2,1,0:T(8,128)(2,1)}), bf16[8,128,256]{2,1,0:T(8,128)(2,1)S(1)}, u32[]{:S(2)}, u32[]{:S(2)}) %all-to-all-start) | async-done | bytes 524320 | tf_op jit(solution)/shard_map/all_to_all | solution.py:88
  27.6 0.3 fusion.14
  27.9 0.0 copy-start.2
  27.9 0.0 copy-start.6
  27.9 0.3 fusion.11
  28.3 0.0 collective-permute-done
  28.3 0.0 collective-permute-done.1
  28.3 1.2 %fusion.5 = f32[256,256]{1,0:T(8,128)S(1)} fusion(f32[256,256]{1,0:T(8,128)S(1)} %fusion.11, f32[256,256]{1,0:T(8,128)S(1)} %fusion.14, bf16[256,256]{1,0:T(8,128)(2,1)} %collective-permute-done.1, bf16[256,256]{1,0:T(8,128)(2,1)S(1)} %convolution_convert_fusion.5, bf16[256,256]{1,0:T(8,128)(2,1)} %collective-permute-done, ...), kind=kOutput, calls=%fused_computation.10 | convolution fusion | flops 101974016 | bytes 1572864 | tf_op jit(solution)/shard_map/dot_general | solution.py:80
  29.5 0.0 copy-done.2
  29.5 0.0 copy-done.6
  29.5 0.0 copy-start.7
  29.6 0.2 fusion.6
  29.8 0.4 fusion.9
  30.2 0.1 copy-done.7
  30.3 1.2 %fusion.3 = bf16[1024,256]{1,0:T(8,128)(2,1)} fusion(f32[1024,256]{1,0:T(8,128)S(1)} %fusion.9, bf16[256,256]{1,0:T(8,128)(2,1)S(1)} %fusion.6, f32[32,8,8,128]{3,2,1,0:T(8,128)S(1)} %bitcast.99), kind=kOutput, calls=%fused_computation.6 | convolution fusion | flops 135790592 | bytes 2752512 | tf_op jit(solution)/shard_map/dot_general | solution.py:125
  31.4 3.6 %all-to-all-start.1 = ((bf16[8,128,256]{2,1,0:T(8,128)(2,1)}), bf16[8,128,256]{2,1,0:T(8,128)(2,1)S(1)}, u32[]{:S(2)}, u32[]{:S(2)}) async-start(bf16[8,128,256]{2,1,0:T(8,128)(2,1)} %bitcast.19), calls=%async_computation.1 | async-start | bytes 1048576 | tf_op jit(solution)/shard_map/all_to_all | solution.py:127
  35.1 0.3 fusion.60
  35.4 0.1 collective-permute-start.2
  35.5 1.7 %collective-permute-start.3 = (bf16[256,256]{1,0:T(8,128)(2,1)S(1)}, bf16[256,256]{1,0:T(8,128)(2,1)S(1)}, u32[]{:S(2)}, u32[]{:S(2)}) collective-permute-start(bf16[256,256]{1,0:T(8,128)(2,1)S(1)} %get-tuple-element.46), channel_id=1, source_target_pairs={{8,0},{16,8},{24,16},{0,24},{9,1},{17,9},{25,17},{1,25},{10,2},{18... | collective-permute-start | bytes 393224 | tf_op jit(solution)/shard_map/ppermute | solution.py:18
  37.2 12.5 %all-to-all-done.1 = bf16[8,128,256]{2,1,0:T(8,128)(2,1)S(1)} async-done(((bf16[8,128,256]{2,1,0:T(8,128)(2,1)}), bf16[8,128,256]{2,1,0:T(8,128)(2,1)S(1)}, u32[]{:S(2)}, u32[]{:S(2)}) %all-to-all-start.1) | async-done | bytes 524320 | tf_op jit(solution)/shard_map/all_to_all | solution.py:127
  49.7 0.0 copy-done.3
  49.7 0.4 fusion.18
  50.2 0.0 collective-permute-done.2
  50.2 0.0 collective-permute-done.3
  50.2 0.0 copy-start.8
  50.2 0.1 fusion.33
  50.3 0.2 convolution_bitcast_fusion
  50.5 13.2 %all_to_all.20 = f32[32,8,256]{2,1,0:T(8,128)S(1)} all-to-all(f32[32,8,256]{2,1,0:T(8,128)S(1)} %convolution_bitcast_fusion), channel_id=1, replica_groups=mesh['row'=4,'col'=8] {'row','col'}, dimensions={0} | all-to-all | bytes 524288 | tf_op jit(solution)/shard_map/all_to_all | solution.py:31
  63.7 0.7 broadcast_in_dim.2
  64.4 2.6 %all-to-all-start.3 = ((bf16[32,8,256]{2,1,0:T(8,128)(2,1)}), bf16[32,8,256]{2,1,0:T(8,128)(2,1)S(1)}, u32[]{:S(2)}, u32[]{:S(2)}) async-start(bf16[32,8,256]{2,1,0:T(8,128)(2,1)} %broadcast_in_dim.2), calls=%async_computation.3 | async-start | bytes 262144 | tf_op jit(solution)/shard_map/all_to_all | solution.py:34
  66.9 1.0 %convolution_convert_fusion.4 = bf16[256,256]{1,0:T(8,128)(2,1)} fusion(s32[256]{0:T(256)S(1)} %bitcast.109, f32[256,256]{1,0:T(8,128)S(1)} %copy-done.8), kind=kOutput, calls=%fused_computation.15 | convolution fusion | flops 34013184 | bytes 394240 | tf_op jit(solution)/shard_map/dot_general | solution.py:107
  67.9 1.1 %convolution_convert_fusion.2 = bf16[256,256]{1,0:T(8,128)(2,1)} fusion(bf16[256,256]{1,0:T(8,128)(2,1)S(1)} %fusion.33, bf16[256,256]{1,0:T(8,128)(2,1)S(1)} %copy-done, s32[256]{0:T(256)S(1)} %bitcast.110), kind=kOutput, calls=%fused_computation.13 | convolution fusion | flops 67305472 | bytes 394240 | tf_op jit(solution)/shard_map/dot_general | solution.py:142
  69.0 5.7 %all-to-all-done.3 = bf16[32,8,256]{2,1,0:T(8,128)(2,1)S(1)} async-done(((bf16[32,8,256]{2,1,0:T(8,128)(2,1)}), bf16[32,8,256]{2,1,0:T(8,128)(2,1)S(1)}, u32[]{:S(2)}, u32[]{:S(2)}) %all-to-all-start.3) | async-done | bytes 131104 | tf_op jit(solution)/shard_map/all_to_all | solution.py:34
  74.7 0.7 bitcast_convert_fusion.3
  (16 shorter events, 0.1 us)
Async XLA Ops:
  0.6 1.2 %copy-start = (bf16[256,256]{1,0:T(8,128)(2,1)S(1)}, bf16[256,256]{1,0:T(8,128)(2,1)}, u32[]{:S(2)}) copy-start(bf16[256,256]{1,0:T(8,128)(2,1)} %param.20) | copy-start | bytes 393220
  2.0 26.2 %collective-permute-start = (bf16[256,256]{1,0:T(8,128)(2,1)S(1)}, bf16[256,256]{1,0:T(8,128)(2,1)}, u32[]{:S(2)}, u32[]{:S(2)}) collective-permute-start(bf16[256,256]{1,0:T(8,128)(2,1)S(1)} %convolution_convert_fusion.5), channel_id=1, source_target_pairs={{0,8},{8,16},{16,24},{24,0},{1,9},{9,17},{17,25},{25,1},{2,10},{10... | collective-permute-start | bytes 393224 | tf_op jit(solution)/shard_map/ppermute | solution.py:16
  2.5 25.7 %collective-permute-start.1 = (bf16[256,256]{1,0:T(8,128)(2,1)S(1)}, bf16[256,256]{1,0:T(8,128)(2,1)}, u32[]{:S(2)}, u32[]{:S(2)}) collective-permute-start(bf16[256,256]{1,0:T(8,128)(2,1)S(1)} %convolution_convert_fusion.5), channel_id=1, source_target_pairs={{8,0},{16,8},{24,16},{0,24},{9,1},{17,9},{25,17},{1,25},{10,2},{18... | collective-permute-start | bytes 393224 | tf_op jit(solution)/shard_map/ppermute | solution.py:18
  4.6 8.5 %copy-start.4 = (s32[40,2]{0,1:T(2,128)S(1)}, s32[40,2]{0,1:T(2,128)}, u32[]{:S(2)}) copy-start(s32[40,2]{0,1:T(2,128)} %param.25) | copy-start | bytes 964
  4.6 8.5 %copy-start.5 = (s32[12,2]{0,1:T(2,128)S(1)}, s32[12,2]{0,1:T(2,128)}, u32[]{:S(2)}) copy-start(s32[12,2]{0,1:T(2,128)} %param.23) | copy-start | bytes 292
  4.6 9.3 %copy-start.1 = (bf16[12,128,128]{2,1,0:T(8,128)(2,1)S(1)}, bf16[12,128,128]{2,1,0:T(8,128)(2,1)}, u32[]{:S(2)}) copy-start(bf16[12,128,128]{2,1,0:T(8,128)(2,1)} %param.22) | copy-start | bytes 1179652
  6.5 21.1 %all-to-all-start = ((bf16[8,128,256]{2,1,0:T(8,128)(2,1)}), bf16[8,128,256]{2,1,0:T(8,128)(2,1)S(1)}, u32[]{:S(2)}, u32[]{:S(2)}) async-start(bf16[8,128,256]{2,1,0:T(8,128)(2,1)} %copy.29), calls=%async_computation | async-start | bytes 1048576 | tf_op jit(solution)/shard_map/all_to_all | solution.py:88
  27.9 1.6 %copy-start.2 = (s32[1,256]{1,0:T(1,128)S(1)}, s32[1,256]{1,0:T(1,128)}, u32[]{:S(2)}) copy-start(s32[1,256]{1,0:T(1,128)} %param.28) | copy-start | bytes 3076
  27.9 1.6 %copy-start.6 = (bf16[256,256]{1,0:T(8,128)(2,1)S(1)}, bf16[256,256]{1,0:T(8,128)(2,1)}, u32[]{:S(2)}) copy-start(bf16[256,256]{1,0:T(8,128)(2,1)} %param.21) | copy-start | bytes 393220
  29.5 0.7 copy-start.7
  31.4 18.3 %all-to-all-start.1 = ((bf16[8,128,256]{2,1,0:T(8,128)(2,1)}), bf16[8,128,256]{2,1,0:T(8,128)(2,1)S(1)}, u32[]{:S(2)}, u32[]{:S(2)}) async-start(bf16[8,128,256]{2,1,0:T(8,128)(2,1)} %bitcast.19), calls=%async_computation.1 | async-start | bytes 1048576 | tf_op jit(solution)/shard_map/all_to_all | solution.py:127
  35.1 14.7 %copy-start.3 = (s32[1,8]{1,0:T(1,128)S(1)}, s32[1,8]{1,0:T(1,128)}, u32[]{:S(2)}) copy-start(s32[1,8]{1,0:T(1,128)} %param.27) | copy-start | bytes 100
  35.4 14.8 %collective-permute-start.2 = (bf16[256,256]{1,0:T(8,128)(2,1)S(1)}, bf16[256,256]{1,0:T(8,128)(2,1)S(1)}, u32[]{:S(2)}, u32[]{:S(2)}) collective-permute-start(bf16[256,256]{1,0:T(8,128)(2,1)S(1)} %get-tuple-element.45), channel_id=1, source_target_pairs={{0,8},{8,16},{16,24},{24,0},{1,9},{9,17},{17,25},{25,1},{2,10},{10... | collective-permute-start | bytes 393224 | tf_op jit(solution)/shard_map/ppermute | solution.py:16
  35.5 14.7 %collective-permute-start.3 = (bf16[256,256]{1,0:T(8,128)(2,1)S(1)}, bf16[256,256]{1,0:T(8,128)(2,1)S(1)}, u32[]{:S(2)}, u32[]{:S(2)}) collective-permute-start(bf16[256,256]{1,0:T(8,128)(2,1)S(1)} %get-tuple-element.46), channel_id=1, source_target_pairs={{8,0},{16,8},{24,16},{0,24},{9,1},{17,9},{25,17},{1,25},{10,2},{18... | collective-permute-start | bytes 393224 | tf_op jit(solution)/shard_map/ppermute | solution.py:18
  50.2 16.8 %copy-start.8 = (f32[256,256]{1,0:T(8,128)S(1)}, f32[256,256]{1,0:T(8,128)}, u32[]{:S(2)}) copy-start(f32[256,256]{1,0:T(8,128)} %copy-done.7) | copy-start | bytes 786436
  64.4 10.3 %all-to-all-start.3 = ((bf16[32,8,256]{2,1,0:T(8,128)(2,1)}), bf16[32,8,256]{2,1,0:T(8,128)(2,1)S(1)}, u32[]{:S(2)}, u32[]{:S(2)}) async-start(bf16[32,8,256]{2,1,0:T(8,128)(2,1)} %broadcast_in_dim.2), calls=%async_computation.3 | async-start | bytes 262144 | tf_op jit(solution)/shard_map/all_to_all | solution.py:34

commit v12 on v11

--- a/solution.py
+++ b/solution.py
@@ -30,7 +30,8 @@
         piece = (count, value.size // count // 128, 128)
     gathered = lax.all_to_all(value.reshape(piece), axes, 0, 0, tiled=True)
     owned = (jnp.sum(gathered, axis=0, keepdims=True) * scale).astype(jnp.bfloat16)
-    copies = jnp.broadcast_to(owned, piece)
+    narrow = (count, value.size // count // 128, 128)
+    copies = jnp.broadcast_to(owned.reshape((1,) + narrow[1:]), narrow)
     spread = lax.all_to_all(copies, axes, 0, 0, tiled=True)
     return spread.astype(jnp.float32).reshape(value.shape)
 

time: 75.8 us -> 75.9 us (level)
  local copies, waits for them, and re-layouts: 1.74 us -> 2.5 us
where the time goes in v12:
time: 75.9 us; the launch traced here: 75.4 us
  waiting for transfers between devices  29.3 us (39%)
  starting transfers between devices  17 us (22%)
  blocking collectives  13.2 us (17%)
  matrix products  11.7 us (15%)
  local copies, waits for them, and re-layouts  2.5 us (3%)
  between operations  1.6 us (2%)
    all_to_all x1, blocking collectives, spread_sum(): gathered = lax.all_to_all(value.reshape(piece), axes, 0, 0, tiled=True)  13.2 us
    all_to_all x1, waiting for transfers between devices, on_device(): lax.all_to_all(to_owner, 'col', split_axis=0, concat_axis=0, tiled=True)  12.5 us
    all_to_all x1, waiting for transfers between devices, on_device(): lax.all_to_all(outgoing, 'col', split_axis=0, concat_axis=0, tiled=True)  11.1 us
    all_to_all x1, starting transfers between devices, on_device(): lax.all_to_all(outgoing, 'col', split_axis=0, concat_axis=0, tiled=True)  6.53 us
    all_to_all x1, waiting for transfers between devices, spread_sum(): spread = lax.all_to_all(copies, axes, 0, 0, tiled=True)  5.65 us
    ppermute x2, starting transfers between devices, padded_2(): lax.ppermute(head, axis, [((i + 1) % count, i) for i in range(count)])  3.75 us
    all_to_all x1, starting transfers between devices, on_device(): lax.all_to_all(to_owner, 'col', split_axis=0, concat_axis=0, tiled=True)  3.63 us
    all_to_all x1, starting transfers between devices, spread_sum(): spread = lax.all_to_all(copies, axes, 0, 0, tiled=True)  2.56 us
  transfers between devices with their start and end apart: 7, of which 3 were waited for; matrix products, arithmetic and copies ran while one was open for 11% of the time, Pallas kernels for 0%

profile of v12, /device:TPU:0, one launch (start us, length us, event | category | flops | bytes accessed | tf_op | source)
XLA Modules:
  0.0 75.4 jit_solution(6078124128989193340)
XLA Ops:
  0.6 0.0 copy-start
  0.6 1.2 %convolution_convert_fusion.6 = bf16[256,256]{1,0:T(8,128)(2,1)S(1)} fusion(bf16[256,256]{1,0:T(8,128)(2,1)} %param.19, s32[256]{0:T(256)} %bitcast.104), kind=kOutput, calls=%fused_computation.17 | convolution fusion | flops 33685504 | bytes 263168 | tf_op jit(solution)/shard_map/dot_general | solution.py:65
  1.8 0.0 copy-done
  1.8 0.2 convolution_convert_fusion.5
  2.0 0.5 collective-permute-start
  2.5 2.0 %collective-permute-start.1 = (bf16[256,256]{1,0:T(8,128)(2,1)S(1)}, bf16[256,256]{1,0:T(8,128)(2,1)}, u32[]{:S(2)}, u32[]{:S(2)}) collective-permute-start(bf16[256,256]{1,0:T(8,128)(2,1)S(1)} %convolution_convert_fusion.5), channel_id=1, source_target_pairs={{8,0},{16,8},{24,16},{0,24},{9,1},{17,9},{25,17},{1,25},{10,2},{18... | collective-permute-start | bytes 393224 | tf_op jit(solution)/shard_map/ppermute | solution.py:18
  4.6 1.1 %convolution_convert_fusion = bf16[8,128,256]{2,0,1:T(8,128)(2,1)S(1)} fusion(bf16[2,128,256]{2,1,0:T(8,128)(2,1)S(1)} %bitcast.103, s32[8]{0:T(128)} %bitcast.108), kind=kOutput, calls=%fused_computation.4 | convolution fusion | flops 1310736 | bytes 655392 | tf_op jit(solution)/shard_map/sb,baf->saf/dot_general | solution.py:86
  5.6 0.9 %copy.29 = bf16[8,128,256]{2,1,0:T(8,128)(2,1)} copy(bf16[8,128,256]{2,0,1:T(8,128)(2,1)S(1)} %convolution_convert_fusion) | data formatting | bytes 1048576 | tf_op jit(solution)/shard_map/convert_element_type | solution.py:88
  6.5 6.5 %all-to-all-start = ((bf16[8,128,256]{2,1,0:T(8,128)(2,1)}), bf16[8,128,256]{2,1,0:T(8,128)(2,1)S(1)}, u32[]{:S(2)}, u32[]{:S(2)}) async-start(bf16[8,128,256]{2,1,0:T(8,128)(2,1)} %copy.29), calls=%async_computation | async-start | bytes 1048576 | tf_op jit(solution)/shard_map/all_to_all | solution.py:89
  13.1 0.0 copy-done.4
  13.1 0.0 copy-done.5
  13.8 0.0 copy-done.1
  13.8 0.4 convolution_convert_fusion.1
  14.2 2.3 %fusion.8 = (bf16[2,128,8,128]{3,2,1,0:T(8,128)(2,1)S(1)}, bf16[2,128,8,128]{3,2,1,0:T(8,128)(2,1)S(1)}, f32[2,8,128,128]{3,1,2,0:T(8,128)S(1)}) fusion(bf16[40,128,128]{2,1,0:T(8,128)(2,1)} %param.24, pred[40]{0:T(512)(128)(4,1)S(1)} %iota_compare_fusion.9, pred[40,8]{0,1:T(8,128)(4,1)S(1)} %iota_compare_fusion.5, pred[40,2]{0,1:T(4,128)(4,1)S(1)} %iota_compare_fusion.7), kind=kOutput, calls=%fused_computation.23 | convolution fusion | flops 22021376 | bytes 3408312 | tf_op jit(solution)/shard_map/krs,kab->rasb/dot_general | solution.py:99
  16.5 11.1 %all-to-all-done = bf16[8,128,256]{2,1,0:T(8,128)(2,1)S(1)} async-done(((bf16[8,128,256]{2,1,0:T(8,128)(2,1)}), bf16[8,128,256]{2,1,0:T(8,128)(2,1)S(1)}, u32[]{:S(2)}, u32[]{:S(2)}) %all-to-all-start) | async-done | bytes 524320 | tf_op jit(solution)/shard_map/all_to_all | solution.py:89
  27.6 0.3 fusion.14
  27.9 0.0 copy-start.2
  27.9 0.0 copy-start.6
  27.9 0.3 fusion.11
  28.3 0.0 collective-permute-done
  28.3 0.0 collective-permute-done.1
  28.3 1.2 %fusion.5 = f32[256,256]{1,0:T(8,128)S(1)} fusion(f32[256,256]{1,0:T(8,128)S(1)} %fusion.11, f32[256,256]{1,0:T(8,128)S(1)} %fusion.14, bf16[256,256]{1,0:T(8,128)(2,1)} %collective-permute-done.1, bf16[256,256]{1,0:T(8,128)(2,1)S(1)} %convolution_convert_fusion.5, bf16[256,256]{1,0:T(8,128)(2,1)} %collective-permute-done, ...), kind=kOutput, calls=%fused_computation.10 | convolution fusion | flops 101974016 | bytes 1572864 | tf_op jit(solution)/shard_map/dot_general | solution.py:81
  29.5 0.0 copy-done.2
  29.5 0.0 copy-done.6
  29.5 0.0 copy-start.7
  29.6 0.2 fusion.6
  29.8 0.4 fusion.9
  30.2 0.1 copy-done.7
  30.3 1.2 %fusion.3 = bf16[1024,256]{1,0:T(8,128)(2,1)} fusion(f32[1024,256]{1,0:T(8,128)S(1)} %fusion.9, bf16[256,256]{1,0:T(8,128)(2,1)S(1)} %fusion.6, f32[32,8,8,128]{3,2,1,0:T(8,128)S(1)} %bitcast.96), kind=kOutput, calls=%fused_computation.6 | convolution fusion | flops 135790592 | bytes 2752512 | tf_op jit(solution)/shard_map/dot_general | solution.py:126
  31.4 3.6 %all-to-all-start.1 = ((bf16[8,128,256]{2,1,0:T(8,128)(2,1)}), bf16[8,128,256]{2,1,0:T(8,128)(2,1)S(1)}, u32[]{:S(2)}, u32[]{:S(2)}) async-start(bf16[8,128,256]{2,1,0:T(8,128)(2,1)} %bitcast.19), calls=%async_computation.1 | async-start | bytes 1048576 | tf_op jit(solution)/shard_map/all_to_all | solution.py:128
  35.1 0.3 fusion.60
  35.4 0.1 collective-permute-start.2
  35.5 1.7 %collective-permute-start.3 = (bf16[256,256]{1,0:T(8,128)(2,1)S(1)}, bf16[256,256]{1,0:T(8,128)(2,1)S(1)}, u32[]{:S(2)}, u32[]{:S(2)}) collective-permute-start(bf16[256,256]{1,0:T(8,128)(2,1)S(1)} %get-tuple-element.46), channel_id=1, source_target_pairs={{8,0},{16,8},{24,16},{0,24},{9,1},{17,9},{25,17},{1,25},{10,2},{18... | collective-permute-start | bytes 393224 | tf_op jit(solution)/shard_map/ppermute | solution.py:18
  37.2 12.5 %all-to-all-done.1 = bf16[8,128,256]{2,1,0:T(8,128)(2,1)S(1)} async-done(((bf16[8,128,256]{2,1,0:T(8,128)(2,1)}), bf16[8,128,256]{2,1,0:T(8,128)(2,1)S(1)}, u32[]{:S(2)}, u32[]{:S(2)}) %all-to-all-start.1) | async-done | bytes 524320 | tf_op jit(solution)/shard_map/all_to_all | solution.py:128
  49.7 0.0 copy-done.3
  49.7 0.4 fusion.18
  50.2 0.0 collective-permute-done.2
  50.2 0.0 collective-permute-done.3
  50.2 0.0 copy-start.8
  50.2 0.1 fusion.33
  50.3 0.2 convolution_bitcast_fusion
  50.5 13.2 %all_to_all.20 = f32[32,8,256]{2,1,0:T(8,128)S(1)} all-to-all(f32[32,8,256]{2,1,0:T(8,128)S(1)} %convolution_bitcast_fusion), channel_id=1, replica_groups=mesh['row'=4,'col'=8] {'row','col'}, dimensions={0} | all-to-all | bytes 524288 | tf_op jit(solution)/shard_map/all_to_all | solution.py:31
  63.7 0.7 broadcast_in_dim.2
  64.4 2.6 %all-to-all-start.3 = ((bf16[32,16,128]{2,1,0:T(8,128)(2,1)}), bf16[32,16,128]{2,1,0:T(8,128)(2,1)S(1)}, u32[]{:S(2)}, u32[]{:S(2)}) async-start(bf16[32,16,128]{2,1,0:T(8,128)(2,1)} %broadcast_in_dim.2), calls=%async_computation.3 | async-start | bytes 262144 | tf_op jit(solution)/shard_map/all_to_all | solution.py:35
  67.0 1.0 %convolution_convert_fusion.4 = bf16[256,256]{1,0:T(8,128)(2,1)} fusion(s32[256]{0:T(256)S(1)} %bitcast.106, f32[256,256]{1,0:T(8,128)S(1)} %copy-done.8), kind=kOutput, calls=%fused_computation.15 | convolution fusion | flops 34013184 | bytes 394240 | tf_op jit(solution)/shard_map/dot_general | solution.py:108
  68.0 1.1 %convolution_convert_fusion.2 = bf16[256,256]{1,0:T(8,128)(2,1)} fusion(bf16[256,256]{1,0:T(8,128)(2,1)S(1)} %fusion.33, bf16[256,256]{1,0:T(8,128)(2,1)S(1)} %copy-done, s32[256]{0:T(256)S(1)} %bitcast.107), kind=kOutput, calls=%fused_computation.13 | convolution fusion | flops 67305472 | bytes 394240 | tf_op jit(solution)/shard_map/dot_general | solution.py:143
  69.0 5.7 %all-to-all-done.3 = bf16[32,16,128]{2,1,0:T(8,128)(2,1)S(1)} async-done(((bf16[32,16,128]{2,1,0:T(8,128)(2,1)}), bf16[32,16,128]{2,1,0:T(8,128)(2,1)S(1)}, u32[]{:S(2)}, u32[]{:S(2)}) %all-to-all-start.3) | async-done | bytes 131104 | tf_op jit(solution)/shard_map/all_to_all | solution.py:35
  74.7 0.7 reshape.214
  (17 shorter events, 0.1 us)
Async XLA Ops:
  0.6 1.2 %copy-start = (bf16[256,256]{1,0:T(8,128)(2,1)S(1)}, bf16[256,256]{1,0:T(8,128)(2,1)}, u32[]{:S(2)}) copy-start(bf16[256,256]{1,0:T(8,128)(2,1)} %param.20) | copy-start | bytes 393220
  2.0 26.2 %collective-permute-start = (bf16[256,256]{1,0:T(8,128)(2,1)S(1)}, bf16[256,256]{1,0:T(8,128)(2,1)}, u32[]{:S(2)}, u32[]{:S(2)}) collective-permute-start(bf16[256,256]{1,0:T(8,128)(2,1)S(1)} %convolution_convert_fusion.5), channel_id=1, source_target_pairs={{0,8},{8,16},{16,24},{24,0},{1,9},{9,17},{17,25},{25,1},{2,10},{10... | collective-permute-start | bytes 393224 | tf_op jit(solution)/shard_map/ppermute | solution.py:16
  2.5 25.7 %collective-permute-start.1 = (bf16[256,256]{1,0:T(8,128)(2,1)S(1)}, bf16[256,256]{1,0:T(8,128)(2,1)}, u32[]{:S(2)}, u32[]{:S(2)}) collective-permute-start(bf16[256,256]{1,0:T(8,128)(2,1)S(1)} %convolution_convert_fusion.5), channel_id=1, source_target_pairs={{8,0},{16,8},{24,16},{0,24},{9,1},{17,9},{25,17},{1,25},{10,2},{18... | collective-permute-start | bytes 393224 | tf_op jit(solution)/shard_map/ppermute | solution.py:18
  4.6 8.5 %copy-start.4 = (s32[40,2]{0,1:T(2,128)S(1)}, s32[40,2]{0,1:T(2,128)}, u32[]{:S(2)}) copy-start(s32[40,2]{0,1:T(2,128)} %param.25) | copy-start | bytes 964
  4.6 8.5 %copy-start.5 = (s32[12,2]{0,1:T(2,128)S(1)}, s32[12,2]{0,1:T(2,128)}, u32[]{:S(2)}) copy-start(s32[12,2]{0,1:T(2,128)} %param.23) | copy-start | bytes 292
  4.6 9.3 %copy-start.1 = (bf16[12,128,128]{2,1,0:T(8,128)(2,1)S(1)}, bf16[12,128,128]{2,1,0:T(8,128)(2,1)}, u32[]{:S(2)}) copy-start(bf16[12,128,128]{2,1,0:T(8,128)(2,1)} %param.22) | copy-start | bytes 1179652
  6.5 21.1 %all-to-all-start = ((bf16[8,128,256]{2,1,0:T(8,128)(2,1)}), bf16[8,128,256]{2,1,0:T(8,128)(2,1)S(1)}, u32[]{:S(2)}, u32[]{:S(2)}) async-start(bf16[8,128,256]{2,1,0:T(8,128)(2,1)} %copy.29), calls=%async_computation | async-start | bytes 1048576 | tf_op jit(solution)/shard_map/all_to_all | solution.py:89
  27.9 1.6 %copy-start.2 = (s32[1,256]{1,0:T(1,128)S(1)}, s32[1,256]{1,0:T(1,128)}, u32[]{:S(2)}) copy-start(s32[1,256]{1,0:T(1,128)} %param.28) | copy-start | bytes 3076
  27.9 1.6 %copy-start.6 = (bf16[256,256]{1,0:T(8,128)(2,1)S(1)}, bf16[256,256]{1,0:T(8,128)(2,1)}, u32[]{:S(2)}) copy-start(bf16[256,256]{1,0:T(8,128)(2,1)} %param.21) | copy-start | bytes 393220
  29.5 0.7 copy-start.7
  31.4 18.3 %all-to-all-start.1 = ((bf16[8,128,256]{2,1,0:T(8,128)(2,1)}), bf16[8,128,256]{2,1,0:T(8,128)(2,1)S(1)}, u32[]{:S(2)}, u32[]{:S(2)}) async-start(bf16[8,128,256]{2,1,0:T(8,128)(2,1)} %bitcast.19), calls=%async_computation.1 | async-start | bytes 1048576 | tf_op jit(solution)/shard_map/all_to_all | solution.py:128
  35.1 14.7 %copy-start.3 = (s32[1,8]{1,0:T(1,128)S(1)}, s32[1,8]{1,0:T(1,128)}, u32[]{:S(2)}) copy-start(s32[1,8]{1,0:T(1,128)} %param.27) | copy-start | bytes 100
  35.4 14.8 %collective-permute-start.2 = (bf16[256,256]{1,0:T(8,128)(2,1)S(1)}, bf16[256,256]{1,0:T(8,128)(2,1)S(1)}, u32[]{:S(2)}, u32[]{:S(2)}) collective-permute-start(bf16[256,256]{1,0:T(8,128)(2,1)S(1)} %get-tuple-element.45), channel_id=1, source_target_pairs={{0,8},{8,16},{16,24},{24,0},{1,9},{9,17},{17,25},{25,1},{2,10},{10... | collective-permute-start | bytes 393224 | tf_op jit(solution)/shard_map/ppermute | solution.py:16
  35.5 14.7 %collective-permute-start.3 = (bf16[256,256]{1,0:T(8,128)(2,1)S(1)}, bf16[256,256]{1,0:T(8,128)(2,1)S(1)}, u32[]{:S(2)}, u32[]{:S(2)}) collective-permute-start(bf16[256,256]{1,0:T(8,128)(2,1)S(1)} %get-tuple-element.46), channel_id=1, source_target_pairs={{8,0},{16,8},{24,16},{0,24},{9,1},{17,9},{25,17},{1,25},{10,2},{18... | collective-permute-start | bytes 393224 | tf_op jit(solution)/shard_map/ppermute | solution.py:18
  50.2 16.8 %copy-start.8 = (f32[256,256]{1,0:T(8,128)S(1)}, f32[256,256]{1,0:T(8,128)}, u32[]{:S(2)}) copy-start(f32[256,256]{1,0:T(8,128)} %copy-done.7) | copy-start | bytes 786436
  64.4 10.3 %all-to-all-start.3 = ((bf16[32,16,128]{2,1,0:T(8,128)(2,1)}), bf16[32,16,128]{2,1,0:T(8,128)(2,1)S(1)}, u32[]{:S(2)}, u32[]{:S(2)}) async-start(bf16[32,16,128]{2,1,0:T(8,128)(2,1)} %broadcast_in_dim.2), calls=%async_computation.3 | async-start | bytes 262144 | tf_op jit(solution)/shard_map/all_to_all | solution.py:35

commit v13 on v10

--- a/solution.py
+++ b/solution.py
@@ -29,9 +29,10 @@
     else:
         piece = (count, value.size // count // 128, 128)
     gathered = lax.all_to_all(value.reshape(piece), axes, 0, 0, tiled=True)
-    owned = jnp.sum(gathered, axis=0, keepdims=True) * scale
+    owned = (jnp.sum(gathered, axis=0, keepdims=True) * scale).astype(jnp.bfloat16)
     copies = jnp.broadcast_to(owned, piece)
-    return lax.all_to_all(copies, axes, 0, 0, tiled=True).reshape(value.shape)
+    spread = lax.all_to_all(copies, axes, 0, 0, tiled=True)
+    return spread.astype(jnp.float32).reshape(value.shape)
 
 
 def on_device(

time: 79 us -> 76.1 us (0.963)
  waiting for transfers between devices: 30.2 us -> 27.3 us
    all_to_all x1, waiting for transfers between devices: 8.57 us -> 5.67 us  [spread_sum(): spread = lax.all_to_all(copies, axes, 0, 0, tiled=True)]
where the time goes in v13:
time: 76.1 us; the launch traced here: 75.6 us
  waiting for transfers between devices  27.3 us (36%)
  starting transfers between devices  17.1 us (22%)
  matrix products  13.5 us (18%)
  blocking collectives  13.2 us (17%)
  other arithmetic  2.24 us (3%)
  between operations  1.57 us (2%)
    all_to_all x1, blocking collectives, spread_sum(): gathered = lax.all_to_all(value.reshape(piece), axes, 0, 0, tiled=True)  13.2 us
    all_to_all x1, waiting for transfers between devices, on_device(): lax.all_to_all(to_owner, 'col', split_axis=0, concat_axis=0, tiled=True)  12.5 us
    all_to_all x1, waiting for transfers between devices, on_device(): lax.all_to_all(outgoing, 'col', split_axis=0, concat_axis=0, tiled=True)  9.1 us
    all_to_all x1, starting transfers between devices, on_device(): lax.all_to_all(outgoing, 'col', split_axis=0, concat_axis=0, tiled=True)  6.53 us
    all_to_all x1, waiting for transfers between devices, spread_sum(): spread = lax.all_to_all(copies, axes, 0, 0, tiled=True)  5.67 us
    ppermute x2, starting transfers between devices, padded_2(): lax.ppermute(head, axis, [((i + 1) % count, i) for i in range(count)])  3.75 us
    all_to_all x1, starting transfers between devices, on_device(): lax.all_to_all(to_owner, 'col', split_axis=0, concat_axis=0, tiled=True)  3.64 us
    all_to_all x1, starting transfers between devices, spread_sum(): spread = lax.all_to_all(copies, axes, 0, 0, tiled=True)  2.58 us
  transfers between devices with their start and end apart: 7, of which 3 were waited for; matrix products, arithmetic and copies ran while one was open for 13% of the time, Pallas kernels for 0%

profile of v13, /device:TPU:0, one launch (start us, length us, event | category | flops | bytes accessed | tf_op | source)
XLA Modules:
  0.0 75.6 jit_solution(73933268948502212)
XLA Ops:
  0.6 0.0 copy-start
  0.6 0.0 copy-start.3
  0.7 0.0 copy-start.4
  0.7 1.2 %convolution_convert_fusion.6 = bf16[256,256]{1,0:T(8,128)(2,1)S(1)} fusion(bf16[256,256]{1,0:T(8,128)(2,1)} %param.19, s32[256]{0:T(256)} %bitcast.108), kind=kOutput, calls=%fused_computation.17 | convolution fusion | flops 33685504 | bytes 263168 | tf_op jit(solution)/shard_map/dot_general | solution.py:64
  1.9 0.0 copy-done
  1.9 0.2 convolution_convert_fusion.5
  2.1 0.5 collective-permute-start
  2.6 2.0 %collective-permute-start.1 = (bf16[256,256]{1,0:T(8,128)(2,1)S(1)}, bf16[256,256]{1,0:T(8,128)(2,1)}, u32[]{:S(2)}, u32[]{:S(2)}) collective-permute-start(bf16[256,256]{1,0:T(8,128)(2,1)S(1)} %convolution_convert_fusion.5), channel_id=1, source_target_pairs={{8,0},{16,8},{24,16},{0,24},{9,1},{17,9},{25,17},{1,25},{10,2},{18... | collective-permute-start | bytes 393224 | tf_op jit(solution)/shard_map/ppermute | solution.py:18
  4.6 0.7 broadcast_compare_fusion
  5.3 0.7 broadcast_multiply_fusion
  5.9 0.1 select_bitcast_fusion
  6.0 1.2 %convolution_convert_fusion = bf16[1024,256]{1,0:T(8,128)(2,1)} fusion(bf16[256,256]{1,0:T(8,128)(2,1)S(1)} %convolution_convert_fusion.5, s32[1024]{0:T(1024)S(1)} %select_bitcast_fusion), kind=kOutput, calls=%fused_computation.4 | convolution fusion | flops 134742016 | bytes 659456 | tf_op jit(solution)/shard_map/dot_general | solution.py:90
  7.2 6.5 %all-to-all-start = ((bf16[8,128,256]{2,1,0:T(8,128)(2,1)}), bf16[8,128,256]{2,1,0:T(8,128)(2,1)S(1)}, u32[]{:S(2)}, u32[]{:S(2)}) async-start(bf16[8,128,256]{2,1,0:T(8,128)(2,1)} %bitcast.9), calls=%async_computation | async-start | bytes 1048576 | tf_op jit(solution)/shard_map/all_to_all | solution.py:94
  13.7 0.0 copy-done.3
  13.7 0.0 copy-done.4
  14.4 0.0 copy-start.1
  14.5 2.3 %fusion.7 = (bf16[2,128,8,128]{3,2,1,0:T(8,128)(2,1)S(1)}, bf16[2,128,8,128]{3,2,1,0:T(8,128)(2,1)S(1)}, f32[2,8,128,128]{3,1,2,0:T(8,128)S(1)}) fusion(bf16[40,128,128]{2,1,0:T(8,128)(2,1)} %param.24, pred[40]{0:T(512)(128)(4,1)S(1)} %iota_compare_fusion.11, pred[40,8]{0,1:T(8,128)(4,1)S(1)} %iota_compare_fusion.7, pred[40,2]{0,1:T(4,128)(4,1)S(1)} %iota_compare_fusion.9), kind=kOutput, calls=%fused_computation.23 | convolution fusion | flops 22021376 | bytes 3408312 | tf_op jit(solution)/shard_map/krs,kab->rasb/dot_general | solution.py:104
  16.8 0.0 copy-done.1
  16.8 0.4 convolution_convert_fusion.1
  17.2 0.0 collective-permute-done
  17.2 0.0 collective-permute-done.1
  17.2 1.9 %fusion.19 = f32[256,256]{1,0:T(8,128)} fusion(bf16[256,256]{1,0:T(8,128)(2,1)} %collective-permute-done.1, bf16[256,256]{1,0:T(8,128)(2,1)S(1)} %convolution_convert_fusion.5, bf16[256,256]{1,0:T(8,128)(2,1)} %collective-permute-done, bf16[32,8,6,128]{3,2,1,0:T(8,128)(2,1)S(1)} %bitcast.106), kind=kOutput, calls=%fused_computation.35 | convolution fusion | flops 101842944 | bytes 1048576 | tf_op jit(solution)/shard_map/dot_general | solution.py:80
  19.1 9.1 %all-to-all-done = bf16[8,128,256]{2,1,0:T(8,128)(2,1)S(1)} async-done(((bf16[8,128,256]{2,1,0:T(8,128)(2,1)}), bf16[8,128,256]{2,1,0:T(8,128)(2,1)S(1)}, u32[]{:S(2)}, u32[]{:S(2)}) %all-to-all-start) | async-done | bytes 524320 | tf_op jit(solution)/shard_map/all_to_all | solution.py:94
  28.2 1.3 %convolution_add_fusion.2 = f32[256,256]{1,0:T(8,128)S(1)} fusion(f32[256,256]{1,0:T(8,128)} %fusion.19, bf16[1024,256]{1,0:T(8,128)(2,1)S(1)} %bitcast.102, bf16[32,8,8,128]{3,2,1,0:T(8,128)(2,1)S(1)} %bitcast.105), kind=kOutput, calls=%fused_computation.11 | convolution fusion | flops 134283264 | bytes 1572864 | tf_op jit(solution)/shard_map/dot_general | solution.py:111
  29.5 0.3 convolution_add_fusion.1
  29.8 0.0 copy-done.2
  29.9 0.0 copy-done.6
  29.9 0.2 fusion.5
  30.1 0.4 fusion.8
  30.5 1.2 %fusion.3 = bf16[1024,256]{1,0:T(8,128)(2,1)} fusion(f32[1024,256]{1,0:T(8,128)S(1)} %fusion.8, bf16[256,256]{1,0:T(8,128)(2,1)S(1)} %fusion.5, f32[32,8,8,128]{3,2,1,0:T(8,128)S(1)} %bitcast.101), kind=kOutput, calls=%fused_computation.6 | convolution fusion | flops 135790592 | bytes 2752512 | tf_op jit(solution)/shard_map/dot_general | solution.py:132
  31.6 3.6 %all-to-all-start.1 = ((bf16[8,128,256]{2,1,0:T(8,128)(2,1)}), bf16[8,128,256]{2,1,0:T(8,128)(2,1)S(1)}, u32[]{:S(2)}, u32[]{:S(2)}) async-start(bf16[8,128,256]{2,1,0:T(8,128)(2,1)} %bitcast.19), calls=%async_computation.1 | async-start | bytes 1048576 | tf_op jit(solution)/shard_map/all_to_all | solution.py:134
  35.3 0.3 fusion.54
  35.6 0.1 collective-permute-start.2
  35.7 1.7 %collective-permute-start.3 = (bf16[256,256]{1,0:T(8,128)(2,1)S(1)}, bf16[256,256]{1,0:T(8,128)(2,1)S(1)}, u32[]{:S(2)}, u32[]{:S(2)}) collective-permute-start(bf16[256,256]{1,0:T(8,128)(2,1)S(1)} %get-tuple-element.50), channel_id=1, source_target_pairs={{8,0},{16,8},{24,16},{0,24},{9,1},{17,9},{25,17},{1,25},{10,2},{18... | collective-permute-start | bytes 393224 | tf_op jit(solution)/shard_map/ppermute | solution.py:18
  37.4 12.5 %all-to-all-done.1 = bf16[8,128,256]{2,1,0:T(8,128)(2,1)S(1)} async-done(((bf16[8,128,256]{2,1,0:T(8,128)(2,1)}), bf16[8,128,256]{2,1,0:T(8,128)(2,1)S(1)}, u32[]{:S(2)}, u32[]{:S(2)}) %all-to-all-start.1) | async-done | bytes 524320 | tf_op jit(solution)/shard_map/all_to_all | solution.py:134
  49.9 0.0 copy-done.5
  49.9 0.4 fusion.15
  50.4 0.0 collective-permute-done.2
  50.4 0.0 collective-permute-done.3
  50.4 0.1 fusion.32
  50.4 0.2 convolution_bitcast_fusion
  50.7 13.2 %all_to_all.20 = f32[32,8,256]{2,1,0:T(8,128)S(1)} all-to-all(f32[32,8,256]{2,1,0:T(8,128)S(1)} %convolution_bitcast_fusion), channel_id=1, replica_groups=mesh['row'=4,'col'=8] {'row','col'}, dimensions={0} | all-to-all | bytes 524288 | tf_op jit(solution)/shard_map/all_to_all | solution.py:31
  63.9 0.7 broadcast_in_dim.16
  64.6 2.6 %all-to-all-start.3 = ((bf16[32,8,256]{2,1,0:T(8,128)(2,1)}), bf16[32,8,256]{2,1,0:T(8,128)(2,1)S(1)}, u32[]{:S(2)}, u32[]{:S(2)}) async-start(bf16[32,8,256]{2,1,0:T(8,128)(2,1)} %broadcast_in_dim.16), calls=%async_computation.3 | async-start | bytes 262144 | tf_op jit(solution)/shard_map/all_to_all | solution.py:34
  67.2 1.0 %convolution_convert_fusion.4 = bf16[256,256]{1,0:T(8,128)(2,1)} fusion(s32[256]{0:T(256)S(1)} %bitcast.110, f32[256,256]{1,0:T(8,128)S(1)} %convolution_add_fusion.1), kind=kOutput, calls=%fused_computation.15 | convolution fusion | flops 34013184 | bytes 394240 | tf_op jit(solution)/shard_map/dot_general | solution.py:114
  68.1 1.1 %convolution_convert_fusion.2 = bf16[256,256]{1,0:T(8,128)(2,1)} fusion(bf16[256,256]{1,0:T(8,128)(2,1)S(1)} %fusion.32, bf16[256,256]{1,0:T(8,128)(2,1)S(1)} %copy-done, s32[256]{0:T(256)S(1)} %bitcast.111), kind=kOutput, calls=%fused_computation.13 | convolution fusion | flops 67305472 | bytes 394240 | tf_op jit(solution)/shard_map/dot_general | solution.py:149
  69.2 5.7 %all-to-all-done.3 = bf16[32,8,256]{2,1,0:T(8,128)(2,1)S(1)} async-done(((bf16[32,8,256]{2,1,0:T(8,128)(2,1)}), bf16[32,8,256]{2,1,0:T(8,128)(2,1)S(1)}, u32[]{:S(2)}, u32[]{:S(2)}) %all-to-all-start.3) | async-done | bytes 131104 | tf_op jit(solution)/shard_map/all_to_all | solution.py:34
  74.9 0.7 bitcast_convert_fusion.3
  (14 shorter events, 0.1 us)
Async XLA Ops:
  0.6 1.3 %copy-start = (bf16[256,256]{1,0:T(8,128)(2,1)S(1)}, bf16[256,256]{1,0:T(8,128)(2,1)}, u32[]{:S(2)}) copy-start(bf16[256,256]{1,0:T(8,128)(2,1)} %param.20) | copy-start | bytes 393220
  0.6 13.0 %copy-start.3 = (s32[12,2]{0,1:T(2,128)S(1)}, s32[12,2]{0,1:T(2,128)}, u32[]{:S(2)}) copy-start(s32[12,2]{0,1:T(2,128)} %param.23) | copy-start | bytes 292
  0.7 13.1 %copy-start.4 = (s32[40,2]{0,1:T(2,128)S(1)}, s32[40,2]{0,1:T(2,128)}, u32[]{:S(2)}) copy-start(s32[40,2]{0,1:T(2,128)} %param.25) | copy-start | bytes 964
  2.1 15.1 %collective-permute-start = (bf16[256,256]{1,0:T(8,128)(2,1)S(1)}, bf16[256,256]{1,0:T(8,128)(2,1)}, u32[]{:S(2)}, u32[]{:S(2)}) collective-permute-start(bf16[256,256]{1,0:T(8,128)(2,1)S(1)} %convolution_convert_fusion.5), channel_id=1, source_target_pairs={{0,8},{8,16},{16,24},{24,0},{1,9},{9,17},{17,25},{25,1},{2,10},{10... | collective-permute-start | bytes 393224 | tf_op jit(solution)/shard_map/ppermute | solution.py:16
  2.6 14.6 %collective-permute-start.1 = (bf16[256,256]{1,0:T(8,128)(2,1)S(1)}, bf16[256,256]{1,0:T(8,128)(2,1)}, u32[]{:S(2)}, u32[]{:S(2)}) collective-permute-start(bf16[256,256]{1,0:T(8,128)(2,1)S(1)} %convolution_convert_fusion.5), channel_id=1, source_target_pairs={{8,0},{16,8},{24,16},{0,24},{9,1},{17,9},{25,17},{1,25},{10,2},{18... | collective-permute-start | bytes 393224 | tf_op jit(solution)/shard_map/ppermute | solution.py:18
  7.2 21.1 %all-to-all-start = ((bf16[8,128,256]{2,1,0:T(8,128)(2,1)}), bf16[8,128,256]{2,1,0:T(8,128)(2,1)S(1)}, u32[]{:S(2)}, u32[]{:S(2)}) async-start(bf16[8,128,256]{2,1,0:T(8,128)(2,1)} %bitcast.9), calls=%async_computation | async-start | bytes 1048576 | tf_op jit(solution)/shard_map/all_to_all | solution.py:94
  14.4 2.4 %copy-start.1 = (bf16[12,128,128]{2,1,0:T(8,128)(2,1)S(1)}, bf16[12,128,128]{2,1,0:T(8,128)(2,1)}, u32[]{:S(2)}) copy-start(bf16[12,128,128]{2,1,0:T(8,128)(2,1)} %param.22) | copy-start | bytes 1179652
  28.2 1.6 %copy-start.2 = (s32[1,256]{1,0:T(1,128)S(1)}, s32[1,256]{1,0:T(1,128)}, u32[]{:S(2)}) copy-start(s32[1,256]{1,0:T(1,128)} %param.28) | copy-start | bytes 3076
  28.2 1.6 %copy-start.6 = (bf16[256,256]{1,0:T(8,128)(2,1)S(1)}, bf16[256,256]{1,0:T(8,128)(2,1)}, u32[]{:S(2)}) copy-start(bf16[256,256]{1,0:T(8,128)(2,1)} %param.21) | copy-start | bytes 393220
  31.6 18.3 %all-to-all-start.1 = ((bf16[8,128,256]{2,1,0:T(8,128)(2,1)}), bf16[8,128,256]{2,1,0:T(8,128)(2,1)S(1)}, u32[]{:S(2)}, u32[]{:S(2)}) async-start(bf16[8,128,256]{2,1,0:T(8,128)(2,1)} %bitcast.19), calls=%async_computation.1 | async-start | bytes 1048576 | tf_op jit(solution)/shard_map/all_to_all | solution.py:134
  35.3 14.7 %copy-start.5 = (s32[1,8]{1,0:T(1,128)S(1)}, s32[1,8]{1,0:T(1,128)}, u32[]{:S(2)}) copy-start(s32[1,8]{1,0:T(1,128)} %param.27) | copy-start | bytes 100
  35.6 14.8 %collective-permute-start.2 = (bf16[256,256]{1,0:T(8,128)(2,1)S(1)}, bf16[256,256]{1,0:T(8,128)(2,1)S(1)}, u32[]{:S(2)}, u32[]{:S(2)}) collective-permute-start(bf16[256,256]{1,0:T(8,128)(2,1)S(1)} %get-tuple-element.49), channel_id=1, source_target_pairs={{0,8},{8,16},{16,24},{24,0},{1,9},{9,17},{17,25},{25,1},{2,10},{10... | collective-permute-start | bytes 393224 | tf_op jit(solution)/shard_map/ppermute | solution.py:16
  35.7 14.7 %collective-permute-start.3 = (bf16[256,256]{1,0:T(8,128)(2,1)S(1)}, bf16[256,256]{1,0:T(8,128)(2,1)S(1)}, u32[]{:S(2)}, u32[]{:S(2)}) collective-permute-start(bf16[256,256]{1,0:T(8,128)(2,1)S(1)} %get-tuple-element.50), channel_id=1, source_target_pairs={{8,0},{16,8},{24,16},{0,24},{9,1},{17,9},{25,17},{1,25},{10,2},{18... | collective-permute-start | bytes 393224 | tf_op jit(solution)/shard_map/ppermute | solution.py:18
  64.6 10.3 %all-to-all-start.3 = ((bf16[32,8,256]{2,1,0:T(8,128)(2,1)}), bf16[32,8,256]{2,1,0:T(8,128)(2,1)S(1)}, u32[]{:S(2)}, u32[]{:S(2)}) async-start(bf16[32,8,256]{2,1,0:T(8,128)(2,1)} %broadcast_in_dim.16), calls=%async_computation.3 | async-start | bytes 262144 | tf_op jit(solution)/shard_map/all_to_all | solution.py:34

commit v14 on v11

--- a/solution.py
+++ b/solution.py
@@ -121,8 +121,11 @@
     grad_hidden = grad_hidden.at[:BW].add(padded[:BW].astype(jnp.float32))
     grad_hidden = grad_hidden.at[row_count - BW :].add(padded[3 * BW :].astype(jnp.float32))
     owner_terms = lax.dot_general(
-        dense_high, slope, contract_rows, preferred_element_type=jnp.float32
-    ) + lax.dot_general(dense_low, slope, contract_rows, preferred_element_type=jnp.float32)
+        jnp.concatenate([dense_high, dense_low], axis=0),
+        jnp.concatenate([slope, slope], axis=0),
+        contract_rows,
+        preferred_element_type=jnp.float32,
+    )
     to_owner = owner_terms.astype(jnp.bfloat16).reshape(peers, tile_size, width_feat)
     returned = lax.all_to_all(to_owner, "col", split_axis=0, concat_axis=0, tiled=True)
     block_onehot = (giving[None, :] == tile_range[:, None]).astype(jnp.bfloat16)

time: 75.8 us -> 75.3 us (level)
  matrix products: 11.7 us -> 9.21 us
  local copies, waits for them, and re-layouts: 1.74 us -> 3.34 us
  other arithmetic: 0.85 us -> 1.83 us
    unnamed x18 -> x25, local copies, waits for them, and re-layouts: 0.14 us -> 1.74 us
    dot_general x1, matrix products: 2.28 us -> 0.96 us  [on_device(): jnp.einsum('krs,kab->rasb', slot_onehot, bound_tiles, preferred_element_t...]
    convert_element_type x0 -> x1, other arithmetic: none -> 0.98 us  [on_device(): (bound_dense - dense_high.astype(jnp.float32)).astype(jnp.bfloat16)]
    dot_general x1, matrix products: 1.24 us -> 0.27 us  [on_device(): mixed = jnp.dot(band_dense, extended, preferred_element_type=jnp.float32)]
    dot_general x2 -> x1, matrix products: 1.53 us -> 1.3 us  [on_device(): lax.dot_general(jnp.concatenate([dense_high, dense_low], axis=0), jnp.con...]
  transfers between devices with their start and end apart: 7 -> 7, of which waited for: 3 -> 3; matrix products, arithmetic and copies ran while one was open for 11% -> 12% of each run, Pallas kernels for 0% -> 0%
where the time goes in v14:
time: 75.3 us; the launch traced here: 74.8 us
  waiting for transfers between devices  28.6 us (38%)
  starting transfers between devices  17 us (23%)
  blocking collectives  13.2 us (18%)
  matrix products  9.21 us (12%)
  local copies, waits for them, and re-layouts  3.34 us (4%)
  other arithmetic  1.83 us (2%)
  between operations  1.59 us (2%)
    all_to_all x1, blocking collectives, spread_sum(): gathered = lax.all_to_all(value.reshape(piece), axes, 0, 0, tiled=True)  13.2 us
    all_to_all x1, waiting for transfers between devices, on_device(): lax.all_to_all(to_owner, 'col', split_axis=0, concat_axis=0, tiled=True)  12.5 us
    all_to_all x1, waiting for transfers between devices, on_device(): lax.all_to_all(outgoing, 'col', split_axis=0, concat_axis=0, tiled=True)  10.4 us
    all_to_all x1, starting transfers between devices, on_device(): lax.all_to_all(outgoing, 'col', split_axis=0, concat_axis=0, tiled=True)  6.53 us
    all_to_all x1, waiting for transfers between devices, spread_sum(): spread = lax.all_to_all(copies, axes, 0, 0, tiled=True)  5.65 us
    ppermute x2, starting transfers between devices, padded_2(): lax.ppermute(head, axis, [((i + 1) % count, i) for i in range(count)])  3.75 us
    all_to_all x1, starting transfers between devices, on_device(): lax.all_to_all(to_owner, 'col', split_axis=0, concat_axis=0, tiled=True)  3.64 us
    all_to_all x1, starting transfers between devices, spread_sum(): spread = lax.all_to_all(copies, axes, 0, 0, tiled=True)  2.56 us
  transfers between devices with their start and end apart: 7, of which 3 were waited for; matrix products, arithmetic and copies ran while one was open for 12% of the time, Pallas kernels for 0%

profile of v14, /device:TPU:0, one launch (start us, length us, event | category | flops | bytes accessed | tf_op | source)
XLA Modules:
  0.0 74.8 jit_solution(17187514401887022753)
XLA Ops:
  0.6 0.0 copy-start
  0.6 1.2 %convolution_convert_fusion.7 = bf16[256,256]{1,0:T(8,128)(2,1)S(1)} fusion(bf16[256,256]{1,0:T(8,128)(2,1)} %param.19, s32[256]{0:T(256)} %bitcast.105), kind=kOutput, calls=%fused_computation.16 | convolution fusion | flops 33685504 | bytes 263168 | tf_op jit(solution)/shard_map/dot_general | solution.py:64
  1.8 0.2 convolution_convert_fusion.6
  2.0 0.5 collective-permute-start
  2.5 2.0 %collective-permute-start.1 = (bf16[256,256]{1,0:T(8,128)(2,1)S(1)}, bf16[256,256]{1,0:T(8,128)(2,1)S(1)}, u32[]{:S(2)}, u32[]{:S(2)}) collective-permute-start(bf16[256,256]{1,0:T(8,128)(2,1)S(1)} %convolution_convert_fusion.6), channel_id=1, source_target_pairs={{8,0},{16,8},{24,16},{0,24},{9,1},{17,9},{25,17},{1,25},{10,2},{18... | collective-permute-start | bytes 393224 | tf_op jit(solution)/shard_map/ppermute | solution.py:18
  4.6 1.1 %convolution_convert_fusion.1 = bf16[8,128,256]{2,0,1:T(8,128)(2,1)S(1)} fusion(bf16[2,128,256]{2,1,0:T(8,128)(2,1)S(1)} %bitcast.104, s32[8]{0:T(128)} %bitcast.109), kind=kOutput, calls=%fused_computation.4 | convolution fusion | flops 1310736 | bytes 655392 | tf_op jit(solution)/shard_map/sb,baf->saf/dot_general | solution.py:85
  5.7 0.9 %copy.29 = bf16[8,128,256]{2,1,0:T(8,128)(2,1)} copy(bf16[8,128,256]{2,0,1:T(8,128)(2,1)S(1)} %convolution_convert_fusion.1) | data formatting | bytes 1048576 | tf_op jit(solution)/shard_map/convert_element_type | solution.py:87
  6.6 6.5 %all-to-all-start = ((bf16[8,128,256]{2,1,0:T(8,128)(2,1)}), bf16[8,128,256]{2,1,0:T(8,128)(2,1)S(1)}, u32[]{:S(2)}, u32[]{:S(2)}) async-start(bf16[8,128,256]{2,1,0:T(8,128)(2,1)} %copy.29), calls=%async_computation | async-start | bytes 1048576 | tf_op jit(solution)/shard_map/all_to_all | solution.py:88
  13.8 0.0 copy-done.1
  13.9 1.0 %fusion.10 = (bf16[2,128,8,128]{3,2,1,0:T(8,128)(2,1)S(1)}, bf16[2,128,8,128]{3,2,1,0:T(8,128)(2,1)S(1)}, f32[2,8,128,128]{3,1,2,0:T(8,128)S(1)}) fusion(bf16[40,128,128]{2,1,0:T(8,128)(2,1)S(1)} %copy-done.1, pred[40]{0:T(512)(128)(4,1)S(1)} %iota_compare_fusion.9, pred[40,8]{0,1:T(8,128)(4,1)S(1)} %iota_compare_fusion.5, ...), kind=kOutput, calls=%fused_computation.25 | convolution fusion | flops 22021376 | bytes 3408312 | tf_op jit(solution)/shard_map/krs,kab->rasb/dot_general | solution.py:98
  14.8 0.0 copy-start.2
  14.8 1.0 %copy.75 = bf16[32,8,8,128]{3,1,2,0:T(8,128)(2,1)} copy(f32[32,8,8,128]{3,2,1,0:T(8,128)S(1)} %bitcast.95) | data formatting | bytes 1572864
  15.9 0.4 convolution_convert_fusion.2
  16.2 1.0 %fusion.6 = bf16[256,1024]{1,0:T(8,128)(2,1)} fusion(f32[32,8,8,128]{3,2,1,0:T(8,128)S(1)} %bitcast.96), kind=kLoop, calls=%fused_computation.19 | loop fusion | flops 1048576 | bytes 1572864 | tf_op jit(solution)/shard_map/convert_element_type | solution.py:102
  17.2 10.4 %all-to-all-done = bf16[8,128,256]{2,1,0:T(8,128)(2,1)S(1)} async-done(((bf16[8,128,256]{2,1,0:T(8,128)(2,1)}), bf16[8,128,256]{2,1,0:T(8,128)(2,1)S(1)}, u32[]{:S(2)}, u32[]{:S(2)}) %all-to-all-start) | async-done | bytes 524320 | tf_op jit(solution)/shard_map/all_to_all | solution.py:88
  27.7 0.3 fusion.14
  28.0 0.0 copy-start.5
  28.0 0.0 copy-start.9
  28.0 0.3 fusion.11
  28.3 0.0 collective-permute-done
  28.3 0.0 collective-permute-done.1
  28.4 0.3 fusion.4
  28.6 0.0 copy-done.5
  28.7 0.2 copy-done.9
  28.9 0.2 fusion.5
  29.1 0.2 copy-done.3
  29.4 0.2 copy-done.4
  29.5 1.3 %convolution_convert_fusion = bf16[1024,256]{1,0:T(8,128)(2,1)} fusion(bf16[256,1024]{1,0:T(8,128)(2,1)S(1)} %copy-done.4, bf16[256,1024]{1,0:T(8,128)(2,1)S(1)} %bitcast.103, bf16[256,256]{1,0:T(8,128)(2,1)S(1)} %fusion.5), kind=kOutput, calls=%fused_computation.3 | convolution fusion | flops 271319040 | bytes 1703936 | tf_op jit(solution)/shard_map/dot_general | solution.py:123
  30.8 0.0 copy-done.10
  30.9 3.6 %all-to-all-start.1 = ((bf16[8,128,256]{2,1,0:T(8,128)(2,1)}), bf16[8,128,256]{2,1,0:T(8,128)(2,1)S(1)}, u32[]{:S(2)}, u32[]{:S(2)}) async-start(bf16[8,128,256]{2,1,0:T(8,128)(2,1)} %bitcast.19), calls=%async_computation.1 | async-start | bytes 1048576 | tf_op jit(solution)/shard_map/all_to_all | solution.py:130
  34.5 0.3 fusion.64
  34.8 0.1 collective-permute-start.2
  34.9 1.7 %collective-permute-start.3 = (bf16[256,256]{1,0:T(8,128)(2,1)S(1)}, bf16[256,256]{1,0:T(8,128)(2,1)S(1)}, u32[]{:S(2)}, u32[]{:S(2)}) collective-permute-start(bf16[256,256]{1,0:T(8,128)(2,1)S(1)} %get-tuple-element.46), channel_id=1, source_target_pairs={{8,0},{16,8},{24,16},{0,24},{9,1},{17,9},{25,17},{1,25},{10,2},{18... | collective-permute-start | bytes 393224 | tf_op jit(solution)/shard_map/ppermute | solution.py:18
  36.6 12.5 %all-to-all-done.1 = bf16[8,128,256]{2,1,0:T(8,128)(2,1)S(1)} async-done(((bf16[8,128,256]{2,1,0:T(8,128)(2,1)}), bf16[8,128,256]{2,1,0:T(8,128)(2,1)S(1)}, u32[]{:S(2)}, u32[]{:S(2)}) %all-to-all-start.1) | async-done | bytes 524320 | tf_op jit(solution)/shard_map/all_to_all | solution.py:130
  49.2 0.4 fusion.18
  49.6 0.0 collective-permute-done.2
  49.6 0.0 collective-permute-done.3
  49.6 0.0 copy-start.11
  49.6 0.1 fusion.33
  49.7 0.2 convolution_bitcast_fusion
  49.9 13.2 %all_to_all.20 = f32[32,8,256]{2,1,0:T(8,128)S(1)} all-to-all(f32[32,8,256]{2,1,0:T(8,128)S(1)} %convolution_bitcast_fusion), channel_id=1, replica_groups=mesh['row'=4,'col'=8] {'row','col'}, dimensions={0} | all-to-all | bytes 524288 | tf_op jit(solution)/shard_map/all_to_all | solution.py:31
  63.1 0.7 broadcast_in_dim.2
  63.8 2.6 %all-to-all-start.3 = ((bf16[32,8,256]{2,1,0:T(8,128)(2,1)}), bf16[32,8,256]{2,1,0:T(8,128)(2,1)S(1)}, u32[]{:S(2)}, u32[]{:S(2)}) async-start(bf16[32,8,256]{2,1,0:T(8,128)(2,1)} %broadcast_in_dim.2), calls=%async_computation.3 | async-start | bytes 262144 | tf_op jit(solution)/shard_map/all_to_all | solution.py:34
  66.4 0.0 copy-done.11
  66.4 1.0 %convolution_convert_fusion.5 = bf16[256,256]{1,0:T(8,128)(2,1)} fusion(s32[256]{0:T(256)S(1)} %bitcast.107, f32[256,256]{1,0:T(8,128)S(1)} %copy-done.11), kind=kOutput, calls=%fused_computation.14 | convolution fusion | flops 34013184 | bytes 394240 | tf_op jit(solution)/shard_map/dot_general | solution.py:107
  67.4 1.1 %convolution_convert_fusion.3 = bf16[256,256]{1,0:T(8,128)(2,1)} fusion(bf16[256,256]{1,0:T(8,128)(2,1)S(1)} %fusion.33, bf16[256,256]{1,0:T(8,128)(2,1)S(1)} %copy-done, s32[256]{0:T(256)S(1)} %bitcast.108), kind=kOutput, calls=%fused_computation.12 | convolution fusion | flops 67305472 | bytes 394240 | tf_op jit(solution)/shard_map/dot_general | solution.py:145
  68.4 5.7 %all-to-all-done.3 = bf16[32,8,256]{2,1,0:T(8,128)(2,1)S(1)} async-done(((bf16[32,8,256]{2,1,0:T(8,128)(2,1)}), bf16[32,8,256]{2,1,0:T(8,128)(2,1)S(1)}, u32[]{:S(2)}, u32[]{:S(2)}) %all-to-all-start.3) | async-done | bytes 131104 | tf_op jit(solution)/shard_map/all_to_all | solution.py:34
  74.1 0.7 bitcast_convert_fusion.2
  (23 shorter events, 0.1 us)
Async XLA Ops:
  0.6 1.2 %copy-start = (bf16[256,256]{1,0:T(8,128)(2,1)S(1)}, bf16[256,256]{1,0:T(8,128)(2,1)}, u32[]{:S(2)}) copy-start(bf16[256,256]{1,0:T(8,128)(2,1)} %param.20) | copy-start | bytes 393220
  2.0 26.3 %collective-permute-start = (bf16[256,256]{1,0:T(8,128)(2,1)S(1)}, bf16[256,256]{1,0:T(8,128)(2,1)S(1)}, u32[]{:S(2)}, u32[]{:S(2)}) collective-permute-start(bf16[256,256]{1,0:T(8,128)(2,1)S(1)} %convolution_convert_fusion.6), channel_id=1, source_target_pairs={{0,8},{8,16},{16,24},{24,0},{1,9},{9,17},{17,25},{25,1},{2,10},{10... | collective-permute-start | bytes 393224 | tf_op jit(solution)/shard_map/ppermute | solution.py:16
  2.5 25.8 %collective-permute-start.1 = (bf16[256,256]{1,0:T(8,128)(2,1)S(1)}, bf16[256,256]{1,0:T(8,128)(2,1)S(1)}, u32[]{:S(2)}, u32[]{:S(2)}) collective-permute-start(bf16[256,256]{1,0:T(8,128)(2,1)S(1)} %convolution_convert_fusion.6), channel_id=1, source_target_pairs={{8,0},{16,8},{24,16},{0,24},{9,1},{17,9},{25,17},{1,25},{10,2},{18... | collective-permute-start | bytes 393224 | tf_op jit(solution)/shard_map/ppermute | solution.py:18
  4.6 8.6 %copy-start.7 = (s32[40,2]{0,1:T(2,128)S(1)}, s32[40,2]{0,1:T(2,128)}, u32[]{:S(2)}) copy-start(s32[40,2]{0,1:T(2,128)} %param.25) | copy-start | bytes 964
  4.6 9.3 %copy-start.8 = (s32[12,2]{0,1:T(2,128)S(1)}, s32[12,2]{0,1:T(2,128)}, u32[]{:S(2)}) copy-start(s32[12,2]{0,1:T(2,128)} %param.23) | copy-start | bytes 292
  4.6 9.3 %copy-start.1 = (bf16[40,128,128]{2,1,0:T(8,128)(2,1)S(1)}, bf16[40,128,128]{2,1,0:T(8,128)(2,1)}, u32[]{:S(2)}) copy-start(bf16[40,128,128]{2,1,0:T(8,128)(2,1)} %param.24) | copy-start | bytes 3932164
  6.6 21.1 %all-to-all-start = ((bf16[8,128,256]{2,1,0:T(8,128)(2,1)}), bf16[8,128,256]{2,1,0:T(8,128)(2,1)S(1)}, u32[]{:S(2)}, u32[]{:S(2)}) async-start(bf16[8,128,256]{2,1,0:T(8,128)(2,1)} %copy.29), calls=%async_computation | async-start | bytes 1048576 | tf_op jit(solution)/shard_map/all_to_all | solution.py:88
  14.8 1.0 %copy-start.2 = (bf16[12,128,128]{2,1,0:T(8,128)(2,1)S(1)}, bf16[12,128,128]{2,1,0:T(8,128)(2,1)}, u32[]{:S(2)}) copy-start(bf16[12,128,128]{2,1,0:T(8,128)(2,1)} %param.22) | copy-start | bytes 1179652
  28.0 0.7 copy-start.5
  28.0 0.9 %copy-start.9 = (bf16[256,256]{1,0:T(8,128)(2,1)S(1)}, bf16[256,256]{1,0:T(8,128)(2,1)}, u32[]{:S(2)}) copy-start(bf16[256,256]{1,0:T(8,128)(2,1)} %param.21) | copy-start | bytes 393220
  28.3 1.1 %copy-start.3 = (bf16[32,8,8,128]{3,1,2,0:T(8,128)(2,1)S(1)}, bf16[32,8,8,128]{3,1,2,0:T(8,128)(2,1)}, u32[]{:S(2)}) copy-start(bf16[32,8,8,128]{3,1,2,0:T(8,128)(2,1)} %copy.75) | copy-start | bytes 1572868
  28.3 1.2 %copy-start.4 = (bf16[256,1024]{1,0:T(8,128)(2,1)S(1)}, bf16[256,1024]{1,0:T(8,128)(2,1)}, u32[]{:S(2)}) copy-start(bf16[256,1024]{1,0:T(8,128)(2,1)} %fusion.6) | copy-start | bytes 1572868
  28.9 1.9 %copy-start.10 = (f32[256,256]{1,0:T(8,128)}, f32[256,256]{1,0:T(8,128)S(1)}, u32[]{:S(2)}) copy-start(f32[256,256]{1,0:T(8,128)S(1)} %fusion.4) | copy-start | bytes 786436
  30.9 18.3 %all-to-all-start.1 = ((bf16[8,128,256]{2,1,0:T(8,128)(2,1)}), bf16[8,128,256]{2,1,0:T(8,128)(2,1)S(1)}, u32[]{:S(2)}, u32[]{:S(2)}) async-start(bf16[8,128,256]{2,1,0:T(8,128)(2,1)} %bitcast.19), calls=%async_computation.1 | async-start | bytes 1048576 | tf_op jit(solution)/shard_map/all_to_all | solution.py:130
  34.5 14.7 %copy-start.6 = (s32[1,8]{1,0:T(1,128)S(1)}, s32[1,8]{1,0:T(1,128)}, u32[]{:S(2)}) copy-start(s32[1,8]{1,0:T(1,128)} %param.27) | copy-start | bytes 100
  34.8 14.8 %collective-permute-start.2 = (bf16[256,256]{1,0:T(8,128)(2,1)S(1)}, bf16[256,256]{1,0:T(8,128)(2,1)S(1)}, u32[]{:S(2)}, u32[]{:S(2)}) collective-permute-start(bf16[256,256]{1,0:T(8,128)(2,1)S(1)} %get-tuple-element.45), channel_id=1, source_target_pairs={{0,8},{8,16},{16,24},{24,0},{1,9},{9,17},{17,25},{25,1},{2,10},{10... | collective-permute-start | bytes 393224 | tf_op jit(solution)/shard_map/ppermute | solution.py:16
  34.9 14.7 %collective-permute-start.3 = (bf16[256,256]{1,0:T(8,128)(2,1)S(1)}, bf16[256,256]{1,0:T(8,128)(2,1)S(1)}, u32[]{:S(2)}, u32[]{:S(2)}) collective-permute-start(bf16[256,256]{1,0:T(8,128)(2,1)S(1)} %get-tuple-element.46), channel_id=1, source_target_pairs={{8,0},{16,8},{24,16},{0,24},{9,1},{17,9},{25,17},{1,25},{10,2},{18... | collective-permute-start | bytes 393224 | tf_op jit(solution)/shard_map/ppermute | solution.py:18
  49.6 16.7 %copy-start.11 = (f32[256,256]{1,0:T(8,128)S(1)}, f32[256,256]{1,0:T(8,128)}, u32[]{:S(2)}) copy-start(f32[256,256]{1,0:T(8,128)} %copy-done.10) | copy-start | bytes 786436
  63.8 10.3 %all-to-all-start.3 = ((bf16[32,8,256]{2,1,0:T(8,128)(2,1)}), bf16[32,8,256]{2,1,0:T(8,128)(2,1)S(1)}, u32[]{:S(2)}, u32[]{:S(2)}) async-start(bf16[32,8,256]{2,1,0:T(8,128)(2,1)} %broadcast_in_dim.2), calls=%async_computation.3 | async-start | bytes 262144 | tf_op jit(solution)/shard_map/all_to_all | solution.py:34

commit v15 on v14

--- a/solution.py
+++ b/solution.py
@@ -101,8 +101,11 @@
     dense_high = bound_dense.astype(jnp.bfloat16)
     dense_low = (bound_dense - dense_high.astype(jnp.float32)).astype(jnp.bfloat16)
     arrived_rows = arrived.reshape(peers * tile_size, width_feat)
-    mixed = mixed + jnp.dot(dense_high, arrived_rows, preferred_element_type=jnp.float32)
-    mixed = mixed + jnp.dot(dense_low, arrived_rows, preferred_element_type=jnp.float32)
+    mixed = mixed + jnp.dot(
+        jnp.concatenate([dense_high, dense_low], axis=1),
+        jnp.concatenate([arrived_rows, arrived_rows], axis=0),
+        preferred_element_type=jnp.float32,
+    )
     out_band = jax.nn.silu(mixed).astype(jnp.bfloat16)
     node_out = lax.dot_general(
         band_perm, out_band, contract_rows, preferred_element_type=jnp.float32

time: 75.3 us -> 75 us (level)
  waiting for transfers between devices: 28.6 us -> 29.5 us
  other arithmetic: 1.83 us -> 1.02 us
    all_to_all x1, waiting for transfers between devices: 10.4 us -> 11.3 us  [on_device(): lax.all_to_all(outgoing, 'col', split_axis=0, concat_axis=0, tiled=True)]
    convert_element_type x1, other arithmetic: 0.98 us -> 0.17 us  [on_device(): (bound_dense - dense_high.astype(jnp.float32)).astype(jnp.bfloat16)]
    unnamed x25 -> x17, local copies, waits for them, and re-layouts: 1.74 us -> 1.68 us
  transfers between devices with their start and end apart: 7 -> 7, of which waited for: 3 -> 3; matrix products, arithmetic and copies ran while one was open for 12% -> 9% of each run, Pallas kernels for 0% -> 0%
where the time goes in v15:
time: 75 us; the launch traced here: 74.6 us
  waiting for transfers between devices  29.5 us (39%)
  starting transfers between devices  17.1 us (23%)
  blocking collectives  13.2 us (18%)
  matrix products  8.99 us (12%)
  local copies, waits for them, and re-layouts  3.29 us (4%)
  between operations  1.55 us (2%)
  other arithmetic  1.02 us (1%)
    all_to_all x1, blocking collectives, spread_sum(): gathered = lax.all_to_all(value.reshape(piece), axes, 0, 0, tiled=True)  13.2 us
    all_to_all x1, waiting for transfers between devices, on_device(): lax.all_to_all(to_owner, 'col', split_axis=0, concat_axis=0, tiled=True)  12.5 us
    all_to_all x1, waiting for transfers between devices, on_device(): lax.all_to_all(outgoing, 'col', split_axis=0, concat_axis=0, tiled=True)  11.3 us
    all_to_all x1, starting transfers between devices, on_device(): lax.all_to_all(outgoing, 'col', split_axis=0, concat_axis=0, tiled=True)  6.53 us
    all_to_all x1, waiting for transfers between devices, spread_sum(): spread = lax.all_to_all(copies, axes, 0, 0, tiled=True)  5.66 us
    ppermute x2, starting transfers between devices, padded_2(): lax.ppermute(head, axis, [((i + 1) % count, i) for i in range(count)])  3.75 us
    all_to_all x1, starting transfers between devices, on_device(): lax.all_to_all(to_owner, 'col', split_axis=0, concat_axis=0, tiled=True)  3.64 us
    all_to_all x1, starting transfers between devices, spread_sum(): spread = lax.all_to_all(copies, axes, 0, 0, tiled=True)  2.58 us
  transfers between devices with their start and end apart: 7, of which 3 were waited for; matrix products, arithmetic and copies ran while one was open for 9% of the time, Pallas kernels for 0%

profile of v15, /device:TPU:0, one launch (start us, length us, event | category | flops | bytes accessed | tf_op | source)
XLA Modules:
  0.0 74.6 jit_solution(5878788806615532038)
XLA Ops:
  0.6 0.0 copy-start
  0.6 1.2 %convolution_convert_fusion.7 = bf16[256,256]{1,0:T(8,128)(2,1)S(1)} fusion(bf16[256,256]{1,0:T(8,128)(2,1)} %param.19, s32[256]{0:T(256)} %bitcast.82), kind=kOutput, calls=%fused_computation.15 | convolution fusion | flops 33685504 | bytes 263168 | tf_op jit(solution)/shard_map/dot_general | solution.py:64
  1.8 0.0 copy-done
  1.8 0.2 convolution_convert_fusion.6
  2.0 0.5 collective-permute-start
  2.5 2.0 %collective-permute-start.1 = (bf16[256,256]{1,0:T(8,128)(2,1)S(1)}, bf16[256,256]{1,0:T(8,128)(2,1)S(1)}, u32[]{:S(2)}, u32[]{:S(2)}) collective-permute-start(bf16[256,256]{1,0:T(8,128)(2,1)S(1)} %convolution_convert_fusion.6), channel_id=1, source_target_pairs={{8,0},{16,8},{24,16},{0,24},{9,1},{17,9},{25,17},{1,25},{10,2},{18... | collective-permute-start | bytes 393224 | tf_op jit(solution)/shard_map/ppermute | solution.py:18
  4.6 0.0 copy-start.5
  4.6 0.0 copy-start.6
  4.6 1.1 %convolution_convert_fusion.1 = bf16[8,128,256]{2,0,1:T(8,128)(2,1)S(1)} fusion(bf16[2,128,256]{2,1,0:T(8,128)(2,1)S(1)} %bitcast.81, s32[8]{0:T(128)} %bitcast.86), kind=kOutput, calls=%fused_computation.4 | convolution fusion | flops 1310736 | bytes 655392 | tf_op jit(solution)/shard_map/sb,baf->saf/dot_general | solution.py:85
  5.7 0.9 %copy.29 = bf16[8,128,256]{2,1,0:T(8,128)(2,1)} copy(bf16[8,128,256]{2,0,1:T(8,128)(2,1)S(1)} %convolution_convert_fusion.1) | data formatting | bytes 1048576 | tf_op jit(solution)/shard_map/convert_element_type | solution.py:87
  6.6 6.5 %all-to-all-start = ((bf16[8,128,256]{2,1,0:T(8,128)(2,1)}), bf16[8,128,256]{2,1,0:T(8,128)(2,1)S(1)}, u32[]{:S(2)}, u32[]{:S(2)}) async-start(bf16[8,128,256]{2,1,0:T(8,128)(2,1)} %copy.29), calls=%async_computation | async-start | bytes 1048576 | tf_op jit(solution)/shard_map/all_to_all | solution.py:88
  13.1 0.0 copy-done.5
  13.2 0.0 copy-done.6
  13.9 0.0 copy-done.1
  13.9 0.9 %fusion = f32[2,8,128,128]{3,1,2,0:T(8,128)S(1)} fusion(bf16[40,128,128]{2,1,0:T(8,128)(2,1)S(1)} %copy-done.1, pred[40]{0:T(512)(128)(4,1)S(1)} %iota_compare_fusion.9, pred[40,8]{0,1:T(8,128)(4,1)S(1)} %iota_compare_fusion.5, pred[40,2]{0,1:T(4,128)(4,1)S(1)} %iota_compare_fusion.7), kind=kOutput, calls=%fused_computation | convolution fusion | flops 20972800 | bytes 2359736 | tf_op jit(solution)/shard_map/krs,kab->rasb/dot_general | solution.py:98
  14.8 0.2 fusion.5
  15.0 0.8 %copy-done.2 = bf16[12,128,128]{2,1,0:T(8,128)(2,1)S(1)} copy-done((bf16[12,128,128]{2,1,0:T(8,128)(2,1)S(1)}, bf16[12,128,128]{2,1,0:T(8,128)(2,1)}, u32[]{:S(2)}) %copy-start.2) | copy-done | bytes 393240
  15.8 0.4 convolution_convert_fusion.2
  16.2 0.2 copy.63
  16.4 11.3 %all-to-all-done = bf16[8,128,256]{2,1,0:T(8,128)(2,1)S(1)} async-done(((bf16[8,128,256]{2,1,0:T(8,128)(2,1)}), bf16[8,128,256]{2,1,0:T(8,128)(2,1)S(1)}, u32[]{:S(2)}, u32[]{:S(2)}) %all-to-all-start) | async-done | bytes 524320 | tf_op jit(solution)/shard_map/all_to_all | solution.py:88
  27.7 0.4 fusion.6
  28.1 0.0 copy-start.3
  28.1 0.0 copy-start.7
  28.1 0.0 collective-permute-done
  28.1 0.0 collective-permute-done.1
  28.1 0.3 convolution_add_fusion
  28.4 0.4 copy-done.3
  28.8 0.2 copy-done.7
  29.0 0.2 fusion.4
  29.3 1.3 %convolution_convert_fusion = bf16[1024,256]{1,0:T(8,128)(2,1)} fusion(bf16[256,1024]{1,0:T(8,128)(2,1)S(1)} %fusion.5, bf16[256,1024]{1,0:T(8,128)(2,1)S(1)} %bitcast.79, bf16[256,256]{1,0:T(8,128)(2,1)S(1)} %fusion.4), kind=kOutput, calls=%fused_computation.3 | convolution fusion | flops 271319040 | bytes 1703936 | tf_op jit(solution)/shard_map/dot_general | solution.py:126
  30.6 3.6 %all-to-all-start.1 = ((bf16[8,128,256]{2,1,0:T(8,128)(2,1)}), bf16[8,128,256]{2,1,0:T(8,128)(2,1)S(1)}, u32[]{:S(2)}, u32[]{:S(2)}) async-start(bf16[8,128,256]{2,1,0:T(8,128)(2,1)} %bitcast.19), calls=%async_computation.1 | async-start | bytes 1048576 | tf_op jit(solution)/shard_map/all_to_all | solution.py:133
  34.2 0.3 fusion.64
  34.5 0.1 collective-permute-start.2
  34.6 1.7 %collective-permute-start.3 = (bf16[256,256]{1,0:T(8,128)(2,1)S(1)}, bf16[256,256]{1,0:T(8,128)(2,1)S(1)}, u32[]{:S(2)}, u32[]{:S(2)}) collective-permute-start(bf16[256,256]{1,0:T(8,128)(2,1)S(1)} %get-tuple-element.44), channel_id=1, source_target_pairs={{8,0},{16,8},{24,16},{0,24},{9,1},{17,9},{25,17},{1,25},{10,2},{18... | collective-permute-start | bytes 393224 | tf_op jit(solution)/shard_map/ppermute | solution.py:18
  36.3 12.5 %all-to-all-done.1 = bf16[8,128,256]{2,1,0:T(8,128)(2,1)S(1)} async-done(((bf16[8,128,256]{2,1,0:T(8,128)(2,1)}), bf16[8,128,256]{2,1,0:T(8,128)(2,1)S(1)}, u32[]{:S(2)}, u32[]{:S(2)}) %all-to-all-start.1) | async-done | bytes 524320 | tf_op jit(solution)/shard_map/all_to_all | solution.py:133
  48.9 0.0 copy-done.4
  48.9 0.4 fusion.17
  49.3 0.0 collective-permute-done.2
  49.3 0.0 collective-permute-done.3
  49.3 0.1 fusion.32
  49.4 0.2 convolution_bitcast_fusion
  49.6 13.2 %all_to_all.20 = f32[32,8,256]{2,1,0:T(8,128)S(1)} all-to-all(f32[32,8,256]{2,1,0:T(8,128)S(1)} %convolution_bitcast_fusion), channel_id=1, replica_groups=mesh['row'=4,'col'=8] {'row','col'}, dimensions={0} | all-to-all | bytes 524288 | tf_op jit(solution)/shard_map/all_to_all | solution.py:31
  62.9 0.7 broadcast_in_dim.2
  63.5 2.6 %all-to-all-start.3 = ((bf16[32,8,256]{2,1,0:T(8,128)(2,1)}), bf16[32,8,256]{2,1,0:T(8,128)(2,1)S(1)}, u32[]{:S(2)}, u32[]{:S(2)}) async-start(bf16[32,8,256]{2,1,0:T(8,128)(2,1)} %broadcast_in_dim.2), calls=%async_computation.3 | async-start | bytes 262144 | tf_op jit(solution)/shard_map/all_to_all | solution.py:34
  66.1 1.0 %convolution_convert_fusion.5 = bf16[256,256]{1,0:T(8,128)(2,1)} fusion(s32[256]{0:T(256)S(1)} %bitcast.84, f32[256,256]{1,0:T(8,128)S(1)} %convolution_add_fusion), kind=kOutput, calls=%fused_computation.13 | convolution fusion | flops 34013184 | bytes 394240 | tf_op jit(solution)/shard_map/dot_general | solution.py:110
  67.1 1.1 %convolution_convert_fusion.3 = bf16[256,256]{1,0:T(8,128)(2,1)} fusion(bf16[256,256]{1,0:T(8,128)(2,1)S(1)} %fusion.32, bf16[256,256]{1,0:T(8,128)(2,1)S(1)} %copy-done, s32[256]{0:T(256)S(1)} %bitcast.85), kind=kOutput, calls=%fused_computation.11 | convolution fusion | flops 67305472 | bytes 394240 | tf_op jit(solution)/shard_map/dot_general | solution.py:148
  68.2 5.7 %all-to-all-done.3 = bf16[32,8,256]{2,1,0:T(8,128)(2,1)S(1)} async-done(((bf16[32,8,256]{2,1,0:T(8,128)(2,1)}), bf16[32,8,256]{2,1,0:T(8,128)(2,1)S(1)}, u32[]{:S(2)}, u32[]{:S(2)}) %all-to-all-start.3) | async-done | bytes 131104 | tf_op jit(solution)/shard_map/all_to_all | solution.py:34
  73.8 0.7 bitcast_convert_fusion.1
  (14 shorter events, 0.1 us)
Async XLA Ops:
  0.6 1.2 %copy-start = (bf16[256,256]{1,0:T(8,128)(2,1)S(1)}, bf16[256,256]{1,0:T(8,128)(2,1)}, u32[]{:S(2)}) copy-start(bf16[256,256]{1,0:T(8,128)(2,1)} %param.20) | copy-start | bytes 393220
  2.0 26.1 %collective-permute-start = (bf16[256,256]{1,0:T(8,128)(2,1)S(1)}, bf16[256,256]{1,0:T(8,128)(2,1)S(1)}, u32[]{:S(2)}, u32[]{:S(2)}) collective-permute-start(bf16[256,256]{1,0:T(8,128)(2,1)S(1)} %convolution_convert_fusion.6), channel_id=1, source_target_pairs={{0,8},{8,16},{16,24},{24,0},{1,9},{9,17},{17,25},{25,1},{2,10},{10... | collective-permute-start | bytes 393224 | tf_op jit(solution)/shard_map/ppermute | solution.py:16
  2.5 25.6 %collective-permute-start.1 = (bf16[256,256]{1,0:T(8,128)(2,1)S(1)}, bf16[256,256]{1,0:T(8,128)(2,1)S(1)}, u32[]{:S(2)}, u32[]{:S(2)}) collective-permute-start(bf16[256,256]{1,0:T(8,128)(2,1)S(1)} %convolution_convert_fusion.6), channel_id=1, source_target_pairs={{8,0},{16,8},{24,16},{0,24},{9,1},{17,9},{25,17},{1,25},{10,2},{18... | collective-permute-start | bytes 393224 | tf_op jit(solution)/shard_map/ppermute | solution.py:18
  4.6 8.6 %copy-start.5 = (s32[40,2]{0,1:T(2,128)S(1)}, s32[40,2]{0,1:T(2,128)}, u32[]{:S(2)}) copy-start(s32[40,2]{0,1:T(2,128)} %param.25) | copy-start | bytes 964
  4.6 8.6 %copy-start.6 = (s32[12,2]{0,1:T(2,128)S(1)}, s32[12,2]{0,1:T(2,128)}, u32[]{:S(2)}) copy-start(s32[12,2]{0,1:T(2,128)} %param.23) | copy-start | bytes 292
  4.6 9.3 %copy-start.1 = (bf16[40,128,128]{2,1,0:T(8,128)(2,1)S(1)}, bf16[40,128,128]{2,1,0:T(8,128)(2,1)}, u32[]{:S(2)}) copy-start(bf16[40,128,128]{2,1,0:T(8,128)(2,1)} %param.24) | copy-start | bytes 3932164
  6.6 21.1 %all-to-all-start = ((bf16[8,128,256]{2,1,0:T(8,128)(2,1)}), bf16[8,128,256]{2,1,0:T(8,128)(2,1)S(1)}, u32[]{:S(2)}, u32[]{:S(2)}) async-start(bf16[8,128,256]{2,1,0:T(8,128)(2,1)} %copy.29), calls=%async_computation | async-start | bytes 1048576 | tf_op jit(solution)/shard_map/all_to_all | solution.py:88
  14.8 1.0 %copy-start.2 = (bf16[12,128,128]{2,1,0:T(8,128)(2,1)S(1)}, bf16[12,128,128]{2,1,0:T(8,128)(2,1)}, u32[]{:S(2)}) copy-start(bf16[12,128,128]{2,1,0:T(8,128)(2,1)} %param.22) | copy-start | bytes 1179652
  28.1 0.7 copy-start.3
  28.1 0.9 %copy-start.7 = (bf16[256,256]{1,0:T(8,128)(2,1)S(1)}, bf16[256,256]{1,0:T(8,128)(2,1)}, u32[]{:S(2)}) copy-start(bf16[256,256]{1,0:T(8,128)(2,1)} %param.21) | copy-start | bytes 393220
  30.6 18.3 %all-to-all-start.1 = ((bf16[8,128,256]{2,1,0:T(8,128)(2,1)}), bf16[8,128,256]{2,1,0:T(8,128)(2,1)S(1)}, u32[]{:S(2)}, u32[]{:S(2)}) async-start(bf16[8,128,256]{2,1,0:T(8,128)(2,1)} %bitcast.19), calls=%async_computation.1 | async-start | bytes 1048576 | tf_op jit(solution)/shard_map/all_to_all | solution.py:133
  34.2 14.7 %copy-start.4 = (s32[1,8]{1,0:T(1,128)S(1)}, s32[1,8]{1,0:T(1,128)}, u32[]{:S(2)}) copy-start(s32[1,8]{1,0:T(1,128)} %param.27) | copy-start | bytes 100
  34.5 14.8 %collective-permute-start.2 = (bf16[256,256]{1,0:T(8,128)(2,1)S(1)}, bf16[256,256]{1,0:T(8,128)(2,1)S(1)}, u32[]{:S(2)}, u32[]{:S(2)}) collective-permute-start(bf16[256,256]{1,0:T(8,128)(2,1)S(1)} %get-tuple-element.43), channel_id=1, source_target_pairs={{0,8},{8,16},{16,24},{24,0},{1,9},{9,17},{17,25},{25,1},{2,10},{10... | collective-permute-start | bytes 393224 | tf_op jit(solution)/shard_map/ppermute | solution.py:16
  34.6 14.7 %collective-permute-start.3 = (bf16[256,256]{1,0:T(8,128)(2,1)S(1)}, bf16[256,256]{1,0:T(8,128)(2,1)S(1)}, u32[]{:S(2)}, u32[]{:S(2)}) collective-permute-start(bf16[256,256]{1,0:T(8,128)(2,1)S(1)} %get-tuple-element.44), channel_id=1, source_target_pairs={{8,0},{16,8},{24,16},{0,24},{9,1},{17,9},{25,17},{1,25},{10,2},{18... | collective-permute-start | bytes 393224 | tf_op jit(solution)/shard_map/ppermute | solution.py:18
  63.5 10.3 %all-to-all-start.3 = ((bf16[32,8,256]{2,1,0:T(8,128)(2,1)}), bf16[32,8,256]{2,1,0:T(8,128)(2,1)S(1)}, u32[]{:S(2)}, u32[]{:S(2)}) async-start(bf16[32,8,256]{2,1,0:T(8,128)(2,1)} %broadcast_in_dim.2), calls=%async_computation.3 | async-start | bytes 262144 | tf_op jit(solution)/shard_map/all_to_all | solution.py:34

commit v16 on v15

--- a/solution.py
+++ b/solution.py
@@ -77,7 +77,6 @@
         .reshape(row_count, ext_count)
     )
     extended = padded_2(hidden, (("row", 0),), BW)
-    mixed = jnp.dot(band_dense, extended, preferred_element_type=jnp.float32)
     blocks = hidden.reshape(tile_rows, tile_size, width_feat)
     giving = send_lists[0]
     tile_range = jnp.arange(tile_rows, dtype=jnp.int32)
@@ -101,9 +100,9 @@
     dense_high = bound_dense.astype(jnp.bfloat16)
     dense_low = (bound_dense - dense_high.astype(jnp.float32)).astype(jnp.bfloat16)
     arrived_rows = arrived.reshape(peers * tile_size, width_feat)
-    mixed = mixed + jnp.dot(
-        jnp.concatenate([dense_high, dense_low], axis=1),
-        jnp.concatenate([arrived_rows, arrived_rows], axis=0),
+    mixed = jnp.dot(
+        jnp.concatenate([band_dense, dense_high, dense_low], axis=1),
+        jnp.concatenate([extended, arrived_rows, arrived_rows], axis=0),
         preferred_element_type=jnp.float32,
     )
     out_band = jax.nn.silu(mixed).astype(jnp.bfloat16)

time: 75 us -> 77.3 us (1.031)
  local copies, waits for them, and re-layouts: 3.29 us -> 6.14 us
  waiting for transfers between devices: 29.5 us -> 27.6 us
  matrix products: 8.99 us -> 10.1 us
    unnamed x17 -> x22, local copies, waits for them, and re-layouts: 1.68 us -> 3.69 us
    all_to_all x1, waiting for transfers between devices: 11.3 us -> 9.45 us  [on_device(): lax.all_to_all(outgoing, 'col', split_axis=0, concat_axis=0, tiled=True)]
    dot_general x2 -> x1, matrix products: 0.7 us -> 1.93 us  [on_device(): jnp.dot(jnp.concatenate([band_dense, dense_high, dense_low], axis=1), jnp...]
    concatenate x0 -> x1, local copies, waits for them, and re-layouts: none -> 0.85 us  [on_device(): jnp.concatenate([extended, arrived_rows, arrived_rows], axis=0)]
  transfers between devices with their start and end apart: 7 -> 7, of which waited for: 3 -> 3; matrix products, arithmetic and copies ran while one was open for 9% -> 11% of each run, Pallas kernels for 0% -> 0%
where the time goes in v16:
time: 77.3 us; the launch traced here: 76.9 us
  waiting for transfers between devices  27.6 us (36%)
  starting transfers between devices  17.2 us (22%)
  blocking collectives  13.2 us (17%)
  matrix products  10.1 us (13%)
  local copies, waits for them, and re-layouts  6.14 us (8%)
  between operations  1.57 us (2%)
  other arithmetic  1.02 us (1%)
    all_to_all x1, blocking collectives, spread_sum(): gathered = lax.all_to_all(value.reshape(piece), axes, 0, 0, tiled=True)  13.2 us
    all_to_all x1, waiting for transfers between devices, on_device(): lax.all_to_all(to_owner, 'col', split_axis=0, concat_axis=0, tiled=True)  12.5 us
    all_to_all x1, waiting for transfers between devices, on_device(): lax.all_to_all(outgoing, 'col', split_axis=0, concat_axis=0, tiled=True)  9.45 us
    all_to_all x1, starting transfers between devices, on_device(): lax.all_to_all(outgoing, 'col', split_axis=0, concat_axis=0, tiled=True)  6.53 us
    all_to_all x1, waiting for transfers between devices, spread_sum(): spread = lax.all_to_all(copies, axes, 0, 0, tiled=True)  5.66 us
    all_to_all x1, starting transfers between devices, on_device(): lax.all_to_all(to_owner, 'col', split_axis=0, concat_axis=0, tiled=True)  3.77 us
    ppermute x2, starting transfers between devices, padded_2(): lax.ppermute(head, axis, [((i + 1) % count, i) for i in range(count)])  3.75 us
    unnamed x22, local copies, waits for them, and re-layouts  3.69 us
  transfers between devices with their start and end apart: 7, of which 3 were waited for; matrix products, arithmetic and copies ran while one was open for 11% of the time, Pallas kernels for 0%

profile of v16, /device:TPU:0, one launch (start us, length us, event | category | flops | bytes accessed | tf_op | source)
XLA Modules:
  0.0 76.9 jit_solution(13756155246022745655)
XLA Ops:
  0.6 0.0 copy-start
  0.6 1.2 %convolution_convert_fusion.7 = bf16[256,256]{1,0:T(8,128)(2,1)S(1)} fusion(bf16[256,256]{1,0:T(8,128)(2,1)} %param.19, s32[256]{0:T(256)} %bitcast.82), kind=kOutput, calls=%fused_computation.20 | convolution fusion | flops 33685504 | bytes 263168 | tf_op jit(solution)/shard_map/dot_general | solution.py:64
  1.8 0.0 copy-done
  1.8 0.2 convolution_convert_fusion.6
  2.0 0.0 copy-start.5
  2.0 0.0 copy-start.6
  2.1 0.0 copy-start.1
  2.1 0.5 collective-permute-start
  2.6 2.0 %collective-permute-start.1 = (bf16[256,256]{1,0:T(8,128)(2,1)S(1)}, bf16[256,256]{1,0:T(8,128)(2,1)S(1)}, u32[]{:S(2)}, u32[]{:S(2)}) collective-permute-start(bf16[256,256]{1,0:T(8,128)(2,1)S(1)} %convolution_convert_fusion.6), channel_id=1, source_target_pairs={{8,0},{16,8},{24,16},{0,24},{9,1},{17,9},{25,17},{1,25},{10,2},{18... | collective-permute-start | bytes 393224 | tf_op jit(solution)/shard_map/ppermute | solution.py:18
  4.6 1.0 %convolution_convert_fusion.1 = bf16[8,128,256]{2,0,1:T(8,128)(2,1)S(1)} fusion(bf16[2,128,256]{2,1,0:T(8,128)(2,1)S(1)} %bitcast.79, s32[8]{0:T(128)} %bitcast.86), kind=kOutput, calls=%fused_computation.10 | convolution fusion | flops 1310736 | bytes 655392 | tf_op jit(solution)/shard_map/sb,baf->saf/dot_general | solution.py:84
  5.6 0.9 %copy.31 = bf16[8,128,256]{2,1,0:T(8,128)(2,1)} copy(bf16[8,128,256]{2,0,1:T(8,128)(2,1)S(1)} %convolution_convert_fusion.1) | data formatting | bytes 1048576 | tf_op jit(solution)/shard_map/convert_element_type | solution.py:86
  6.5 6.5 %all-to-all-start = ((bf16[8,128,256]{2,1,0:T(8,128)(2,1)}), bf16[8,128,256]{2,1,0:T(8,128)(2,1)S(1)}, u32[]{:S(2)}, u32[]{:S(2)}) async-start(bf16[8,128,256]{2,1,0:T(8,128)(2,1)} %copy.31), calls=%async_computation | async-start | bytes 1048576 | tf_op jit(solution)/shard_map/all_to_all | solution.py:87
  13.0 0.0 copy-done.5
  13.8 0.9 %fusion.6 = f32[2,8,128,128]{3,1,2,0:T(8,128)S(1)} fusion(bf16[40,128,128]{2,1,0:T(8,128)(2,1)S(1)} %copy-done.1, pred[40]{0:T(512)(128)(4,1)S(1)} %iota_compare_fusion.9, pred[40,8]{0,1:T(8,128)(4,1)S(1)} %iota_compare_fusion.5, pred[40,2]{0,1:T(4,128)(4,1)S(1)} %iota_compare_fusion.7), kind=kOutput, calls=%fused_computation.6 | convolution fusion | flops 20972800 | bytes 2359736 | tf_op jit(solution)/shard_map/krs,kab->rasb/dot_general | solution.py:97
  14.7 0.0 copy-start.2
  14.7 0.2 copy.56
  15.0 0.2 fusion.11
  15.1 0.6 copy-done.2
  15.7 0.4 convolution_convert_fusion.2
  16.1 0.1 copy.57
  16.1 0.0 collective-permute-done
  16.2 0.7 constant_dynamic-update-slice_fusion.4
  16.8 0.7 constant_dynamic-update-slice_fusion.3
  17.5 0.0 collective-permute-done.1
  17.5 0.6 constant_dynamic-update-slice_fusion.2
  18.1 9.4 %all-to-all-done = bf16[8,128,256]{2,1,0:T(8,128)(2,1)S(1)} async-done(((bf16[8,128,256]{2,1,0:T(8,128)(2,1)}), bf16[8,128,256]{2,1,0:T(8,128)(2,1)S(1)}, u32[]{:S(2)}, u32[]{:S(2)}) %all-to-all-start) | async-done | bytes 524320 | tf_op jit(solution)/shard_map/all_to_all | solution.py:87
  27.6 0.8 %constant_dynamic-update-slice_fusion.1 = bf16[2816,256]{1,0:T(8,128)(2,1)} fusion(bf16[2816,256]{1,0:T(8,128)(2,1)} %constant_dynamic-update-slice_fusion.2, bf16[1024,256]{1,0:T(8,128)(2,1)S(1)} %bitcast.74), kind=kLoop, calls=%fused_computation.49 | loop fusion | bytes 1048576
  28.4 0.9 %constant_dynamic-update-slice_fusion = bf16[2816,256]{1,0:T(8,128)(2,1)} fusion(bf16[2816,256]{1,0:T(8,128)(2,1)} %constant_dynamic-update-slice_fusion.1, bf16[1024,256]{1,0:T(8,128)(2,1)S(1)} %bitcast.75), kind=kLoop, calls=%fused_computation.48 | loop fusion | bytes 1048576 | tf_op jit(solution)/shard_map/concatenate | solution.py:105
  29.2 1.9 %fusion = f32[256,256]{1,0:T(8,128)S(1)} fusion(bf16[2816,256]{1,0:T(8,128)(2,1)} %constant_dynamic-update-slice_fusion, bf16[256,1024]{1,0:T(8,128)(2,1)S(1)} %fusion.11, bf16[256,1024]{1,0:T(8,128)(2,1)S(1)} %bitcast.80, bf16[256,768]{1,0:T(8,128)(2,1)S(1)} %bitcast.77), kind=kOutput, calls=%fused_computation | convolution fusion | flops 373424128 | bytes 3145728 | tf_op jit(solution)/shard_map/dot_general | solution.py:103
  31.2 0.2 fusion.10
  31.5 1.3 %convolution_convert_fusion = bf16[1024,256]{1,0:T(8,128)(2,1)} fusion(bf16[256,1024]{1,0:T(8,128)(2,1)S(1)} %fusion.11, bf16[256,1024]{1,0:T(8,128)(2,1)S(1)} %bitcast.81, bf16[256,256]{1,0:T(8,128)(2,1)S(1)} %fusion.10), kind=kOutput, calls=%fused_computation.9 | convolution fusion | flops 271319040 | bytes 1703936 | tf_op jit(solution)/shard_map/dot_general | solution.py:125
  32.7 3.8 %all-to-all-start.1 = ((bf16[8,128,256]{2,1,0:T(8,128)(2,1)}), bf16[8,128,256]{2,1,0:T(8,128)(2,1)S(1)}, u32[]{:S(2)}, u32[]{:S(2)}) async-start(bf16[8,128,256]{2,1,0:T(8,128)(2,1)} %bitcast.19), calls=%async_computation.1 | async-start | bytes 1048576 | tf_op jit(solution)/shard_map/all_to_all | solution.py:132
  36.5 0.3 fusion.52
  36.9 0.1 collective-permute-start.2
  36.9 1.7 %collective-permute-start.3 = (bf16[256,256]{1,0:T(8,128)(2,1)S(1)}, bf16[256,256]{1,0:T(8,128)(2,1)S(1)}, u32[]{:S(2)}, u32[]{:S(2)}) collective-permute-start(bf16[256,256]{1,0:T(8,128)(2,1)S(1)} %get-tuple-element.44), channel_id=1, source_target_pairs={{8,0},{16,8},{24,16},{0,24},{9,1},{17,9},{25,17},{1,25},{10,2},{18... | collective-permute-start | bytes 393224 | tf_op jit(solution)/shard_map/ppermute | solution.py:18
  38.7 12.5 %all-to-all-done.1 = bf16[8,128,256]{2,1,0:T(8,128)(2,1)S(1)} async-done(((bf16[8,128,256]{2,1,0:T(8,128)(2,1)}), bf16[8,128,256]{2,1,0:T(8,128)(2,1)S(1)}, u32[]{:S(2)}, u32[]{:S(2)}) %all-to-all-start.1) | async-done | bytes 524320 | tf_op jit(solution)/shard_map/all_to_all | solution.py:132
  51.2 0.4 fusion.16
  51.6 0.0 collective-permute-done.2
  51.6 0.0 collective-permute-done.3
  51.6 0.1 fusion.21
  51.7 0.2 convolution_bitcast_fusion
  51.9 13.2 %all_to_all.20 = f32[32,8,256]{2,1,0:T(8,128)S(1)} all-to-all(f32[32,8,256]{2,1,0:T(8,128)S(1)} %convolution_bitcast_fusion), channel_id=1, replica_groups=mesh['row'=4,'col'=8] {'row','col'}, dimensions={0} | all-to-all | bytes 524288 | tf_op jit(solution)/shard_map/all_to_all | solution.py:31
  65.2 0.7 broadcast_in_dim.2
  65.8 2.6 %all-to-all-start.3 = ((bf16[32,8,256]{2,1,0:T(8,128)(2,1)}), bf16[32,8,256]{2,1,0:T(8,128)(2,1)S(1)}, u32[]{:S(2)}, u32[]{:S(2)}) async-start(bf16[32,8,256]{2,1,0:T(8,128)(2,1)} %broadcast_in_dim.2), calls=%async_computation.3 | async-start | bytes 262144 | tf_op jit(solution)/shard_map/all_to_all | solution.py:34
  68.4 1.0 %convolution_convert_fusion.5 = bf16[256,256]{1,0:T(8,128)(2,1)} fusion(s32[256]{0:T(256)S(1)} %bitcast.84, f32[256,256]{1,0:T(8,128)S(1)} %fusion), kind=kOutput, calls=%fused_computation.18 | convolution fusion | flops 34013184 | bytes 394240 | tf_op jit(solution)/shard_map/dot_general | solution.py:109
  69.4 1.1 %convolution_convert_fusion.3 = bf16[256,256]{1,0:T(8,128)(2,1)} fusion(bf16[256,256]{1,0:T(8,128)(2,1)S(1)} %fusion.21, bf16[256,256]{1,0:T(8,128)(2,1)S(1)} %copy-done, s32[256]{0:T(256)S(1)} %bitcast.85), kind=kOutput, calls=%fused_computation.16 | convolution fusion | flops 67305472 | bytes 394240 | tf_op jit(solution)/shard_map/dot_general | solution.py:147
  70.5 5.7 %all-to-all-done.3 = bf16[32,8,256]{2,1,0:T(8,128)(2,1)S(1)} async-done(((bf16[32,8,256]{2,1,0:T(8,128)(2,1)}), bf16[32,8,256]{2,1,0:T(8,128)(2,1)S(1)}, u32[]{:S(2)}, u32[]{:S(2)}) %all-to-all-start.3) | async-done | bytes 131104 | tf_op jit(solution)/shard_map/all_to_all | solution.py:34
  76.1 0.7 bitcast_convert_fusion.1
  (19 shorter events, 0.1 us)
Async XLA Ops:
  0.6 1.2 %copy-start = (bf16[256,256]{1,0:T(8,128)(2,1)S(1)}, bf16[256,256]{1,0:T(8,128)(2,1)}, u32[]{:S(2)}) copy-start(bf16[256,256]{1,0:T(8,128)(2,1)} %param.20) | copy-start | bytes 393220
  2.0 11.0 %copy-start.5 = (s32[40,2]{0,1:T(2,128)S(1)}, s32[40,2]{0,1:T(2,128)}, u32[]{:S(2)}) copy-start(s32[40,2]{0,1:T(2,128)} %param.25) | copy-start | bytes 964
  2.0 11.7 %copy-start.6 = (s32[12,2]{0,1:T(2,128)S(1)}, s32[12,2]{0,1:T(2,128)}, u32[]{:S(2)}) copy-start(s32[12,2]{0,1:T(2,128)} %param.23) | copy-start | bytes 292
  2.1 11.7 %copy-start.1 = (bf16[40,128,128]{2,1,0:T(8,128)(2,1)S(1)}, bf16[40,128,128]{2,1,0:T(8,128)(2,1)}, u32[]{:S(2)}) copy-start(bf16[40,128,128]{2,1,0:T(8,128)(2,1)} %param.24) | copy-start | bytes 3932164
  2.1 14.1 %collective-permute-start = (bf16[256,256]{1,0:T(8,128)(2,1)S(1)}, bf16[256,256]{1,0:T(8,128)(2,1)S(1)}, u32[]{:S(2)}, u32[]{:S(2)}) collective-permute-start(bf16[256,256]{1,0:T(8,128)(2,1)S(1)} %convolution_convert_fusion.6), channel_id=1, source_target_pairs={{0,8},{8,16},{16,24},{24,0},{1,9},{9,17},{17,25},{25,1},{2,10},{10... | collective-permute-start | bytes 393224 | tf_op jit(solution)/shard_map/ppermute | solution.py:16
  2.6 14.9 %collective-permute-start.1 = (bf16[256,256]{1,0:T(8,128)(2,1)S(1)}, bf16[256,256]{1,0:T(8,128)(2,1)S(1)}, u32[]{:S(2)}, u32[]{:S(2)}) collective-permute-start(bf16[256,256]{1,0:T(8,128)(2,1)S(1)} %convolution_convert_fusion.6), channel_id=1, source_target_pairs={{8,0},{16,8},{24,16},{0,24},{9,1},{17,9},{25,17},{1,25},{10,2},{18... | collective-permute-start | bytes 393224 | tf_op jit(solution)/shard_map/ppermute | solution.py:18
  6.5 21.1 %all-to-all-start = ((bf16[8,128,256]{2,1,0:T(8,128)(2,1)}), bf16[8,128,256]{2,1,0:T(8,128)(2,1)S(1)}, u32[]{:S(2)}, u32[]{:S(2)}) async-start(bf16[8,128,256]{2,1,0:T(8,128)(2,1)} %copy.31), calls=%async_computation | async-start | bytes 1048576 | tf_op jit(solution)/shard_map/all_to_all | solution.py:87
  14.7 1.0 %copy-start.2 = (bf16[12,128,128]{2,1,0:T(8,128)(2,1)S(1)}, bf16[12,128,128]{2,1,0:T(8,128)(2,1)}, u32[]{:S(2)}) copy-start(bf16[12,128,128]{2,1,0:T(8,128)(2,1)} %param.22) | copy-start | bytes 1179652
  29.2 1.9 %copy-start.3 = (s32[1,256]{1,0:T(1,128)S(1)}, s32[1,256]{1,0:T(1,128)}, u32[]{:S(2)}) copy-start(s32[1,256]{1,0:T(1,128)} %param.28) | copy-start | bytes 3076
  29.2 2.0 %copy-start.7 = (bf16[256,256]{1,0:T(8,128)(2,1)S(1)}, bf16[256,256]{1,0:T(8,128)(2,1)}, u32[]{:S(2)}) copy-start(bf16[256,256]{1,0:T(8,128)(2,1)} %param.21) | copy-start | bytes 393220
  32.7 18.4 %copy-start.4 = (s32[1,8]{1,0:T(1,128)S(1)}, s32[1,8]{1,0:T(1,128)}, u32[]{:S(2)}) copy-start(s32[1,8]{1,0:T(1,128)} %param.27) | copy-start | bytes 100
  32.7 18.4 %all-to-all-start.1 = ((bf16[8,128,256]{2,1,0:T(8,128)(2,1)}), bf16[8,128,256]{2,1,0:T(8,128)(2,1)S(1)}, u32[]{:S(2)}, u32[]{:S(2)}) async-start(bf16[8,128,256]{2,1,0:T(8,128)(2,1)} %bitcast.19), calls=%async_computation.1 | async-start | bytes 1048576 | tf_op jit(solution)/shard_map/all_to_all | solution.py:132
  36.9 14.8 %collective-permute-start.2 = (bf16[256,256]{1,0:T(8,128)(2,1)S(1)}, bf16[256,256]{1,0:T(8,128)(2,1)S(1)}, u32[]{:S(2)}, u32[]{:S(2)}) collective-permute-start(bf16[256,256]{1,0:T(8,128)(2,1)S(1)} %get-tuple-element.43), channel_id=1, source_target_pairs={{0,8},{8,16},{16,24},{24,0},{1,9},{9,17},{17,25},{25,1},{2,10},{10... | collective-permute-start | bytes 393224 | tf_op jit(solution)/shard_map/ppermute | solution.py:16
  36.9 14.7 %collective-permute-start.3 = (bf16[256,256]{1,0:T(8,128)(2,1)S(1)}, bf16[256,256]{1,0:T(8,128)(2,1)S(1)}, u32[]{:S(2)}, u32[]{:S(2)}) collective-permute-start(bf16[256,256]{1,0:T(8,128)(2,1)S(1)} %get-tuple-element.44), channel_id=1, source_target_pairs={{8,0},{16,8},{24,16},{0,24},{9,1},{17,9},{25,17},{1,25},{10,2},{18... | collective-permute-start | bytes 393224 | tf_op jit(solution)/shard_map/ppermute | solution.py:18
  65.8 10.3 %all-to-all-start.3 = ((bf16[32,8,256]{2,1,0:T(8,128)(2,1)}), bf16[32,8,256]{2,1,0:T(8,128)(2,1)S(1)}, u32[]{:S(2)}, u32[]{:S(2)}) async-start(bf16[32,8,256]{2,1,0:T(8,128)(2,1)} %broadcast_in_dim.2), calls=%async_computation.3 | async-start | bytes 262144 | tf_op jit(solution)/shard_map/all_to_all | solution.py:34

commit v17 on v15

--- a/solution.py
+++ b/solution.py
@@ -77,7 +77,7 @@
         .reshape(row_count, ext_count)
     )
     extended = padded_2(hidden, (("row", 0),), BW)
-    mixed = jnp.dot(band_dense, extended, preferred_element_type=jnp.float32)
+    band_mixed = jnp.dot(band_dense, extended, preferred_element_type=jnp.float32)
     blocks = hidden.reshape(tile_rows, tile_size, width_feat)
     giving = send_lists[0]
     tile_range = jnp.arange(tile_rows, dtype=jnp.int32)
@@ -100,8 +100,9 @@
     ).reshape(row_count, peers * tile_size)
     dense_high = bound_dense.astype(jnp.bfloat16)
     dense_low = (bound_dense - dense_high.astype(jnp.float32)).astype(jnp.bfloat16)
+    band_mixed, arrived = lax.optimization_barrier((band_mixed, arrived))
     arrived_rows = arrived.reshape(peers * tile_size, width_feat)
-    mixed = mixed + jnp.dot(
+    mixed = band_mixed + jnp.dot(
         jnp.concatenate([dense_high, dense_low], axis=1),
         jnp.concatenate([arrived_rows, arrived_rows], axis=0),
         preferred_element_type=jnp.float32,

time: 75 us -> 75.6 us (level)
  blocking collectives: 13.2 us -> 14.1 us
  starting transfers between devices: 17.1 us -> 16.3 us
  waiting for transfers between devices: 29.5 us -> 30.3 us
    all_to_all x1, blocking collectives: 13.2 us -> 14.1 us  [spread_sum(): gathered = lax.all_to_all(value.reshape(piece), axes, 0, 0, tiled=True)]
    all_to_all x1, waiting for transfers between devices: 11.3 us -> 12.1 us  [on_device(): lax.all_to_all(outgoing, 'col', split_axis=0, concat_axis=0, tiled=True)]
where the time goes in v17:
time: 75.6 us; the launch traced here: 75.1 us
  waiting for transfers between devices  30.3 us (40%)
  starting transfers between devices  16.3 us (22%)
  blocking collectives  14.1 us (19%)
  matrix products  9.01 us (12%)
  local copies, waits for them, and re-layouts  2.9 us (4%)
  between operations  1.55 us (2%)
  other arithmetic  1.02 us (1%)
    all_to_all x1, blocking collectives, spread_sum(): gathered = lax.all_to_all(value.reshape(piece), axes, 0, 0, tiled=True)  14.1 us
    all_to_all x1, waiting for transfers between devices, on_device(): lax.all_to_all(to_owner, 'col', split_axis=0, concat_axis=0, tiled=True)  12.6 us
    all_to_all x1, waiting for transfers between devices, on_device(): lax.all_to_all(outgoing, 'col', split_axis=0, concat_axis=0, tiled=True)  12.1 us
    all_to_all x1, starting transfers between devices, on_device(): lax.all_to_all(outgoing, 'col', split_axis=0, concat_axis=0, tiled=True)  5.8 us
    all_to_all x1, waiting for transfers between devices, spread_sum(): spread = lax.all_to_all(copies, axes, 0, 0, tiled=True)  5.66 us
    ppermute x2, starting transfers between devices, padded_2(): lax.ppermute(head, axis, [((i + 1) % count, i) for i in range(count)])  4.19 us
    all_to_all x1, starting transfers between devices, on_device(): lax.all_to_all(to_owner, 'col', split_axis=0, concat_axis=0, tiled=True)  3.64 us
    all_to_all x1, starting transfers between devices, spread_sum(): spread = lax.all_to_all(copies, axes, 0, 0, tiled=True)  2.58 us
  transfers between devices with their start and end apart: 7, of which 3 were waited for; matrix products, arithmetic and copies ran while one was open for 9% of the time, Pallas kernels for 0%

profile of v17, /device:TPU:0, one launch (start us, length us, event | category | flops | bytes accessed | tf_op | source)
XLA Modules:
  0.0 75.1 jit_solution(3925074972130065818)
XLA Ops:
  0.6 0.0 copy-start
  0.6 1.2 %convolution_convert_fusion.7 = bf16[256,256]{1,0:T(8,128)(2,1)S(1)} fusion(bf16[256,256]{1,0:T(8,128)(2,1)} %param.19, s32[256]{0:T(256)} %bitcast.82), kind=kOutput, calls=%fused_computation.15 | convolution fusion | flops 33685504 | bytes 263168 | tf_op jit(solution)/shard_map/dot_general | solution.py:64
  1.8 0.0 copy-done
  1.8 0.2 convolution_convert_fusion.6
  2.0 2.5 %collective-permute-start.1 = (bf16[256,256]{1,0:T(8,128)(2,1)S(1)}, bf16[256,256]{1,0:T(8,128)(2,1)S(1)}, u32[]{:S(2)}, u32[]{:S(2)}) collective-permute-start(bf16[256,256]{1,0:T(8,128)(2,1)S(1)} %convolution_convert_fusion.6), channel_id=1, source_target_pairs={{8,0},{16,8},{24,16},{0,24},{9,1},{17,9},{25,17},{1,25},{10,2},{18... | collective-permute-start | bytes 393224 | tf_op jit(solution)/shard_map/ppermute | solution.py:18
  4.5 0.0 collective-permute-start
  4.5 0.0 copy-start.5
  4.5 0.0 copy-start.6
  4.5 0.0 copy-start.1
  4.5 1.1 %convolution_convert_fusion.1 = bf16[8,128,256]{2,0,1:T(8,128)(2,1)S(1)} fusion(bf16[2,128,256]{2,1,0:T(8,128)(2,1)S(1)} %bitcast.81, s32[8]{0:T(128)} %bitcast.86), kind=kOutput, calls=%fused_computation.4 | convolution fusion | flops 1310736 | bytes 655392 | tf_op jit(solution)/shard_map/sb,baf->saf/dot_general | solution.py:85
  5.6 0.9 %copy.28 = bf16[8,128,256]{2,1,0:T(8,128)(2,1)} copy(bf16[8,128,256]{2,0,1:T(8,128)(2,1)S(1)} %convolution_convert_fusion.1) | data formatting | bytes 1048576 | tf_op jit(solution)/shard_map/convert_element_type | solution.py:87
  6.5 5.8 %all-to-all-start = ((bf16[8,128,256]{2,1,0:T(8,128)(2,1)}), bf16[8,128,256]{2,1,0:T(8,128)(2,1)S(1)}, u32[]{:S(2)}, u32[]{:S(2)}) async-start(bf16[8,128,256]{2,1,0:T(8,128)(2,1)} %copy.28), calls=%async_computation | async-start | bytes 1048576 | tf_op jit(solution)/shard_map/all_to_all | solution.py:88
  13.0 0.0 copy-done.5
  13.0 0.0 copy-done.6
  13.1 0.0 copy-done.1
  13.1 0.9 %fusion = f32[2,8,128,128]{3,1,2,0:T(8,128)S(1)} fusion(bf16[40,128,128]{2,1,0:T(8,128)(2,1)S(1)} %copy-done.1, pred[40]{0:T(512)(128)(4,1)S(1)} %iota_compare_fusion.9, pred[40,8]{0,1:T(8,128)(4,1)S(1)} %iota_compare_fusion.5, pred[40,2]{0,1:T(4,128)(4,1)S(1)} %iota_compare_fusion.7), kind=kOutput, calls=%fused_computation | convolution fusion | flops 20972800 | bytes 2359736 | tf_op jit(solution)/shard_map/krs,kab->rasb/dot_general | solution.py:98
  14.0 0.0 copy-start.2
  14.0 0.2 copy.63
  14.3 0.2 fusion.5
  14.4 0.6 copy-done.2
  15.0 0.4 convolution_convert_fusion.2
  15.4 0.0 collective-permute-done.1
  15.4 0.0 collective-permute-done
  15.4 0.3 fusion.19
  15.7 12.1 %all-to-all-done = bf16[8,128,256]{2,1,0:T(8,128)(2,1)S(1)} async-done(((bf16[8,128,256]{2,1,0:T(8,128)(2,1)}), bf16[8,128,256]{2,1,0:T(8,128)(2,1)S(1)}, u32[]{:S(2)}, u32[]{:S(2)}) %all-to-all-start) | async-done | bytes 524320 | tf_op jit(solution)/shard_map/all_to_all | solution.py:88
  27.8 0.5 convolution_add_fusion
  28.2 0.2 copy-done.3
  28.4 0.2 copy-done.7
  28.7 0.2 fusion.4
  28.9 1.3 %convolution_convert_fusion = bf16[1024,256]{1,0:T(8,128)(2,1)} fusion(bf16[256,1024]{1,0:T(8,128)(2,1)S(1)} %fusion.5, bf16[256,1024]{1,0:T(8,128)(2,1)S(1)} %bitcast.79, bf16[256,256]{1,0:T(8,128)(2,1)S(1)} %fusion.4), kind=kOutput, calls=%fused_computation.3 | convolution fusion | flops 271319040 | bytes 1703936 | tf_op jit(solution)/shard_map/dot_general | solution.py:127
  30.2 3.6 %all-to-all-start.1 = ((bf16[8,128,256]{2,1,0:T(8,128)(2,1)}), bf16[8,128,256]{2,1,0:T(8,128)(2,1)S(1)}, u32[]{:S(2)}, u32[]{:S(2)}) async-start(bf16[8,128,256]{2,1,0:T(8,128)(2,1)} %bitcast.19), calls=%async_computation.1 | async-start | bytes 1048576 | tf_op jit(solution)/shard_map/all_to_all | solution.py:134
  33.9 0.3 fusion.64
  34.2 0.1 collective-permute-start.2
  34.3 1.7 %collective-permute-start.3 = (bf16[256,256]{1,0:T(8,128)(2,1)S(1)}, bf16[256,256]{1,0:T(8,128)(2,1)S(1)}, u32[]{:S(2)}, u32[]{:S(2)}) collective-permute-start(bf16[256,256]{1,0:T(8,128)(2,1)S(1)} %get-tuple-element.48), channel_id=1, source_target_pairs={{8,0},{16,8},{24,16},{0,24},{9,1},{17,9},{25,17},{1,25},{10,2},{18... | collective-permute-start | bytes 393224 | tf_op jit(solution)/shard_map/ppermute | solution.py:18
  36.0 12.6 %all-to-all-done.1 = bf16[8,128,256]{2,1,0:T(8,128)(2,1)S(1)} async-done(((bf16[8,128,256]{2,1,0:T(8,128)(2,1)}), bf16[8,128,256]{2,1,0:T(8,128)(2,1)S(1)}, u32[]{:S(2)}, u32[]{:S(2)}) %all-to-all-start.1) | async-done | bytes 524320 | tf_op jit(solution)/shard_map/all_to_all | solution.py:134
  48.6 0.0 copy-done.4
  48.6 0.4 fusion.16
  49.0 0.0 collective-permute-done.2
  49.0 0.0 collective-permute-done.3
  49.0 0.1 fusion.32
  49.1 0.2 convolution_bitcast_fusion
  49.3 14.1 %all_to_all.20 = f32[32,8,256]{2,1,0:T(8,128)S(1)} all-to-all(f32[32,8,256]{2,1,0:T(8,128)S(1)} %convolution_bitcast_fusion), channel_id=1, replica_groups=mesh['row'=4,'col'=8] {'row','col'}, dimensions={0} | all-to-all | bytes 524288 | tf_op jit(solution)/shard_map/all_to_all | solution.py:31
  63.4 0.7 broadcast_in_dim.2
  64.1 2.6 %all-to-all-start.3 = ((bf16[32,8,256]{2,1,0:T(8,128)(2,1)}), bf16[32,8,256]{2,1,0:T(8,128)(2,1)S(1)}, u32[]{:S(2)}, u32[]{:S(2)}) async-start(bf16[32,8,256]{2,1,0:T(8,128)(2,1)} %broadcast_in_dim.2), calls=%async_computation.3 | async-start | bytes 262144 | tf_op jit(solution)/shard_map/all_to_all | solution.py:34
  66.7 1.0 %convolution_convert_fusion.5 = bf16[256,256]{1,0:T(8,128)(2,1)} fusion(s32[256]{0:T(256)S(1)} %bitcast.84, f32[256,256]{1,0:T(8,128)S(1)} %convolution_add_fusion), kind=kOutput, calls=%fused_computation.13 | convolution fusion | flops 34013184 | bytes 394240 | tf_op jit(solution)/shard_map/dot_general | solution.py:111
  67.7 1.1 %convolution_convert_fusion.3 = bf16[256,256]{1,0:T(8,128)(2,1)} fusion(bf16[256,256]{1,0:T(8,128)(2,1)S(1)} %fusion.32, bf16[256,256]{1,0:T(8,128)(2,1)S(1)} %copy-done, s32[256]{0:T(256)S(1)} %bitcast.85), kind=kOutput, calls=%fused_computation.11 | convolution fusion | flops 67305472 | bytes 394240 | tf_op jit(solution)/shard_map/dot_general | solution.py:149
  68.7 5.7 %all-to-all-done.3 = bf16[32,8,256]{2,1,0:T(8,128)(2,1)S(1)} async-done(((bf16[32,8,256]{2,1,0:T(8,128)(2,1)}), bf16[32,8,256]{2,1,0:T(8,128)(2,1)S(1)}, u32[]{:S(2)}, u32[]{:S(2)}) %all-to-all-start.3) | async-done | bytes 131104 | tf_op jit(solution)/shard_map/all_to_all | solution.py:34
  74.4 0.7 bitcast_convert_fusion.1
  (14 shorter events, 0.1 us)
Async XLA Ops:
  0.6 1.2 %copy-start = (bf16[256,256]{1,0:T(8,128)(2,1)S(1)}, bf16[256,256]{1,0:T(8,128)(2,1)}, u32[]{:S(2)}) copy-start(bf16[256,256]{1,0:T(8,128)(2,1)} %param.20) | copy-start | bytes 393220
  2.0 13.3 %collective-permute-start.1 = (bf16[256,256]{1,0:T(8,128)(2,1)S(1)}, bf16[256,256]{1,0:T(8,128)(2,1)S(1)}, u32[]{:S(2)}, u32[]{:S(2)}) collective-permute-start(bf16[256,256]{1,0:T(8,128)(2,1)S(1)} %convolution_convert_fusion.6), channel_id=1, source_target_pairs={{8,0},{16,8},{24,16},{0,24},{9,1},{17,9},{25,17},{1,25},{10,2},{18... | collective-permute-start | bytes 393224 | tf_op jit(solution)/shard_map/ppermute | solution.py:18
  4.5 10.9 %collective-permute-start = (bf16[256,256]{1,0:T(8,128)(2,1)S(1)}, bf16[256,256]{1,0:T(8,128)(2,1)S(1)}, u32[]{:S(2)}, u32[]{:S(2)}) collective-permute-start(bf16[256,256]{1,0:T(8,128)(2,1)S(1)} %convolution_convert_fusion.6), channel_id=1, source_target_pairs={{0,8},{8,16},{16,24},{24,0},{1,9},{9,17},{17,25},{25,1},{2,10},{10... | collective-permute-start | bytes 393224 | tf_op jit(solution)/shard_map/ppermute | solution.py:16
  4.5 8.5 %copy-start.5 = (s32[12,2]{0,1:T(2,128)S(1)}, s32[12,2]{0,1:T(2,128)}, u32[]{:S(2)}) copy-start(s32[12,2]{0,1:T(2,128)} %param.23) | copy-start | bytes 292
  4.5 8.5 %copy-start.6 = (s32[40,2]{0,1:T(2,128)S(1)}, s32[40,2]{0,1:T(2,128)}, u32[]{:S(2)}) copy-start(s32[40,2]{0,1:T(2,128)} %param.25) | copy-start | bytes 964
  4.5 8.6 %copy-start.1 = (bf16[40,128,128]{2,1,0:T(8,128)(2,1)S(1)}, bf16[40,128,128]{2,1,0:T(8,128)(2,1)}, u32[]{:S(2)}) copy-start(bf16[40,128,128]{2,1,0:T(8,128)(2,1)} %param.24) | copy-start | bytes 3932164
  6.5 21.2 %all-to-all-start = ((bf16[8,128,256]{2,1,0:T(8,128)(2,1)}), bf16[8,128,256]{2,1,0:T(8,128)(2,1)S(1)}, u32[]{:S(2)}, u32[]{:S(2)}) async-start(bf16[8,128,256]{2,1,0:T(8,128)(2,1)} %copy.28), calls=%async_computation | async-start | bytes 1048576 | tf_op jit(solution)/shard_map/all_to_all | solution.py:88
  14.0 1.0 %copy-start.2 = (bf16[12,128,128]{2,1,0:T(8,128)(2,1)S(1)}, bf16[12,128,128]{2,1,0:T(8,128)(2,1)}, u32[]{:S(2)}) copy-start(bf16[12,128,128]{2,1,0:T(8,128)(2,1)} %param.22) | copy-start | bytes 1179652
  27.8 0.7 copy-start.3
  27.8 0.9 %copy-start.7 = (bf16[256,256]{1,0:T(8,128)(2,1)S(1)}, bf16[256,256]{1,0:T(8,128)(2,1)}, u32[]{:S(2)}) copy-start(bf16[256,256]{1,0:T(8,128)(2,1)} %param.21) | copy-start | bytes 393220
  30.2 18.4 %all-to-all-start.1 = ((bf16[8,128,256]{2,1,0:T(8,128)(2,1)}), bf16[8,128,256]{2,1,0:T(8,128)(2,1)S(1)}, u32[]{:S(2)}, u32[]{:S(2)}) async-start(bf16[8,128,256]{2,1,0:T(8,128)(2,1)} %bitcast.19), calls=%async_computation.1 | async-start | bytes 1048576 | tf_op jit(solution)/shard_map/all_to_all | solution.py:134
  33.9 14.7 %copy-start.4 = (s32[1,8]{1,0:T(1,128)S(1)}, s32[1,8]{1,0:T(1,128)}, u32[]{:S(2)}) copy-start(s32[1,8]{1,0:T(1,128)} %param.27) | copy-start | bytes 100
  34.2 14.8 %collective-permute-start.2 = (bf16[256,256]{1,0:T(8,128)(2,1)S(1)}, bf16[256,256]{1,0:T(8,128)(2,1)S(1)}, u32[]{:S(2)}, u32[]{:S(2)}) collective-permute-start(bf16[256,256]{1,0:T(8,128)(2,1)S(1)} %get-tuple-element.47), channel_id=1, source_target_pairs={{0,8},{8,16},{16,24},{24,0},{1,9},{9,17},{17,25},{25,1},{2,10},{10... | collective-permute-start | bytes 393224 | tf_op jit(solution)/shard_map/ppermute | solution.py:16
  34.3 14.7 %collective-permute-start.3 = (bf16[256,256]{1,0:T(8,128)(2,1)S(1)}, bf16[256,256]{1,0:T(8,128)(2,1)S(1)}, u32[]{:S(2)}, u32[]{:S(2)}) collective-permute-start(bf16[256,256]{1,0:T(8,128)(2,1)S(1)} %get-tuple-element.48), channel_id=1, source_target_pairs={{8,0},{16,8},{24,16},{0,24},{9,1},{17,9},{25,17},{1,25},{10,2},{18... | collective-permute-start | bytes 393224 | tf_op jit(solution)/shard_map/ppermute | solution.py:18
  64.1 10.3 %all-to-all-start.3 = ((bf16[32,8,256]{2,1,0:T(8,128)(2,1)}), bf16[32,8,256]{2,1,0:T(8,128)(2,1)S(1)}, u32[]{:S(2)}, u32[]{:S(2)}) async-start(bf16[32,8,256]{2,1,0:T(8,128)(2,1)} %broadcast_in_dim.2), calls=%async_computation.3 | async-start | bytes 262144 | tf_op jit(solution)/shard_map/all_to_all | solution.py:34

commit v18 on v15

--- a/solution.py
+++ b/solution.py
@@ -78,13 +78,19 @@
     )
     extended = padded_2(hidden, (("row", 0),), BW)
     mixed = jnp.dot(band_dense, extended, preferred_element_type=jnp.float32)
-    blocks = hidden.reshape(tile_rows, tile_size, width_feat)
     giving = send_lists[0]
     tile_range = jnp.arange(tile_rows, dtype=jnp.int32)
-    give_onehot = (giving[:, None] == tile_range[None, :]).astype(jnp.bfloat16)
-    outgoing = jnp.einsum(
-        "sb,baf->saf", give_onehot, blocks, preferred_element_type=jnp.float32
-    ).astype(jnp.bfloat16)
+    send_rows = jnp.where(
+        giving[:, None] >= 0,
+        giving[:, None] * tile_size + jnp.arange(tile_size, dtype=jnp.int32)[None, :],
+        -1,
+    ).reshape(peers * tile_size)
+    send_pick = (send_rows[:, None] == node_range[None, :]).astype(jnp.bfloat16)
+    outgoing = (
+        jnp.dot(send_pick, hidden, preferred_element_type=jnp.float32)
+        .astype(jnp.bfloat16)
+        .reshape(peers, tile_size, width_feat)
+    )
     arrived = lax.all_to_all(outgoing, "col", split_axis=0, concat_axis=0, tiled=True)
     owner_range = jnp.arange(peers, dtype=jnp.int32)
     live_slots = jnp.arange(slot_total, dtype=jnp.int32) < bound_count[0]

time: 75 us -> 75.6 us (level)
  other arithmetic: 1.02 us -> 2.41 us
  local copies, waits for them, and re-layouts: 3.29 us -> 2.39 us
    convert_element_type x1 -> x0, local copies, waits for them, and re-layouts: 0.9 us -> none  [on_device(): outgoing = jnp.einsum('sb,baf->saf', give_onehot, blocks, preferred_eleme...]
  transfers between devices with their start and end apart: 7 -> 7, of which waited for: 3 -> 3; matrix products, arithmetic and copies ran while one was open for 9% -> 10% of each run, Pallas kernels for 0% -> 0%
where the time goes in v18:
time: 75.6 us; the launch traced here: 75.2 us
  waiting for transfers between devices  29.5 us (39%)
  starting transfers between devices  17.1 us (23%)
  blocking collectives  13.2 us (17%)
  matrix products  9.11 us (12%)
  other arithmetic  2.41 us (3%)
  local copies, waits for them, and re-layouts  2.39 us (3%)
  between operations  1.57 us (2%)
    all_to_all x1, blocking collectives, spread_sum(): gathered = lax.all_to_all(value.reshape(piece), axes, 0, 0, tiled=True)  13.2 us
    all_to_all x1, waiting for transfers between devices, on_device(): lax.all_to_all(to_owner, 'col', split_axis=0, concat_axis=0, tiled=True)  12.5 us
    all_to_all x1, waiting for transfers between devices, on_device(): lax.all_to_all(outgoing, 'col', split_axis=0, concat_axis=0, tiled=True)  11.3 us
    all_to_all x1, starting transfers between devices, on_device(): lax.all_to_all(outgoing, 'col', split_axis=0, concat_axis=0, tiled=True)  6.53 us
    all_to_all x1, waiting for transfers between devices, spread_sum(): spread = lax.all_to_all(copies, axes, 0, 0, tiled=True)  5.66 us
    ppermute x2, starting transfers between devices, padded_2(): lax.ppermute(head, axis, [((i + 1) % count, i) for i in range(count)])  3.75 us
    all_to_all x1, starting transfers between devices, on_device(): lax.all_to_all(to_owner, 'col', split_axis=0, concat_axis=0, tiled=True)  3.64 us
    all_to_all x1, starting transfers between devices, spread_sum(): spread = lax.all_to_all(copies, axes, 0, 0, tiled=True)  2.58 us
  transfers between devices with their start and end apart: 7, of which 3 were waited for; matrix products, arithmetic and copies ran while one was open for 10% of the time, Pallas kernels for 0%

profile of v18, /device:TPU:0, one launch (start us, length us, event | category | flops | bytes accessed | tf_op | source)
XLA Modules:
  0.0 75.2 jit_solution(1296389309267915976)
XLA Ops:
  0.6 0.0 copy-start
  0.6 0.0 copy-start.4
  0.7 0.0 copy-start.5
  0.7 0.0 copy-start.1
  0.7 1.3 %convolution_convert_fusion.7 = bf16[256,256]{1,0:T(8,128)(2,1)S(1)} fusion(bf16[256,256]{1,0:T(8,128)(2,1)} %param.19, s32[256]{0:T(256)} %bitcast.83), kind=kOutput, calls=%fused_computation.15 | convolution fusion | flops 33685504 | bytes 263168 | tf_op jit(solution)/shard_map/dot_general | solution.py:64
  1.9 0.2 convolution_convert_fusion.6
  2.1 0.5 collective-permute-start
  2.6 2.0 %collective-permute-start.1 = (bf16[256,256]{1,0:T(8,128)(2,1)S(1)}, bf16[256,256]{1,0:T(8,128)(2,1)S(1)}, u32[]{:S(2)}, u32[]{:S(2)}) collective-permute-start(bf16[256,256]{1,0:T(8,128)(2,1)S(1)} %convolution_convert_fusion.6), channel_id=1, source_target_pairs={{8,0},{16,8},{24,16},{0,24},{9,1},{17,9},{25,17},{1,25},{10,2},{18... | collective-permute-start | bytes 393224 | tf_op jit(solution)/shard_map/ppermute | solution.py:18
  4.7 0.7 broadcast_compare_fusion
  5.3 0.7 broadcast_multiply_fusion
  6.0 0.1 select_bitcast_fusion
  6.1 1.2 %convolution_convert_fusion.1 = bf16[1024,256]{1,0:T(8,128)(2,1)} fusion(bf16[256,256]{1,0:T(8,128)(2,1)S(1)} %convolution_convert_fusion.6, s32[1024]{0:T(1024)S(1)} %select_bitcast_fusion), kind=kOutput, calls=%fused_computation.4 | convolution fusion | flops 134742016 | bytes 659456 | tf_op jit(solution)/shard_map/dot_general | solution.py:90
  7.2 6.5 %all-to-all-start = ((bf16[8,128,256]{2,1,0:T(8,128)(2,1)}), bf16[8,128,256]{2,1,0:T(8,128)(2,1)S(1)}, u32[]{:S(2)}, u32[]{:S(2)}) async-start(bf16[8,128,256]{2,1,0:T(8,128)(2,1)} %bitcast.16), calls=%async_computation | async-start | bytes 1048576 | tf_op jit(solution)/shard_map/all_to_all | solution.py:94
  14.5 0.0 copy-done.1
  14.5 0.9 %fusion = f32[2,8,128,128]{3,1,2,0:T(8,128)S(1)} fusion(bf16[40,128,128]{2,1,0:T(8,128)(2,1)S(1)} %copy-done.1, pred[40]{0:T(512)(128)(4,1)S(1)} %iota_compare_fusion.11, pred[40,8]{0,1:T(8,128)(4,1)S(1)} %iota_compare_fusion.7, pred[40,2]{0,1:T(4,128)(4,1)S(1)} %iota_compare_fusion.9), kind=kOutput, calls=%fused_computation | convolution fusion | flops 20972800 | bytes 2359736 | tf_op jit(solution)/shard_map/krs,kab->rasb/dot_general | solution.py:104
  15.4 0.2 fusion.5
  15.6 0.8 %copy-done.2 = bf16[12,128,128]{2,1,0:T(8,128)(2,1)S(1)} copy-done((bf16[12,128,128]{2,1,0:T(8,128)(2,1)S(1)}, bf16[12,128,128]{2,1,0:T(8,128)(2,1)}, u32[]{:S(2)}) %copy-start.2) | copy-done | bytes 393240
  16.4 0.4 convolution_convert_fusion.2
  16.8 0.2 copy.56
  17.0 11.3 %all-to-all-done = bf16[8,128,256]{2,1,0:T(8,128)(2,1)S(1)} async-done(((bf16[8,128,256]{2,1,0:T(8,128)(2,1)}), bf16[8,128,256]{2,1,0:T(8,128)(2,1)S(1)}, u32[]{:S(2)}, u32[]{:S(2)}) %all-to-all-start) | async-done | bytes 524320 | tf_op jit(solution)/shard_map/all_to_all | solution.py:94
  28.3 0.4 fusion.6
  28.7 0.0 copy-start.3
  28.7 0.0 copy-start.7
  28.8 0.0 collective-permute-done
  28.8 0.0 collective-permute-done.1
  28.8 0.3 convolution_add_fusion
  29.1 0.4 copy-done.3
  29.4 0.2 copy-done.7
  29.7 0.2 fusion.4
  29.9 1.3 %convolution_convert_fusion = bf16[1024,256]{1,0:T(8,128)(2,1)} fusion(bf16[256,1024]{1,0:T(8,128)(2,1)S(1)} %fusion.5, bf16[256,1024]{1,0:T(8,128)(2,1)S(1)} %bitcast.81, bf16[256,256]{1,0:T(8,128)(2,1)S(1)} %fusion.4), kind=kOutput, calls=%fused_computation.3 | convolution fusion | flops 271319040 | bytes 1703936 | tf_op jit(solution)/shard_map/dot_general | solution.py:132
  31.2 3.6 %all-to-all-start.1 = ((bf16[8,128,256]{2,1,0:T(8,128)(2,1)}), bf16[8,128,256]{2,1,0:T(8,128)(2,1)S(1)}, u32[]{:S(2)}, u32[]{:S(2)}) async-start(bf16[8,128,256]{2,1,0:T(8,128)(2,1)} %bitcast.19), calls=%async_computation.1 | async-start | bytes 1048576 | tf_op jit(solution)/shard_map/all_to_all | solution.py:139
  34.8 0.3 fusion.60
  35.2 0.1 collective-permute-start.2
  35.2 1.7 %collective-permute-start.3 = (bf16[256,256]{1,0:T(8,128)(2,1)S(1)}, bf16[256,256]{1,0:T(8,128)(2,1)S(1)}, u32[]{:S(2)}, u32[]{:S(2)}) collective-permute-start(bf16[256,256]{1,0:T(8,128)(2,1)S(1)} %get-tuple-element.44), channel_id=1, source_target_pairs={{8,0},{16,8},{24,16},{0,24},{9,1},{17,9},{25,17},{1,25},{10,2},{18... | collective-permute-start | bytes 393224 | tf_op jit(solution)/shard_map/ppermute | solution.py:18
  37.0 12.5 %all-to-all-done.1 = bf16[8,128,256]{2,1,0:T(8,128)(2,1)S(1)} async-done(((bf16[8,128,256]{2,1,0:T(8,128)(2,1)}), bf16[8,128,256]{2,1,0:T(8,128)(2,1)S(1)}, u32[]{:S(2)}, u32[]{:S(2)}) %all-to-all-start.1) | async-done | bytes 524320 | tf_op jit(solution)/shard_map/all_to_all | solution.py:139
  49.5 0.0 copy-done.6
  49.5 0.4 fusion.17
  49.9 0.0 collective-permute-done.2
  50.0 0.0 collective-permute-done.3
  50.0 0.1 fusion.33
  50.0 0.2 convolution_bitcast_fusion
  50.3 13.2 %all_to_all.20 = f32[32,8,256]{2,1,0:T(8,128)S(1)} all-to-all(f32[32,8,256]{2,1,0:T(8,128)S(1)} %convolution_bitcast_fusion), channel_id=1, replica_groups=mesh['row'=4,'col'=8] {'row','col'}, dimensions={0} | all-to-all | bytes 524288 | tf_op jit(solution)/shard_map/all_to_all | solution.py:31
  63.5 0.7 broadcast_in_dim.16
  64.1 2.6 %all-to-all-start.3 = ((bf16[32,8,256]{2,1,0:T(8,128)(2,1)}), bf16[32,8,256]{2,1,0:T(8,128)(2,1)S(1)}, u32[]{:S(2)}, u32[]{:S(2)}) async-start(bf16[32,8,256]{2,1,0:T(8,128)(2,1)} %broadcast_in_dim.16), calls=%async_computation.3 | async-start | bytes 262144 | tf_op jit(solution)/shard_map/all_to_all | solution.py:34
  66.7 1.0 %convolution_convert_fusion.5 = bf16[256,256]{1,0:T(8,128)(2,1)} fusion(s32[256]{0:T(256)S(1)} %bitcast.85, f32[256,256]{1,0:T(8,128)S(1)} %convolution_add_fusion), kind=kOutput, calls=%fused_computation.13 | convolution fusion | flops 34013184 | bytes 394240 | tf_op jit(solution)/shard_map/dot_general | solution.py:116
  67.7 1.1 %convolution_convert_fusion.3 = bf16[256,256]{1,0:T(8,128)(2,1)} fusion(bf16[256,256]{1,0:T(8,128)(2,1)S(1)} %fusion.33, bf16[256,256]{1,0:T(8,128)(2,1)S(1)} %copy-done, s32[256]{0:T(256)S(1)} %bitcast.86), kind=kOutput, calls=%fused_computation.11 | convolution fusion | flops 67305472 | bytes 394240 | tf_op jit(solution)/shard_map/dot_general | solution.py:154
  68.8 5.7 %all-to-all-done.3 = bf16[32,8,256]{2,1,0:T(8,128)(2,1)S(1)} async-done(((bf16[32,8,256]{2,1,0:T(8,128)(2,1)}), bf16[32,8,256]{2,1,0:T(8,128)(2,1)S(1)}, u32[]{:S(2)}, u32[]{:S(2)}) %all-to-all-start.3) | async-done | bytes 131104 | tf_op jit(solution)/shard_map/all_to_all | solution.py:34
  74.5 0.7 bitcast_convert_fusion.1
  (16 shorter events, 0.1 us)
Async XLA Ops:
  0.6 1.3 %copy-start = (bf16[256,256]{1,0:T(8,128)(2,1)S(1)}, bf16[256,256]{1,0:T(8,128)(2,1)}, u32[]{:S(2)}) copy-start(bf16[256,256]{1,0:T(8,128)(2,1)} %param.20) | copy-start | bytes 393220
  0.6 13.1 %copy-start.4 = (s32[40,2]{0,1:T(2,128)S(1)}, s32[40,2]{0,1:T(2,128)}, u32[]{:S(2)}) copy-start(s32[40,2]{0,1:T(2,128)} %param.25) | copy-start | bytes 964
  0.7 13.1 %copy-start.5 = (s32[12,2]{0,1:T(2,128)S(1)}, s32[12,2]{0,1:T(2,128)}, u32[]{:S(2)}) copy-start(s32[12,2]{0,1:T(2,128)} %param.23) | copy-start | bytes 292
  0.7 13.8 %copy-start.1 = (bf16[40,128,128]{2,1,0:T(8,128)(2,1)S(1)}, bf16[40,128,128]{2,1,0:T(8,128)(2,1)}, u32[]{:S(2)}) copy-start(bf16[40,128,128]{2,1,0:T(8,128)(2,1)} %param.24) | copy-start | bytes 3932164
  2.1 26.6 %collective-permute-start = (bf16[256,256]{1,0:T(8,128)(2,1)S(1)}, bf16[256,256]{1,0:T(8,128)(2,1)S(1)}, u32[]{:S(2)}, u32[]{:S(2)}) collective-permute-start(bf16[256,256]{1,0:T(8,128)(2,1)S(1)} %convolution_convert_fusion.6), channel_id=1, source_target_pairs={{0,8},{8,16},{16,24},{24,0},{1,9},{9,17},{17,25},{25,1},{2,10},{10... | collective-permute-start | bytes 393224 | tf_op jit(solution)/shard_map/ppermute | solution.py:16
  2.6 26.1 %collective-permute-start.1 = (bf16[256,256]{1,0:T(8,128)(2,1)S(1)}, bf16[256,256]{1,0:T(8,128)(2,1)S(1)}, u32[]{:S(2)}, u32[]{:S(2)}) collective-permute-start(bf16[256,256]{1,0:T(8,128)(2,1)S(1)} %convolution_convert_fusion.6), channel_id=1, source_target_pairs={{8,0},{16,8},{24,16},{0,24},{9,1},{17,9},{25,17},{1,25},{10,2},{18... | collective-permute-start | bytes 393224 | tf_op jit(solution)/shard_map/ppermute | solution.py:18
  7.2 21.1 %all-to-all-start = ((bf16[8,128,256]{2,1,0:T(8,128)(2,1)}), bf16[8,128,256]{2,1,0:T(8,128)(2,1)S(1)}, u32[]{:S(2)}, u32[]{:S(2)}) async-start(bf16[8,128,256]{2,1,0:T(8,128)(2,1)} %bitcast.16), calls=%async_computation | async-start | bytes 1048576 | tf_op jit(solution)/shard_map/all_to_all | solution.py:94
  15.4 1.0 %copy-start.2 = (bf16[12,128,128]{2,1,0:T(8,128)(2,1)S(1)}, bf16[12,128,128]{2,1,0:T(8,128)(2,1)}, u32[]{:S(2)}) copy-start(bf16[12,128,128]{2,1,0:T(8,128)(2,1)} %param.22) | copy-start | bytes 1179652
  28.7 0.7 copy-start.3
  28.7 0.9 %copy-start.7 = (bf16[256,256]{1,0:T(8,128)(2,1)S(1)}, bf16[256,256]{1,0:T(8,128)(2,1)}, u32[]{:S(2)}) copy-start(bf16[256,256]{1,0:T(8,128)(2,1)} %param.21) | copy-start | bytes 393220
  31.2 18.3 %all-to-all-start.1 = ((bf16[8,128,256]{2,1,0:T(8,128)(2,1)}), bf16[8,128,256]{2,1,0:T(8,128)(2,1)S(1)}, u32[]{:S(2)}, u32[]{:S(2)}) async-start(bf16[8,128,256]{2,1,0:T(8,128)(2,1)} %bitcast.19), calls=%async_computation.1 | async-start | bytes 1048576 | tf_op jit(solution)/shard_map/all_to_all | solution.py:139
  34.8 14.7 %copy-start.6 = (s32[1,8]{1,0:T(1,128)S(1)}, s32[1,8]{1,0:T(1,128)}, u32[]{:S(2)}) copy-start(s32[1,8]{1,0:T(1,128)} %param.27) | copy-start | bytes 100
  35.2 14.8 %collective-permute-start.2 = (bf16[256,256]{1,0:T(8,128)(2,1)S(1)}, bf16[256,256]{1,0:T(8,128)(2,1)S(1)}, u32[]{:S(2)}, u32[]{:S(2)}) collective-permute-start(bf16[256,256]{1,0:T(8,128)(2,1)S(1)} %get-tuple-element.43), channel_id=1, source_target_pairs={{0,8},{8,16},{16,24},{24,0},{1,9},{9,17},{17,25},{25,1},{2,10},{10... | collective-permute-start | bytes 393224 | tf_op jit(solution)/shard_map/ppermute | solution.py:16
  35.2 14.7 %collective-permute-start.3 = (bf16[256,256]{1,0:T(8,128)(2,1)S(1)}, bf16[256,256]{1,0:T(8,128)(2,1)S(1)}, u32[]{:S(2)}, u32[]{:S(2)}) collective-permute-start(bf16[256,256]{1,0:T(8,128)(2,1)S(1)} %get-tuple-element.44), channel_id=1, source_target_pairs={{8,0},{16,8},{24,16},{0,24},{9,1},{17,9},{25,17},{1,25},{10,2},{18... | collective-permute-start | bytes 393224 | tf_op jit(solution)/shard_map/ppermute | solution.py:18
  64.1 10.3 %all-to-all-start.3 = ((bf16[32,8,256]{2,1,0:T(8,128)(2,1)}), bf16[32,8,256]{2,1,0:T(8,128)(2,1)S(1)}, u32[]{:S(2)}, u32[]{:S(2)}) async-start(bf16[32,8,256]{2,1,0:T(8,128)(2,1)} %broadcast_in_dim.16), calls=%async_computation.3 | async-start | bytes 262144 | tf_op jit(solution)/shard_map/all_to_all | solution.py:34

commit v19 on v15

--- a/solution.py
+++ b/solution.py
@@ -100,6 +100,11 @@
     ).reshape(row_count, peers * tile_size)
     dense_high = bound_dense.astype(jnp.bfloat16)
     dense_low = (bound_dense - dense_high.astype(jnp.float32)).astype(jnp.bfloat16)
+    bound_dense_t = jnp.einsum(
+        "krs,kab->sbra", slot_onehot, bound_tiles, preferred_element_type=jnp.float32
+    ).reshape(peers * tile_size, row_count)
+    dense_high_t = bound_dense_t.astype(jnp.bfloat16)
+    dense_low_t = (bound_dense_t - dense_high_t.astype(jnp.float32)).astype(jnp.bfloat16)
     arrived_rows = arrived.reshape(peers * tile_size, width_feat)
     mixed = mixed + jnp.dot(
         jnp.concatenate([dense_high, dense_low], axis=1),
@@ -123,10 +128,9 @@
     grad_hidden = ext_grad[BW : BW + row_count]
     grad_hidden = grad_hidden.at[:BW].add(padded[:BW].astype(jnp.float32))
     grad_hidden = grad_hidden.at[row_count - BW :].add(padded[3 * BW :].astype(jnp.float32))
-    owner_terms = lax.dot_general(
-        jnp.concatenate([dense_high, dense_low], axis=0),
+    owner_terms = jnp.dot(
+        jnp.concatenate([dense_high_t, dense_low_t], axis=1),
         jnp.concatenate([slope, slope], axis=0),
-        contract_rows,
         preferred_element_type=jnp.float32,
     )
     to_owner = owner_terms.astype(jnp.bfloat16).reshape(peers, tile_size, width_feat)

time: 75 us -> 75 us (level)
  transfers between devices with their start and end apart: 7 -> 7, of which waited for: 3 -> 3; matrix products, arithmetic and copies ran while one was open for 9% -> 10% of each run, Pallas kernels for 0% -> 0%
where the time goes in v19:
time: 75 us; the launch traced here: 74.6 us
  waiting for transfers between devices  29.5 us (39%)
  starting transfers between devices  17.1 us (23%)
  blocking collectives  13.2 us (18%)
  matrix products  8.99 us (12%)
  local copies, waits for them, and re-layouts  3.1 us (4%)
  between operations  1.56 us (2%)
  other arithmetic  1.19 us (2%)
    all_to_all x1, blocking collectives, spread_sum(): gathered = lax.all_to_all(value.reshape(piece), axes, 0, 0, tiled=True)  13.2 us
    all_to_all x1, waiting for transfers between devices, on_device(): lax.all_to_all(to_owner, 'col', split_axis=0, concat_axis=0, tiled=True)  12.5 us
    all_to_all x1, waiting for transfers between devices, on_device(): lax.all_to_all(outgoing, 'col', split_axis=0, concat_axis=0, tiled=True)  11.3 us
    all_to_all x1, starting transfers between devices, on_device(): lax.all_to_all(outgoing, 'col', split_axis=0, concat_axis=0, tiled=True)  6.53 us
    all_to_all x1, waiting for transfers between devices, spread_sum(): spread = lax.all_to_all(copies, axes, 0, 0, tiled=True)  5.66 us
    ppermute x2, starting transfers between devices, padded_2(): lax.ppermute(head, axis, [((i + 1) % count, i) for i in range(count)])  3.75 us
    all_to_all x1, starting transfers between devices, on_device(): lax.all_to_all(to_owner, 'col', split_axis=0, concat_axis=0, tiled=True)  3.64 us
    all_to_all x1, starting transfers between devices, spread_sum(): spread = lax.all_to_all(copies, axes, 0, 0, tiled=True)  2.58 us
  transfers between devices with their start and end apart: 7, of which 3 were waited for; matrix products, arithmetic and copies ran while one was open for 10% of the time, Pallas kernels for 0%

profile of v19, /device:TPU:0, one launch (start us, length us, event | category | flops | bytes accessed | tf_op | source)
XLA Modules:
  0.0 74.6 jit_solution(1136919719707972097)
XLA Ops:
  0.6 0.0 copy-start
  0.6 1.2 %convolution_convert_fusion.7 = bf16[256,256]{1,0:T(8,128)(2,1)S(1)} fusion(bf16[256,256]{1,0:T(8,128)(2,1)} %param.19, s32[256]{0:T(256)} %bitcast.95), kind=kOutput, calls=%fused_computation.15 | convolution fusion | flops 33685504 | bytes 263168 | tf_op jit(solution)/shard_map/dot_general | solution.py:64
  1.8 0.0 copy-done
  1.8 0.2 convolution_convert_fusion.6
  2.0 0.5 collective-permute-start
  2.5 2.0 %collective-permute-start.1 = (bf16[256,256]{1,0:T(8,128)(2,1)S(1)}, bf16[256,256]{1,0:T(8,128)(2,1)S(1)}, u32[]{:S(2)}, u32[]{:S(2)}) collective-permute-start(bf16[256,256]{1,0:T(8,128)(2,1)S(1)} %convolution_convert_fusion.6), channel_id=1, source_target_pairs={{8,0},{16,8},{24,16},{0,24},{9,1},{17,9},{25,17},{1,25},{10,2},{18... | collective-permute-start | bytes 393224 | tf_op jit(solution)/shard_map/ppermute | solution.py:18
  4.6 1.1 %convolution_convert_fusion.1 = bf16[8,128,256]{2,0,1:T(8,128)(2,1)S(1)} fusion(bf16[2,128,256]{2,1,0:T(8,128)(2,1)S(1)} %bitcast.94, s32[8]{0:T(128)} %bitcast.99), kind=kOutput, calls=%fused_computation.4 | convolution fusion | flops 1310736 | bytes 655392 | tf_op jit(solution)/shard_map/sb,baf->saf/dot_general | solution.py:85
  5.7 0.9 %copy.29 = bf16[8,128,256]{2,1,0:T(8,128)(2,1)} copy(bf16[8,128,256]{2,0,1:T(8,128)(2,1)S(1)} %convolution_convert_fusion.1) | data formatting | bytes 1048576 | tf_op jit(solution)/shard_map/convert_element_type | solution.py:87
  6.6 6.5 %all-to-all-start = ((bf16[8,128,256]{2,1,0:T(8,128)(2,1)}), bf16[8,128,256]{2,1,0:T(8,128)(2,1)S(1)}, u32[]{:S(2)}, u32[]{:S(2)}) async-start(bf16[8,128,256]{2,1,0:T(8,128)(2,1)} %copy.29), calls=%async_computation | async-start | bytes 1048576 | tf_op jit(solution)/shard_map/all_to_all | solution.py:88
  13.1 0.0 copy-done.5
  13.8 0.0 copy-done.6
  13.8 0.0 copy-done.1
  13.9 0.9 %fusion = f32[2,8,128,128]{3,1,2,0:T(8,128)S(1)} fusion(bf16[40,128,128]{2,1,0:T(8,128)(2,1)S(1)} %copy-done.1, pred[40]{0:T(512)(128)(4,1)S(1)} %iota_compare_fusion.9, pred[40,8]{0,1:T(8,128)(4,1)S(1)} %iota_compare_fusion.5, pred[40,2]{0,1:T(4,128)(4,1)S(1)} %iota_compare_fusion.7), kind=kOutput, calls=%fused_computation | convolution fusion | flops 20972800 | bytes 2359736 | tf_op jit(solution)/shard_map/krs,kab->rasb/dot_general | solution.py:98
  14.8 0.0 copy-start.2
  14.8 0.2 fusion.6
  15.0 0.2 fusion.5
  15.2 0.6 copy-done.2
  15.8 0.4 convolution_convert_fusion.2
  16.2 0.2 copy.68
  16.4 11.3 %all-to-all-done = bf16[8,128,256]{2,1,0:T(8,128)(2,1)S(1)} async-done(((bf16[8,128,256]{2,1,0:T(8,128)(2,1)}), bf16[8,128,256]{2,1,0:T(8,128)(2,1)S(1)}, u32[]{:S(2)}, u32[]{:S(2)}) %all-to-all-start) | async-done | bytes 524320 | tf_op jit(solution)/shard_map/all_to_all | solution.py:88
  27.7 0.4 fusion.7
  28.1 0.0 copy-start.3
  28.1 0.0 copy-start.7
  28.1 0.0 collective-permute-done
  28.1 0.0 collective-permute-done.1
  28.1 0.3 convolution_add_fusion
  28.4 0.4 copy-done.3
  28.8 0.2 copy-done.7
  29.0 0.2 fusion.4
  29.3 1.3 %convolution_convert_fusion = bf16[1024,256]{1,0:T(8,128)(2,1)} fusion(bf16[1024,256]{0,1:T(8,128)(2,1)S(1)} %fusion.5, bf16[1024,256]{0,1:T(8,128)(2,1)S(1)} %bitcast.92, bf16[256,256]{1,0:T(8,128)(2,1)S(1)} %fusion.4), kind=kOutput, calls=%fused_computation.3 | convolution fusion | flops 271319040 | bytes 1703936 | tf_op jit(solution)/shard_map/dot_general | solution.py:131
  30.6 3.6 %all-to-all-start.1 = ((bf16[8,128,256]{2,1,0:T(8,128)(2,1)}), bf16[8,128,256]{2,1,0:T(8,128)(2,1)S(1)}, u32[]{:S(2)}, u32[]{:S(2)}) async-start(bf16[8,128,256]{2,1,0:T(8,128)(2,1)} %bitcast.20), calls=%async_computation.1 | async-start | bytes 1048576 | tf_op jit(solution)/shard_map/all_to_all | solution.py:137
  34.2 0.3 fusion.65
  34.5 0.1 collective-permute-start.2
  34.6 1.7 %collective-permute-start.3 = (bf16[256,256]{1,0:T(8,128)(2,1)S(1)}, bf16[256,256]{1,0:T(8,128)(2,1)S(1)}, u32[]{:S(2)}, u32[]{:S(2)}) collective-permute-start(bf16[256,256]{1,0:T(8,128)(2,1)S(1)} %get-tuple-element.46), channel_id=1, source_target_pairs={{8,0},{16,8},{24,16},{0,24},{9,1},{17,9},{25,17},{1,25},{10,2},{18... | collective-permute-start | bytes 393224 | tf_op jit(solution)/shard_map/ppermute | solution.py:18
  36.3 12.5 %all-to-all-done.1 = bf16[8,128,256]{2,1,0:T(8,128)(2,1)S(1)} async-done(((bf16[8,128,256]{2,1,0:T(8,128)(2,1)}), bf16[8,128,256]{2,1,0:T(8,128)(2,1)S(1)}, u32[]{:S(2)}, u32[]{:S(2)}) %all-to-all-start.1) | async-done | bytes 524320 | tf_op jit(solution)/shard_map/all_to_all | solution.py:137
  48.9 0.0 copy-done.4
  48.9 0.4 fusion.18
  49.3 0.0 collective-permute-done.2
  49.3 0.0 collective-permute-done.3
  49.3 0.1 fusion.33
  49.4 0.2 convolution_bitcast_fusion
  49.6 13.2 %all_to_all.20 = f32[32,8,256]{2,1,0:T(8,128)S(1)} all-to-all(f32[32,8,256]{2,1,0:T(8,128)S(1)} %convolution_bitcast_fusion), channel_id=1, replica_groups=mesh['row'=4,'col'=8] {'row','col'}, dimensions={0} | all-to-all | bytes 524288 | tf_op jit(solution)/shard_map/all_to_all | solution.py:31
  62.9 0.7 broadcast_in_dim.2
  63.5 2.6 %all-to-all-start.3 = ((bf16[32,8,256]{2,1,0:T(8,128)(2,1)}), bf16[32,8,256]{2,1,0:T(8,128)(2,1)S(1)}, u32[]{:S(2)}, u32[]{:S(2)}) async-start(bf16[32,8,256]{2,1,0:T(8,128)(2,1)} %broadcast_in_dim.2), calls=%async_computation.3 | async-start | bytes 262144 | tf_op jit(solution)/shard_map/all_to_all | solution.py:34
  66.1 1.0 %convolution_convert_fusion.5 = bf16[256,256]{1,0:T(8,128)(2,1)} fusion(s32[256]{0:T(256)S(1)} %bitcast.97, f32[256,256]{1,0:T(8,128)S(1)} %convolution_add_fusion), kind=kOutput, calls=%fused_computation.13 | convolution fusion | flops 34013184 | bytes 394240 | tf_op jit(solution)/shard_map/dot_general | solution.py:115
  67.1 1.1 %convolution_convert_fusion.3 = bf16[256,256]{1,0:T(8,128)(2,1)} fusion(bf16[256,256]{1,0:T(8,128)(2,1)S(1)} %fusion.33, bf16[256,256]{1,0:T(8,128)(2,1)S(1)} %copy-done, s32[256]{0:T(256)S(1)} %bitcast.98), kind=kOutput, calls=%fused_computation.11 | convolution fusion | flops 67305472 | bytes 394240 | tf_op jit(solution)/shard_map/dot_general | solution.py:152
  68.2 5.7 %all-to-all-done.3 = bf16[32,8,256]{2,1,0:T(8,128)(2,1)S(1)} async-done(((bf16[32,8,256]{2,1,0:T(8,128)(2,1)}), bf16[32,8,256]{2,1,0:T(8,128)(2,1)S(1)}, u32[]{:S(2)}, u32[]{:S(2)}) %all-to-all-start.3) | async-done | bytes 131104 | tf_op jit(solution)/shard_map/all_to_all | solution.py:34
  73.8 0.7 bitcast_convert_fusion.2
  (15 shorter events, 0.1 us)
Async XLA Ops:
  0.6 1.2 %copy-start = (bf16[256,256]{1,0:T(8,128)(2,1)S(1)}, bf16[256,256]{1,0:T(8,128)(2,1)}, u32[]{:S(2)}) copy-start(bf16[256,256]{1,0:T(8,128)(2,1)} %param.20) | copy-start | bytes 393220
  2.0 26.1 %collective-permute-start = (bf16[256,256]{1,0:T(8,128)(2,1)S(1)}, bf16[256,256]{1,0:T(8,128)(2,1)S(1)}, u32[]{:S(2)}, u32[]{:S(2)}) collective-permute-start(bf16[256,256]{1,0:T(8,128)(2,1)S(1)} %convolution_convert_fusion.6), channel_id=1, source_target_pairs={{0,8},{8,16},{16,24},{24,0},{1,9},{9,17},{17,25},{25,1},{2,10},{10... | collective-permute-start | bytes 393224 | tf_op jit(solution)/shard_map/ppermute | solution.py:16
  2.5 25.6 %collective-permute-start.1 = (bf16[256,256]{1,0:T(8,128)(2,1)S(1)}, bf16[256,256]{1,0:T(8,128)(2,1)S(1)}, u32[]{:S(2)}, u32[]{:S(2)}) collective-permute-start(bf16[256,256]{1,0:T(8,128)(2,1)S(1)} %convolution_convert_fusion.6), channel_id=1, source_target_pairs={{8,0},{16,8},{24,16},{0,24},{9,1},{17,9},{25,17},{1,25},{10,2},{18... | collective-permute-start | bytes 393224 | tf_op jit(solution)/shard_map/ppermute | solution.py:18
  4.6 8.6 %copy-start.5 = (s32[40,2]{0,1:T(2,128)S(1)}, s32[40,2]{0,1:T(2,128)}, u32[]{:S(2)}) copy-start(s32[40,2]{0,1:T(2,128)} %param.25) | copy-start | bytes 964
  4.6 9.3 %copy-start.6 = (s32[12,2]{0,1:T(2,128)S(1)}, s32[12,2]{0,1:T(2,128)}, u32[]{:S(2)}) copy-start(s32[12,2]{0,1:T(2,128)} %param.23) | copy-start | bytes 292
  4.6 9.3 %copy-start.1 = (bf16[40,128,128]{2,1,0:T(8,128)(2,1)S(1)}, bf16[40,128,128]{2,1,0:T(8,128)(2,1)}, u32[]{:S(2)}) copy-start(bf16[40,128,128]{2,1,0:T(8,128)(2,1)} %param.24) | copy-start | bytes 3932164
  6.6 21.1 %all-to-all-start = ((bf16[8,128,256]{2,1,0:T(8,128)(2,1)}), bf16[8,128,256]{2,1,0:T(8,128)(2,1)S(1)}, u32[]{:S(2)}, u32[]{:S(2)}) async-start(bf16[8,128,256]{2,1,0:T(8,128)(2,1)} %copy.29), calls=%async_computation | async-start | bytes 1048576 | tf_op jit(solution)/shard_map/all_to_all | solution.py:88
  14.8 1.0 %copy-start.2 = (bf16[12,128,128]{2,1,0:T(8,128)(2,1)S(1)}, bf16[12,128,128]{2,1,0:T(8,128)(2,1)}, u32[]{:S(2)}) copy-start(bf16[12,128,128]{2,1,0:T(8,128)(2,1)} %param.22) | copy-start | bytes 1179652
  28.1 0.7 copy-start.3
  28.1 0.9 %copy-start.7 = (bf16[256,256]{1,0:T(8,128)(2,1)S(1)}, bf16[256,256]{1,0:T(8,128)(2,1)}, u32[]{:S(2)}) copy-start(bf16[256,256]{1,0:T(8,128)(2,1)} %param.21) | copy-start | bytes 393220
  30.6 18.3 %all-to-all-start.1 = ((bf16[8,128,256]{2,1,0:T(8,128)(2,1)}), bf16[8,128,256]{2,1,0:T(8,128)(2,1)S(1)}, u32[]{:S(2)}, u32[]{:S(2)}) async-start(bf16[8,128,256]{2,1,0:T(8,128)(2,1)} %bitcast.20), calls=%async_computation.1 | async-start | bytes 1048576 | tf_op jit(solution)/shard_map/all_to_all | solution.py:137
  34.2 14.7 %copy-start.4 = (s32[1,8]{1,0:T(1,128)S(1)}, s32[1,8]{1,0:T(1,128)}, u32[]{:S(2)}) copy-start(s32[1,8]{1,0:T(1,128)} %param.27) | copy-start | bytes 100
  34.5 14.8 %collective-permute-start.2 = (bf16[256,256]{1,0:T(8,128)(2,1)S(1)}, bf16[256,256]{1,0:T(8,128)(2,1)S(1)}, u32[]{:S(2)}, u32[]{:S(2)}) collective-permute-start(bf16[256,256]{1,0:T(8,128)(2,1)S(1)} %get-tuple-element.45), channel_id=1, source_target_pairs={{0,8},{8,16},{16,24},{24,0},{1,9},{9,17},{17,25},{25,1},{2,10},{10... | collective-permute-start | bytes 393224 | tf_op jit(solution)/shard_map/ppermute | solution.py:16
  34.6 14.7 %collective-permute-start.3 = (bf16[256,256]{1,0:T(8,128)(2,1)S(1)}, bf16[256,256]{1,0:T(8,128)(2,1)S(1)}, u32[]{:S(2)}, u32[]{:S(2)}) collective-permute-start(bf16[256,256]{1,0:T(8,128)(2,1)S(1)} %get-tuple-element.46), channel_id=1, source_target_pairs={{8,0},{16,8},{24,16},{0,24},{9,1},{17,9},{25,17},{1,25},{10,2},{18... | collective-permute-start | bytes 393224 | tf_op jit(solution)/shard_map/ppermute | solution.py:18
  63.5 10.3 %all-to-all-start.3 = ((bf16[32,8,256]{2,1,0:T(8,128)(2,1)}), bf16[32,8,256]{2,1,0:T(8,128)(2,1)S(1)}, u32[]{:S(2)}, u32[]{:S(2)}) async-start(bf16[32,8,256]{2,1,0:T(8,128)(2,1)} %broadcast_in_dim.2), calls=%async_computation.3 | async-start | bytes 262144 | tf_op jit(solution)/shard_map/all_to_all | solution.py:34

commit v20 on v15

--- a/solution.py
+++ b/solution.py
@@ -141,7 +141,7 @@
         x_band, grad_round, (((0,), (0,)), ((), ())), preferred_element_type=jnp.float32
     )
     nodes_all = row_count * lax.axis_size("row") * peers
-    weight_grad = spread_sum(partial_weight, ("row", "col"), nodes_all ** (-0.5))
+    weight_grad = spread_sum(partial_weight, ("col", "row"), nodes_all ** (-0.5))
     feat_band = lax.dot_general(
         grad_round, weight, (((1,), (1,)), ((), ())), preferred_element_type=jnp.float32
     ).astype(jnp.bfloat16)

time: 75 us -> 75.5 us (level)
  no operation moved by 1% of the time
where the time goes in v20:
time: 75.5 us; the launch traced here: 75 us
  waiting for transfers between devices  30 us (40%)
  starting transfers between devices  17.1 us (23%)
  blocking collectives  13.1 us (17%)
  matrix products  8.99 us (12%)
  local copies, waits for them, and re-layouts  3.29 us (4%)
  between operations  1.55 us (2%)
  other arithmetic  1.02 us (1%)
    all_to_all x1, blocking collectives, spread_sum(): gathered = lax.all_to_all(value.reshape(piece), axes, 0, 0, tiled=True)  13.1 us
    all_to_all x1, waiting for transfers between devices, on_device(): lax.all_to_all(to_owner, 'col', split_axis=0, concat_axis=0, tiled=True)  12.5 us
    all_to_all x1, waiting for transfers between devices, on_device(): lax.all_to_all(outgoing, 'col', split_axis=0, concat_axis=0, tiled=True)  11.3 us
    all_to_all x1, starting transfers between devices, on_device(): lax.all_to_all(outgoing, 'col', split_axis=0, concat_axis=0, tiled=True)  6.53 us
    all_to_all x1, waiting for transfers between devices, spread_sum(): spread = lax.all_to_all(copies, axes, 0, 0, tiled=True)  6.16 us
    ppermute x2, starting transfers between devices, padded_2(): lax.ppermute(head, axis, [((i + 1) % count, i) for i in range(count)])  3.75 us
    all_to_all x1, starting transfers between devices, on_device(): lax.all_to_all(to_owner, 'col', split_axis=0, concat_axis=0, tiled=True)  3.64 us
    all_to_all x1, starting transfers between devices, spread_sum(): spread = lax.all_to_all(copies, axes, 0, 0, tiled=True)  2.58 us
  transfers between devices with their start and end apart: 7, of which 3 were waited for; matrix products, arithmetic and copies ran while one was open for 9% of the time, Pallas kernels for 0%

profile of v20, /device:TPU:0, one launch (start us, length us, event | category | flops | bytes accessed | tf_op | source)
XLA Modules:
  0.0 75.0 jit_solution(5126200154196014109)
XLA Ops:
  0.6 0.0 copy-start
  0.6 1.2 %convolution_convert_fusion.7 = bf16[256,256]{1,0:T(8,128)(2,1)S(1)} fusion(bf16[256,256]{1,0:T(8,128)(2,1)} %param.19, s32[256]{0:T(256)} %bitcast.82), kind=kOutput, calls=%fused_computation.15 | convolution fusion | flops 33685504 | bytes 263168 | tf_op jit(solution)/shard_map/dot_general | solution.py:64
  1.8 0.0 copy-done
  1.8 0.2 convolution_convert_fusion.6
  2.0 0.5 collective-permute-start
  2.5 2.0 %collective-permute-start.1 = (bf16[256,256]{1,0:T(8,128)(2,1)S(1)}, bf16[256,256]{1,0:T(8,128)(2,1)S(1)}, u32[]{:S(2)}, u32[]{:S(2)}) collective-permute-start(bf16[256,256]{1,0:T(8,128)(2,1)S(1)} %convolution_convert_fusion.6), channel_id=1, source_target_pairs={{8,0},{16,8},{24,16},{0,24},{9,1},{17,9},{25,17},{1,25},{10,2},{18... | collective-permute-start | bytes 393224 | tf_op jit(solution)/shard_map/ppermute | solution.py:18
  4.6 0.0 copy-start.5
  4.6 0.0 copy-start.6
  4.6 1.1 %convolution_convert_fusion.1 = bf16[8,128,256]{2,0,1:T(8,128)(2,1)S(1)} fusion(bf16[2,128,256]{2,1,0:T(8,128)(2,1)S(1)} %bitcast.81, s32[8]{0:T(128)} %bitcast.86), kind=kOutput, calls=%fused_computation.4 | convolution fusion | flops 1310736 | bytes 655392 | tf_op jit(solution)/shard_map/sb,baf->saf/dot_general | solution.py:85
  5.7 0.9 %copy.29 = bf16[8,128,256]{2,1,0:T(8,128)(2,1)} copy(bf16[8,128,256]{2,0,1:T(8,128)(2,1)S(1)} %convolution_convert_fusion.1) | data formatting | bytes 1048576 | tf_op jit(solution)/shard_map/convert_element_type | solution.py:87
  6.6 6.5 %all-to-all-start = ((bf16[8,128,256]{2,1,0:T(8,128)(2,1)}), bf16[8,128,256]{2,1,0:T(8,128)(2,1)S(1)}, u32[]{:S(2)}, u32[]{:S(2)}) async-start(bf16[8,128,256]{2,1,0:T(8,128)(2,1)} %copy.29), calls=%async_computation | async-start | bytes 1048576 | tf_op jit(solution)/shard_map/all_to_all | solution.py:88
  13.1 0.0 copy-done.5
  13.2 0.0 copy-done.6
  13.9 0.0 copy-done.1
  13.9 0.9 %fusion = f32[2,8,128,128]{3,1,2,0:T(8,128)S(1)} fusion(bf16[40,128,128]{2,1,0:T(8,128)(2,1)S(1)} %copy-done.1, pred[40]{0:T(512)(128)(4,1)S(1)} %iota_compare_fusion.9, pred[40,8]{0,1:T(8,128)(4,1)S(1)} %iota_compare_fusion.5, pred[40,2]{0,1:T(4,128)(4,1)S(1)} %iota_compare_fusion.7), kind=kOutput, calls=%fused_computation | convolution fusion | flops 20972800 | bytes 2359736 | tf_op jit(solution)/shard_map/krs,kab->rasb/dot_general | solution.py:98
  14.8 0.2 fusion.5
  15.0 0.8 %copy-done.2 = bf16[12,128,128]{2,1,0:T(8,128)(2,1)S(1)} copy-done((bf16[12,128,128]{2,1,0:T(8,128)(2,1)S(1)}, bf16[12,128,128]{2,1,0:T(8,128)(2,1)}, u32[]{:S(2)}) %copy-start.2) | copy-done | bytes 393240
  15.8 0.4 convolution_convert_fusion.2
  16.2 0.2 copy.63
  16.4 11.3 %all-to-all-done = bf16[8,128,256]{2,1,0:T(8,128)(2,1)S(1)} async-done(((bf16[8,128,256]{2,1,0:T(8,128)(2,1)}), bf16[8,128,256]{2,1,0:T(8,128)(2,1)S(1)}, u32[]{:S(2)}, u32[]{:S(2)}) %all-to-all-start) | async-done | bytes 524320 | tf_op jit(solution)/shard_map/all_to_all | solution.py:88
  27.7 0.4 fusion.6
  28.1 0.0 copy-start.3
  28.1 0.0 copy-start.7
  28.1 0.0 collective-permute-done
  28.1 0.0 collective-permute-done.1
  28.1 0.3 convolution_add_fusion
  28.4 0.4 copy-done.3
  28.8 0.2 copy-done.7
  29.0 0.2 fusion.4
  29.3 1.3 %convolution_convert_fusion = bf16[1024,256]{1,0:T(8,128)(2,1)} fusion(bf16[256,1024]{1,0:T(8,128)(2,1)S(1)} %fusion.5, bf16[256,1024]{1,0:T(8,128)(2,1)S(1)} %bitcast.79, bf16[256,256]{1,0:T(8,128)(2,1)S(1)} %fusion.4), kind=kOutput, calls=%fused_computation.3 | convolution fusion | flops 271319040 | bytes 1703936 | tf_op jit(solution)/shard_map/dot_general | solution.py:126
  30.6 3.6 %all-to-all-start.1 = ((bf16[8,128,256]{2,1,0:T(8,128)(2,1)}), bf16[8,128,256]{2,1,0:T(8,128)(2,1)S(1)}, u32[]{:S(2)}, u32[]{:S(2)}) async-start(bf16[8,128,256]{2,1,0:T(8,128)(2,1)} %bitcast.19), calls=%async_computation.1 | async-start | bytes 1048576 | tf_op jit(solution)/shard_map/all_to_all | solution.py:133
  34.2 0.3 fusion.64
  34.5 0.1 collective-permute-start.2
  34.6 1.7 %collective-permute-start.3 = (bf16[256,256]{1,0:T(8,128)(2,1)S(1)}, bf16[256,256]{1,0:T(8,128)(2,1)S(1)}, u32[]{:S(2)}, u32[]{:S(2)}) collective-permute-start(bf16[256,256]{1,0:T(8,128)(2,1)S(1)} %get-tuple-element.44), channel_id=1, source_target_pairs={{8,0},{16,8},{24,16},{0,24},{9,1},{17,9},{25,17},{1,25},{10,2},{18... | collective-permute-start | bytes 393224 | tf_op jit(solution)/shard_map/ppermute | solution.py:18
  36.3 12.5 %all-to-all-done.1 = bf16[8,128,256]{2,1,0:T(8,128)(2,1)S(1)} async-done(((bf16[8,128,256]{2,1,0:T(8,128)(2,1)}), bf16[8,128,256]{2,1,0:T(8,128)(2,1)S(1)}, u32[]{:S(2)}, u32[]{:S(2)}) %all-to-all-start.1) | async-done | bytes 524320 | tf_op jit(solution)/shard_map/all_to_all | solution.py:133
  48.9 0.0 copy-done.4
  48.9 0.4 fusion.17
  49.3 0.0 collective-permute-done.2
  49.3 0.0 collective-permute-done.3
  49.3 0.1 fusion.32
  49.4 0.2 convolution_bitcast_fusion
  49.6 13.1 %all_to_all.20 = f32[32,8,256]{2,1,0:T(8,128)S(1)} all-to-all(f32[32,8,256]{2,1,0:T(8,128)S(1)} %convolution_bitcast_fusion), channel_id=1, replica_groups=mesh['row'=4,'col'=8] {'col','row'}, dimensions={0} | all-to-all | bytes 524288 | tf_op jit(solution)/shard_map/all_to_all | solution.py:31
  62.8 0.7 broadcast_in_dim.2
  63.5 2.6 %all-to-all-start.3 = ((bf16[32,8,256]{2,1,0:T(8,128)(2,1)}), bf16[32,8,256]{2,1,0:T(8,128)(2,1)S(1)}, u32[]{:S(2)}, u32[]{:S(2)}) async-start(bf16[32,8,256]{2,1,0:T(8,128)(2,1)} %broadcast_in_dim.2), calls=%async_computation.3 | async-start | bytes 262144 | tf_op jit(solution)/shard_map/all_to_all | solution.py:34
  66.0 1.0 %convolution_convert_fusion.5 = bf16[256,256]{1,0:T(8,128)(2,1)} fusion(s32[256]{0:T(256)S(1)} %bitcast.84, f32[256,256]{1,0:T(8,128)S(1)} %convolution_add_fusion), kind=kOutput, calls=%fused_computation.13 | convolution fusion | flops 34013184 | bytes 394240 | tf_op jit(solution)/shard_map/dot_general | solution.py:110
  67.0 1.1 %convolution_convert_fusion.3 = bf16[256,256]{1,0:T(8,128)(2,1)} fusion(bf16[256,256]{1,0:T(8,128)(2,1)S(1)} %fusion.32, bf16[256,256]{1,0:T(8,128)(2,1)S(1)} %copy-done, s32[256]{0:T(256)S(1)} %bitcast.85), kind=kOutput, calls=%fused_computation.11 | convolution fusion | flops 67305472 | bytes 394240 | tf_op jit(solution)/shard_map/dot_general | solution.py:148
  68.1 6.2 %all-to-all-done.3 = bf16[32,8,256]{2,1,0:T(8,128)(2,1)S(1)} async-done(((bf16[32,8,256]{2,1,0:T(8,128)(2,1)}), bf16[32,8,256]{2,1,0:T(8,128)(2,1)S(1)}, u32[]{:S(2)}, u32[]{:S(2)}) %all-to-all-start.3) | async-done | bytes 131104 | tf_op jit(solution)/shard_map/all_to_all | solution.py:34
  74.3 0.7 bitcast_convert_fusion.1
  (14 shorter events, 0.1 us)
Async XLA Ops:
  0.6 1.2 %copy-start = (bf16[256,256]{1,0:T(8,128)(2,1)S(1)}, bf16[256,256]{1,0:T(8,128)(2,1)}, u32[]{:S(2)}) copy-start(bf16[256,256]{1,0:T(8,128)(2,1)} %param.20) | copy-start | bytes 393220
  2.0 26.1 %collective-permute-start = (bf16[256,256]{1,0:T(8,128)(2,1)S(1)}, bf16[256,256]{1,0:T(8,128)(2,1)S(1)}, u32[]{:S(2)}, u32[]{:S(2)}) collective-permute-start(bf16[256,256]{1,0:T(8,128)(2,1)S(1)} %convolution_convert_fusion.6), channel_id=1, source_target_pairs={{0,8},{8,16},{16,24},{24,0},{1,9},{9,17},{17,25},{25,1},{2,10},{10... | collective-permute-start | bytes 393224 | tf_op jit(solution)/shard_map/ppermute | solution.py:16
  2.5 25.6 %collective-permute-start.1 = (bf16[256,256]{1,0:T(8,128)(2,1)S(1)}, bf16[256,256]{1,0:T(8,128)(2,1)S(1)}, u32[]{:S(2)}, u32[]{:S(2)}) collective-permute-start(bf16[256,256]{1,0:T(8,128)(2,1)S(1)} %convolution_convert_fusion.6), channel_id=1, source_target_pairs={{8,0},{16,8},{24,16},{0,24},{9,1},{17,9},{25,17},{1,25},{10,2},{18... | collective-permute-start | bytes 393224 | tf_op jit(solution)/shard_map/ppermute | solution.py:18
  4.6 8.6 %copy-start.5 = (s32[40,2]{0,1:T(2,128)S(1)}, s32[40,2]{0,1:T(2,128)}, u32[]{:S(2)}) copy-start(s32[40,2]{0,1:T(2,128)} %param.25) | copy-start | bytes 964
  4.6 8.6 %copy-start.6 = (s32[12,2]{0,1:T(2,128)S(1)}, s32[12,2]{0,1:T(2,128)}, u32[]{:S(2)}) copy-start(s32[12,2]{0,1:T(2,128)} %param.23) | copy-start | bytes 292
  4.6 9.3 %copy-start.1 = (bf16[40,128,128]{2,1,0:T(8,128)(2,1)S(1)}, bf16[40,128,128]{2,1,0:T(8,128)(2,1)}, u32[]{:S(2)}) copy-start(bf16[40,128,128]{2,1,0:T(8,128)(2,1)} %param.24) | copy-start | bytes 3932164
  6.6 21.1 %all-to-all-start = ((bf16[8,128,256]{2,1,0:T(8,128)(2,1)}), bf16[8,128,256]{2,1,0:T(8,128)(2,1)S(1)}, u32[]{:S(2)}, u32[]{:S(2)}) async-start(bf16[8,128,256]{2,1,0:T(8,128)(2,1)} %copy.29), calls=%async_computation | async-start | bytes 1048576 | tf_op jit(solution)/shard_map/all_to_all | solution.py:88
  14.8 1.0 %copy-start.2 = (bf16[12,128,128]{2,1,0:T(8,128)(2,1)S(1)}, bf16[12,128,128]{2,1,0:T(8,128)(2,1)}, u32[]{:S(2)}) copy-start(bf16[12,128,128]{2,1,0:T(8,128)(2,1)} %param.22) | copy-start | bytes 1179652
  28.1 0.7 copy-start.3
  28.1 0.9 %copy-start.7 = (bf16[256,256]{1,0:T(8,128)(2,1)S(1)}, bf16[256,256]{1,0:T(8,128)(2,1)}, u32[]{:S(2)}) copy-start(bf16[256,256]{1,0:T(8,128)(2,1)} %param.21) | copy-start | bytes 393220
  30.6 18.3 %all-to-all-start.1 = ((bf16[8,128,256]{2,1,0:T(8,128)(2,1)}), bf16[8,128,256]{2,1,0:T(8,128)(2,1)S(1)}, u32[]{:S(2)}, u32[]{:S(2)}) async-start(bf16[8,128,256]{2,1,0:T(8,128)(2,1)} %bitcast.19), calls=%async_computation.1 | async-start | bytes 1048576 | tf_op jit(solution)/shard_map/all_to_all | solution.py:133
  34.2 14.7 %copy-start.4 = (s32[1,8]{1,0:T(1,128)S(1)}, s32[1,8]{1,0:T(1,128)}, u32[]{:S(2)}) copy-start(s32[1,8]{1,0:T(1,128)} %param.27) | copy-start | bytes 100
  34.5 14.8 %collective-permute-start.2 = (bf16[256,256]{1,0:T(8,128)(2,1)S(1)}, bf16[256,256]{1,0:T(8,128)(2,1)S(1)}, u32[]{:S(2)}, u32[]{:S(2)}) collective-permute-start(bf16[256,256]{1,0:T(8,128)(2,1)S(1)} %get-tuple-element.43), channel_id=1, source_target_pairs={{0,8},{8,16},{16,24},{24,0},{1,9},{9,17},{17,25},{25,1},{2,10},{10... | collective-permute-start | bytes 393224 | tf_op jit(solution)/shard_map/ppermute | solution.py:16
  34.6 14.7 %collective-permute-start.3 = (bf16[256,256]{1,0:T(8,128)(2,1)S(1)}, bf16[256,256]{1,0:T(8,128)(2,1)S(1)}, u32[]{:S(2)}, u32[]{:S(2)}) collective-permute-start(bf16[256,256]{1,0:T(8,128)(2,1)S(1)} %get-tuple-element.44), channel_id=1, source_target_pairs={{8,0},{16,8},{24,16},{0,24},{9,1},{17,9},{25,17},{1,25},{10,2},{18... | collective-permute-start | bytes 393224 | tf_op jit(solution)/shard_map/ppermute | solution.py:18
  63.5 10.8 %all-to-all-start.3 = ((bf16[32,8,256]{2,1,0:T(8,128)(2,1)}), bf16[32,8,256]{2,1,0:T(8,128)(2,1)S(1)}, u32[]{:S(2)}, u32[]{:S(2)}) async-start(bf16[32,8,256]{2,1,0:T(8,128)(2,1)} %broadcast_in_dim.2), calls=%async_computation.3 | async-start | bytes 262144 | tf_op jit(solution)/shard_map/all_to_all | solution.py:34

commit v21 on v15

--- a/solution.py
+++ b/solution.py
@@ -28,8 +28,13 @@
         piece = (count, value.shape[0] // count, value.shape[1])
     else:
         piece = (count, value.size // count // 128, 128)
-    gathered = lax.all_to_all(value.reshape(piece), axes, 0, 0, tiled=True)
-    owned = (jnp.sum(gathered, axis=0, keepdims=True) * scale).astype(jnp.bfloat16)
+    high = value.astype(jnp.bfloat16)
+    low = (value - high.astype(jnp.float32)).astype(jnp.bfloat16)
+    split = jnp.concatenate([high.reshape(piece), low.reshape(piece)], axis=1)
+    gathered = lax.all_to_all(split, axes, 0, 0, tiled=True).astype(jnp.float32)
+    rows = piece[1]
+    owned = jnp.sum(gathered[:, :rows] + gathered[:, rows:], axis=0, keepdims=True) * scale
+    owned = owned.astype(jnp.bfloat16)
     copies = jnp.broadcast_to(owned, piece)
     spread = lax.all_to_all(copies, axes, 0, 0, tiled=True)
     return spread.astype(jnp.float32).reshape(value.shape)

time: 75 us -> 75.1 us (level)
  no operation moved by 1% of the time
where the time goes in v21:
time: 75.1 us; the launch traced here: 74.6 us
  waiting for transfers between devices  29.5 us (39%)
  starting transfers between devices  17.1 us (23%)
  blocking collectives  13.2 us (18%)
  matrix products  8.99 us (12%)
  local copies, waits for them, and re-layouts  3.29 us (4%)
  between operations  1.56 us (2%)
  other arithmetic  1.1 us (1%)
    all_to_all x1, blocking collectives, spread_sum(): gathered = lax.all_to_all(split, axes, 0, 0, tiled=True).astype(jnp.float32)  13.2 us
    all_to_all x1, waiting for transfers between devices, on_device(): lax.all_to_all(to_owner, 'col', split_axis=0, concat_axis=0, tiled=True)  12.5 us
    all_to_all x1, waiting for transfers between devices, on_device(): lax.all_to_all(outgoing, 'col', split_axis=0, concat_axis=0, tiled=True)  11.3 us
    all_to_all x1, starting transfers between devices, on_device(): lax.all_to_all(outgoing, 'col', split_axis=0, concat_axis=0, tiled=True)  6.53 us
    all_to_all x1, waiting for transfers between devices, spread_sum(): spread = lax.all_to_all(copies, axes, 0, 0, tiled=True)  5.66 us
    ppermute x2, starting transfers between devices, padded_2(): lax.ppermute(head, axis, [((i + 1) % count, i) for i in range(count)])  3.75 us
    all_to_all x1, starting transfers between devices, on_device(): lax.all_to_all(to_owner, 'col', split_axis=0, concat_axis=0, tiled=True)  3.64 us
    all_to_all x1, starting transfers between devices, spread_sum(): spread = lax.all_to_all(copies, axes, 0, 0, tiled=True)  2.58 us
  transfers between devices with their start and end apart: 7, of which 3 were waited for; matrix products, arithmetic and copies ran while one was open for 9% of the time, Pallas kernels for 0%

profile of v21, /device:TPU:0, one launch (start us, length us, event | category | flops | bytes accessed | tf_op | source)
XLA Modules:
  0.0 74.6 jit_solution(9642834415182097726)
XLA Ops:
  0.6 0.0 copy-start
  0.6 1.2 %convolution_convert_fusion.7 = bf16[256,256]{1,0:T(8,128)(2,1)S(1)} fusion(bf16[256,256]{1,0:T(8,128)(2,1)} %param.19, s32[256]{0:T(256)} %bitcast.84), kind=kOutput, calls=%fused_computation.14 | convolution fusion | flops 33685504 | bytes 263168 | tf_op jit(solution)/shard_map/dot_general | solution.py:69
  1.8 0.0 copy-done
  1.8 0.2 convolution_convert_fusion.6
  2.0 0.5 collective-permute-start
  2.5 2.0 %collective-permute-start.1 = (bf16[256,256]{1,0:T(8,128)(2,1)S(1)}, bf16[256,256]{1,0:T(8,128)(2,1)S(1)}, u32[]{:S(2)}, u32[]{:S(2)}) collective-permute-start(bf16[256,256]{1,0:T(8,128)(2,1)S(1)} %convolution_convert_fusion.6), channel_id=1, source_target_pairs={{8,0},{16,8},{24,16},{0,24},{9,1},{17,9},{25,17},{1,25},{10,2},{18... | collective-permute-start | bytes 393224 | tf_op jit(solution)/shard_map/ppermute | solution.py:18
  4.6 0.0 copy-start.5
  4.6 0.0 copy-start.6
  4.6 1.1 %convolution_convert_fusion.1 = bf16[8,128,256]{2,0,1:T(8,128)(2,1)S(1)} fusion(bf16[2,128,256]{2,1,0:T(8,128)(2,1)S(1)} %bitcast.83, s32[8]{0:T(128)} %bitcast.88), kind=kOutput, calls=%fused_computation.4 | convolution fusion | flops 1310736 | bytes 655392 | tf_op jit(solution)/shard_map/sb,baf->saf/dot_general | solution.py:90
  5.7 0.9 %copy.29 = bf16[8,128,256]{2,1,0:T(8,128)(2,1)} copy(bf16[8,128,256]{2,0,1:T(8,128)(2,1)S(1)} %convolution_convert_fusion.1) | data formatting | bytes 1048576 | tf_op jit(solution)/shard_map/convert_element_type | solution.py:92
  6.6 6.5 %all-to-all-start = ((bf16[8,128,256]{2,1,0:T(8,128)(2,1)}), bf16[8,128,256]{2,1,0:T(8,128)(2,1)S(1)}, u32[]{:S(2)}, u32[]{:S(2)}) async-start(bf16[8,128,256]{2,1,0:T(8,128)(2,1)} %copy.29), calls=%async_computation | async-start | bytes 1048576 | tf_op jit(solution)/shard_map/all_to_all | solution.py:93
  13.1 0.0 copy-done.5
  13.1 0.0 copy-done.6
  13.9 0.0 copy-done.1
  13.9 0.9 %fusion = f32[2,8,128,128]{3,1,2,0:T(8,128)S(1)} fusion(bf16[40,128,128]{2,1,0:T(8,128)(2,1)S(1)} %copy-done.1, pred[40]{0:T(512)(128)(4,1)S(1)} %iota_compare_fusion.9, pred[40,8]{0,1:T(8,128)(4,1)S(1)} %iota_compare_fusion.5, pred[40,2]{0,1:T(4,128)(4,1)S(1)} %iota_compare_fusion.7), kind=kOutput, calls=%fused_computation | convolution fusion | flops 20972800 | bytes 2359736 | tf_op jit(solution)/shard_map/krs,kab->rasb/dot_general | solution.py:103
  14.8 0.2 fusion.5
  15.0 0.8 %copy-done.2 = bf16[12,128,128]{2,1,0:T(8,128)(2,1)S(1)} copy-done((bf16[12,128,128]{2,1,0:T(8,128)(2,1)S(1)}, bf16[12,128,128]{2,1,0:T(8,128)(2,1)}, u32[]{:S(2)}) %copy-start.2) | copy-done | bytes 393240
  15.8 0.4 convolution_convert_fusion.2
  16.2 0.2 copy.63
  16.4 11.3 %all-to-all-done = bf16[8,128,256]{2,1,0:T(8,128)(2,1)S(1)} async-done(((bf16[8,128,256]{2,1,0:T(8,128)(2,1)}), bf16[8,128,256]{2,1,0:T(8,128)(2,1)S(1)}, u32[]{:S(2)}, u32[]{:S(2)}) %all-to-all-start) | async-done | bytes 524320 | tf_op jit(solution)/shard_map/all_to_all | solution.py:93
  27.7 0.4 fusion.6
  28.1 0.0 copy-start.3
  28.1 0.0 copy-start.7
  28.1 0.0 collective-permute-done
  28.1 0.0 collective-permute-done.1
  28.1 0.3 convolution_add_fusion
  28.4 0.4 copy-done.3
  28.8 0.2 copy-done.7
  29.0 0.2 fusion.4
  29.3 1.3 %convolution_convert_fusion = bf16[1024,256]{1,0:T(8,128)(2,1)} fusion(bf16[256,1024]{1,0:T(8,128)(2,1)S(1)} %fusion.5, bf16[256,1024]{1,0:T(8,128)(2,1)S(1)} %bitcast.81, bf16[256,256]{1,0:T(8,128)(2,1)S(1)} %fusion.4), kind=kOutput, calls=%fused_computation.3 | convolution fusion | flops 271319040 | bytes 1703936 | tf_op jit(solution)/shard_map/dot_general | solution.py:131
  30.5 3.6 %all-to-all-start.1 = ((bf16[8,128,256]{2,1,0:T(8,128)(2,1)}), bf16[8,128,256]{2,1,0:T(8,128)(2,1)S(1)}, u32[]{:S(2)}, u32[]{:S(2)}) async-start(bf16[8,128,256]{2,1,0:T(8,128)(2,1)} %bitcast.19), calls=%async_computation.1 | async-start | bytes 1048576 | tf_op jit(solution)/shard_map/all_to_all | solution.py:138
  34.2 0.3 fusion.66
  34.5 0.1 collective-permute-start.2
  34.6 1.7 %collective-permute-start.3 = (bf16[256,256]{1,0:T(8,128)(2,1)S(1)}, bf16[256,256]{1,0:T(8,128)(2,1)S(1)}, u32[]{:S(2)}, u32[]{:S(2)}) collective-permute-start(bf16[256,256]{1,0:T(8,128)(2,1)S(1)} %get-tuple-element.44), channel_id=1, source_target_pairs={{8,0},{16,8},{24,16},{0,24},{9,1},{17,9},{25,17},{1,25},{10,2},{18... | collective-permute-start | bytes 393224 | tf_op jit(solution)/shard_map/ppermute | solution.py:18
  36.3 12.5 %all-to-all-done.1 = bf16[8,128,256]{2,1,0:T(8,128)(2,1)S(1)} async-done(((bf16[8,128,256]{2,1,0:T(8,128)(2,1)}), bf16[8,128,256]{2,1,0:T(8,128)(2,1)S(1)}, u32[]{:S(2)}, u32[]{:S(2)}) %all-to-all-start.1) | async-done | bytes 524320 | tf_op jit(solution)/shard_map/all_to_all | solution.py:138
  48.8 0.0 copy-done.4
  48.9 0.4 fusion.17
  49.3 0.0 collective-permute-done.2
  49.3 0.0 collective-permute-done.3
  49.3 0.1 fusion.33
  49.4 0.2 convert_bitcast_fusion
  49.6 13.2 %all_to_all.20 = bf16[32,16,256]{2,1,0:T(8,128)(2,1)S(1)} all-to-all(bf16[32,16,256]{2,1,0:T(8,128)(2,1)S(1)} %pad_maximum_fusion), channel_id=1, replica_groups=mesh['row'=4,'col'=8] {'row','col'}, dimensions={0} | all-to-all | bytes 524288 | tf_op jit(solution)/shard_map/all_to_all | solution.py:34
  62.9 0.7 broadcast_in_dim.2
  63.6 2.6 %all-to-all-start.3 = ((bf16[32,8,256]{2,1,0:T(8,128)(2,1)}), bf16[32,8,256]{2,1,0:T(8,128)(2,1)S(1)}, u32[]{:S(2)}, u32[]{:S(2)}) async-start(bf16[32,8,256]{2,1,0:T(8,128)(2,1)} %broadcast_in_dim.2), calls=%async_computation.3 | async-start | bytes 262144 | tf_op jit(solution)/shard_map/all_to_all | solution.py:39
  66.2 1.0 %convolution_convert_fusion.5 = bf16[256,256]{1,0:T(8,128)(2,1)} fusion(s32[256]{0:T(256)S(1)} %bitcast.86, f32[256,256]{1,0:T(8,128)S(1)} %convolution_add_fusion), kind=kOutput, calls=%fused_computation.12 | convolution fusion | flops 34013184 | bytes 394240 | tf_op jit(solution)/shard_map/dot_general | solution.py:115
  67.1 1.1 %convolution_convert_fusion.3 = bf16[256,256]{1,0:T(8,128)(2,1)} fusion(bf16[256,256]{1,0:T(8,128)(2,1)S(1)} %fusion.33, bf16[256,256]{1,0:T(8,128)(2,1)S(1)} %copy-done, s32[256]{0:T(256)S(1)} %bitcast.87), kind=kOutput, calls=%fused_computation.10 | convolution fusion | flops 67305472 | bytes 394240 | tf_op jit(solution)/shard_map/dot_general | solution.py:153
  68.2 5.7 %all-to-all-done.3 = bf16[32,8,256]{2,1,0:T(8,128)(2,1)S(1)} async-done(((bf16[32,8,256]{2,1,0:T(8,128)(2,1)}), bf16[32,8,256]{2,1,0:T(8,128)(2,1)S(1)}, u32[]{:S(2)}, u32[]{:S(2)}) %all-to-all-start.3) | async-done | bytes 131104 | tf_op jit(solution)/shard_map/all_to_all | solution.py:39
  73.9 0.7 bitcast_convert_fusion.1
  (16 shorter events, 0.2 us)
Async XLA Ops:
  0.6 1.2 %copy-start = (bf16[256,256]{1,0:T(8,128)(2,1)S(1)}, bf16[256,256]{1,0:T(8,128)(2,1)}, u32[]{:S(2)}) copy-start(bf16[256,256]{1,0:T(8,128)(2,1)} %param.20) | copy-start | bytes 393220
  2.0 26.1 %collective-permute-start = (bf16[256,256]{1,0:T(8,128)(2,1)S(1)}, bf16[256,256]{1,0:T(8,128)(2,1)S(1)}, u32[]{:S(2)}, u32[]{:S(2)}) collective-permute-start(bf16[256,256]{1,0:T(8,128)(2,1)S(1)} %convolution_convert_fusion.6), channel_id=1, source_target_pairs={{0,8},{8,16},{16,24},{24,0},{1,9},{9,17},{17,25},{25,1},{2,10},{10... | collective-permute-start | bytes 393224 | tf_op jit(solution)/shard_map/ppermute | solution.py:16
  2.5 25.6 %collective-permute-start.1 = (bf16[256,256]{1,0:T(8,128)(2,1)S(1)}, bf16[256,256]{1,0:T(8,128)(2,1)S(1)}, u32[]{:S(2)}, u32[]{:S(2)}) collective-permute-start(bf16[256,256]{1,0:T(8,128)(2,1)S(1)} %convolution_convert_fusion.6), channel_id=1, source_target_pairs={{8,0},{16,8},{24,16},{0,24},{9,1},{17,9},{25,17},{1,25},{10,2},{18... | collective-permute-start | bytes 393224 | tf_op jit(solution)/shard_map/ppermute | solution.py:18
  4.6 8.5 %copy-start.5 = (s32[40,2]{0,1:T(2,128)S(1)}, s32[40,2]{0,1:T(2,128)}, u32[]{:S(2)}) copy-start(s32[40,2]{0,1:T(2,128)} %param.25) | copy-start | bytes 964
  4.6 8.6 %copy-start.6 = (s32[12,2]{0,1:T(2,128)S(1)}, s32[12,2]{0,1:T(2,128)}, u32[]{:S(2)}) copy-start(s32[12,2]{0,1:T(2,128)} %param.23) | copy-start | bytes 292
  4.6 9.3 %copy-start.1 = (bf16[40,128,128]{2,1,0:T(8,128)(2,1)S(1)}, bf16[40,128,128]{2,1,0:T(8,128)(2,1)}, u32[]{:S(2)}) copy-start(bf16[40,128,128]{2,1,0:T(8,128)(2,1)} %param.24) | copy-start | bytes 3932164
  6.6 21.1 %all-to-all-start = ((bf16[8,128,256]{2,1,0:T(8,128)(2,1)}), bf16[8,128,256]{2,1,0:T(8,128)(2,1)S(1)}, u32[]{:S(2)}, u32[]{:S(2)}) async-start(bf16[8,128,256]{2,1,0:T(8,128)(2,1)} %copy.29), calls=%async_computation | async-start | bytes 1048576 | tf_op jit(solution)/shard_map/all_to_all | solution.py:93
  14.8 1.0 %copy-start.2 = (bf16[12,128,128]{2,1,0:T(8,128)(2,1)S(1)}, bf16[12,128,128]{2,1,0:T(8,128)(2,1)}, u32[]{:S(2)}) copy-start(bf16[12,128,128]{2,1,0:T(8,128)(2,1)} %param.22) | copy-start | bytes 1179652
  28.1 0.7 copy-start.3
  28.1 0.9 %copy-start.7 = (bf16[256,256]{1,0:T(8,128)(2,1)S(1)}, bf16[256,256]{1,0:T(8,128)(2,1)}, u32[]{:S(2)}) copy-start(bf16[256,256]{1,0:T(8,128)(2,1)} %param.21) | copy-start | bytes 393220
  30.5 18.3 %all-to-all-start.1 = ((bf16[8,128,256]{2,1,0:T(8,128)(2,1)}), bf16[8,128,256]{2,1,0:T(8,128)(2,1)S(1)}, u32[]{:S(2)}, u32[]{:S(2)}) async-start(bf16[8,128,256]{2,1,0:T(8,128)(2,1)} %bitcast.19), calls=%async_computation.1 | async-start | bytes 1048576 | tf_op jit(solution)/shard_map/all_to_all | solution.py:138
  34.2 14.7 %copy-start.4 = (s32[1,8]{1,0:T(1,128)S(1)}, s32[1,8]{1,0:T(1,128)}, u32[]{:S(2)}) copy-start(s32[1,8]{1,0:T(1,128)} %param.27) | copy-start | bytes 100
  34.5 14.8 %collective-permute-start.2 = (bf16[256,256]{1,0:T(8,128)(2,1)S(1)}, bf16[256,256]{1,0:T(8,128)(2,1)S(1)}, u32[]{:S(2)}, u32[]{:S(2)}) collective-permute-start(bf16[256,256]{1,0:T(8,128)(2,1)S(1)} %get-tuple-element.43), channel_id=1, source_target_pairs={{0,8},{8,16},{16,24},{24,0},{1,9},{9,17},{17,25},{25,1},{2,10},{10... | collective-permute-start | bytes 393224 | tf_op jit(solution)/shard_map/ppermute | solution.py:16
  34.6 14.7 %collective-permute-start.3 = (bf16[256,256]{1,0:T(8,128)(2,1)S(1)}, bf16[256,256]{1,0:T(8,128)(2,1)S(1)}, u32[]{:S(2)}, u32[]{:S(2)}) collective-permute-start(bf16[256,256]{1,0:T(8,128)(2,1)S(1)} %get-tuple-element.44), channel_id=1, source_target_pairs={{8,0},{16,8},{24,16},{0,24},{9,1},{17,9},{25,17},{1,25},{10,2},{18... | collective-permute-start | bytes 393224 | tf_op jit(solution)/shard_map/ppermute | solution.py:18
  63.6 10.3 %all-to-all-start.3 = ((bf16[32,8,256]{2,1,0:T(8,128)(2,1)}), bf16[32,8,256]{2,1,0:T(8,128)(2,1)S(1)}, u32[]{:S(2)}, u32[]{:S(2)}) async-start(bf16[32,8,256]{2,1,0:T(8,128)(2,1)} %broadcast_in_dim.2), calls=%async_computation.3 | async-start | bytes 262144 | tf_op jit(solution)/shard_map/all_to_all | solution.py:39

commit v22 on v19

--- a/solution.py
+++ b/solution.py
@@ -28,8 +28,13 @@
         piece = (count, value.shape[0] // count, value.shape[1])
     else:
         piece = (count, value.size // count // 128, 128)
-    gathered = lax.all_to_all(value.reshape(piece), axes, 0, 0, tiled=True)
-    owned = (jnp.sum(gathered, axis=0, keepdims=True) * scale).astype(jnp.bfloat16)
+    high = value.astype(jnp.bfloat16)
+    low = (value - high.astype(jnp.float32)).astype(jnp.bfloat16)
+    split = jnp.concatenate([high.reshape(piece), low.reshape(piece)], axis=1)
+    gathered = lax.all_to_all(split, axes, 0, 0, tiled=True).astype(jnp.float32)
+    rows = piece[1]
+    owned = jnp.sum(gathered[:, :rows] + gathered[:, rows:], axis=0, keepdims=True) * scale
+    owned = owned.astype(jnp.bfloat16)
     copies = jnp.broadcast_to(owned, piece)
     spread = lax.all_to_all(copies, axes, 0, 0, tiled=True)
     return spread.astype(jnp.float32).reshape(value.shape)

time: 75 us -> 75.1 us (level)
  no operation moved by 1% of the time
where the time goes in v22:
time: 75.1 us; the launch traced here: 74.6 us
  waiting for transfers between devices  29.5 us (39%)
  starting transfers between devices  17.1 us (23%)
  blocking collectives  13.2 us (18%)
  matrix products  8.99 us (12%)
  local copies, waits for them, and re-layouts  3.1 us (4%)
  between operations  1.57 us (2%)
  other arithmetic  1.27 us (2%)
    all_to_all x1, blocking collectives, spread_sum(): gathered = lax.all_to_all(split, axes, 0, 0, tiled=True).astype(jnp.float32)  13.2 us
    all_to_all x1, waiting for transfers between devices, on_device(): lax.all_to_all(to_owner, 'col', split_axis=0, concat_axis=0, tiled=True)  12.5 us
    all_to_all x1, waiting for transfers between devices, on_device(): lax.all_to_all(outgoing, 'col', split_axis=0, concat_axis=0, tiled=True)  11.3 us
    all_to_all x1, starting transfers between devices, on_device(): lax.all_to_all(outgoing, 'col', split_axis=0, concat_axis=0, tiled=True)  6.53 us
    all_to_all x1, waiting for transfers between devices, spread_sum(): spread = lax.all_to_all(copies, axes, 0, 0, tiled=True)  5.66 us
    ppermute x2, starting transfers between devices, padded_2(): lax.ppermute(head, axis, [((i + 1) % count, i) for i in range(count)])  3.75 us
    all_to_all x1, starting transfers between devices, on_device(): lax.all_to_all(to_owner, 'col', split_axis=0, concat_axis=0, tiled=True)  3.64 us
    all_to_all x1, starting transfers between devices, spread_sum(): spread = lax.all_to_all(copies, axes, 0, 0, tiled=True)  2.58 us
  transfers between devices with their start and end apart: 7, of which 3 were waited for; matrix products, arithmetic and copies ran while one was open for 10% of the time, Pallas kernels for 0%

profile of v22, /device:TPU:0, one launch (start us, length us, event | category | flops | bytes accessed | tf_op | source)
XLA Modules:
  0.0 74.6 jit_solution(17266522183552336389)
XLA Ops:
  0.6 0.0 copy-start
  0.6 1.2 %convolution_convert_fusion.7 = bf16[256,256]{1,0:T(8,128)(2,1)S(1)} fusion(bf16[256,256]{1,0:T(8,128)(2,1)} %param.19, s32[256]{0:T(256)} %bitcast.97), kind=kOutput, calls=%fused_computation.14 | convolution fusion | flops 33685504 | bytes 263168 | tf_op jit(solution)/shard_map/dot_general | solution.py:69
  1.8 0.0 copy-done
  1.8 0.2 convolution_convert_fusion.6
  2.0 0.5 collective-permute-start
  2.5 2.0 %collective-permute-start.1 = (bf16[256,256]{1,0:T(8,128)(2,1)S(1)}, bf16[256,256]{1,0:T(8,128)(2,1)S(1)}, u32[]{:S(2)}, u32[]{:S(2)}) collective-permute-start(bf16[256,256]{1,0:T(8,128)(2,1)S(1)} %convolution_convert_fusion.6), channel_id=1, source_target_pairs={{8,0},{16,8},{24,16},{0,24},{9,1},{17,9},{25,17},{1,25},{10,2},{18... | collective-permute-start | bytes 393224 | tf_op jit(solution)/shard_map/ppermute | solution.py:18
  4.6 1.1 %convolution_convert_fusion.1 = bf16[8,128,256]{2,0,1:T(8,128)(2,1)S(1)} fusion(bf16[2,128,256]{2,1,0:T(8,128)(2,1)S(1)} %bitcast.96, s32[8]{0:T(128)} %bitcast.101), kind=kOutput, calls=%fused_computation.4 | convolution fusion | flops 1310736 | bytes 655392 | tf_op jit(solution)/shard_map/sb,baf->saf/dot_general | solution.py:90
  5.7 0.9 %copy.29 = bf16[8,128,256]{2,1,0:T(8,128)(2,1)} copy(bf16[8,128,256]{2,0,1:T(8,128)(2,1)S(1)} %convolution_convert_fusion.1) | data formatting | bytes 1048576 | tf_op jit(solution)/shard_map/convert_element_type | solution.py:92
  6.6 6.5 %all-to-all-start = ((bf16[8,128,256]{2,1,0:T(8,128)(2,1)}), bf16[8,128,256]{2,1,0:T(8,128)(2,1)S(1)}, u32[]{:S(2)}, u32[]{:S(2)}) async-start(bf16[8,128,256]{2,1,0:T(8,128)(2,1)} %copy.29), calls=%async_computation | async-start | bytes 1048576 | tf_op jit(solution)/shard_map/all_to_all | solution.py:93
  13.1 0.0 copy-done.5
  13.8 0.0 copy-done.6
  13.8 0.0 copy-done.1
  13.8 0.9 %fusion = f32[2,8,128,128]{3,1,2,0:T(8,128)S(1)} fusion(bf16[40,128,128]{2,1,0:T(8,128)(2,1)S(1)} %copy-done.1, pred[40]{0:T(512)(128)(4,1)S(1)} %iota_compare_fusion.9, pred[40,8]{0,1:T(8,128)(4,1)S(1)} %iota_compare_fusion.5, pred[40,2]{0,1:T(4,128)(4,1)S(1)} %iota_compare_fusion.7), kind=kOutput, calls=%fused_computation | convolution fusion | flops 20972800 | bytes 2359736 | tf_op jit(solution)/shard_map/krs,kab->rasb/dot_general | solution.py:103
  14.8 0.0 copy-start.2
  14.8 0.2 fusion.6
  15.0 0.2 fusion.5
  15.2 0.6 copy-done.2
  15.8 0.4 convolution_convert_fusion.2
  16.2 0.2 copy.68
  16.4 11.3 %all-to-all-done = bf16[8,128,256]{2,1,0:T(8,128)(2,1)S(1)} async-done(((bf16[8,128,256]{2,1,0:T(8,128)(2,1)}), bf16[8,128,256]{2,1,0:T(8,128)(2,1)S(1)}, u32[]{:S(2)}, u32[]{:S(2)}) %all-to-all-start) | async-done | bytes 524320 | tf_op jit(solution)/shard_map/all_to_all | solution.py:93
  27.7 0.4 fusion.7
  28.1 0.0 copy-start.3
  28.1 0.0 copy-start.7
  28.1 0.0 collective-permute-done
  28.1 0.0 collective-permute-done.1
  28.1 0.3 convolution_add_fusion
  28.4 0.4 copy-done.3
  28.8 0.2 copy-done.7
  29.0 0.2 fusion.4
  29.3 1.3 %convolution_convert_fusion = bf16[1024,256]{1,0:T(8,128)(2,1)} fusion(bf16[1024,256]{0,1:T(8,128)(2,1)S(1)} %fusion.5, bf16[1024,256]{0,1:T(8,128)(2,1)S(1)} %bitcast.94, bf16[256,256]{1,0:T(8,128)(2,1)S(1)} %fusion.4), kind=kOutput, calls=%fused_computation.3 | convolution fusion | flops 271319040 | bytes 1703936 | tf_op jit(solution)/shard_map/dot_general | solution.py:136
  30.5 3.6 %all-to-all-start.1 = ((bf16[8,128,256]{2,1,0:T(8,128)(2,1)}), bf16[8,128,256]{2,1,0:T(8,128)(2,1)S(1)}, u32[]{:S(2)}, u32[]{:S(2)}) async-start(bf16[8,128,256]{2,1,0:T(8,128)(2,1)} %bitcast.20), calls=%async_computation.1 | async-start | bytes 1048576 | tf_op jit(solution)/shard_map/all_to_all | solution.py:142
  34.2 0.3 fusion.67
  34.5 0.1 collective-permute-start.2
  34.6 1.7 %collective-permute-start.3 = (bf16[256,256]{1,0:T(8,128)(2,1)S(1)}, bf16[256,256]{1,0:T(8,128)(2,1)S(1)}, u32[]{:S(2)}, u32[]{:S(2)}) collective-permute-start(bf16[256,256]{1,0:T(8,128)(2,1)S(1)} %get-tuple-element.46), channel_id=1, source_target_pairs={{8,0},{16,8},{24,16},{0,24},{9,1},{17,9},{25,17},{1,25},{10,2},{18... | collective-permute-start | bytes 393224 | tf_op jit(solution)/shard_map/ppermute | solution.py:18
  36.3 12.5 %all-to-all-done.1 = bf16[8,128,256]{2,1,0:T(8,128)(2,1)S(1)} async-done(((bf16[8,128,256]{2,1,0:T(8,128)(2,1)}), bf16[8,128,256]{2,1,0:T(8,128)(2,1)S(1)}, u32[]{:S(2)}, u32[]{:S(2)}) %all-to-all-start.1) | async-done | bytes 524320 | tf_op jit(solution)/shard_map/all_to_all | solution.py:142
  48.8 0.0 copy-done.4
  48.9 0.4 fusion.18
  49.3 0.0 collective-permute-done.2
  49.3 0.0 collective-permute-done.3
  49.3 0.1 fusion.34
  49.4 0.2 convert_bitcast_fusion
  49.6 13.2 %all_to_all.20 = bf16[32,16,256]{2,1,0:T(8,128)(2,1)S(1)} all-to-all(bf16[32,16,256]{2,1,0:T(8,128)(2,1)S(1)} %pad_maximum_fusion), channel_id=1, replica_groups=mesh['row'=4,'col'=8] {'row','col'}, dimensions={0} | all-to-all | bytes 524288 | tf_op jit(solution)/shard_map/all_to_all | solution.py:34
  62.9 0.7 broadcast_in_dim.2
  63.6 2.6 %all-to-all-start.3 = ((bf16[32,8,256]{2,1,0:T(8,128)(2,1)}), bf16[32,8,256]{2,1,0:T(8,128)(2,1)S(1)}, u32[]{:S(2)}, u32[]{:S(2)}) async-start(bf16[32,8,256]{2,1,0:T(8,128)(2,1)} %broadcast_in_dim.2), calls=%async_computation.3 | async-start | bytes 262144 | tf_op jit(solution)/shard_map/all_to_all | solution.py:39
  66.2 1.0 %convolution_convert_fusion.5 = bf16[256,256]{1,0:T(8,128)(2,1)} fusion(s32[256]{0:T(256)S(1)} %bitcast.99, f32[256,256]{1,0:T(8,128)S(1)} %convolution_add_fusion), kind=kOutput, calls=%fused_computation.12 | convolution fusion | flops 34013184 | bytes 394240 | tf_op jit(solution)/shard_map/dot_general | solution.py:120
  67.1 1.1 %convolution_convert_fusion.3 = bf16[256,256]{1,0:T(8,128)(2,1)} fusion(bf16[256,256]{1,0:T(8,128)(2,1)S(1)} %fusion.34, bf16[256,256]{1,0:T(8,128)(2,1)S(1)} %copy-done, s32[256]{0:T(256)S(1)} %bitcast.100), kind=kOutput, calls=%fused_computation.10 | convolution fusion | flops 67305472 | bytes 394240 | tf_op jit(solution)/shard_map/dot_general | solution.py:157
  68.2 5.7 %all-to-all-done.3 = bf16[32,8,256]{2,1,0:T(8,128)(2,1)S(1)} async-done(((bf16[32,8,256]{2,1,0:T(8,128)(2,1)}), bf16[32,8,256]{2,1,0:T(8,128)(2,1)S(1)}, u32[]{:S(2)}, u32[]{:S(2)}) %all-to-all-start.3) | async-done | bytes 131104 | tf_op jit(solution)/shard_map/all_to_all | solution.py:39
  73.9 0.7 bitcast_convert_fusion.2
  (17 shorter events, 0.2 us)
Async XLA Ops:
  0.6 1.2 %copy-start = (bf16[256,256]{1,0:T(8,128)(2,1)S(1)}, bf16[256,256]{1,0:T(8,128)(2,1)}, u32[]{:S(2)}) copy-start(bf16[256,256]{1,0:T(8,128)(2,1)} %param.20) | copy-start | bytes 393220
  2.0 26.1 %collective-permute-start = (bf16[256,256]{1,0:T(8,128)(2,1)S(1)}, bf16[256,256]{1,0:T(8,128)(2,1)S(1)}, u32[]{:S(2)}, u32[]{:S(2)}) collective-permute-start(bf16[256,256]{1,0:T(8,128)(2,1)S(1)} %convolution_convert_fusion.6), channel_id=1, source_target_pairs={{0,8},{8,16},{16,24},{24,0},{1,9},{9,17},{17,25},{25,1},{2,10},{10... | collective-permute-start | bytes 393224 | tf_op jit(solution)/shard_map/ppermute | solution.py:16
  2.5 25.6 %collective-permute-start.1 = (bf16[256,256]{1,0:T(8,128)(2,1)S(1)}, bf16[256,256]{1,0:T(8,128)(2,1)S(1)}, u32[]{:S(2)}, u32[]{:S(2)}) collective-permute-start(bf16[256,256]{1,0:T(8,128)(2,1)S(1)} %convolution_convert_fusion.6), channel_id=1, source_target_pairs={{8,0},{16,8},{24,16},{0,24},{9,1},{17,9},{25,17},{1,25},{10,2},{18... | collective-permute-start | bytes 393224 | tf_op jit(solution)/shard_map/ppermute | solution.py:18
  4.6 8.5 %copy-start.5 = (s32[40,2]{0,1:T(2,128)S(1)}, s32[40,2]{0,1:T(2,128)}, u32[]{:S(2)}) copy-start(s32[40,2]{0,1:T(2,128)} %param.25) | copy-start | bytes 964
  4.6 9.2 %copy-start.6 = (s32[12,2]{0,1:T(2,128)S(1)}, s32[12,2]{0,1:T(2,128)}, u32[]{:S(2)}) copy-start(s32[12,2]{0,1:T(2,128)} %param.23) | copy-start | bytes 292
  4.6 9.3 %copy-start.1 = (bf16[40,128,128]{2,1,0:T(8,128)(2,1)S(1)}, bf16[40,128,128]{2,1,0:T(8,128)(2,1)}, u32[]{:S(2)}) copy-start(bf16[40,128,128]{2,1,0:T(8,128)(2,1)} %param.24) | copy-start | bytes 3932164
  6.6 21.1 %all-to-all-start = ((bf16[8,128,256]{2,1,0:T(8,128)(2,1)}), bf16[8,128,256]{2,1,0:T(8,128)(2,1)S(1)}, u32[]{:S(2)}, u32[]{:S(2)}) async-start(bf16[8,128,256]{2,1,0:T(8,128)(2,1)} %copy.29), calls=%async_computation | async-start | bytes 1048576 | tf_op jit(solution)/shard_map/all_to_all | solution.py:93
  14.8 1.0 %copy-start.2 = (bf16[12,128,128]{2,1,0:T(8,128)(2,1)S(1)}, bf16[12,128,128]{2,1,0:T(8,128)(2,1)}, u32[]{:S(2)}) copy-start(bf16[12,128,128]{2,1,0:T(8,128)(2,1)} %param.22) | copy-start | bytes 1179652
  28.1 0.7 copy-start.3
  28.1 0.9 %copy-start.7 = (bf16[256,256]{1,0:T(8,128)(2,1)S(1)}, bf16[256,256]{1,0:T(8,128)(2,1)}, u32[]{:S(2)}) copy-start(bf16[256,256]{1,0:T(8,128)(2,1)} %param.21) | copy-start | bytes 393220
  30.5 18.3 %all-to-all-start.1 = ((bf16[8,128,256]{2,1,0:T(8,128)(2,1)}), bf16[8,128,256]{2,1,0:T(8,128)(2,1)S(1)}, u32[]{:S(2)}, u32[]{:S(2)}) async-start(bf16[8,128,256]{2,1,0:T(8,128)(2,1)} %bitcast.20), calls=%async_computation.1 | async-start | bytes 1048576 | tf_op jit(solution)/shard_map/all_to_all | solution.py:142
  34.2 14.7 %copy-start.4 = (s32[1,8]{1,0:T(1,128)S(1)}, s32[1,8]{1,0:T(1,128)}, u32[]{:S(2)}) copy-start(s32[1,8]{1,0:T(1,128)} %param.27) | copy-start | bytes 100
  34.5 14.8 %collective-permute-start.2 = (bf16[256,256]{1,0:T(8,128)(2,1)S(1)}, bf16[256,256]{1,0:T(8,128)(2,1)S(1)}, u32[]{:S(2)}, u32[]{:S(2)}) collective-permute-start(bf16[256,256]{1,0:T(8,128)(2,1)S(1)} %get-tuple-element.45), channel_id=1, source_target_pairs={{0,8},{8,16},{16,24},{24,0},{1,9},{9,17},{17,25},{25,1},{2,10},{10... | collective-permute-start | bytes 393224 | tf_op jit(solution)/shard_map/ppermute | solution.py:16
  34.6 14.7 %collective-permute-start.3 = (bf16[256,256]{1,0:T(8,128)(2,1)S(1)}, bf16[256,256]{1,0:T(8,128)(2,1)S(1)}, u32[]{:S(2)}, u32[]{:S(2)}) collective-permute-start(bf16[256,256]{1,0:T(8,128)(2,1)S(1)} %get-tuple-element.46), channel_id=1, source_target_pairs={{8,0},{16,8},{24,16},{0,24},{9,1},{17,9},{25,17},{1,25},{10,2},{18... | collective-permute-start | bytes 393224 | tf_op jit(solution)/shard_map/ppermute | solution.py:18
  63.6 10.3 %all-to-all-start.3 = ((bf16[32,8,256]{2,1,0:T(8,128)(2,1)}), bf16[32,8,256]{2,1,0:T(8,128)(2,1)S(1)}, u32[]{:S(2)}, u32[]{:S(2)}) async-start(bf16[32,8,256]{2,1,0:T(8,128)(2,1)} %broadcast_in_dim.2), calls=%async_computation.3 | async-start | bytes 262144 | tf_op jit(solution)/shard_map/all_to_all | solution.py:39
